TPU v7x, 256 devices: a whole 4x4x8 slice. The times are simulated.
256 devices in a mesh: sec: 2 (over y_hi), gx: 32 (over z, y_lo, core), gy: 4 (over x).
Axes of the slice: x: 4, y: 4 (y_hi: 2, y_lo: 2; y = y_hi * 2 + y_lo), z: 8, core: 2. Of those that a mesh axis runs over, the one named last changes fastest.
Arguments:
- model_state: float32 [2, 3, 32, 512, 2048], P('sec', None, None, 'gx', 'gy'), may hold values from -6 to 6
- wave_speed: float32 [2, 512, 2048], P('sec', 'gx', 'gy'), may hold values from 0.05 to 0.45
- wet_mask: int32 [2, 512, 2048], P('sec', 'gx', 'gy'), may hold values 0 or 1
- vertical: float32 [2, 32, 32], P('sec'), may hold values from -1 to 1
- surface_temp: float32 [2, 512, 2048], P('sec', 'gx', 'gy'), may hold values from -6 to 6
- flux_coef: float32 [8, 4], replicated, may hold values from -3 to 3
- heat_gain: float32 [8], replicated, may hold values from -2.5 to 2.5
- pair_tile: int32 [32, 4, 64, 1], P('gx', 'gy'), may hold values from 0 to 31; in each aligned block of 64 rows (0 to 63, 64 to 127, ..., all dimensions but the last counted through in order) at most 4 rows name the same one
- pair_source: int32 [32, 4, 64], P('gx', 'gy'), may hold values from 0 to 31
- pair_target: int32 [32, 4, 64], P('gx', 'gy'), may hold values from 0 to 63
- intersection_weights: bfloat16 [32, 4, 64, 256, 128], P('gx', 'gy'), may hold values from -0.375 to 0.375
Outputs:
- final_state: float32 [2, 3, 32, 512, 2048], P('sec', None, None, 'gx', 'gy')
- surface_temps: float32 [2, 512, 2048], P('sec', 'gx', 'gy')
Inputs may be any that keep to these rules, and one draw needn't show every extreme that they name: `pair_tile`: the destination lies in the source tile's column along gy; at most 4 pairs of one atmosphere tile name one ocean tile, and in some tile exactly 4 do.
All inputs are finite; a program needn't handle non-finite values. No bound on the sum of `wet_mask` on one device may be relied on, other than what follows from the above.
Results may differ from a plain program's by a relative error of at most 0.0033.
Values may be sent and summed in bfloat16 or wider, within the bound.
No kernel may reach another device: no remote copies, remote signals or barrier semaphores. Data moves between devices by JAX's collectives and lax.ppermute only.
A program may use at most 64 MiB of HBM per device.

v0:
```python
import jax
import jax.numpy as jnp
from jax import lax
from jax.sharding import PartitionSpec as P

SUBSTEPS = 2


HIGHEST_PRECISION = lax.Precision.HIGHEST


def extended(cells, sides, width):
    for axis, dim in sides:
        count = lax.axis_size(axis)
        ends = count - 1
        head = lax.slice_in_dim(cells, 0, width, axis=dim)
        tail = lax.slice_in_dim(cells, cells.shape[dim] - width, cells.shape[dim], axis=dim)
        cells = jnp.concatenate(
            [
                lax.ppermute(tail, axis, [(i, (i + 1) % count) for i in range(ends)]),
                cells,
                lax.ppermute(head, axis, [((i + 1) % count, i) for i in range(ends)]),
            ],
            axis=dim,
        )
    return cells


def shifted_2(value, axis, by):
    size = lax.axis_size(axis)
    pairs = [(i, i + by) for i in range(size) if 0 <= i + by < size]
    return lax.ppermute(value, axis, pairs)


def vertical_mix(matrix, right_side):
    return right_side + jnp.einsum("lm,mxy->lxy", matrix, right_side, precision=HIGHEST_PRECISION)


def velocity_divergence(eastward, northward):
    padded_east = extended(eastward, (("gx", 1),), 1)
    padded_north = extended(northward, (("gy", 2),), 1)
    return (
        padded_east[:, 2:, :]
        - padded_east[:, :-2, :]
        + (padded_north[:, :, 2:] - padded_north[:, :, :-2])
    )


def substep_single(pressure, eastward, northward, sound_speed, wetness, matrix):
    divergence = velocity_divergence(eastward, northward)
    pressure = vertical_mix(matrix, pressure - sound_speed * divergence)
    padded = extended(pressure, (("gx", 1), ("gy", 2)), 1)
    eastward = wetness * (eastward - 0.5 * (padded[:, 2:, 1:-1] - padded[:, :-2, 1:-1]))
    northward = wetness * (northward - 0.5 * (padded[:, 1:-1, 2:] - padded[:, 1:-1, :-2]))
    return (pressure, eastward, northward)


def local(
    model_state,
    wave_speed,
    wet_mask,
    vertical,
    surface_temp,
    flux_coef,
    heat_gain,
    pair_tile,
    pair_source,
    pair_target,
    intersection_weights,
):
    pressure = model_state[0, 0]
    eastward = model_state[0, 1]
    northward = model_state[0, 2]
    sound_speed = wave_speed[0]
    wetness = wet_mask[0].astype(jnp.float32)
    matrix = vertical[0]
    for substep in range(SUBSTEPS):
        pressure, eastward, northward = substep_single(
            pressure, eastward, northward, sound_speed, wetness, matrix
        )
    final_state = jnp.stack([pressure, eastward, northward])[None]
    tile_count = lax.axis_size("gx")
    weights = intersection_weights[0, 0]
    pair_count = weights.shape[0]
    in_width = weights.shape[1]
    out_width = weights.shape[2]
    capacity = max(2, 2 * pair_count // tile_count)
    slot_count = tile_count * capacity
    grid_shape = surface_temp.shape[1:]
    cell_count = grid_shape[0] * grid_shape[1]
    in_blocks = cell_count // in_width
    out_blocks = cell_count // out_width
    sources = pair_source[0, 0]
    targets = pair_target[0, 0]
    target_tile = pair_tile[0, 0, :, 0]
    drivers = jnp.stack(
        [model_state[0, 0, 0], model_state[0, 1, 0], model_state[0, 2, 0], surface_temp[0]]
    ).reshape(4, cell_count)
    fluxes = jnp.tanh(jnp.dot(flux_coef, drivers, precision=HIGHEST_PRECISION)).astype(jnp.bfloat16)
    flux_count = fluxes.shape[0]
    blocks = fluxes.reshape(flux_count, in_blocks, in_width)
    picked = jnp.take(blocks, sources, axis=1)
    regridded = jnp.einsum(
        "fpi,pio->pfo", picked, weights, preferred_element_type=jnp.float32
    ).astype(jnp.bfloat16)
    positions = jnp.arange(pair_count)
    same_tile = target_tile[None, :] == target_tile[:, None]
    is_before = positions[None, :] < positions[:, None]
    earlier = jnp.sum(same_tile & is_before, axis=1)
    slot_of = target_tile * capacity + earlier
    placing = jnp.arange(slot_count)[:, None] == slot_of[None, :]
    outgoing = jnp.dot(
        placing.astype(jnp.bfloat16),
        regridded.reshape(pair_count, flux_count * out_width),
        preferred_element_type=jnp.float32,
    )
    outgoing = outgoing.astype(jnp.bfloat16).reshape(tile_count, capacity, flux_count, out_width)
    offsets = (jnp.sum(jnp.where(placing, targets[None, :] + 1, 0), axis=1) - 1).reshape(
        tile_count, capacity
    )
    shifted = shifted_2((outgoing, offsets), "sec", 1)
    arrived, arrived_at = (
        lax.all_to_all(shifted[0], "gx", split_axis=0, concat_axis=0, tiled=True),
        lax.all_to_all(shifted[1], "gx", split_axis=0, concat_axis=0, tiled=True),
    )
    landing = jnp.arange(out_blocks)[:, None] == arrived_at.reshape(slot_count)[None, :]
    gathered = jnp.dot(
        landing.astype(jnp.bfloat16),
        arrived.reshape(slot_count, flux_count * out_width),
        preferred_element_type=jnp.float32,
    )
    ocean_flux = (
        gathered.reshape(out_blocks, flux_count, out_width)
        .transpose(1, 0, 2)
        .reshape(flux_count, cell_count)
    )
    heating = jnp.dot(heat_gain, ocean_flux, precision=HIGHEST_PRECISION).reshape(grid_shape)
    ocean_temp = surface_temp[0] + wetness * heating
    returning = jnp.dot(
        landing.T.astype(jnp.bfloat16),
        ocean_temp.astype(jnp.bfloat16).reshape(out_blocks, out_width),
        preferred_element_type=jnp.float32,
    )
    returning = returning.astype(jnp.bfloat16).reshape(tile_count, capacity, out_width)
    exchanged_back = lax.all_to_all(returning, "gx", split_axis=0, concat_axis=0, tiled=True)
    delivered = shifted_2(exchanged_back, "sec", -1)
    per_pair = jnp.dot(
        placing.T.astype(jnp.bfloat16),
        delivered.reshape(slot_count, out_width),
        preferred_element_type=jnp.float32,
    ).astype(jnp.bfloat16)
    pieces = jnp.einsum("pio,po->pi", weights, per_pair, preferred_element_type=jnp.float32)
    owning = (jnp.arange(in_blocks)[:, None] == sources[None, :]).astype(jnp.float32)
    atmos_temp = jnp.dot(owning, pieces, precision=HIGHEST_PRECISION).reshape(grid_shape)
    section = lax.axis_index("sec")
    surface_temps = jnp.where(section == 0, atmos_temp, ocean_temp)[None]
    return (final_state, surface_temps)


def solution(mesh):
    return jax.shard_map(
        local,
        mesh=mesh,
        in_specs=(
            P("sec", None, None, "gx", "gy"),
            P("sec", "gx", "gy"),
            P("sec", "gx", "gy"),
            P("sec", None, None),
            P("sec", "gx", "gy"),
            P(),
            P(),
            P("gx", "gy", None, None),
            P("gx", "gy", None),
            P("gx", "gy", None),
            P("gx", "gy", None, None, None),
        ),
        out_specs=(P("sec", None, None, "gx", "gy"), P("sec", "gx", "gy")),
        check_vma=False,
    )
```

profile of v0, /device:TPU:1, one launch (start us, length us, event | category | flops | bytes accessed | tf_op | source)
XLA Modules:
  0.0 158.2 jit_solution(17208287649903211362)
XLA Ops:
  0.6 3.2 %fusion.90 = (f32[1,1,32,16,512]{4,3,2,1,0:T(8,128)}, f32[1,1,32,16,512]{4,3,2,1,0:T(8,128)S(1)}, f32[1,1,32,16,512]{4,3,2,1,0:T(8,128)S(1)}) fusion(f32[1,3,32,16,512]{4,3,2,1,0:T(8,128)} %param.11), kind=kLoop, calls=%fused_computation.145 | loop fusion | bytes 6291456 | tf_op jit(solution)/shard_map/slice | solution.py:71
  7.0 5.3 %collective-permute-start.3 = (f32[32,16,1]{2,0,1:T(8,128)S(1)}, f32[32,16,1]{2,0,1:T(8,128)}, u32[]{:S(2)}, u32[]{:S(2)}) collective-permute-start(f32[32,16,1]{2,0,1:T(8,128)S(1)} %get-tuple-element.35), channel_id=1, source_target_pairs={{0,1},{1,2},{2,3},{4,5},{5,6},{6,7},{8,9},{9,10},{10,11},{12,13},{... | collective-permute-start | bytes 6152 | tf_op jit(solution)/shard_map/ppermute | solution.py:20
  13.9 5.1 %collective-permute-start = (f32[32,1,512]{2,0,1:T(8,128)S(1)}, f32[32,1,512]{2,0,1:T(8,128)S(1)}, u32[]{:S(2)}, u32[]{:S(2)}) collective-permute-start(f32[32,1,512]{2,0,1:T(8,128)S(1)} %get-tuple-element.32), channel_id=1, source_target_pairs={{4,0},{8,4},{12,8},{16,12},{20,16},{24,20},{28,24},{32,28},{36,32}... | collective-permute-start | bytes 196616 | tf_op jit(solution)/shard_map/ppermute | solution.py:22
  19.0 1.9 %collective-permute-start.1 = (f32[32,1,512]{2,0,1:T(8,128)S(1)}, f32[32,1,512]{2,0,1:T(8,128)}, u32[]{:S(2)}, u32[]{:S(2)}) collective-permute-start(f32[32,1,512]{2,0,1:T(8,128)S(1)} %get-tuple-element.33), channel_id=1, source_target_pairs={{0,4},{4,8},{8,12},{12,16},{16,20},{20,24},{24,28},{28,32},{32,36}... | collective-permute-start | bytes 196616 | tf_op jit(solution)/shard_map/ppermute | solution.py:20
  23.3 2.9 %fusion.8 = bf16[64,8,128]{2,1,0:T(8,128)(2,1)S(1)} fusion(bf16[1,1,64,256,128]{4,3,2,1,0:T(8,128)(2,1)} %param.21, bf16[64,8,256]{2,1,0:T(8,128)(2,1)S(1)} %gather_fusion, pred[64]{0:T(512)(128)(4,1)S(1)} %compare_and_fusion), kind=kOutput, calls=%fused_computation.15 | convolution fusion | flops 33751040 | bytes 4587584 | tf_op jit(solution)/shard_map/fpi,pio->pfo/dot_general | solution.py:103
  27.3 4.7 %collective-permute-start.17 = (bf16[32,4,8,128]{3,2,1,0:T(8,128)(2,1)}, bf16[32,4,8,128]{3,2,1,0:T(8,128)(2,1)}, u32[]{:S(2)}, u32[]{:S(2)}) collective-permute-start(bf16[32,4,8,128]{3,2,1,0:T(8,128)(2,1)} %bitcast.54), channel_id=1, source_target_pairs={{0,128},{1,129},{2,130},{3,131},{4,132},{5,133},{6,134},{7,135},{8... | collective-permute-start | bytes 786440 | tf_op jit(solution)/shard_map/ppermute | solution.py:32
  32.8 7.7 %fusion.6 = f32[32,16,512]{2,0,1:T(8,128)S(1)} fusion(f32[32,16,512]{2,0,1:T(8,128)} %bitcast.125, f32[32,16,1]{2,0,1:T(8,128)} %collective-permute-done.3, f32[32,16,1]{2,0,1:T(8,128)} %copy-done.13, f32[32,16,512]{2,0,1:T(8,128)} %bitcast.127, f32[32,1,512]{2,0,1:T(8,128)} %collective-permute-done.1, f32[32,1,512]{2,0,1:T(8,128)S(1)} %collective-permute-done, ...), kind=kOutput, calls=%fused_computation.11 | convolution fusion | flops 105644032 | bytes 4366336 | tf_op jit(solution)/shard_map/lm,mxy->lxy/dot_general | solution.py:36
  40.5 2.4 %collective-permute-start.4 = (f32[32,1,512]{2,0,1:T(8,128)S(1)}, f32[32,1,512]{2,0,1:T(8,128)S(1)}, u32[]{:S(2)}, u32[]{:S(2)}) collective-permute-start(f32[32,1,512]{2,0,1:T(8,128)S(1)} %get-tuple-element.31), channel_id=1, source_target_pairs={{4,0},{8,4},{12,8},{16,12},{20,16},{24,20},{28,24},{32,28},{36,32}... | collective-permute-start | bytes 196616 | tf_op jit(solution)/shard_map/ppermute | solution.py:22
  42.9 3.2 %collective-permute-start.5 = (f32[32,1,512]{2,0,1:T(8,128)S(1)}, f32[32,1,512]{2,0,1:T(8,128)S(1)}, u32[]{:S(2)}, u32[]{:S(2)}) collective-permute-start(f32[32,1,512]{2,0,1:T(8,128)S(1)} %get-tuple-element.30), channel_id=1, source_target_pairs={{0,4},{4,8},{8,12},{12,16},{16,20},{20,24},{24,28},{28,32},{32,36}... | collective-permute-start | bytes 196616 | tf_op jit(solution)/shard_map/ppermute | solution.py:20
  49.0 4.0 %collective-permute-start.9 = (f32[32,18,1]{2,0,1:T(8,128)S(1)}, f32[32,18,1]{2,0,1:T(8,128)S(1)}, u32[]{:S(2)}, u32[]{:S(2)}) collective-permute-start(f32[32,18,1]{2,0,1:T(8,128)S(1)} %get-tuple-element.23), channel_id=1, source_target_pairs={{0,1},{1,2},{2,3},{4,5},{5,6},{6,7},{8,9},{9,10},{10,11},{12,13},{... | collective-permute-start | bytes 6920 | tf_op jit(solution)/shard_map/ppermute | solution.py:20
  53.6 4.4 %collective-permute-done.8 = f32[32,18,1]{2,0,1:T(8,128)S(1)} collective-permute-done((f32[32,18,1]{2,0,1:T(8,128)S(1)}, f32[32,18,1]{2,0,1:T(8,128)S(1)}, u32[]{:S(2)}, u32[]{:S(2)}) %collective-permute-start.8) | collective-permute-done | bytes 2336 | tf_op jit(solution)/shard_map/ppermute | solution.py:22
  58.1 1.7 %collective-permute-done.9 = f32[32,18,1]{2,0,1:T(8,128)S(1)} collective-permute-done((f32[32,18,1]{2,0,1:T(8,128)S(1)}, f32[32,18,1]{2,0,1:T(8,128)S(1)}, u32[]{:S(2)}, u32[]{:S(2)}) %collective-permute-start.9) | collective-permute-done | bytes 2336 | tf_op jit(solution)/shard_map/ppermute | solution.py:20
  59.8 4.3 %fusion.40 = (f32[32,16,512]{2,0,1:T(8,128)S(1)}, f32[32,16,512]{2,0,1:T(8,128)S(1)}) fusion(f32[32,16,512]{2,0,1:T(8,128)} %copy-done.1, f32[32,1,512]{2,0,1:T(8,128)S(1)} %collective-permute-done.5, f32[32,1,512]{2,0,1:T(8,128)S(1)} %collective-permute-done.4, f32[16,512]{1,0:T(8,128)S(1)} %get-tuple-element.37, ...), kind=kLoop, calls=%fused_computation.64 | loop fusion | flops 4194304 | bytes 5411328 | tf_op jit(solution)/shard_map/mul | solution.py:53
  65.1 2.3 %collective-permute-start.6 = (f32[32,1,512]{2,0,1:T(8,128)S(1)}, f32[32,1,512]{2,0,1:T(8,128)S(1)}, u32[]{:S(2)}, u32[]{:S(2)}) collective-permute-start(f32[32,1,512]{2,0,1:T(8,128)S(1)} %get-tuple-element.26), channel_id=1, source_target_pairs={{4,0},{8,4},{12,8},{16,12},{20,16},{24,20},{28,24},{32,28},{36,32}... | collective-permute-start | bytes 196616 | tf_op jit(solution)/shard_map/ppermute | solution.py:22
  67.4 3.9 %collective-permute-start.7 = (f32[32,1,512]{2,0,1:T(8,128)S(1)}, f32[32,1,512]{2,0,1:T(8,128)S(1)}, u32[]{:S(2)}, u32[]{:S(2)}) collective-permute-start(f32[32,1,512]{2,0,1:T(8,128)S(1)} %get-tuple-element.27), channel_id=1, source_target_pairs={{0,4},{4,8},{8,12},{12,16},{16,20},{20,24},{24,28},{28,32},{32,36}... | collective-permute-start | bytes 196616 | tf_op jit(solution)/shard_map/ppermute | solution.py:20
  72.8 4.8 %collective-permute-start.11 = (f32[32,16,1]{2,0,1:T(8,128)S(1)}, f32[32,16,1]{2,0,1:T(8,128)S(1)}, u32[]{:S(2)}, u32[]{:S(2)}) collective-permute-start(f32[32,16,1]{2,0,1:T(8,128)S(1)} %get-tuple-element.29), channel_id=1, source_target_pairs={{0,1},{1,2},{2,3},{4,5},{5,6},{6,7},{8,9},{9,10},{10,11},{12,13},{... | collective-permute-start | bytes 6152 | tf_op jit(solution)/shard_map/ppermute | solution.py:20
  77.6 18.0 %all_to_all.19 = s32[32,1,4]{2,1,0:T(1,128)} all-to-all(s32[32,1,4]{2,1,0:T(1,128)S(1)} %bitcast.140), channel_id=1, replica_groups=mesh['sec'=2,'gx'=32,'gy'=4] {'gx'}, dimensions={0} | all-to-all | bytes 1024 | tf_op jit(solution)/shard_map/all_to_all | solution.py:124
  95.5 4.3 %all-to-all-start.1 = ((bf16[32,4,8,128]{3,2,1,0:T(8,128)(2,1)}), bf16[32,4,8,128]{3,2,1,0:T(8,128)(2,1)S(1)}, u32[]{:S(2)}, u32[]{:S(2)}) async-start(bf16[32,4,8,128]{3,2,1,0:T(8,128)(2,1)} %collective-permute-done.17), calls=%async_computation.1 | async-start | bytes 524288 | tf_op jit(solution)/shard_map/all_to_all | solution.py:123
  99.9 5.0 %fusion.5 = f32[32,16,512]{2,0,1:T(8,128)S(1)} fusion(f32[32,16,512]{2,0,1:T(8,128)} %copy-done.1, f32[32,16,512]{2,0,1:T(8,128)S(1)} %get-tuple-element.19, f32[32,16,1]{2,0,1:T(8,128)S(1)} %collective-permute-done.11, f32[32,16,1]{2,0,1:T(8,128)S(1)} %collective-permute-done.10, f32[32,16,512]{2,0,1:T(8,128)} %copy-done.2, ...), kind=kOutput, calls=%fused_computation.9 | convolution fusion | flops 105644032 | bytes 4366336 | tf_op jit(solution)/shard_map/lm,mxy->lxy/dot_general | solution.py:36
  105.5 2.4 %collective-permute-start.12 = (f32[32,1,512]{2,0,1:T(8,128)}, f32[32,1,512]{2,0,1:T(8,128)S(1)}, u32[]{:S(2)}, u32[]{:S(2)}) collective-permute-start(f32[32,1,512]{2,0,1:T(8,128)} %get-tuple-element.25), channel_id=1, source_target_pairs={{4,0},{8,4},{12,8},{16,12},{20,16},{24,20},{28,24},{32,28},{36,32}... | collective-permute-start | bytes 196616 | tf_op jit(solution)/shard_map/ppermute | solution.py:22
  108.0 3.1 %collective-permute-start.13 = (f32[32,1,512]{2,0,1:T(8,128)}, f32[32,1,512]{2,0,1:T(8,128)}, u32[]{:S(2)}, u32[]{:S(2)}) collective-permute-start(f32[32,1,512]{2,0,1:T(8,128)} %get-tuple-element.24), channel_id=1, source_target_pairs={{0,4},{4,8},{8,12},{12,16},{16,20},{20,24},{24,28},{28,32},{32,36}... | collective-permute-start | bytes 196616 | tf_op jit(solution)/shard_map/ppermute | solution.py:20
  111.7 1.4 convert_element_type.41
  113.6 1.9 %reduce.3 = s32[32,4]{1,0:T(8,128)} reduce(s32[32,1,4]{2,1,0:T(1,128)} %all_to_all.19, s32[]{:T(128)} %broadcast.70), dimensions={1}, to_apply=%all_to_all.13.reduce_sub_computation.3 | reduce | bytes 1028 | tf_op jit(solution)/shard_map/all_to_all | solution.py:124
  116.9 1.6 %pad_maximum_fusion.30 = (f32[32,18,1]{2,0,1:T(8,128)}, f32[32,18,1]{2,0,1:T(8,128)}) fusion(f32[32,1,512]{2,0,1:T(8,128)S(1)} %collective-permute-done.12, f32[32,16,512]{2,0,1:T(8,128)S(1)} %fusion.5, f32[32,1,512]{2,0,1:T(8,128)} %collective-permute-done.13), kind=kLoop, calls=%fused_computation.86 | loop fusion | flops 2304 | bytes 1184256 | tf_op jit(solution)/shard_map/slice | solution.py:16
  119.8 4.7 %collective-permute-start.15 = (f32[32,18,1]{2,0,1:T(8,128)}, f32[32,18,1]{2,0,1:T(8,128)}, u32[]{:S(2)}, u32[]{:S(2)}) collective-permute-start(f32[32,18,1]{2,0,1:T(8,128)} %get-tuple-element.21), channel_id=1, source_target_pairs={{0,1},{1,2},{2,3},{4,5},{5,6},{6,7},{8,9},{9,10},{10,11},{12,13},{... | collective-permute-start | bytes 6920 | tf_op jit(solution)/shard_map/ppermute | solution.py:20
  128.3 1.6 %convolution_convert_fusion.1 = bf16[128,128]{1,0:T(8,128)(2,1)} fusion(f32[64,128]{1,0:T(8,128)} %squeeze.30, f32[64,128]{1,0:T(8,128)} %convert_element_type.41, f32[64,128]{1,0:T(8,128)S(1)} %bitcast.134, s32[128]{0:T(128)} %eq.71), kind=kOutput, calls=%fused_computation.16 | convolution fusion | flops 2146304 | bytes 131584 | tf_op jit(solution)/shard_map/dot_general | solution.py:139
  130.0 9.0 %all-to-all-start.2 = ((bf16[32,4,128]{2,1,0:T(4,128)(2,1)}), bf16[32,4,128]{2,1,0:T(4,128)(2,1)S(1)}, u32[]{:S(2)}, u32[]{:S(2)}) async-start(bf16[32,4,128]{2,1,0:T(4,128)(2,1)} %bitcast.30), calls=%async_computation.2 | async-start | bytes 65536 | tf_op jit(solution)/shard_map/all_to_all | solution.py:145
  139.0 3.2 %fusion.21 = (f32[1,32,16,512]{3,1,2,0:T(8,128)}, f32[1,32,16,512]{3,1,2,0:T(8,128)}) fusion(f32[32,16,512]{2,0,1:T(8,128)S(1)} %copy-done.3, f32[32,16,512]{2,0,1:T(8,128)S(1)} %fusion.5, f32[32,1,512]{2,0,1:T(8,128)} %collective-permute-done.13, f32[32,1,512]{2,0,1:T(8,128)S(1)} %collective-permute-done.12, f32[16,512]{1,0:T(8,128)S(1)} %get-tuple-element.37, ...), kind=kLoop, calls=%fused_computation.35 | loop fusion | flops 4194304 | bytes 5411328 | tf_op jit(solution)/shard_map/stack | solution.py:81
  142.2 4.9 %all-to-all-done.2 = bf16[32,4,128]{2,1,0:T(4,128)(2,1)S(1)} async-done(((bf16[32,4,128]{2,1,0:T(4,128)(2,1)}), bf16[32,4,128]{2,1,0:T(4,128)(2,1)S(1)}, u32[]{:S(2)}, u32[]{:S(2)}) %all-to-all-start.2) | async-done | bytes 32800 | tf_op jit(solution)/shard_map/all_to_all | solution.py:145
  148.4 1.8 %maximum_bitcast_fusion = f32[1,3,32,16,512]{4,2,3,1,0:T(8,128)S(1)} fusion(f32[1,32,16,512]{3,1,2,0:T(8,128)} %get-tuple-element.17, f32[1,32,16,512]{3,1,2,0:T(8,128)} %get-tuple-element.16, f32[1,32,16,512]{3,1,2,0:T(8,128)S(1)} %bitcast.123), kind=kLoop, calls=%fused_computation.7 | loop fusion | flops 1572864 | bytes 6291456 | tf_op jit(solution)/shard_map/broadcast_in_dim | solution.py:81
  150.3 3.5 %copy.40 = f32[1,3,32,16,512]{4,3,2,1,0:T(8,128)} copy(f32[1,3,32,16,512]{4,2,3,1,0:T(8,128)S(1)} %maximum_bitcast_fusion) | data formatting | bytes 6291456
  154.0 3.4 %fusion.1 = f32[64,1,256]{2,1,0:T(1,128)S(1)} fusion(bf16[1,1,64,256,128]{4,3,2,1,0:T(8,128)(2,1)} %param.21, bf16[64,128,1]{1,0,2:T(8,128)(2,1)S(1)} %fusion.11), kind=kOutput, calls=%fused_computation.3 | convolution fusion | flops 4194304 | bytes 4276224 | tf_op jit(solution)/shard_map/pio,po->pi/dot_general | solution.py:152
  (102 shorter events, 25.3 us)
Async XLA Ops:
  0.6 32.2 %copy-start = (f32[1,32,32]{2,1,0:T(8,128)S(1)}, f32[1,32,32]{2,1,0:T(8,128)}, u32[]{:S(2)}) copy-start(f32[1,32,32]{2,1,0:T(8,128)} %param.14) | copy-start | bytes 12292
  3.9 17.8 %copy-start.9 = (s32[1,1,64]{2,1,0:T(1,128)S(1)}, s32[1,1,64]{2,1,0:T(1,128)}, u32[]{:S(2)}) copy-start(s32[1,1,64]{2,1,0:T(1,128)} %param.19) | copy-start | bytes 772
  3.9 18.0 %copy-start.6 = (f32[1,16,512]{2,1,0:T(8,128)S(1)}, f32[1,16,512]{2,1,0:T(8,128)}, u32[]{:S(2)}) copy-start(f32[1,16,512]{2,1,0:T(8,128)} %param.15) | copy-start | bytes 98308
  3.9 18.1 %copy-start.17 = (s32[1,1,64,1]{2,3,1,0:T(1,128)S(1)}, s32[1,1,64,1]{2,3,1,0:T(1,128)}, u32[]{:S(2)}) copy-start(s32[1,1,64,1]{2,3,1,0:T(1,128)} %param.18) | copy-start | bytes 772
  3.9 18.3 %copy-start.16 = (f32[8,4]{0,1:T(4,128)S(1)}, f32[8,4]{0,1:T(4,128)}, u32[]{:S(2)}) copy-start(f32[8,4]{0,1:T(4,128)} %param.16) | copy-start | bytes 388
  5.7 26.4 %collective-permute-start.2 = (f32[32,16,1]{2,0,1:T(8,128)S(1)}, f32[32,16,1]{2,0,1:T(8,128)S(1)}, u32[]{:S(2)}, u32[]{:S(2)}) collective-permute-start(f32[32,16,1]{2,0,1:T(8,128)S(1)} %get-tuple-element.34), channel_id=1, source_target_pairs={{1,0},{2,1},{3,2},{5,4},{6,5},{7,6},{9,8},{10,9},{11,10},{13,12},{... | collective-permute-start | bytes 6152 | tf_op jit(solution)/shard_map/ppermute | solution.py:22
  7.0 25.1 %collective-permute-start.3 = (f32[32,16,1]{2,0,1:T(8,128)S(1)}, f32[32,16,1]{2,0,1:T(8,128)}, u32[]{:S(2)}, u32[]{:S(2)}) collective-permute-start(f32[32,16,1]{2,0,1:T(8,128)S(1)} %get-tuple-element.35), channel_id=1, source_target_pairs={{0,1},{1,2},{2,3},{4,5},{5,6},{6,7},{8,9},{9,10},{10,11},{12,13},{... | collective-permute-start | bytes 6152 | tf_op jit(solution)/shard_map/ppermute | solution.py:20
  13.9 18.3 %collective-permute-start = (f32[32,1,512]{2,0,1:T(8,128)S(1)}, f32[32,1,512]{2,0,1:T(8,128)S(1)}, u32[]{:S(2)}, u32[]{:S(2)}) collective-permute-start(f32[32,1,512]{2,0,1:T(8,128)S(1)} %get-tuple-element.32), channel_id=1, source_target_pairs={{4,0},{8,4},{12,8},{16,12},{20,16},{24,20},{28,24},{32,28},{36,32}... | collective-permute-start | bytes 196616 | tf_op jit(solution)/shard_map/ppermute | solution.py:22
  19.0 13.1 %collective-permute-start.1 = (f32[32,1,512]{2,0,1:T(8,128)S(1)}, f32[32,1,512]{2,0,1:T(8,128)}, u32[]{:S(2)}, u32[]{:S(2)}) collective-permute-start(f32[32,1,512]{2,0,1:T(8,128)S(1)} %get-tuple-element.33), channel_id=1, source_target_pairs={{0,4},{4,8},{8,12},{12,16},{16,20},{20,24},{24,28},{28,32},{32,36}... | collective-permute-start | bytes 196616 | tf_op jit(solution)/shard_map/ppermute | solution.py:20
  22.1 9.8 %copy-start.11 = (s32[64]{0:T(128)}, s32[64]{0:T(128)S(1)}, u32[]{:S(2)}) copy-start(s32[64]{0:T(128)S(1)} %multiply_add_fusion) | copy-start | bytes 772
  23.3 9.5 %copy-start.14 = (f32[1,16,512]{2,1,0:T(8,128)S(1)}, f32[1,16,512]{2,1,0:T(8,128)}, u32[]{:S(2)}) copy-start(f32[1,16,512]{2,1,0:T(8,128)} %param.12) | copy-start | bytes 98308
  27.3 68.2 %collective-permute-start.17 = (bf16[32,4,8,128]{3,2,1,0:T(8,128)(2,1)}, bf16[32,4,8,128]{3,2,1,0:T(8,128)(2,1)}, u32[]{:S(2)}, u32[]{:S(2)}) collective-permute-start(bf16[32,4,8,128]{3,2,1,0:T(8,128)(2,1)} %bitcast.54), channel_id=1, source_target_pairs={{0,128},{1,129},{2,130},{3,131},{4,132},{5,133},{6,134},{7,135},{8... | collective-permute-start | bytes 786440 | tf_op jit(solution)/shard_map/ppermute | solution.py:32
  32.8 20.2 %copy-start.7 = (s32[1,16,512]{2,1,0:T(8,128)S(1)}, s32[1,16,512]{2,1,0:T(8,128)}, u32[]{:S(2)}) copy-start(s32[1,16,512]{2,1,0:T(8,128)} %param.13) | copy-start | bytes 98308
  40.5 19.3 %copy-start.1 = (f32[32,16,512]{2,0,1:T(8,128)}, f32[32,16,512]{2,0,1:T(8,128)S(1)}, u32[]{:S(2)}) copy-start(f32[32,16,512]{2,0,1:T(8,128)S(1)} %fusion.6) | copy-start | bytes 3145732
  40.5 7.0 %collective-permute-start.4 = (f32[32,1,512]{2,0,1:T(8,128)S(1)}, f32[32,1,512]{2,0,1:T(8,128)S(1)}, u32[]{:S(2)}, u32[]{:S(2)}) collective-permute-start(f32[32,1,512]{2,0,1:T(8,128)S(1)} %get-tuple-element.31), channel_id=1, source_target_pairs={{4,0},{8,4},{12,8},{16,12},{20,16},{24,20},{28,24},{32,28},{36,32}... | collective-permute-start | bytes 196616 | tf_op jit(solution)/shard_map/ppermute | solution.py:22
  42.9 4.6 %collective-permute-start.5 = (f32[32,1,512]{2,0,1:T(8,128)S(1)}, f32[32,1,512]{2,0,1:T(8,128)S(1)}, u32[]{:S(2)}, u32[]{:S(2)}) collective-permute-start(f32[32,1,512]{2,0,1:T(8,128)S(1)} %get-tuple-element.30), channel_id=1, source_target_pairs={{0,4},{4,8},{8,12},{12,16},{16,20},{20,24},{24,28},{28,32},{32,36}... | collective-permute-start | bytes 196616 | tf_op jit(solution)/shard_map/ppermute | solution.py:20
  46.2 26.6 %collective-permute-start.16 = (s32[32,4]{1,0:T(8,128)S(1)}, s32[32,4]{1,0:T(8,128)S(1)}, u32[]{:S(2)}, u32[]{:S(2)}) collective-permute-start(s32[32,4]{1,0:T(8,128)S(1)} %sub.63), channel_id=1, source_target_pairs={{0,128},{1,129},{2,130},{3,131},{4,132},{5,133},{6,134},{7,135},{8... | collective-permute-start | bytes 1544 | tf_op jit(solution)/shard_map/ppermute | solution.py:32
  47.7 10.4 %collective-permute-start.8 = (f32[32,18,1]{2,0,1:T(8,128)S(1)}, f32[32,18,1]{2,0,1:T(8,128)S(1)}, u32[]{:S(2)}, u32[]{:S(2)}) collective-permute-start(f32[32,18,1]{2,0,1:T(8,128)S(1)} %get-tuple-element.22), channel_id=1, source_target_pairs={{1,0},{2,1},{3,2},{5,4},{6,5},{7,6},{9,8},{10,9},{11,10},{13,12},{... | collective-permute-start | bytes 6920 | tf_op jit(solution)/shard_map/ppermute | solution.py:22
  49.0 10.8 %collective-permute-start.9 = (f32[32,18,1]{2,0,1:T(8,128)S(1)}, f32[32,18,1]{2,0,1:T(8,128)S(1)}, u32[]{:S(2)}, u32[]{:S(2)}) collective-permute-start(f32[32,18,1]{2,0,1:T(8,128)S(1)} %get-tuple-element.23), channel_id=1, source_target_pairs={{0,1},{1,2},{2,3},{4,5},{5,6},{6,7},{8,9},{9,10},{10,11},{12,13},{... | collective-permute-start | bytes 6920 | tf_op jit(solution)/shard_map/ppermute | solution.py:20
  59.8 40.1 %copy-start.15 = (f32[1,16,512]{2,1,0:T(8,128)S(1)}, f32[1,16,512]{2,1,0:T(8,128)}, u32[]{:S(2)}) copy-start(f32[1,16,512]{2,1,0:T(8,128)} %param.12) | copy-start | bytes 98308
  65.1 34.7 %collective-permute-start.6 = (f32[32,1,512]{2,0,1:T(8,128)S(1)}, f32[32,1,512]{2,0,1:T(8,128)S(1)}, u32[]{:S(2)}, u32[]{:S(2)}) collective-permute-start(f32[32,1,512]{2,0,1:T(8,128)S(1)} %get-tuple-element.26), channel_id=1, source_target_pairs={{4,0},{8,4},{12,8},{16,12},{20,16},{24,20},{28,24},{32,28},{36,32}... | collective-permute-start | bytes 196616 | tf_op jit(solution)/shard_map/ppermute | solution.py:22
  67.4 32.4 %collective-permute-start.7 = (f32[32,1,512]{2,0,1:T(8,128)S(1)}, f32[32,1,512]{2,0,1:T(8,128)S(1)}, u32[]{:S(2)}, u32[]{:S(2)}) collective-permute-start(f32[32,1,512]{2,0,1:T(8,128)S(1)} %get-tuple-element.27), channel_id=1, source_target_pairs={{0,4},{4,8},{8,12},{12,16},{16,20},{20,24},{24,28},{28,32},{32,36}... | collective-permute-start | bytes 196616 | tf_op jit(solution)/shard_map/ppermute | solution.py:20
  71.5 28.3 %collective-permute-start.10 = (f32[32,16,1]{2,0,1:T(8,128)S(1)}, f32[32,16,1]{2,0,1:T(8,128)S(1)}, u32[]{:S(2)}, u32[]{:S(2)}) collective-permute-start(f32[32,16,1]{2,0,1:T(8,128)S(1)} %get-tuple-element.28), channel_id=1, source_target_pairs={{1,0},{2,1},{3,2},{5,4},{6,5},{7,6},{9,8},{10,9},{11,10},{13,12},{... | collective-permute-start | bytes 6152 | tf_op jit(solution)/shard_map/ppermute | solution.py:22
  72.8 27.0 %collective-permute-start.11 = (f32[32,16,1]{2,0,1:T(8,128)S(1)}, f32[32,16,1]{2,0,1:T(8,128)S(1)}, u32[]{:S(2)}, u32[]{:S(2)}) collective-permute-start(f32[32,16,1]{2,0,1:T(8,128)S(1)} %get-tuple-element.29), channel_id=1, source_target_pairs={{0,1},{1,2},{2,3},{4,5},{5,6},{6,7},{8,9},{9,10},{10,11},{12,13},{... | collective-permute-start | bytes 6152 | tf_op jit(solution)/shard_map/ppermute | solution.py:20
  95.5 29.0 %all-to-all-start.1 = ((bf16[32,4,8,128]{3,2,1,0:T(8,128)(2,1)}), bf16[32,4,8,128]{3,2,1,0:T(8,128)(2,1)S(1)}, u32[]{:S(2)}, u32[]{:S(2)}) async-start(bf16[32,4,8,128]{3,2,1,0:T(8,128)(2,1)} %collective-permute-done.17), calls=%async_computation.1 | async-start | bytes 524288 | tf_op jit(solution)/shard_map/all_to_all | solution.py:123
  104.9 34.2 %copy-start.3 = (f32[32,16,512]{2,0,1:T(8,128)S(1)}, f32[32,16,512]{2,0,1:T(8,128)}, u32[]{:S(2)}) copy-start(f32[32,16,512]{2,0,1:T(8,128)} %copy-done.2) | copy-start | bytes 3145732
  105.5 11.3 %collective-permute-start.12 = (f32[32,1,512]{2,0,1:T(8,128)}, f32[32,1,512]{2,0,1:T(8,128)S(1)}, u32[]{:S(2)}, u32[]{:S(2)}) collective-permute-start(f32[32,1,512]{2,0,1:T(8,128)} %get-tuple-element.25), channel_id=1, source_target_pairs={{4,0},{8,4},{12,8},{16,12},{20,16},{24,20},{28,24},{32,28},{36,32}... | collective-permute-start | bytes 196616 | tf_op jit(solution)/shard_map/ppermute | solution.py:22
  108.0 8.9 %collective-permute-start.13 = (f32[32,1,512]{2,0,1:T(8,128)}, f32[32,1,512]{2,0,1:T(8,128)}, u32[]{:S(2)}, u32[]{:S(2)}) collective-permute-start(f32[32,1,512]{2,0,1:T(8,128)} %get-tuple-element.24), channel_id=1, source_target_pairs={{0,4},{4,8},{8,12},{12,16},{16,20},{20,24},{24,28},{28,32},{32,36}... | collective-permute-start | bytes 196616 | tf_op jit(solution)/shard_map/ppermute | solution.py:20
  118.5 20.5 %collective-permute-start.14 = (f32[32,18,1]{2,0,1:T(8,128)}, f32[32,18,1]{2,0,1:T(8,128)}, u32[]{:S(2)}, u32[]{:S(2)}) collective-permute-start(f32[32,18,1]{2,0,1:T(8,128)} %get-tuple-element.20), channel_id=1, source_target_pairs={{1,0},{2,1},{3,2},{5,4},{6,5},{7,6},{9,8},{10,9},{11,10},{13,12},{... | collective-permute-start | bytes 6920 | tf_op jit(solution)/shard_map/ppermute | solution.py:22
  119.8 19.2 %collective-permute-start.15 = (f32[32,18,1]{2,0,1:T(8,128)}, f32[32,18,1]{2,0,1:T(8,128)}, u32[]{:S(2)}, u32[]{:S(2)}) collective-permute-start(f32[32,18,1]{2,0,1:T(8,128)} %get-tuple-element.21), channel_id=1, source_target_pairs={{0,1},{1,2},{2,3},{4,5},{5,6},{6,7},{8,9},{9,10},{10,11},{12,13},{... | collective-permute-start | bytes 6920 | tf_op jit(solution)/shard_map/ppermute | solution.py:20
  130.0 17.2 %all-to-all-start.2 = ((bf16[32,4,128]{2,1,0:T(4,128)(2,1)}), bf16[32,4,128]{2,1,0:T(4,128)(2,1)S(1)}, u32[]{:S(2)}, u32[]{:S(2)}) async-start(bf16[32,4,128]{2,1,0:T(4,128)(2,1)} %bitcast.30), calls=%async_computation.2 | async-start | bytes 65536 | tf_op jit(solution)/shard_map/all_to_all | solution.py:145
  147.1 6.7 %collective-permute-start.18 = (bf16[32,4,128]{2,1,0:T(4,128)(2,1)S(1)}, bf16[32,4,128]{2,1,0:T(4,128)(2,1)S(1)}, u32[]{:S(2)}, u32[]{:S(2)}) collective-permute-start(bf16[32,4,128]{2,1,0:T(4,128)(2,1)S(1)} %all-to-all-done.2), channel_id=1, source_target_pairs={{128,0},{129,1},{130,2},{131,3},{132,4},{133,5},{134,6},{135,7},{1... | collective-permute-start | bytes 98312 | tf_op jit(solution)/shard_map/ppermute | solution.py:32
  (8 other events, 23.9 us)
where the time goes:
time: 160 us; the launch traced here: 158 us
  starting transfers between devices  68.9 us (43%)
  matrix products  23.7 us (15%)
  local copies, waits for them, and re-layouts  20.7 us (13%)
  blocking collectives  18 us (11%)
  other arithmetic  14.6 us (9%)
  waiting for transfers between devices  11.1 us (7%)
    ppermute x8, starting transfers between devices, extended(): lax.ppermute(tail, axis, [(i, (i + 1) % count) for i in range(ends)])  30.9 us
    all_to_all x1, blocking collectives, local(): lax.all_to_all(shifted[1], 'gx', split_axis=0, concat_axis=0, tiled=True)  18 us
    ppermute x8, starting transfers between devices, extended(): lax.ppermute(head, axis, [((i + 1) % count, i) for i in range(ends)])  17.4 us
    dot_general x2, matrix products, vertical_mix(): jnp.einsum('lm,mxy->lxy', matrix, right_side, precision=HIGHEST_PRECISION)  12.6 us
    unnamed x48, local copies, waits for them, and re-layouts  10.9 us
    all_to_all x1, starting transfers between devices, local(): lax.all_to_all(returning, 'gx', split_axis=0, concat_axis=0, tiled=True)  9.04 us
    ppermute x3, starting transfers between devices, shifted_2(): return lax.ppermute(value, axis, pairs)  7.24 us
    all_to_all x1, waiting for transfers between devices, local(): lax.all_to_all(returning, 'gx', split_axis=0, concat_axis=0, tiled=True)  4.91 us
  transfers between devices with their start and end apart: 21, of which 3 were waited for; matrix products, arithmetic and copies ran while one was open for 30% of the time, Pallas kernels for 0%

commit v1 on v0

v1 whole, which is shorter than its diff:
```python
import jax
import jax.numpy as jnp
from jax import lax
from jax.sharding import PartitionSpec as P

SUBSTEPS = 2


HIGHEST_PRECISION = lax.Precision.HIGHEST


def neighbours(head, tail, axis):
    count = lax.axis_size(axis)
    lo = lax.ppermute(tail, axis, [(i, i + 1) for i in range(count - 1)])
    hi = lax.ppermute(head, axis, [(i + 1, i) for i in range(count - 1)])
    return lo, hi


def vertical_mix(matrix, right_side):
    return right_side + jnp.einsum("lm,mxy->lxy", matrix, right_side, precision=HIGHEST_PRECISION)


def stencil(pressure, eastward, northward, sound_speed, wetness, matrix):
    wet3 = wetness[None]
    lo_x, hi_x = neighbours(
        jnp.concatenate([eastward[:, :1], wet3[:, :1]], axis=0),
        jnp.concatenate([eastward[:, -1:], wet3[:, -1:]], axis=0),
        "gx",
    )
    lo_y, hi_y = neighbours(
        jnp.concatenate([northward[:, :, :1], wet3[:, :, :1]], axis=0),
        jnp.concatenate([northward[:, :, -1:], wet3[:, :, -1:]], axis=0),
        "gy",
    )
    levels = eastward.shape[0]
    u_ext = jnp.concatenate([lo_x[:levels], eastward, hi_x[:levels]], axis=1)
    wet_x = jnp.concatenate([lo_x[levels:], wet3, hi_x[levels:]], axis=1)
    v_ext = jnp.concatenate([lo_y[:levels], northward, hi_y[:levels]], axis=2)
    wet_y = jnp.concatenate([lo_y[levels:], wet3, hi_y[levels:]], axis=2)

    divergence = (u_ext[:, 2:] - u_ext[:, :-2]) + (v_ext[:, :, 2:] - v_ext[:, :, :-2])
    p1 = vertical_mix(matrix, pressure - sound_speed * divergence)

    lo2x, hi2x = neighbours(p1[:, :2], p1[:, -2:], "gx")
    lo2y, hi2y = neighbours(p1[:, :, :2], p1[:, :, -2:], "gy")
    p1_x = jnp.concatenate([lo2x, p1, hi2x], axis=1)
    p1_y = jnp.concatenate([lo2y, p1, hi2y], axis=2)
    u1_ext = wet_x * (u_ext - 0.5 * (p1_x[:, 2:] - p1_x[:, :-2]))
    v1_ext = wet_y * (v_ext - 0.5 * (p1_y[:, :, 2:] - p1_y[:, :, :-2]))

    divergence = (u1_ext[:, 2:] - u1_ext[:, :-2]) + (v1_ext[:, :, 2:] - v1_ext[:, :, :-2])
    p2 = vertical_mix(matrix, p1 - sound_speed * divergence)

    lo3x, hi3x = neighbours(p2[:, :1], p2[:, -1:], "gx")
    lo3y, hi3y = neighbours(p2[:, :, :1], p2[:, :, -1:], "gy")
    p2_x = jnp.concatenate([lo3x, p2, hi3x], axis=1)
    p2_y = jnp.concatenate([lo3y, p2, hi3y], axis=2)
    u1 = u1_ext[:, 1:-1]
    v1 = v1_ext[:, :, 1:-1]
    u2 = wetness * (u1 - 0.5 * (p2_x[:, 2:] - p2_x[:, :-2]))
    v2 = wetness * (v1 - 0.5 * (p2_y[:, :, 2:] - p2_y[:, :, :-2]))
    return p2, u2, v2


def local(
    model_state,
    wave_speed,
    wet_mask,
    vertical,
    surface_temp,
    flux_coef,
    heat_gain,
    pair_tile,
    pair_source,
    pair_target,
    intersection_weights,
):
    pressure = model_state[0, 0]
    eastward = model_state[0, 1]
    northward = model_state[0, 2]
    sound_speed = wave_speed[0]
    wetness = wet_mask[0].astype(jnp.float32)
    matrix = vertical[0]
    assert SUBSTEPS == 2
    p2, u2, v2 = stencil(pressure, eastward, northward, sound_speed, wetness, matrix)
    final_state = jnp.stack([p2, u2, v2])[None]

    weights = intersection_weights[0, 0]
    pair_count, in_width, out_width = weights.shape
    tile_count = lax.axis_size("gx")
    grid_shape = surface_temp.shape[1:]
    cell_count = grid_shape[0] * grid_shape[1]
    in_blocks = cell_count // in_width
    out_blocks = cell_count // out_width
    sources = pair_source[0, 0]
    targets = pair_target[0, 0]
    target_tile = pair_tile[0, 0, :, 0]
    is_atmos = lax.axis_index("sec") == 0
    me = lax.axis_index("gx")

    own_st = surface_temp[0].reshape(cell_count)
    own_wet = wetness.reshape(cell_count)
    drivers = jnp.stack(
        [model_state[0, 0, 0].reshape(cell_count), model_state[0, 1, 0].reshape(cell_count),
         model_state[0, 2, 0].reshape(cell_count), own_st]
    )
    zeros = jnp.zeros_like(own_st)
    sent = jnp.where(is_atmos, drivers, jnp.stack([own_st, own_wet, zeros, zeros]))
    got = lax.ppermute(sent, "sec", [(0, 1), (1, 0)])
    atmos_drivers = jnp.where(is_atmos, drivers, got)
    ocean_st = jnp.where(is_atmos, got[0], own_st)
    ocean_wet = jnp.where(is_atmos, got[1], own_wet)

    pad = jnp.zeros((out_width - pair_count,), jnp.float32)
    table = jnp.concatenate(
        [
            ocean_st.reshape(out_blocks, out_width),
            ocean_wet.reshape(out_blocks, out_width),
            jnp.concatenate([target_tile.astype(jnp.float32), pad])[None],
            jnp.concatenate([targets.astype(jnp.float32), pad])[None],
        ]
    )
    tables = lax.all_gather(table, "gx")
    st_blocks = tables[:, :out_blocks].reshape(tile_count * out_blocks, out_width)
    wet_blocks = tables[:, out_blocks:2 * out_blocks].reshape(tile_count * out_blocks, out_width)
    all_tiles = tables[:, 2 * out_blocks, :pair_count].reshape(tile_count * pair_count).astype(jnp.int32)
    all_targets = tables[:, 2 * out_blocks + 1, :pair_count].reshape(tile_count * pair_count).astype(jnp.int32)

    fluxes = jnp.tanh(jnp.dot(flux_coef, atmos_drivers, precision=HIGHEST_PRECISION)).astype(jnp.bfloat16)
    flux_count = fluxes.shape[0]
    blocks = fluxes.reshape(flux_count, in_blocks, in_width)
    picked = jnp.take(blocks, sources, axis=1)
    regridded = jnp.einsum(
        "fpi,pio->pfo", picked, weights, preferred_element_type=jnp.float32
    ).astype(jnp.bfloat16)
    heat = jnp.einsum(
        "f,pfo->po", heat_gain, regridded.astype(jnp.float32), precision=HIGHEST_PRECISION
    )
    heats = lax.all_gather(heat, "gx").reshape(tile_count * pair_count, out_width)

    own_match = (all_tiles[None, :] == me) & (all_targets[None, :] == jnp.arange(out_blocks)[:, None])
    heating = jnp.dot(own_match.astype(jnp.float32), heats, precision=HIGHEST_PRECISION)
    ocean_temp = own_st + own_wet * heating.reshape(cell_count)

    pair_match = (all_tiles[None, :] == target_tile[:, None]) & (all_targets[None, :] == targets[:, None])
    pair_heating = jnp.dot(pair_match.astype(jnp.float32), heats, precision=HIGHEST_PRECISION)
    rows = target_tile * out_blocks + targets
    pair_temp = jnp.take(st_blocks, rows, axis=0) + jnp.take(wet_blocks, rows, axis=0) * pair_heating
    returned = pair_temp.astype(jnp.bfloat16)
    pieces = jnp.einsum("pio,po->pi", weights, returned, preferred_element_type=jnp.float32)
    owning = (jnp.arange(in_blocks)[:, None] == sources[None, :]).astype(jnp.float32)
    atmos_temp = jnp.dot(owning, pieces, precision=HIGHEST_PRECISION)

    surface_temps = jnp.where(is_atmos, atmos_temp.reshape(grid_shape), ocean_temp.reshape(grid_shape))[None]
    return (final_state, surface_temps)


def solution(mesh):
    return jax.shard_map(
        local,
        mesh=mesh,
        in_specs=(
            P("sec", None, None, "gx", "gy"),
            P("sec", "gx", "gy"),
            P("sec", "gx", "gy"),
            P("sec", None, None),
            P("sec", "gx", "gy"),
            P(),
            P(),
            P("gx", "gy", None, None),
            P("gx", "gy", None),
            P("gx", "gy", None),
            P("gx", "gy", None, None, None),
        ),
        out_specs=(P("sec", None, None, "gx", "gy"), P("sec", "gx", "gy")),
        check_vma=False,
    )
```

time: 160 us -> 168 us (1.050)
  waiting for transfers between devices: 11.1 us -> 70.1 us
  starting transfers between devices: 68.9 us -> 37.5 us
  blocking collectives: 18 us -> 0 us
  between operations: 1.27 us -> 14.8 us
  matrix products: 23.7 us -> 15.8 us
  other arithmetic: 14.6 us -> 9.72 us
  local copies, waits for them, and re-layouts: 20.7 us -> 18.9 us
    all_gather x0 -> x2, waiting for transfers between devices: none -> 61.2 us  [the longest x1 61.2 us: local(): lax.all_gather(heat, 'gx').reshape(tile_count * pair_count, out_width)]
    ppermute x19 -> x13, starting transfers between devices: 55.5 us -> 37.5 us  [the longest x6 22.9 us: neighbours(): lo = lax.ppermute(tail, axis, [(i, i + 1) for i in range(count - 1)])]
    all_to_all x1 -> x0, blocking collectives: 18 us -> none  [local(): lax.all_to_all(shifted[1], 'gx', split_axis=0, concat_axis=0, tiled=True)]
    all_to_all x2 -> x0, starting transfers between devices: 13.3 us -> none  [the longest x1 9.04 us: local(): lax.all_to_all(returning, 'gx', split_axis=0, concat_axis=0, tiled=True)]
    dot_general x2, matrix products: 12.6 us -> 4.73 us  [vertical_mix(): jnp.einsum('lm,mxy->lxy', matrix, right_side, precision=HIGHEST_PRECISION)]
    all_to_all x2 -> x0, waiting for transfers between devices: 4.91 us -> none  [the longest x1 4.91 us: local(): lax.all_to_all(returning, 'gx', split_axis=0, concat_axis=0, tiled=True)]
    slice x6 -> x18, local copies, waits for them, and re-layouts: 0.97 us -> 3.72 us  [the longest x1 1.71 us: local(): tables[:, :out_blocks].reshape(tile_count * out_blocks, out_width)]
    unnamed x48 -> x70, local copies, waits for them, and re-layouts: 10.9 us -> 8.18 us
  transfers between devices with their start and end apart: 21 -> 15, of which waited for: 3 -> 5; matrix products, arithmetic and copies ran while one was open for 30% -> 20% of each run, Pallas kernels for 0% -> 0%
where the time goes in v1:
time: 168 us; the launch traced here: 167 us
  waiting for transfers between devices  70.1 us (42%)
  starting transfers between devices  37.5 us (22%)
  local copies, waits for them, and re-layouts  18.9 us (11%)
  matrix products  15.8 us (9%)
  between operations  14.8 us (9%)
  other arithmetic  9.72 us (6%)
    all_gather x1, waiting for transfers between devices, local(): lax.all_gather(heat, 'gx').reshape(tile_count * pair_count, out_width)  61.2 us
    ppermute x6, starting transfers between devices, neighbours(): lo = lax.ppermute(tail, axis, [(i, i + 1) for i in range(count - 1)])  22.9 us
    ppermute x6, starting transfers between devices, neighbours(): hi = lax.ppermute(head, axis, [(i + 1, i) for i in range(count - 1)])  10.7 us
    unnamed x70, local copies, waits for them, and re-layouts  8.18 us
    ppermute x6, waiting for transfers between devices, neighbours(): hi = lax.ppermute(head, axis, [(i + 1, i) for i in range(count - 1)])  7.35 us
    dot_general x2, matrix products, vertical_mix(): jnp.einsum('lm,mxy->lxy', matrix, right_side, precision=HIGHEST_PRECISION)  4.73 us
    ppermute x1, starting transfers between devices, local(): got = lax.ppermute(sent, 'sec', [(0, 1), (1, 0)])  3.79 us
    dot_general x1, matrix products, local(): jnp.einsum('pio,po->pi', weights, returned, preferred_element_type=jnp.fl...  3.45 us
  transfers between devices with their start and end apart: 15, of which 5 were waited for; matrix products, arithmetic and copies ran while one was open for 20% of the time, Pallas kernels for 0%

profile of v1, /device:TPU:1, one launch (start us, length us, event | category | flops | bytes accessed | tf_op | source)
XLA Modules:
  0.0 166.8 jit_solution(39620544912601809)
XLA Ops:
  10.4 3.8 %collective-permute-start.12 = (f32[4,8192]{1,0:T(4,128)S(1)}, f32[4,8192]{1,0:T(4,128)S(1)}, u32[]{:S(2)}, u32[]{:S(2)}) collective-permute-start(f32[4,8192]{1,0:T(4,128)S(1)} %maximum_select_fusion), channel_id=1, source_target_pairs={{0,128},{128,0},{1,129},{129,1},{2,130},{130,2},{3,131},{131,3},{4... | collective-permute-start | bytes 393224 | tf_op jit(solution)/shard_map/ppermute | solution.py:109
  14.2 3.2 %fusion.79 = (f32[1,1,32,16,512]{4,3,2,1,0:T(8,128)}, f32[1,1,32,16,512]{4,3,2,1,0:T(8,128)S(1)}, f32[1,1,32,16,512]{4,3,2,1,0:T(8,128)S(1)}) fusion(f32[1,3,32,16,512]{4,3,2,1,0:T(8,128)} %param.13), kind=kLoop, calls=%fused_computation.134 | loop fusion | bytes 6291456 | tf_op jit(solution)/shard_map/slice | solution.py:78
  19.2 3.1 %collective-permute-start.3 = (f32[33,16,1]{2,0,1:T(8,128)S(1)}, f32[33,16,1]{2,0,1:T(8,128)S(1)}, u32[]{:S(2)}, u32[]{:S(2)}) collective-permute-start(f32[33,16,1]{2,0,1:T(8,128)S(1)} %pad_maximum_fusion.11), channel_id=1, source_target_pairs={{0,1},{1,2},{2,3},{4,5},{5,6},{6,7},{8,9},{9,10},{10,11},{12,13},{... | collective-permute-start | bytes 6344 | tf_op jit(solution)/shard_map/ppermute | solution.py:14
  22.4 1.3 collective-permute-start.2
  24.4 4.7 %collective-permute-start.1 = (f32[33,1,512]{2,0,1:T(8,128)S(1)}, f32[33,1,512]{2,0,1:T(8,128)S(1)}, u32[]{:S(2)}, u32[]{:S(2)}) collective-permute-start(f32[33,1,512]{2,0,1:T(8,128)S(1)} %pad_maximum_fusion.14), channel_id=1, source_target_pairs={{0,4},{4,8},{8,12},{12,16},{16,20},{20,24},{24,28},{28,32},{32,36}... | collective-permute-start | bytes 202760 | tf_op jit(solution)/shard_map/ppermute | solution.py:14
  29.1 1.9 %collective-permute-start = (f32[33,1,512]{2,0,1:T(8,128)S(1)}, f32[33,1,512]{2,0,1:T(8,128)S(1)}, u32[]{:S(2)}, u32[]{:S(2)}) collective-permute-start(f32[33,1,512]{2,0,1:T(8,128)S(1)} %pad_maximum_fusion.13), channel_id=1, source_target_pairs={{4,0},{8,4},{12,8},{16,12},{20,16},{24,20},{28,24},{32,28},{36,32}... | collective-permute-start | bytes 202760 | tf_op jit(solution)/shard_map/ppermute | solution.py:15
  33.1 1.7 %collective-permute-done = f32[33,1,512]{2,0,1:T(8,128)S(1)} collective-permute-done((f32[33,1,512]{2,0,1:T(8,128)S(1)}, f32[33,1,512]{2,0,1:T(8,128)S(1)}, u32[]{:S(2)}, u32[]{:S(2)}) %collective-permute-start) | collective-permute-done | bytes 67616 | tf_op jit(solution)/shard_map/ppermute | solution.py:15
  34.9 2.9 %fusion.6 = f32[32,16,512]{2,0,1:T(8,128)S(1)} fusion(f32[32,16,512]{2,0,1:T(8,128)S(1)} %bitcast.115, f32[32,16,1]{2,0,1:T(8,128)S(1)} %slice.233, f32[32,16,1]{2,0,1:T(8,128)S(1)} %slice.230, f32[32,16,512]{2,0,1:T(8,128)S(1)} %bitcast.118, f32[32,1,512]{2,0,1:T(8,128)S(1)} %slice.227, f32[32,1,512]{2,0,1:T(8,128)S(1)} %slice.224, ...), kind=kOutput, calls=%fused_computation.13 | convolution fusion | flops 105644032 | bytes 4366336 | tf_op jit(solution)/shard_map/lm,mxy->lxy/dot_general | solution.py:20
  38.0 5.4 %collective-permute-start.7 = (f32[32,16,2]{2,0,1:T(8,128)S(1)}, f32[32,16,2]{2,0,1:T(8,128)S(1)}, u32[]{:S(2)}, u32[]{:S(2)}) collective-permute-start(f32[32,16,2]{2,0,1:T(8,128)S(1)} %get-tuple-element.29), channel_id=1, source_target_pairs={{0,1},{1,2},{2,3},{4,5},{5,6},{6,7},{8,9},{9,10},{10,11},{12,13},{... | collective-permute-start | bytes 12296 | tf_op jit(solution)/shard_map/ppermute | solution.py:14
  43.4 1.3 collective-permute-start.6
  46.1 1.9 %collective-permute-start.5 = (f32[32,2,512]{2,0,1:T(8,128)}, f32[32,2,512]{2,0,1:T(8,128)}, u32[]{:S(2)}, u32[]{:S(2)}) collective-permute-start(f32[32,2,512]{2,0,1:T(8,128)} %get-tuple-element.27), channel_id=1, source_target_pairs={{0,4},{4,8},{8,12},{12,16},{16,20},{20,24},{24,28},{28,32},{32,36}... | collective-permute-start | bytes 393224 | tf_op jit(solution)/shard_map/ppermute | solution.py:14
  48.0 3.0 %collective-permute-start.4 = (f32[32,2,512]{2,0,1:T(8,128)}, f32[32,2,512]{2,0,1:T(8,128)}, u32[]{:S(2)}, u32[]{:S(2)}) collective-permute-start(f32[32,2,512]{2,0,1:T(8,128)} %get-tuple-element.28), channel_id=1, source_target_pairs={{4,0},{8,4},{12,8},{16,12},{20,16},{24,20},{28,24},{32,28},{36,32}... | collective-permute-start | bytes 393224 | tf_op jit(solution)/shard_map/ppermute | solution.py:15
  51.1 1.0 collective-permute-done.6
  53.0 1.1 fusion
  54.2 2.3 %gather_fusion = bf16[64,8,256]{2,1,0:T(8,128)(2,1)} fusion(bf16[8,32,256]{2,0,1:T(8,128)(2,1)} %bitcast.124, s32[1024]{0:T(1024)} %pad_clamp_fusion), kind=kCustom, calls=%fused_computation.2 | custom fusion | bytes 524544 | tf_op jit(solution)/shard_map/jit(_take)/gather | solution.py:132
  56.5 3.0 %fusion.11 = bf16[64,8,128]{2,1,0:T(8,128)(2,1)S(1)} fusion(bf16[1,1,64,256,128]{4,3,2,1,0:T(8,128)(2,1)} %param.23, bf16[64,8,256]{2,1,0:T(8,128)(2,1)} %gather_fusion, pred[64]{0:T(512)(128)(4,1)} %compare_and_fusion.1), kind=kOutput, calls=%fused_computation.22 | convolution fusion | flops 33751040 | bytes 4587584 | tf_op jit(solution)/shard_map/fpi,pio->pfo/dot_general | solution.py:133
  59.5 0.9 fusion.74
  60.5 1.3 fusion.9
  61.8 1.8 %fusion.5 = f32[32,16,512]{2,0,1:T(8,128)S(1)} fusion(f32[32,16,512]{2,0,1:T(8,128)S(1)} %fusion.6, f32[32,16,514]{2,0,1:T(8,128)S(1)} %fusion.7, f32[32,18,512]{2,0,1:T(8,128)S(1)} %fusion.9, f32[16,512]{1,0:T(8,128)S(1)} %bitcast.145, f32[1,32,32]{2,1,0:T(8,128)S(1)} %copy-done), kind=kOutput, calls=%fused_computation.11 | convolution fusion | flops 103546880 | bytes 11616256 | tf_op jit(solution)/shard_map/lm,mxy->lxy/dot_general | solution.py:20
  64.3 1.9 %collective-permute-start.8 = (f32[32,1,512]{2,0,1:T(8,128)}, f32[32,1,512]{2,0,1:T(8,128)}, u32[]{:S(2)}, u32[]{:S(2)}) collective-permute-start(f32[32,1,512]{2,0,1:T(8,128)} %get-tuple-element.23), channel_id=1, source_target_pairs={{4,0},{8,4},{12,8},{16,12},{20,16},{24,20},{28,24},{32,28},{36,32}... | collective-permute-start | bytes 196616 | tf_op jit(solution)/shard_map/ppermute | solution.py:15
  66.2 3.8 %collective-permute-start.9 = (f32[32,1,512]{2,0,1:T(8,128)}, f32[32,1,512]{2,0,1:T(8,128)}, u32[]{:S(2)}, u32[]{:S(2)}) collective-permute-start(f32[32,1,512]{2,0,1:T(8,128)} %get-tuple-element.24), channel_id=1, source_target_pairs={{0,4},{4,8},{8,12},{12,16},{16,20},{20,24},{24,28},{28,32},{32,36}... | collective-permute-start | bytes 196616 | tf_op jit(solution)/shard_map/ppermute | solution.py:14
  70.2 1.3 collective-permute-start.10
  71.5 4.0 %collective-permute-start.11 = (f32[32,16,1]{2,0,1:T(8,128)S(1)}, f32[32,16,1]{2,0,1:T(8,128)S(1)}, u32[]{:S(2)}, u32[]{:S(2)}) collective-permute-start(f32[32,16,1]{2,0,1:T(8,128)S(1)} %get-tuple-element.26), channel_id=1, source_target_pairs={{0,1},{1,2},{2,3},{4,5},{5,6},{6,7},{8,9},{9,10},{10,11},{12,13},{... | collective-permute-start | bytes 6152 | tf_op jit(solution)/shard_map/ppermute | solution.py:14
  75.5 4.6 %collective-permute-done.10 = f32[32,16,1]{2,0,1:T(8,128)S(1)} collective-permute-done((f32[32,16,1]{2,0,1:T(8,128)S(1)}, f32[32,16,1]{2,0,1:T(8,128)S(1)}, u32[]{:S(2)}, u32[]{:S(2)}) %collective-permute-start.10) | collective-permute-done | bytes 2080 | tf_op jit(solution)/shard_map/ppermute | solution.py:15
  80.2 1.4 collective-permute-done.11
  81.6 2.3 %fusion.26 = (f32[1,32,16,512]{3,1,2,0:T(8,128)S(1)}, f32[1,32,16,512]{3,1,2,0:T(8,128)S(1)}) fusion(f32[32,16,512]{2,0,1:T(8,128)S(1)} %fusion.5, f32[32,1,512]{2,0,1:T(8,128)} %collective-permute-done.9, f32[32,1,512]{2,0,1:T(8,128)} %collective-permute-done.8, f32[32,18,512]{2,0,1:T(8,128)} %copy-done.1, f32[16,512]{1,0:T(8,128)S(1)} %bitcast.128, ...), kind=kLoop, calls=%fused_computation.39 | loop fusion | flops 3145728 | bytes 5410816 | tf_op jit(solution)/shard_map/stack | solution.py:86
  84.2 3.5 %copy.38 = f32[1,3,32,16,512]{4,3,2,1,0:T(8,128)} copy(f32[1,3,32,16,512]{4,2,3,1,0:T(8,128)S(1)} %maximum_bitcast_fusion) | data formatting | bytes 6291456
  87.7 1.7 %fusion.80 = (f32[32,64,128]{2,1,0:T(8,128)S(1)}, f32[32,64,128]{2,1,0:T(8,128)S(1)}) fusion(f32[32,130,128]{2,1,0:T(8,128)} %all-gather.8.cloned.1.call-done), kind=kLoop, calls=%fused_computation.135 | loop fusion | bytes 4194304 | tf_op jit(solution)/shard_map/slice | solution.py:124
  90.6 1.1 fusion.69
  91.9 61.2 %all-gather.6.cloned.1.call-done = f32[2048,128]{1,0:T(8,128)} async-done(((f32[64,128]{1,0:T(8,128)}), f32[2048,128]{1,0:T(8,128)}) %all-gather.6.cloned.1.call-update) | async-done | bytes 1048592 | tf_op jit(solution)/shard_map/all_gather | solution.py:139
  153.2 1.8 %fusion.16 = bf16[64,128,1]{1,0,2:T(8,128)(2,1)S(1)} fusion(f32[2048,128]{1,0:T(8,128)} %all-gather.6.cloned.1.call-done, s32[2048]{0:T(1024)S(1)} %convert_element_type.74, s32[2048]{0:T(1024)S(1)} %convert_element_type.72, s32[64]{0:T(128)S(1)} %bitcast.141, s32[64]{0:T(128)S(1)} %bitcast.142, f32[64,128]{1,0:T(8,128)S(1)} %gather_fusion.2, ...), kind=kOutput, calls=%fused_computation.26 | convolution fusion | flops 201760768 | bytes 1147456 | tf_op jit(solution)/shard_map/dot_general | solution.py:146
  155.0 3.5 %fusion.1 = f32[64,1,256]{2,1,0:T(1,128)S(1)} fusion(bf16[1,1,64,256,128]{4,3,2,1,0:T(8,128)(2,1)} %param.23, bf16[64,128,1]{1,0,2:T(8,128)(2,1)S(1)} %fusion.16), kind=kOutput, calls=%fused_computation.5 | convolution fusion | flops 4194304 | bytes 4276224 | tf_op jit(solution)/shard_map/pio,po->pi/dot_general | solution.py:150
  (133 shorter events, 14.0 us)
Async XLA Ops:
  7.2 27.7 %copy-start = (f32[1,32,32]{2,1,0:T(8,128)S(1)}, f32[1,32,32]{2,1,0:T(8,128)}, u32[]{:S(2)}) copy-start(f32[1,32,32]{2,1,0:T(8,128)} %param.16) | copy-start | bytes 12292
  7.2 80.5 %all-gather.8.cloned.1.call-start = ((), (), s32[]{:S(2)}) async-start(), calls=%async_computation.1 | async-start | bytes 2297856 | tf_op jit(solution)/shard_map/all_gather | solution.py:123
  10.4 7.0 %copy-start.19 = (s32[1,1,64,1]{2,3,1,0:T(1,128)S(1)}, s32[1,1,64,1]{2,3,1,0:T(1,128)}, u32[]{:S(2)}) copy-start(s32[1,1,64,1]{2,3,1,0:T(1,128)} %param.20) | copy-start | bytes 772
  10.4 7.0 %copy-start.17 = (s32[1,1,64]{2,1,0:T(1,128)S(1)}, s32[1,1,64]{2,1,0:T(1,128)}, u32[]{:S(2)}) copy-start(s32[1,1,64]{2,1,0:T(1,128)} %param.22) | copy-start | bytes 772
  10.4 7.1 %copy-start.4 = (f32[1,16,512]{2,1,0:T(8,128)S(1)}, f32[1,16,512]{2,1,0:T(8,128)}, u32[]{:S(2)}) copy-start(f32[1,16,512]{2,1,0:T(8,128)} %param.17) | copy-start | bytes 98308
  10.4 7.1 %collective-permute-start.12 = (f32[4,8192]{1,0:T(4,128)S(1)}, f32[4,8192]{1,0:T(4,128)S(1)}, u32[]{:S(2)}, u32[]{:S(2)}) collective-permute-start(f32[4,8192]{1,0:T(4,128)S(1)} %maximum_select_fusion), channel_id=1, source_target_pairs={{0,128},{128,0},{1,129},{129,1},{2,130},{130,2},{3,131},{131,3},{4... | collective-permute-start | bytes 393224 | tf_op jit(solution)/shard_map/ppermute | solution.py:109
  18.3 134.9 %all-gather.6.cloned.1.call-start = ((), (), s32[]{:S(2)}) async-start(), calls=%async_computation | async-start | bytes 1081344 | tf_op jit(solution)/shard_map/all_gather | solution.py:139
  19.2 13.6 %collective-permute-start.3 = (f32[33,16,1]{2,0,1:T(8,128)S(1)}, f32[33,16,1]{2,0,1:T(8,128)S(1)}, u32[]{:S(2)}, u32[]{:S(2)}) collective-permute-start(f32[33,16,1]{2,0,1:T(8,128)S(1)} %pad_maximum_fusion.11), channel_id=1, source_target_pairs={{0,1},{1,2},{2,3},{4,5},{5,6},{6,7},{8,9},{9,10},{10,11},{12,13},{... | collective-permute-start | bytes 6344 | tf_op jit(solution)/shard_map/ppermute | solution.py:14
  22.4 10.4 %collective-permute-start.2 = (f32[33,16,1]{2,0,1:T(8,128)S(1)}, f32[33,16,1]{2,0,1:T(8,128)S(1)}, u32[]{:S(2)}, u32[]{:S(2)}) collective-permute-start(f32[33,16,1]{2,0,1:T(8,128)S(1)} %pad_maximum_fusion.10), channel_id=1, source_target_pairs={{1,0},{2,1},{3,2},{5,4},{6,5},{7,6},{9,8},{10,9},{11,10},{13,12},{... | collective-permute-start | bytes 6344 | tf_op jit(solution)/shard_map/ppermute | solution.py:15
  23.7 7.3 %copy-start.24 = (s32[1,1,64]{2,1,0:T(1,128)S(1)}, s32[1,1,64]{2,1,0:T(1,128)}, u32[]{:S(2)}) copy-start(s32[1,1,64]{2,1,0:T(1,128)} %param.21) | copy-start | bytes 772
  24.3 10.6 %copy-start.3 = (f32[1,1,32,16,512]{4,3,2,1,0:T(8,128)S(1)}, f32[1,1,32,16,512]{4,3,2,1,0:T(8,128)}, u32[]{:S(2)}) copy-start(f32[1,1,32,16,512]{4,3,2,1,0:T(8,128)} %get-tuple-element.16) | copy-start | bytes 3145732
  24.3 10.6 %copy-start.26 = (f32[1,16,512]{2,1,0:T(8,128)S(1)}, f32[1,16,512]{2,1,0:T(8,128)}, u32[]{:S(2)}) copy-start(f32[1,16,512]{2,1,0:T(8,128)} %param.14) | copy-start | bytes 98308
  24.4 8.7 %collective-permute-start.1 = (f32[33,1,512]{2,0,1:T(8,128)S(1)}, f32[33,1,512]{2,0,1:T(8,128)S(1)}, u32[]{:S(2)}, u32[]{:S(2)}) collective-permute-start(f32[33,1,512]{2,0,1:T(8,128)S(1)} %pad_maximum_fusion.14), channel_id=1, source_target_pairs={{0,4},{4,8},{8,12},{12,16},{16,20},{20,24},{24,28},{28,32},{32,36}... | collective-permute-start | bytes 202760 | tf_op jit(solution)/shard_map/ppermute | solution.py:14
  29.1 5.8 %collective-permute-start = (f32[33,1,512]{2,0,1:T(8,128)S(1)}, f32[33,1,512]{2,0,1:T(8,128)S(1)}, u32[]{:S(2)}, u32[]{:S(2)}) collective-permute-start(f32[33,1,512]{2,0,1:T(8,128)S(1)} %pad_maximum_fusion.13), channel_id=1, source_target_pairs={{4,0},{8,4},{12,8},{16,12},{20,16},{24,20},{28,24},{32,28},{36,32}... | collective-permute-start | bytes 202760 | tf_op jit(solution)/shard_map/ppermute | solution.py:15
  34.9 3.0 %copy-start.5 = (f32[32,1,512]{2,0,1:T(8,128)}, f32[32,1,512]{2,0,1:T(8,128)S(1)}, u32[]{:S(2)}) copy-start(f32[32,1,512]{2,0,1:T(8,128)S(1)} %slice.224) | copy-start | bytes 196612
  38.0 13.1 %collective-permute-start.7 = (f32[32,16,2]{2,0,1:T(8,128)S(1)}, f32[32,16,2]{2,0,1:T(8,128)S(1)}, u32[]{:S(2)}, u32[]{:S(2)}) collective-permute-start(f32[32,16,2]{2,0,1:T(8,128)S(1)} %get-tuple-element.29), channel_id=1, source_target_pairs={{0,1},{1,2},{2,3},{4,5},{5,6},{6,7},{8,9},{9,10},{10,11},{12,13},{... | collective-permute-start | bytes 12296 | tf_op jit(solution)/shard_map/ppermute | solution.py:14
  43.4 8.6 %collective-permute-start.6 = (f32[32,16,2]{2,0,1:T(8,128)S(1)}, f32[32,16,2]{2,0,1:T(8,128)S(1)}, u32[]{:S(2)}, u32[]{:S(2)}) collective-permute-start(f32[32,16,2]{2,0,1:T(8,128)S(1)} %get-tuple-element.30), channel_id=1, source_target_pairs={{1,0},{2,1},{3,2},{5,4},{6,5},{7,6},{9,8},{10,9},{11,10},{13,12},{... | collective-permute-start | bytes 12296 | tf_op jit(solution)/shard_map/ppermute | solution.py:15
  46.1 14.3 %collective-permute-start.5 = (f32[32,2,512]{2,0,1:T(8,128)}, f32[32,2,512]{2,0,1:T(8,128)}, u32[]{:S(2)}, u32[]{:S(2)}) collective-permute-start(f32[32,2,512]{2,0,1:T(8,128)} %get-tuple-element.27), channel_id=1, source_target_pairs={{0,4},{4,8},{8,12},{12,16},{16,20},{20,24},{24,28},{28,32},{32,36}... | collective-permute-start | bytes 393224 | tf_op jit(solution)/shard_map/ppermute | solution.py:14
  48.0 12.4 %collective-permute-start.4 = (f32[32,2,512]{2,0,1:T(8,128)}, f32[32,2,512]{2,0,1:T(8,128)}, u32[]{:S(2)}, u32[]{:S(2)}) collective-permute-start(f32[32,2,512]{2,0,1:T(8,128)} %get-tuple-element.28), channel_id=1, source_target_pairs={{4,0},{8,4},{12,8},{16,12},{20,16},{24,20},{28,24},{32,28},{36,32}... | collective-permute-start | bytes 393224 | tf_op jit(solution)/shard_map/ppermute | solution.py:15
  56.5 3.0 %copy-start.23 = (f32[8]{0:T(128)S(1)}, f32[8]{0:T(128)}, u32[]{:S(2)}) copy-start(f32[8]{0:T(128)} %param.19) | copy-start | bytes 100
  61.8 1.8 %copy-start.1 = (f32[32,18,512]{2,0,1:T(8,128)}, f32[32,18,512]{2,0,1:T(8,128)S(1)}, u32[]{:S(2)}) copy-start(f32[32,18,512]{2,0,1:T(8,128)S(1)} %fusion.9) | copy-start | bytes 3538948
  63.6 11.9 %copy-start.22 = (s32[64]{0:T(128)S(1)}, s32[64]{0:T(128)}, u32[]{:S(2)}) copy-start(s32[64]{0:T(128)} %get-tuple-element.12) | copy-start | bytes 772
  64.3 17.3 %collective-permute-start.8 = (f32[32,1,512]{2,0,1:T(8,128)}, f32[32,1,512]{2,0,1:T(8,128)}, u32[]{:S(2)}, u32[]{:S(2)}) collective-permute-start(f32[32,1,512]{2,0,1:T(8,128)} %get-tuple-element.23), channel_id=1, source_target_pairs={{4,0},{8,4},{12,8},{16,12},{20,16},{24,20},{28,24},{32,28},{36,32}... | collective-permute-start | bytes 196616 | tf_op jit(solution)/shard_map/ppermute | solution.py:15
  66.2 15.4 %collective-permute-start.9 = (f32[32,1,512]{2,0,1:T(8,128)}, f32[32,1,512]{2,0,1:T(8,128)}, u32[]{:S(2)}, u32[]{:S(2)}) collective-permute-start(f32[32,1,512]{2,0,1:T(8,128)} %get-tuple-element.24), channel_id=1, source_target_pairs={{0,4},{4,8},{8,12},{12,16},{16,20},{20,24},{24,28},{28,32},{32,36}... | collective-permute-start | bytes 196616 | tf_op jit(solution)/shard_map/ppermute | solution.py:14
  70.2 10.0 %collective-permute-start.10 = (f32[32,16,1]{2,0,1:T(8,128)S(1)}, f32[32,16,1]{2,0,1:T(8,128)S(1)}, u32[]{:S(2)}, u32[]{:S(2)}) collective-permute-start(f32[32,16,1]{2,0,1:T(8,128)S(1)} %get-tuple-element.25), channel_id=1, source_target_pairs={{1,0},{2,1},{3,2},{5,4},{6,5},{7,6},{9,8},{10,9},{11,10},{13,12},{... | collective-permute-start | bytes 6152 | tf_op jit(solution)/shard_map/ppermute | solution.py:15
  71.5 10.1 %collective-permute-start.11 = (f32[32,16,1]{2,0,1:T(8,128)S(1)}, f32[32,16,1]{2,0,1:T(8,128)S(1)}, u32[]{:S(2)}, u32[]{:S(2)}) collective-permute-start(f32[32,16,1]{2,0,1:T(8,128)S(1)} %get-tuple-element.26), channel_id=1, source_target_pairs={{0,1},{1,2},{2,3},{4,5},{5,6},{6,7},{8,9},{9,10},{10,11},{12,13},{... | collective-permute-start | bytes 6152 | tf_op jit(solution)/shard_map/ppermute | solution.py:14
  87.7 65.4 %copy-start.18 = (s32[1,1,64]{2,1,0:T(1,128)S(1)}, s32[1,1,64]{2,1,0:T(1,128)}, u32[]{:S(2)}) copy-start(s32[1,1,64]{2,1,0:T(1,128)} %param.22) | copy-start | bytes 772
  87.7 65.4 %copy-start.20 = (s32[1,1,64,1]{2,3,1,0:T(1,128)S(1)}, s32[1,1,64,1]{2,3,1,0:T(1,128)}, u32[]{:S(2)}) copy-start(s32[1,1,64,1]{2,3,1,0:T(1,128)} %param.20) | copy-start | bytes 772
  87.7 65.4 %copy-start.21 = (pred[64]{0:T(512)(128)(4,1)S(1)}, pred[64]{0:T(512)(128)(4,1)}, u32[]{:S(2)}) copy-start(pred[64]{0:T(512)(128)(4,1)} %get-tuple-element.11) | copy-start | bytes 196
  155.0 3.5 %copy-start.25 = (s32[1,1,64]{2,1,0:T(1,128)S(1)}, s32[1,1,64]{2,1,0:T(1,128)}, u32[]{:S(2)}) copy-start(s32[1,1,64]{2,1,0:T(1,128)} %param.21) | copy-start | bytes 772
  155.0 3.7 %copy-start.2 = (f32[2048,128]{1,0:T(8,128)S(1)}, f32[2048,128]{1,0:T(8,128)}, u32[]{:S(2)}) copy-start(f32[2048,128]{1,0:T(8,128)} %all-gather.6.cloned.1.call-done) | copy-start | bytes 3145732
  155.0 4.3 %copy-start.6 = (s32[1,16,512]{2,1,0:T(8,128)S(1)}, s32[1,16,512]{2,1,0:T(8,128)}, u32[]{:S(2)}) copy-start(s32[1,16,512]{2,1,0:T(8,128)} %param.15) | copy-start | bytes 98308
  (12 other events, 11.5 us)
Sparse Core Ops, SparseCore 0:
  18.4 69.0 all-gather.7
  89.9 63.1 all-gather.5

commit v2 on v1

--- a/solution.py
+++ b/solution.py
@@ -96,7 +96,6 @@
     targets = pair_target[0, 0]
     target_tile = pair_tile[0, 0, :, 0]
     is_atmos = lax.axis_index("sec") == 0
-    me = lax.axis_index("gx")
 
     own_st = surface_temp[0].reshape(cell_count)
     own_wet = wetness.reshape(cell_count)
@@ -111,21 +110,6 @@
     ocean_st = jnp.where(is_atmos, got[0], own_st)
     ocean_wet = jnp.where(is_atmos, got[1], own_wet)
 
-    pad = jnp.zeros((out_width - pair_count,), jnp.float32)
-    table = jnp.concatenate(
-        [
-            ocean_st.reshape(out_blocks, out_width),
-            ocean_wet.reshape(out_blocks, out_width),
-            jnp.concatenate([target_tile.astype(jnp.float32), pad])[None],
-            jnp.concatenate([targets.astype(jnp.float32), pad])[None],
-        ]
-    )
-    tables = lax.all_gather(table, "gx")
-    st_blocks = tables[:, :out_blocks].reshape(tile_count * out_blocks, out_width)
-    wet_blocks = tables[:, out_blocks:2 * out_blocks].reshape(tile_count * out_blocks, out_width)
-    all_tiles = tables[:, 2 * out_blocks, :pair_count].reshape(tile_count * pair_count).astype(jnp.int32)
-    all_targets = tables[:, 2 * out_blocks + 1, :pair_count].reshape(tile_count * pair_count).astype(jnp.int32)
-
     fluxes = jnp.tanh(jnp.dot(flux_coef, atmos_drivers, precision=HIGHEST_PRECISION)).astype(jnp.bfloat16)
     flux_count = fluxes.shape[0]
     blocks = fluxes.reshape(flux_count, in_blocks, in_width)
@@ -136,18 +120,45 @@
     heat = jnp.einsum(
         "f,pfo->po", heat_gain, regridded.astype(jnp.float32), precision=HIGHEST_PRECISION
     )
-    heats = lax.all_gather(heat, "gx").reshape(tile_count * pair_count, out_width)
 
-    own_match = (all_tiles[None, :] == me) & (all_targets[None, :] == jnp.arange(out_blocks)[:, None])
-    heating = jnp.dot(own_match.astype(jnp.float32), heats, precision=HIGHEST_PRECISION)
-    ocean_temp = own_st + own_wet * heating.reshape(cell_count)
+    capacity = max(2, 2 * pair_count // tile_count)
+    slot_count = tile_count * capacity
+    positions = jnp.arange(pair_count)
+    same_tile = target_tile[None, :] == target_tile[:, None]
+    is_before = positions[None, :] < positions[:, None]
+    earlier = jnp.sum(same_tile & is_before, axis=1)
+    slot_of = target_tile * capacity + earlier
+    placing = jnp.arange(slot_count)[:, None] == slot_of[None, :]
+    outgoing = jnp.dot(placing.astype(jnp.float32), heat, precision=HIGHEST_PRECISION)
+    offsets = jnp.sum(jnp.where(placing, targets[None, :] + 1, 0), axis=1) - 1
+    offset_row = jnp.zeros((tile_count, 1, out_width), jnp.float32).at[:, 0, :capacity].set(
+        offsets.reshape(tile_count, capacity).astype(jnp.float32)
+    )
+    packet = jnp.concatenate([outgoing.reshape(tile_count, capacity, out_width), offset_row], axis=1)
+    arrived = lax.all_to_all(packet, "gx", split_axis=0, concat_axis=0, tiled=True)
+    arrived_at = arrived[:, capacity, :capacity].reshape(slot_count).astype(jnp.int32)
+    landing = jnp.arange(out_blocks)[:, None] == arrived_at[None, :]
+    heating = jnp.dot(
+        landing.astype(jnp.float32),
+        arrived[:, :capacity].reshape(slot_count, out_width),
+        precision=HIGHEST_PRECISION,
+    )
+    ocean_temp = ocean_st + ocean_wet * heating.reshape(cell_count)
 
-    pair_match = (all_tiles[None, :] == target_tile[:, None]) & (all_targets[None, :] == targets[:, None])
-    pair_heating = jnp.dot(pair_match.astype(jnp.float32), heats, precision=HIGHEST_PRECISION)
-    rows = target_tile * out_blocks + targets
-    pair_temp = jnp.take(st_blocks, rows, axis=0) + jnp.take(wet_blocks, rows, axis=0) * pair_heating
-    returned = pair_temp.astype(jnp.bfloat16)
-    pieces = jnp.einsum("pio,po->pi", weights, returned, preferred_element_type=jnp.float32)
+    returning = jnp.dot(
+        landing.T.astype(jnp.bfloat16),
+        ocean_temp.astype(jnp.bfloat16).reshape(out_blocks, out_width),
+        preferred_element_type=jnp.float32,
+    ).astype(jnp.bfloat16)
+    delivered = lax.all_to_all(
+        returning.reshape(tile_count, capacity, out_width), "gx", split_axis=0, concat_axis=0, tiled=True
+    )
+    per_pair = jnp.dot(
+        placing.T.astype(jnp.bfloat16),
+        delivered.reshape(slot_count, out_width),
+        preferred_element_type=jnp.float32,
+    ).astype(jnp.bfloat16)
+    pieces = jnp.einsum("pio,po->pi", weights, per_pair, preferred_element_type=jnp.float32)
     owning = (jnp.arange(in_blocks)[:, None] == sources[None, :]).astype(jnp.float32)
     atmos_temp = jnp.dot(owning, pieces, precision=HIGHEST_PRECISION)
 

time: 168 us -> 114 us (0.68)
  waiting for transfers between devices: 70.1 us -> 9.67 us
  starting transfers between devices: 37.5 us -> 58.5 us
  between operations: 14.8 us -> 1.39 us
  other arithmetic: 9.72 us -> 7.7 us
    all_gather x2 -> x0, waiting for transfers between devices: 61.2 us -> none  [the longest x1 61.2 us: local(): lax.all_gather(heat, 'gx').reshape(tile_count * pair_count, out_width)]
    all_to_all x0 -> x2, starting transfers between devices: none -> 22.1 us  [the longest x1 13.9 us: local(): lax.all_to_all(packet, 'gx', split_axis=0, concat_axis=0, tiled=True)]
    all_to_all x0 -> x2, waiting for transfers between devices: none -> 4.32 us  [the longest x1 4.32 us: local(): lax.all_to_all(returning.reshape(tile_count, capacity, out_width), 'gx',...]
    ppermute x6, waiting for transfers between devices: 7.35 us -> 3.57 us  [neighbours(): hi = lax.ppermute(head, axis, [(i + 1, i) for i in range(count - 1)])]
    gather x1, local copies, waits for them, and re-layouts: 2.32 us -> 0.6 us  [local(): picked = jnp.take(blocks, sources, axis=1)]
    slice x1, local copies, waits for them, and re-layouts: 1.71 us -> 0.01 us  [local(): arrived[:, :capacity].reshape(slot_count, out_width)]
    dot_general x2, matrix products: 4.73 us -> 6.42 us  [vertical_mix(): jnp.einsum('lm,mxy->lxy', matrix, right_side, precision=HIGHEST_PRECISION)]
    dot_general x3 -> x5, matrix products: 5.83 us -> 4.88 us  [the longest x1 3.38 us: local(): jnp.einsum('pio,po->pi', weights, per_pair, preferred_element_type=jnp.fl...]
  transfers between devices with their start and end apart: 15 -> 15, of which waited for: 5 -> 4; matrix products, arithmetic and copies ran while one was open for 20% -> 29% of each run, Pallas kernels for 0% -> 0%
where the time goes in v2:
time: 114 us; the launch traced here: 112 us
  starting transfers between devices  58.5 us (51%)
  local copies, waits for them, and re-layouts  19.6 us (17%)
  matrix products  15.1 us (13%)
  waiting for transfers between devices  9.67 us (8%)
  other arithmetic  7.7 us (7%)
  between operations  1.39 us (1%)
    ppermute x6, starting transfers between devices, neighbours(): lo = lax.ppermute(tail, axis, [(i, i + 1) for i in range(count - 1)])  22.8 us
    all_to_all x1, starting transfers between devices, local(): lax.all_to_all(packet, 'gx', split_axis=0, concat_axis=0, tiled=True)  13.9 us
    ppermute x6, starting transfers between devices, neighbours(): hi = lax.ppermute(head, axis, [(i + 1, i) for i in range(count - 1)])  9.86 us
    unnamed x54, local copies, waits for them, and re-layouts  8.46 us
    all_to_all x1, starting transfers between devices, local(): lax.all_to_all(returning.reshape(tile_count, capacity, out_width), 'gx',...  8.15 us
    dot_general x2, matrix products, vertical_mix(): jnp.einsum('lm,mxy->lxy', matrix, right_side, precision=HIGHEST_PRECISION)  6.42 us
    all_to_all x1, waiting for transfers between devices, local(): lax.all_to_all(returning.reshape(tile_count, capacity, out_width), 'gx',...  4.32 us
    ppermute x1, starting transfers between devices, local(): got = lax.ppermute(sent, 'sec', [(0, 1), (1, 0)])  3.74 us
  transfers between devices with their start and end apart: 15, of which 4 were waited for; matrix products, arithmetic and copies ran while one was open for 29% of the time, Pallas kernels for 0%

profile of v2, /device:TPU:1, one launch (start us, length us, event | category | flops | bytes accessed | tf_op | source)
XLA Modules:
  0.0 112.0 jit_solution(15795774354128952918)
XLA Ops:
  4.1 3.7 %collective-permute-start.12 = (f32[4,8192]{1,0:T(4,128)}, f32[4,8192]{1,0:T(4,128)}, u32[]{:S(2)}, u32[]{:S(2)}) collective-permute-start(f32[4,8192]{1,0:T(4,128)} %maximum_select_fusion), channel_id=1, source_target_pairs={{0,128},{128,0},{1,129},{129,1},{2,130},{130,2},{3,131},{131,3},{4... | collective-permute-start | bytes 393224 | tf_op jit(solution)/shard_map/ppermute | solution.py:108
  8.0 3.2 %fusion.74 = (f32[1,1,32,16,512]{4,3,2,1,0:T(8,128)}, f32[1,1,32,16,512]{4,3,2,1,0:T(8,128)S(1)}, f32[1,1,32,16,512]{4,3,2,1,0:T(8,128)S(1)}) fusion(f32[1,3,32,16,512]{4,3,2,1,0:T(8,128)} %param.13), kind=kLoop, calls=%fused_computation.127 | loop fusion | bytes 6291456 | tf_op jit(solution)/shard_map/slice | solution.py:78
  12.0 3.1 %collective-permute-start.3 = (f32[33,16,1]{2,0,1:T(8,128)S(1)}, f32[33,16,1]{2,0,1:T(8,128)S(1)}, u32[]{:S(2)}, u32[]{:S(2)}) collective-permute-start(f32[33,16,1]{2,0,1:T(8,128)S(1)} %pad_maximum_fusion.11), channel_id=1, source_target_pairs={{0,1},{1,2},{2,3},{4,5},{5,6},{6,7},{8,9},{9,10},{10,11},{12,13},{... | collective-permute-start | bytes 6344 | tf_op jit(solution)/shard_map/ppermute | solution.py:14
  15.2 1.3 %collective-permute-start.2 = (f32[33,16,1]{2,0,1:T(8,128)S(1)}, f32[33,16,1]{2,0,1:T(8,128)}, u32[]{:S(2)}, u32[]{:S(2)}) collective-permute-start(f32[33,16,1]{2,0,1:T(8,128)S(1)} %pad_maximum_fusion.10), channel_id=1, source_target_pairs={{1,0},{2,1},{3,2},{5,4},{6,5},{7,6},{9,8},{10,9},{11,10},{13,12},{... | collective-permute-start | bytes 6344 | tf_op jit(solution)/shard_map/ppermute | solution.py:15
  17.2 3.4 %collective-permute-start.1 = (f32[33,1,512]{2,0,1:T(8,128)S(1)}, f32[33,1,512]{2,0,1:T(8,128)}, u32[]{:S(2)}, u32[]{:S(2)}) collective-permute-start(f32[33,1,512]{2,0,1:T(8,128)S(1)} %pad_maximum_fusion.15), channel_id=1, source_target_pairs={{0,4},{4,8},{8,12},{12,16},{16,20},{20,24},{24,28},{28,32},{32,36}... | collective-permute-start | bytes 202760 | tf_op jit(solution)/shard_map/ppermute | solution.py:14
  20.6 1.9 %collective-permute-start = (f32[33,1,512]{2,0,1:T(8,128)S(1)}, f32[33,1,512]{2,0,1:T(8,128)S(1)}, u32[]{:S(2)}, u32[]{:S(2)}) collective-permute-start(f32[33,1,512]{2,0,1:T(8,128)S(1)} %pad_maximum_fusion.14), channel_id=1, source_target_pairs={{4,0},{8,4},{12,8},{16,12},{20,16},{24,20},{28,24},{32,28},{36,32}... | collective-permute-start | bytes 202760 | tf_op jit(solution)/shard_map/ppermute | solution.py:15
  25.1 0.8 slice.252
  26.2 1.0 slice.241
  27.2 0.8 slice.238
  28.7 4.6 %fusion.6 = f32[32,16,512]{2,0,1:T(8,128)S(1)} fusion(f32[32,16,512]{2,0,1:T(8,128)S(1)} %bitcast.111, f32[32,16,1]{2,0,1:T(8,128)S(1)} %slice.244, f32[32,16,1]{2,0,1:T(8,128)S(1)} %slice.241, f32[32,16,512]{2,0,1:T(8,128)S(1)} %bitcast.114, f32[32,1,512]{2,0,1:T(8,128)S(1)} %slice.238, f32[32,1,512]{2,0,1:T(8,128)S(1)} %slice.235, ...), kind=kOutput, calls=%fused_computation.11 | convolution fusion | flops 105644032 | bytes 4366336 | tf_op jit(solution)/shard_map/lm,mxy->lxy/dot_general | solution.py:20
  34.1 3.5 %collective-permute-start.7 = (f32[32,16,2]{2,0,1:T(8,128)S(1)}, f32[32,16,2]{2,0,1:T(8,128)S(1)}, u32[]{:S(2)}, u32[]{:S(2)}) collective-permute-start(f32[32,16,2]{2,0,1:T(8,128)S(1)} %get-tuple-element.36), channel_id=1, source_target_pairs={{0,1},{1,2},{2,3},{4,5},{5,6},{6,7},{8,9},{9,10},{10,11},{12,13},{... | collective-permute-start | bytes 12296 | tf_op jit(solution)/shard_map/ppermute | solution.py:14
  37.6 1.3 %collective-permute-start.6 = (f32[32,16,2]{2,0,1:T(8,128)S(1)}, f32[32,16,2]{2,0,1:T(8,128)S(1)}, u32[]{:S(2)}, u32[]{:S(2)}) collective-permute-start(f32[32,16,2]{2,0,1:T(8,128)S(1)} %get-tuple-element.37), channel_id=1, source_target_pairs={{1,0},{2,1},{3,2},{5,4},{6,5},{7,6},{9,8},{10,9},{11,10},{13,12},{... | collective-permute-start | bytes 12296 | tf_op jit(solution)/shard_map/ppermute | solution.py:15
  40.4 4.3 %collective-permute-start.5 = (f32[32,2,512]{2,0,1:T(8,128)}, f32[32,2,512]{2,0,1:T(8,128)}, u32[]{:S(2)}, u32[]{:S(2)}) collective-permute-start(f32[32,2,512]{2,0,1:T(8,128)} %get-tuple-element.34), channel_id=1, source_target_pairs={{0,4},{4,8},{8,12},{12,16},{16,20},{20,24},{24,28},{28,32},{32,36}... | collective-permute-start | bytes 393224 | tf_op jit(solution)/shard_map/ppermute | solution.py:14
  44.7 1.9 %collective-permute-start.4 = (f32[32,2,512]{2,0,1:T(8,128)}, f32[32,2,512]{2,0,1:T(8,128)}, u32[]{:S(2)}, u32[]{:S(2)}) collective-permute-start(f32[32,2,512]{2,0,1:T(8,128)} %get-tuple-element.35), channel_id=1, source_target_pairs={{4,0},{8,4},{12,8},{16,12},{20,16},{24,20},{28,24},{32,28},{36,32}... | collective-permute-start | bytes 393224 | tf_op jit(solution)/shard_map/ppermute | solution.py:15
  46.7 1.9 %fusion.7 = f32[32,16,514]{2,0,1:T(8,128)} fusion(f32[32,16,1]{2,0,1:T(8,128)S(1)} %slice.241, f32[32,16,512]{2,0,1:T(8,128)S(1)} %bitcast.112, f32[32,16,1]{2,0,1:T(8,128)S(1)} %slice.244, f32[32,16,2]{2,0,1:T(8,128)S(1)} %collective-permute-done.6, f32[32,16,512]{2,0,1:T(8,128)S(1)} %fusion.6, f32[32,16,2]{2,0,1:T(8,128)S(1)} %collective-permute-done.7, ...), kind=kLoop, calls=%fused_computation.13 | loop fusion | flops 2105344 | bytes 3195008 | tf_op jit(solution)/shard_map/mul | solution.py:49
  49.7 2.9 %fusion.11 = bf16[64,8,128]{2,1,0:T(8,128)(2,1)S(1)} fusion(bf16[1,1,64,256,128]{4,3,2,1,0:T(8,128)(2,1)} %param.23, bf16[64,8,256]{2,1,0:T(8,128)(2,1)S(1)} %gather_fusion, pred[64]{0:T(512)(128)(4,1)S(1)} %compare_and_fusion), kind=kOutput, calls=%fused_computation.20 | convolution fusion | flops 33751040 | bytes 4587584 | tf_op jit(solution)/shard_map/fpi,pio->pfo/dot_general | solution.py:117
  53.9 13.9 %all-to-all-start = ((f32[32,5,128]{2,1,0:T(8,128)}), f32[32,5,128]{2,1,0:T(8,128)S(1)}, u32[]{:S(2)}, u32[]{:S(2)}) async-start(f32[32,5,128]{2,1,0:T(8,128)} %pad_maximum_fusion.13), calls=%async_computation | async-start | bytes 262144 | tf_op jit(solution)/shard_map/all_to_all | solution.py:138
  67.9 1.4 %fusion.9 = f32[32,18,512]{2,0,1:T(8,128)S(1)} fusion(f32[32,1,512]{2,0,1:T(8,128)S(1)} %slice.235, f32[32,16,512]{2,0,1:T(8,128)S(1)} %bitcast.115, f32[32,1,512]{2,0,1:T(8,128)S(1)} %slice.238, f32[32,2,512]{2,0,1:T(8,128)} %collective-permute-done.4, f32[32,16,512]{2,0,1:T(8,128)S(1)} %fusion.6, f32[32,2,512]{2,0,1:T(8,128)} %collective-permute-done.5, ...), kind=kLoop, calls=%fused_computation.17 | loop fusion | flops 2359296 | bytes 3706880 | tf_op jit(solution)/shard_map/mul | solution.py:48
  69.3 1.9 %fusion.5 = f32[32,16,512]{2,0,1:T(8,128)S(1)} fusion(f32[32,16,512]{2,0,1:T(8,128)S(1)} %fusion.6, f32[32,16,514]{2,0,1:T(8,128)S(1)} %copy-done.1, f32[32,18,512]{2,0,1:T(8,128)S(1)} %fusion.9, f32[16,512]{1,0:T(8,128)S(1)} %bitcast.143, f32[1,32,32]{2,1,0:T(8,128)S(1)} %copy-done), kind=kOutput, calls=%fused_computation.9 | convolution fusion | flops 103546880 | bytes 11616256 | tf_op jit(solution)/shard_map/lm,mxy->lxy/dot_general | solution.py:20
  71.4 2.1 %collective-permute-start.8 = (f32[32,1,512]{2,0,1:T(8,128)S(1)}, f32[32,1,512]{2,0,1:T(8,128)S(1)}, u32[]{:S(2)}, u32[]{:S(2)}) collective-permute-start(f32[32,1,512]{2,0,1:T(8,128)S(1)} %get-tuple-element.30), channel_id=1, source_target_pairs={{4,0},{8,4},{12,8},{16,12},{20,16},{24,20},{28,24},{32,28},{36,32}... | collective-permute-start | bytes 196616 | tf_op jit(solution)/shard_map/ppermute | solution.py:15
  73.5 3.6 %collective-permute-start.9 = (f32[32,1,512]{2,0,1:T(8,128)S(1)}, f32[32,1,512]{2,0,1:T(8,128)S(1)}, u32[]{:S(2)}, u32[]{:S(2)}) collective-permute-start(f32[32,1,512]{2,0,1:T(8,128)S(1)} %get-tuple-element.31), channel_id=1, source_target_pairs={{0,4},{4,8},{8,12},{12,16},{16,20},{20,24},{24,28},{28,32},{32,36}... | collective-permute-start | bytes 196616 | tf_op jit(solution)/shard_map/ppermute | solution.py:14
  77.1 1.3 %collective-permute-start.10 = (f32[32,16,1]{2,0,1:T(8,128)S(1)}, f32[32,16,1]{2,0,1:T(8,128)S(1)}, u32[]{:S(2)}, u32[]{:S(2)}) collective-permute-start(f32[32,16,1]{2,0,1:T(8,128)S(1)} %get-tuple-element.32), channel_id=1, source_target_pairs={{1,0},{2,1},{3,2},{5,4},{6,5},{7,6},{9,8},{10,9},{11,10},{13,12},{... | collective-permute-start | bytes 6152 | tf_op jit(solution)/shard_map/ppermute | solution.py:15
  78.4 4.9 %collective-permute-start.11 = (f32[32,16,1]{2,0,1:T(8,128)S(1)}, f32[32,16,1]{2,0,1:T(8,128)S(1)}, u32[]{:S(2)}, u32[]{:S(2)}) collective-permute-start(f32[32,16,1]{2,0,1:T(8,128)S(1)} %get-tuple-element.33), channel_id=1, source_target_pairs={{0,1},{1,2},{2,3},{4,5},{5,6},{6,7},{8,9},{9,10},{10,11},{12,13},{... | collective-permute-start | bytes 6152 | tf_op jit(solution)/shard_map/ppermute | solution.py:14
  83.4 1.0 fusion.81
  84.4 2.8 %collective-permute-done.10 = f32[32,16,1]{2,0,1:T(8,128)S(1)} collective-permute-done((f32[32,16,1]{2,0,1:T(8,128)S(1)}, f32[32,16,1]{2,0,1:T(8,128)S(1)}, u32[]{:S(2)}, u32[]{:S(2)}) %collective-permute-start.10) | collective-permute-done | bytes 2080 | tf_op jit(solution)/shard_map/ppermute | solution.py:15
  87.2 1.8 %collective-permute-done.11 = f32[32,16,1]{2,0,1:T(8,128)S(1)} collective-permute-done((f32[32,16,1]{2,0,1:T(8,128)S(1)}, f32[32,16,1]{2,0,1:T(8,128)S(1)}, u32[]{:S(2)}, u32[]{:S(2)}) %collective-permute-start.11) | collective-permute-done | bytes 2080 | tf_op jit(solution)/shard_map/ppermute | solution.py:14
  88.9 1.1 fusion.24
  90.4 0.8 convolution_convert_fusion
  91.2 8.2 %all-to-all-start.1 = ((bf16[32,4,128]{2,1,0:T(4,128)(2,1)}), bf16[32,4,128]{2,1,0:T(4,128)(2,1)S(1)}, u32[]{:S(2)}, u32[]{:S(2)}) async-start(bf16[32,4,128]{2,1,0:T(4,128)(2,1)} %bitcast.31), calls=%async_computation.1 | async-start | bytes 65536 | tf_op jit(solution)/shard_map/all_to_all | solution.py:153
  99.7 3.5 %copy.49 = f32[1,3,32,16,512]{4,3,2,1,0:T(8,128)} copy(f32[1,3,32,16,512]{4,2,3,1,0:T(8,128)S(1)} %maximum_bitcast_fusion) | data formatting | bytes 6291456
  103.2 4.3 %all-to-all-done.1 = bf16[32,4,128]{2,1,0:T(4,128)(2,1)S(1)} async-done(((bf16[32,4,128]{2,1,0:T(4,128)(2,1)}), bf16[32,4,128]{2,1,0:T(4,128)(2,1)S(1)}, u32[]{:S(2)}, u32[]{:S(2)}) %all-to-all-start.1) | async-done | bytes 32800 | tf_op jit(solution)/shard_map/all_to_all | solution.py:153
  107.7 3.4 %fusion.1 = f32[64,1,256]{2,1,0:T(1,128)S(1)} fusion(bf16[1,1,64,256,128]{4,3,2,1,0:T(8,128)(2,1)} %param.23, bf16[64,128,1]{1,0,2:T(8,128)(2,1)S(1)} %fusion.14), kind=kOutput, calls=%fused_computation.3 | convolution fusion | flops 4194304 | bytes 4276224 | tf_op jit(solution)/shard_map/pio,po->pi/dot_general | solution.py:161
  (113 shorter events, 15.0 us)
Async XLA Ops:
  0.6 28.0 %copy-start = (f32[1,32,32]{2,1,0:T(8,128)S(1)}, f32[1,32,32]{2,1,0:T(8,128)}, u32[]{:S(2)}) copy-start(f32[1,32,32]{2,1,0:T(8,128)} %param.16) | copy-start | bytes 12292
  2.2 8.9 %copy-start.5 = (f32[1,1,16,512]{3,1,2,0:T(1,128)}, f32[1,1,16,512]{3,1,2,0:T(1,128)S(1)}, u32[]{:S(2)}) copy-start(f32[1,1,16,512]{3,1,2,0:T(1,128)S(1)} %copy.63) | copy-start | bytes 98308
  3.1 8.1 %copy-start.7 = (f32[1,1,16,512]{3,1,2,0:T(1,128)}, f32[1,1,16,512]{3,1,2,0:T(1,128)S(1)}, u32[]{:S(2)}) copy-start(f32[1,1,16,512]{3,1,2,0:T(1,128)S(1)} %copy.60) | copy-start | bytes 98308
  3.2 8.0 %copy-start.9 = (f32[1,1,16,512]{3,1,2,0:T(1,128)}, f32[1,1,16,512]{3,1,2,0:T(1,128)S(1)}, u32[]{:S(2)}) copy-start(f32[1,1,16,512]{3,1,2,0:T(1,128)S(1)} %copy.62) | copy-start | bytes 98308
  3.2 8.0 %copy-start.11 = (f32[1,1,16,512]{3,1,2,0:T(1,128)}, f32[1,1,16,512]{3,1,2,0:T(1,128)S(1)}, u32[]{:S(2)}) copy-start(f32[1,1,16,512]{3,1,2,0:T(1,128)S(1)} %copy.61) | copy-start | bytes 98308
  4.1 44.4 %collective-permute-start.12 = (f32[4,8192]{1,0:T(4,128)}, f32[4,8192]{1,0:T(4,128)}, u32[]{:S(2)}, u32[]{:S(2)}) collective-permute-start(f32[4,8192]{1,0:T(4,128)} %maximum_select_fusion), channel_id=1, source_target_pairs={{0,128},{128,0},{1,129},{129,1},{2,130},{130,2},{3,131},{131,3},{4... | collective-permute-start | bytes 393224 | tf_op jit(solution)/shard_map/ppermute | solution.py:108
  12.0 12.3 %collective-permute-start.3 = (f32[33,16,1]{2,0,1:T(8,128)S(1)}, f32[33,16,1]{2,0,1:T(8,128)S(1)}, u32[]{:S(2)}, u32[]{:S(2)}) collective-permute-start(f32[33,16,1]{2,0,1:T(8,128)S(1)} %pad_maximum_fusion.11), channel_id=1, source_target_pairs={{0,1},{1,2},{2,3},{4,5},{5,6},{6,7},{8,9},{9,10},{10,11},{12,13},{... | collective-permute-start | bytes 6344 | tf_op jit(solution)/shard_map/ppermute | solution.py:14
  15.2 10.0 %collective-permute-start.2 = (f32[33,16,1]{2,0,1:T(8,128)S(1)}, f32[33,16,1]{2,0,1:T(8,128)}, u32[]{:S(2)}, u32[]{:S(2)}) collective-permute-start(f32[33,16,1]{2,0,1:T(8,128)S(1)} %pad_maximum_fusion.10), channel_id=1, source_target_pairs={{1,0},{2,1},{3,2},{5,4},{6,5},{7,6},{9,8},{10,9},{11,10},{13,12},{... | collective-permute-start | bytes 6344 | tf_op jit(solution)/shard_map/ppermute | solution.py:15
  16.5 6.1 %copy-start.16 = (s32[1,1,64]{2,1,0:T(1,128)S(1)}, s32[1,1,64]{2,1,0:T(1,128)}, u32[]{:S(2)}) copy-start(s32[1,1,64]{2,1,0:T(1,128)} %param.21) | copy-start | bytes 772
  16.5 6.1 %copy-start.19 = (s32[1,1,64]{2,1,0:T(1,128)S(1)}, s32[1,1,64]{2,1,0:T(1,128)}, u32[]{:S(2)}) copy-start(s32[1,1,64]{2,1,0:T(1,128)} %param.22) | copy-start | bytes 772
  16.5 6.1 %copy-start.20 = (s32[1,1,64,1]{2,3,1,0:T(1,128)S(1)}, s32[1,1,64,1]{2,3,1,0:T(1,128)}, u32[]{:S(2)}) copy-start(s32[1,1,64,1]{2,3,1,0:T(1,128)} %param.20) | copy-start | bytes 772
  16.5 7.1 %copy-start.2 = (f32[1,16,512]{2,1,0:T(8,128)S(1)}, f32[1,16,512]{2,1,0:T(8,128)}, u32[]{:S(2)}) copy-start(f32[1,16,512]{2,1,0:T(8,128)} %param.17) | copy-start | bytes 98308
  17.1 11.5 %copy-start.17 = (f32[1,16,512]{2,1,0:T(8,128)S(1)}, f32[1,16,512]{2,1,0:T(8,128)}, u32[]{:S(2)}) copy-start(f32[1,16,512]{2,1,0:T(8,128)} %param.14) | copy-start | bytes 98308
  17.2 10.0 %collective-permute-start.1 = (f32[33,1,512]{2,0,1:T(8,128)S(1)}, f32[33,1,512]{2,0,1:T(8,128)}, u32[]{:S(2)}, u32[]{:S(2)}) collective-permute-start(f32[33,1,512]{2,0,1:T(8,128)S(1)} %pad_maximum_fusion.15), channel_id=1, source_target_pairs={{0,4},{4,8},{8,12},{12,16},{16,20},{20,24},{24,28},{28,32},{32,36}... | collective-permute-start | bytes 202760 | tf_op jit(solution)/shard_map/ppermute | solution.py:14
  20.6 7.4 %collective-permute-start = (f32[33,1,512]{2,0,1:T(8,128)S(1)}, f32[33,1,512]{2,0,1:T(8,128)S(1)}, u32[]{:S(2)}, u32[]{:S(2)}) collective-permute-start(f32[33,1,512]{2,0,1:T(8,128)S(1)} %pad_maximum_fusion.14), channel_id=1, source_target_pairs={{4,0},{8,4},{12,8},{16,12},{20,16},{24,20},{28,24},{32,28},{36,32}... | collective-permute-start | bytes 202760 | tf_op jit(solution)/shard_map/ppermute | solution.py:15
  34.1 12.5 %collective-permute-start.7 = (f32[32,16,2]{2,0,1:T(8,128)S(1)}, f32[32,16,2]{2,0,1:T(8,128)S(1)}, u32[]{:S(2)}, u32[]{:S(2)}) collective-permute-start(f32[32,16,2]{2,0,1:T(8,128)S(1)} %get-tuple-element.36), channel_id=1, source_target_pairs={{0,1},{1,2},{2,3},{4,5},{5,6},{6,7},{8,9},{9,10},{10,11},{12,13},{... | collective-permute-start | bytes 12296 | tf_op jit(solution)/shard_map/ppermute | solution.py:14
  37.6 9.0 %collective-permute-start.6 = (f32[32,16,2]{2,0,1:T(8,128)S(1)}, f32[32,16,2]{2,0,1:T(8,128)S(1)}, u32[]{:S(2)}, u32[]{:S(2)}) collective-permute-start(f32[32,16,2]{2,0,1:T(8,128)S(1)} %get-tuple-element.37), channel_id=1, source_target_pairs={{1,0},{2,1},{3,2},{5,4},{6,5},{7,6},{9,8},{10,9},{11,10},{13,12},{... | collective-permute-start | bytes 12296 | tf_op jit(solution)/shard_map/ppermute | solution.py:15
  40.4 27.5 %collective-permute-start.5 = (f32[32,2,512]{2,0,1:T(8,128)}, f32[32,2,512]{2,0,1:T(8,128)}, u32[]{:S(2)}, u32[]{:S(2)}) collective-permute-start(f32[32,2,512]{2,0,1:T(8,128)} %get-tuple-element.34), channel_id=1, source_target_pairs={{0,4},{4,8},{8,12},{12,16},{16,20},{20,24},{24,28},{28,32},{32,36}... | collective-permute-start | bytes 393224 | tf_op jit(solution)/shard_map/ppermute | solution.py:14
  44.7 23.2 %collective-permute-start.4 = (f32[32,2,512]{2,0,1:T(8,128)}, f32[32,2,512]{2,0,1:T(8,128)}, u32[]{:S(2)}, u32[]{:S(2)}) collective-permute-start(f32[32,2,512]{2,0,1:T(8,128)} %get-tuple-element.35), channel_id=1, source_target_pairs={{4,0},{8,4},{12,8},{16,12},{20,16},{24,20},{28,24},{32,28},{36,32}... | collective-permute-start | bytes 393224 | tf_op jit(solution)/shard_map/ppermute | solution.py:15
  46.6 2.0 %copy-start.6 = (f32[1,1,16,512]{3,1,2,0:T(1,128)S(1)}, f32[1,1,16,512]{3,1,2,0:T(1,128)}, u32[]{:S(2)}) copy-start(f32[1,1,16,512]{3,1,2,0:T(1,128)} %copy-done.5) | copy-start | bytes 98308
  46.6 2.0 %copy-start.8 = (f32[1,1,16,512]{3,1,2,0:T(1,128)S(1)}, f32[1,1,16,512]{3,1,2,0:T(1,128)}, u32[]{:S(2)}) copy-start(f32[1,1,16,512]{3,1,2,0:T(1,128)} %copy-done.7) | copy-start | bytes 98308
  46.6 2.0 %copy-start.10 = (f32[1,1,16,512]{3,1,2,0:T(1,128)S(1)}, f32[1,1,16,512]{3,1,2,0:T(1,128)}, u32[]{:S(2)}) copy-start(f32[1,1,16,512]{3,1,2,0:T(1,128)} %copy-done.9) | copy-start | bytes 98308
  46.6 2.0 %copy-start.12 = (f32[1,1,16,512]{3,1,2,0:T(1,128)S(1)}, f32[1,1,16,512]{3,1,2,0:T(1,128)}, u32[]{:S(2)}) copy-start(f32[1,1,16,512]{3,1,2,0:T(1,128)} %copy-done.11) | copy-start | bytes 98308
  49.7 2.9 %copy-start.15 = (f32[8]{0:T(128)S(1)}, f32[8]{0:T(128)}, u32[]{:S(2)}) copy-start(f32[8]{0:T(128)} %param.19) | copy-start | bytes 100
  53.9 36.1 %all-to-all-start = ((f32[32,5,128]{2,1,0:T(8,128)}), f32[32,5,128]{2,1,0:T(8,128)S(1)}, u32[]{:S(2)}, u32[]{:S(2)}) async-start(f32[32,5,128]{2,1,0:T(8,128)} %pad_maximum_fusion.13), calls=%async_computation | async-start | bytes 262144 | tf_op jit(solution)/shard_map/all_to_all | solution.py:138
  71.2 17.7 %copy-start.3 = (f32[1,16,512]{2,1,0:T(8,128)S(1)}, f32[1,16,512]{2,1,0:T(8,128)}, u32[]{:S(2)}) copy-start(f32[1,16,512]{2,1,0:T(8,128)} %copy.90) | copy-start | bytes 98308
  71.4 17.5 %collective-permute-start.8 = (f32[32,1,512]{2,0,1:T(8,128)S(1)}, f32[32,1,512]{2,0,1:T(8,128)S(1)}, u32[]{:S(2)}, u32[]{:S(2)}) collective-permute-start(f32[32,1,512]{2,0,1:T(8,128)S(1)} %get-tuple-element.30), channel_id=1, source_target_pairs={{4,0},{8,4},{12,8},{16,12},{20,16},{24,20},{28,24},{32,28},{36,32}... | collective-permute-start | bytes 196616 | tf_op jit(solution)/shard_map/ppermute | solution.py:15
  73.5 15.4 %collective-permute-start.9 = (f32[32,1,512]{2,0,1:T(8,128)S(1)}, f32[32,1,512]{2,0,1:T(8,128)S(1)}, u32[]{:S(2)}, u32[]{:S(2)}) collective-permute-start(f32[32,1,512]{2,0,1:T(8,128)S(1)} %get-tuple-element.31), channel_id=1, source_target_pairs={{0,4},{4,8},{8,12},{12,16},{16,20},{20,24},{24,28},{28,32},{32,36}... | collective-permute-start | bytes 196616 | tf_op jit(solution)/shard_map/ppermute | solution.py:14
  77.1 10.0 %collective-permute-start.10 = (f32[32,16,1]{2,0,1:T(8,128)S(1)}, f32[32,16,1]{2,0,1:T(8,128)S(1)}, u32[]{:S(2)}, u32[]{:S(2)}) collective-permute-start(f32[32,16,1]{2,0,1:T(8,128)S(1)} %get-tuple-element.32), channel_id=1, source_target_pairs={{1,0},{2,1},{3,2},{5,4},{6,5},{7,6},{9,8},{10,9},{11,10},{13,12},{... | collective-permute-start | bytes 6152 | tf_op jit(solution)/shard_map/ppermute | solution.py:15
  78.4 10.5 %collective-permute-start.11 = (f32[32,16,1]{2,0,1:T(8,128)S(1)}, f32[32,16,1]{2,0,1:T(8,128)S(1)}, u32[]{:S(2)}, u32[]{:S(2)}) collective-permute-start(f32[32,16,1]{2,0,1:T(8,128)S(1)} %get-tuple-element.33), channel_id=1, source_target_pairs={{0,1},{1,2},{2,3},{4,5},{5,6},{6,7},{8,9},{9,10},{10,11},{12,13},{... | collective-permute-start | bytes 6152 | tf_op jit(solution)/shard_map/ppermute | solution.py:14
  91.2 16.3 %all-to-all-start.1 = ((bf16[32,4,128]{2,1,0:T(4,128)(2,1)}), bf16[32,4,128]{2,1,0:T(4,128)(2,1)S(1)}, u32[]{:S(2)}, u32[]{:S(2)}) async-start(bf16[32,4,128]{2,1,0:T(4,128)(2,1)} %bitcast.31), calls=%async_computation.1 | async-start | bytes 65536 | tf_op jit(solution)/shard_map/all_to_all | solution.py:153
  107.7 3.6 %copy-start.4 = (s32[1,16,512]{2,1,0:T(8,128)S(1)}, s32[1,16,512]{2,1,0:T(8,128)}, u32[]{:S(2)}) copy-start(s32[1,16,512]{2,1,0:T(8,128)} %param.15) | copy-start | bytes 98308
  (4 other events, 5.5 us)

commit v3 on v2

--- a/solution.py
+++ b/solution.py
@@ -17,7 +17,7 @@
 
 
 def vertical_mix(matrix, right_side):
-    return right_side + jnp.einsum("lm,mxy->lxy", matrix, right_side, precision=HIGHEST_PRECISION)
+    return right_side + jnp.sum(matrix[:, :, None, None] * right_side[None], axis=1)
 
 
 def stencil(pressure, eastward, northward, sound_speed, wetness, matrix):

time: 114 us -> 129 us (1.13)
  other arithmetic: 7.7 us -> 31.1 us
  waiting for transfers between devices: 9.67 us -> 17.5 us
  matrix products: 15.1 us -> 8.8 us
  local copies, waits for them, and re-layouts: 19.6 us -> 13.9 us
  starting transfers between devices: 58.5 us -> 54.8 us
    reduce_sum x0 -> x2, other arithmetic: none -> 9.56 us  [vertical_mix(): jnp.sum(matrix[:, :, None, None] * right_side[None], axis=1)]
    dot_general x2 -> x0, matrix products: 6.42 us -> none  [vertical_mix(): jnp.einsum('lm,mxy->lxy', matrix, right_side, precision=HIGHEST_PRECISION)]
    ppermute x6, waiting for transfers between devices: 3.57 us -> 9.13 us  [neighbours(): hi = lax.ppermute(head, axis, [(i + 1, i) for i in range(count - 1)])]
    another operation x1, other arithmetic: 1.07 us -> 5.51 us  [local(): final_state = jnp.stack([p2, u2, v2])[None]]
    broadcast_in_dim x1, other arithmetic: 0.31 us -> 4.1 us  [local(): final_state = jnp.stack([p2, u2, v2])[None]]
    unnamed x54 -> x80, local copies, waits for them, and re-layouts: 8.46 us -> 4.68 us
    all_to_all x1, starting transfers between devices: 13.9 us -> 10.3 us  [local(): lax.all_to_all(packet, 'gx', split_axis=0, concat_axis=0, tiled=True)]
    slice x1 -> x0, local copies, waits for them, and re-layouts: 3.2 us -> none  [local(): pressure = model_state[0, 0]]
  transfers between devices with their start and end apart: 15 -> 15, of which waited for: 4 -> 6; matrix products, arithmetic and copies ran while one was open for 29% -> 25% of each run, Pallas kernels for 0% -> 0%
where the time goes in v3:
time: 129 us; the launch traced here: 128 us
  starting transfers between devices  54.8 us (42%)
  other arithmetic  31.1 us (24%)
  waiting for transfers between devices  17.5 us (14%)
  local copies, waits for them, and re-layouts  13.9 us (11%)
  matrix products  8.8 us (7%)
  between operations  1.54 us (1%)
    ppermute x6, starting transfers between devices, neighbours(): lo = lax.ppermute(tail, axis, [(i, i + 1) for i in range(count - 1)])  25 us
    all_to_all x1, starting transfers between devices, local(): lax.all_to_all(packet, 'gx', split_axis=0, concat_axis=0, tiled=True)  10.3 us
    ppermute x6, starting transfers between devices, neighbours(): hi = lax.ppermute(head, axis, [(i + 1, i) for i in range(count - 1)])  9.78 us
    reduce_sum x2, other arithmetic, vertical_mix(): jnp.sum(matrix[:, :, None, None] * right_side[None], axis=1)  9.56 us
    ppermute x6, waiting for transfers between devices, neighbours(): hi = lax.ppermute(head, axis, [(i + 1, i) for i in range(count - 1)])  9.13 us
    all_to_all x1, starting transfers between devices, local(): lax.all_to_all(returning.reshape(tile_count, capacity, out_width), 'gx',...  5.83 us
    another operation x1, other arithmetic, local(): final_state = jnp.stack([p2, u2, v2])[None]  5.51 us
    unnamed x80, local copies, waits for them, and re-layouts  4.68 us
  transfers between devices with their start and end apart: 15, of which 6 were waited for; matrix products, arithmetic and copies ran while one was open for 25% of the time, Pallas kernels for 0%

profile of v3, /device:TPU:1, one launch (start us, length us, event | category | flops | bytes accessed | tf_op | source)
XLA Modules:
  0.0 127.6 jit_solution(1431029846304613386)
XLA Ops:
  1.5 1.4 %convert_bitcast_fusion = (f32[1,1,16,512]{3,2,1,0:T(8,128)S(1)}, f32[16,512]{1,0:T(8,128)}, f32[1,16,512]{2,1,0:T(8,128)S(1)}) fusion(s32[1,16,512]{2,1,0:T(8,128)} %param.15), kind=kLoop, calls=%fused_computation.105 | loop fusion | flops 8192 | bytes 131072
  4.8 3.8 %collective-permute-start.12 = (f32[4,8192]{1,0:T(4,128)}, f32[4,8192]{1,0:T(4,128)}, u32[]{:S(2)}, u32[]{:S(2)}) collective-permute-start(f32[4,8192]{1,0:T(4,128)} %maximum_select_fusion), channel_id=1, source_target_pairs={{0,128},{128,0},{1,129},{129,1},{2,130},{130,2},{3,131},{131,3},{4... | collective-permute-start | bytes 393224 | tf_op jit(solution)/shard_map/ppermute | solution.py:108
  8.6 1.7 %slice_bitcast_fusion.1 = (f32[32,16,512]{2,1,0:T(8,128)S(1)}, f32[32,16,512]{2,1,0:T(8,128)S(1)}) fusion(f32[1,3,32,16,512]{4,3,2,1,0:T(8,128)} %param.13), kind=kLoop, calls=%fused_computation.51 | loop fusion | bytes 4194304 | tf_op jit(solution)/shard_map/squeeze | solution.py:79
  10.6 3.1 %collective-permute-start.1 = (f32[33,1,512]{2,1,0:T(1,128)S(1)}, f32[33,1,512]{2,1,0:T(1,128)S(1)}, u32[]{:S(2)}, u32[]{:S(2)}) collective-permute-start(f32[33,1,512]{2,1,0:T(1,128)S(1)} %pad_maximum_fusion.13), channel_id=1, source_target_pairs={{0,4},{4,8},{8,12},{12,16},{16,20},{20,24},{24,28},{28,32},{32,36}... | collective-permute-start | bytes 202760 | tf_op jit(solution)/shard_map/ppermute | solution.py:14
  14.4 1.9 %collective-permute-start = (f32[33,1,512]{2,1,0:T(1,128)}, f32[33,1,512]{2,1,0:T(1,128)S(1)}, u32[]{:S(2)}, u32[]{:S(2)}) collective-permute-start(f32[33,1,512]{2,1,0:T(1,128)} %pad_maximum_fusion.12), channel_id=1, source_target_pairs={{4,0},{8,4},{12,8},{16,12},{20,16},{24,20},{28,24},{32,28},{36,32}... | collective-permute-start | bytes 202760 | tf_op jit(solution)/shard_map/ppermute | solution.py:15
  16.6 3.1 %collective-permute-start.3 = (f32[33,16,1]{2,1,0:T(8,128)S(1)}, f32[33,16,1]{2,1,0:T(8,128)S(1)}, u32[]{:S(2)}, u32[]{:S(2)}) collective-permute-start(f32[33,16,1]{2,1,0:T(8,128)S(1)} %pad_maximum_fusion.9), channel_id=1, source_target_pairs={{0,1},{1,2},{2,3},{4,5},{5,6},{6,7},{8,9},{9,10},{10,11},{12,13},{... | collective-permute-start | bytes 6344 | tf_op jit(solution)/shard_map/ppermute | solution.py:14
  20.5 1.3 %collective-permute-start.2 = (f32[33,16,1]{2,1,0:T(8,128)}, f32[33,16,1]{2,1,0:T(8,128)S(1)}, u32[]{:S(2)}, u32[]{:S(2)}) collective-permute-start(f32[33,16,1]{2,1,0:T(8,128)} %pad_maximum_fusion.8), channel_id=1, source_target_pairs={{1,0},{2,1},{3,2},{5,4},{6,5},{7,6},{9,8},{10,9},{11,10},{13,12},{... | collective-permute-start | bytes 6344 | tf_op jit(solution)/shard_map/ppermute | solution.py:15
  25.1 5.0 %collective-permute-done.2 = f32[33,16,1]{2,1,0:T(8,128)S(1)} collective-permute-done((f32[33,16,1]{2,1,0:T(8,128)}, f32[33,16,1]{2,1,0:T(8,128)S(1)}, u32[]{:S(2)}, u32[]{:S(2)}) %collective-permute-start.2) | collective-permute-done | bytes 2144 | tf_op jit(solution)/shard_map/ppermute | solution.py:15
  30.4 2.0 %fusion.29 = f32[32,16,512]{2,1,0:T(8,128)S(1)} fusion(f32[32,16,512]{2,1,0:T(8,128)S(1)} %get-tuple-element.22, f32[32,16,1]{2,1,0:T(8,128)S(1)} %slice.244, f32[32,16,1]{2,1,0:T(8,128)S(1)} %slice.241, f32[32,16,512]{2,1,0:T(8,128)S(1)} %get-tuple-element.21, f32[32,1,512]{2,1,0:T(1,128)S(1)} %slice.238, f32[32,1,512]{2,1,0:T(1,128)S(1)} %slice.235, ...), kind=kLoop, calls=%fused_computation.45 | loop fusion | flops 2359296 | bytes 4362240 | tf_op jit(solution)/shard_map/sub | solution.py:42
  32.5 4.8 %multiply_reduce_fusion.1 = f32[32,16,512]{2,1,0:T(8,128)S(1)} fusion(f32[32,16,512]{2,1,0:T(8,128)S(1)} %fusion.29, f32[32,32]{1,0:T(8,128)S(1)} %bitcast.102), kind=kLoop, calls=%fused_computation.2 | loop fusion | flops 16515072 | bytes 2101248 | tf_op jit(solution)/shard_map/reduce_sum | solution.py:20
  38.4 5.5 %collective-permute-start.5 = (f32[32,2,512]{2,1,0:T(2,128)}, f32[32,2,512]{2,1,0:T(2,128)}, u32[]{:S(2)}, u32[]{:S(2)}) collective-permute-start(f32[32,2,512]{2,1,0:T(2,128)} %get-tuple-element.29), channel_id=1, source_target_pairs={{0,4},{4,8},{8,12},{12,16},{16,20},{20,24},{24,28},{28,32},{32,36}... | collective-permute-start | bytes 393224 | tf_op jit(solution)/shard_map/ppermute | solution.py:14
  44.0 1.9 %collective-permute-start.4 = (f32[32,2,512]{2,1,0:T(2,128)}, f32[32,2,512]{2,1,0:T(2,128)}, u32[]{:S(2)}, u32[]{:S(2)}) collective-permute-start(f32[32,2,512]{2,1,0:T(2,128)} %get-tuple-element.30), channel_id=1, source_target_pairs={{4,0},{8,4},{12,8},{16,12},{20,16},{24,20},{28,24},{32,28},{36,32}... | collective-permute-start | bytes 393224 | tf_op jit(solution)/shard_map/ppermute | solution.py:15
  45.9 3.1 %collective-permute-start.7 = (f32[32,16,2]{2,1,0:T(8,128)S(1)}, f32[32,16,2]{2,1,0:T(8,128)S(1)}, u32[]{:S(2)}, u32[]{:S(2)}) collective-permute-start(f32[32,16,2]{2,1,0:T(8,128)S(1)} %get-tuple-element.31), channel_id=1, source_target_pairs={{0,1},{1,2},{2,3},{4,5},{5,6},{6,7},{8,9},{9,10},{10,11},{12,13},{... | collective-permute-start | bytes 12296 | tf_op jit(solution)/shard_map/ppermute | solution.py:14
  49.0 1.5 %collective-permute-start.6 = (f32[32,16,2]{2,1,0:T(8,128)S(1)}, f32[32,16,2]{2,1,0:T(8,128)S(1)}, u32[]{:S(2)}, u32[]{:S(2)}) collective-permute-start(f32[32,16,2]{2,1,0:T(8,128)S(1)} %get-tuple-element.32), channel_id=1, source_target_pairs={{1,0},{2,1},{3,2},{5,4},{6,5},{7,6},{9,8},{10,9},{11,10},{13,12},{... | collective-permute-start | bytes 12296 | tf_op jit(solution)/shard_map/ppermute | solution.py:15
  51.2 1.3 %collective-permute-done.7 = f32[32,16,2]{2,1,0:T(8,128)S(1)} collective-permute-done((f32[32,16,2]{2,1,0:T(8,128)S(1)}, f32[32,16,2]{2,1,0:T(8,128)S(1)}, u32[]{:S(2)}, u32[]{:S(2)}) %collective-permute-start.7) | collective-permute-done | bytes 4128 | tf_op jit(solution)/shard_map/ppermute | solution.py:14
  52.5 4.1 %collective-permute-done.6 = f32[32,16,2]{2,1,0:T(8,128)S(1)} collective-permute-done((f32[32,16,2]{2,1,0:T(8,128)S(1)}, f32[32,16,2]{2,1,0:T(8,128)S(1)}, u32[]{:S(2)}, u32[]{:S(2)}) %collective-permute-start.6) | collective-permute-done | bytes 4128 | tf_op jit(solution)/shard_map/ppermute | solution.py:15
  58.7 3.0 %fusion.9 = bf16[64,8,128]{2,1,0:T(8,128)(2,1)S(1)} fusion(bf16[1,1,64,256,128]{4,3,2,1,0:T(8,128)(2,1)} %param.23, bf16[64,8,256]{2,1,0:T(8,128)(2,1)S(1)} %gather_fusion, pred[64]{0:T(512)(128)(4,1)} %compare_and_fusion), kind=kOutput, calls=%fused_computation.18 | convolution fusion | flops 33751040 | bytes 4587584 | tf_op jit(solution)/shard_map/fpi,pio->pfo/dot_general | solution.py:117
  61.9 1.7 %slice_reduce_fusion.1 = (f32[8192]{0:T(1024)S(1)}, f32[8192]{0:T(1024)S(1)}, f32[1,8192]{1,0:T(1,128)}, f32[1,8192]{1,0:T(1,128)}) fusion(f32[4,8192]{1,0:T(4,128)} %collective-permute-done.12), kind=kLoop, calls=%fused_computation.108 | loop fusion | bytes 196608 | tf_op jit(solution)/shard_map/slice | solution.py:110
  64.0 1.6 %fusion.5 = f32[32,18,512]{2,1,0:T(8,128)S(1)} fusion(f32[32,1,512]{2,1,0:T(1,128)S(1)} %copy-done.7, f32[32,16,512]{2,1,0:T(8,128)S(1)} %copy-done.5, f32[32,1,512]{2,1,0:T(1,128)S(1)} %slice.238, f32[32,2,512]{2,1,0:T(2,128)} %collective-permute-done.4, f32[32,16,512]{2,1,0:T(8,128)S(1)} %add.75, f32[32,2,512]{2,1,0:T(2,128)} %collective-permute-done.5, ...), kind=kLoop, calls=%fused_computation.11 | loop fusion | flops 2359296 | bytes 3706880 | tf_op jit(solution)/shard_map/mul | solution.py:48
  65.6 1.1 copy-done.1
  67.5 4.8 %multiply_reduce_fusion = f32[32,16,512]{2,1,0:T(8,128)S(1)} fusion(f32[32,16,512]{2,1,0:T(8,128)S(1)} %fusion.25, f32[32,32]{1,0:T(8,128)S(1)} %bitcast.103), kind=kLoop, calls=%fused_computation.1 | loop fusion | flops 16515072 | bytes 2101248 | tf_op jit(solution)/shard_map/reduce_sum | solution.py:20
  74.4 1.9 %collective-permute-start.8 = (f32[32,1,512]{2,1,0:T(1,128)}, f32[32,1,512]{2,1,0:T(1,128)S(1)}, u32[]{:S(2)}, u32[]{:S(2)}) collective-permute-start(f32[32,1,512]{2,1,0:T(1,128)} %get-tuple-element.25), channel_id=1, source_target_pairs={{4,0},{8,4},{12,8},{16,12},{20,16},{24,20},{28,24},{32,28},{36,32}... | collective-permute-start | bytes 196616 | tf_op jit(solution)/shard_map/ppermute | solution.py:15
  76.3 5.4 %collective-permute-start.9 = (f32[32,1,512]{2,1,0:T(1,128)}, f32[32,1,512]{2,1,0:T(1,128)S(1)}, u32[]{:S(2)}, u32[]{:S(2)}) collective-permute-start(f32[32,1,512]{2,1,0:T(1,128)} %get-tuple-element.26), channel_id=1, source_target_pairs={{0,4},{4,8},{8,12},{12,16},{16,20},{20,24},{24,28},{28,32},{32,36}... | collective-permute-start | bytes 196616 | tf_op jit(solution)/shard_map/ppermute | solution.py:14
  81.8 1.3 %collective-permute-start.10 = (f32[32,16,1]{2,1,0:T(8,128)}, f32[32,16,1]{2,1,0:T(8,128)S(1)}, u32[]{:S(2)}, u32[]{:S(2)}) collective-permute-start(f32[32,16,1]{2,1,0:T(8,128)} %get-tuple-element.27), channel_id=1, source_target_pairs={{1,0},{2,1},{3,2},{5,4},{6,5},{7,6},{9,8},{10,9},{11,10},{13,12},{... | collective-permute-start | bytes 6152 | tf_op jit(solution)/shard_map/ppermute | solution.py:15
  83.1 4.7 %collective-permute-start.11 = (f32[32,16,1]{2,1,0:T(8,128)}, f32[32,16,1]{2,1,0:T(8,128)}, u32[]{:S(2)}, u32[]{:S(2)}) collective-permute-start(f32[32,16,1]{2,1,0:T(8,128)} %get-tuple-element.28), channel_id=1, source_target_pairs={{0,1},{1,2},{2,3},{4,5},{5,6},{6,7},{8,9},{9,10},{10,11},{12,13},{... | collective-permute-start | bytes 6152 | tf_op jit(solution)/shard_map/ppermute | solution.py:14
  88.5 10.3 %all-to-all-start = ((f32[32,5,128]{2,1,0:T(8,128)}), f32[32,5,128]{2,1,0:T(8,128)S(1)}, u32[]{:S(2)}, u32[]{:S(2)}) async-start(f32[32,5,128]{2,1,0:T(8,128)} %pad_maximum_fusion.11), calls=%async_computation | async-start | bytes 262144 | tf_op jit(solution)/shard_map/all_to_all | solution.py:138
  100.0 5.5 %fusion.22 = (f32[1,32,16,512]{3,2,1,0:T(8,128)}, f32[1,32,16,512]{3,2,1,0:T(8,128)}) fusion(f32[32,16,512]{2,1,0:T(8,128)} %copy-done.3, f32[32,1,512]{2,1,0:T(1,128)} %copy-done.29, f32[32,1,512]{2,1,0:T(1,128)} %copy-done.28, f32[32,18,512]{2,1,0:T(8,128)S(1)} %copy-done.2, f32[16,512]{1,0:T(8,128)S(1)} %copy-done.12, ...), kind=kLoop, calls=%fused_computation.34 | loop fusion | flops 3145728 | bytes 5410816 | tf_op jit(solution)/shard_map/stack | solution.py:86
  105.6 2.4 %all-to-all-done = f32[32,5,128]{2,1,0:T(8,128)S(1)} async-done(((f32[32,5,128]{2,1,0:T(8,128)}), f32[32,5,128]{2,1,0:T(8,128)S(1)}, u32[]{:S(2)}, u32[]{:S(2)}) %all-to-all-start) | async-done | bytes 81952 | tf_op jit(solution)/shard_map/all_to_all | solution.py:138
  109.2 5.8 %all-to-all-start.1 = ((bf16[32,4,128]{2,1,0:T(4,128)(2,1)}), bf16[32,4,128]{2,1,0:T(4,128)(2,1)S(1)}, u32[]{:S(2)}, u32[]{:S(2)}) async-start(bf16[32,4,128]{2,1,0:T(4,128)(2,1)} %bitcast.29), calls=%async_computation.1 | async-start | bytes 65536 | tf_op jit(solution)/shard_map/all_to_all | solution.py:153
  115.1 4.1 %maximum_bitcast_fusion = f32[1,3,32,16,512]{4,3,2,1,0:T(8,128)} fusion(f32[1,32,16,512]{3,2,1,0:T(8,128)} %get-tuple-element.24, f32[1,32,16,512]{3,2,1,0:T(8,128)} %get-tuple-element.23, f32[1,32,16,512]{3,2,1,0:T(8,128)} %bitcast.83), kind=kLoop, calls=%fused_computation.9 | loop fusion | flops 1572864 | bytes 6291456 | tf_op jit(solution)/shard_map/broadcast_in_dim | solution.py:86
  119.2 4.0 %all-to-all-done.1 = bf16[32,4,128]{2,1,0:T(4,128)(2,1)S(1)} async-done(((bf16[32,4,128]{2,1,0:T(4,128)(2,1)}), bf16[32,4,128]{2,1,0:T(4,128)(2,1)S(1)}, u32[]{:S(2)}, u32[]{:S(2)}) %all-to-all-start.1) | async-done | bytes 32800 | tf_op jit(solution)/shard_map/all_to_all | solution.py:153
  123.4 3.4 %fusion.1 = f32[64,1,256]{2,1,0:T(1,128)S(1)} fusion(bf16[1,1,64,256,128]{4,3,2,1,0:T(8,128)(2,1)} %param.23, bf16[64,128,1]{1,0,2:T(8,128)(2,1)S(1)} %fusion.12), kind=kOutput, calls=%fused_computation.5 | convolution fusion | flops 4194304 | bytes 4276224 | tf_op jit(solution)/shard_map/pio,po->pi/dot_general | solution.py:161
  (149 shorter events, 19.3 us)
Async XLA Ops:
  0.6 56.8 %copy-start = (f32[8,4]{0,1:T(4,128)S(1)}, f32[8,4]{0,1:T(4,128)}, u32[]{:S(2)}) copy-start(f32[8,4]{0,1:T(4,128)} %param.18) | copy-start | bytes 388
  4.8 52.7 %collective-permute-start.12 = (f32[4,8192]{1,0:T(4,128)}, f32[4,8192]{1,0:T(4,128)}, u32[]{:S(2)}, u32[]{:S(2)}) collective-permute-start(f32[4,8192]{1,0:T(4,128)} %maximum_select_fusion), channel_id=1, source_target_pairs={{0,128},{128,0},{1,129},{129,1},{2,130},{130,2},{3,131},{131,3},{4... | collective-permute-start | bytes 393224 | tf_op jit(solution)/shard_map/ppermute | solution.py:108
  10.3 20.0 %copy-start.4 = (f32[32,16,512]{2,1,0:T(8,128)}, f32[32,16,512]{2,1,0:T(8,128)S(1)}, u32[]{:S(2)}) copy-start(f32[32,16,512]{2,1,0:T(8,128)S(1)} %get-tuple-element.21) | copy-start | bytes 3145732
  10.3 11.4 %copy-start.34 = (s32[1,1,64]{2,1,0:T(1,128)S(1)}, s32[1,1,64]{2,1,0:T(1,128)}, u32[]{:S(2)}) copy-start(s32[1,1,64]{2,1,0:T(1,128)} %param.21) | copy-start | bytes 772
  10.3 11.9 %copy-start.35 = (s32[1,1,64]{2,1,0:T(1,128)S(1)}, s32[1,1,64]{2,1,0:T(1,128)}, u32[]{:S(2)}) copy-start(s32[1,1,64]{2,1,0:T(1,128)} %param.22) | copy-start | bytes 772
  10.4 11.9 %copy-start.36 = (s32[1,1,64,1]{2,3,1,0:T(1,128)S(1)}, s32[1,1,64,1]{2,3,1,0:T(1,128)}, u32[]{:S(2)}) copy-start(s32[1,1,64,1]{2,3,1,0:T(1,128)} %param.20) | copy-start | bytes 772
  10.4 12.2 %copy-start.8 = (f32[1,16,512]{2,1,0:T(8,128)S(1)}, f32[1,16,512]{2,1,0:T(8,128)}, u32[]{:S(2)}) copy-start(f32[1,16,512]{2,1,0:T(8,128)} %param.17) | copy-start | bytes 98308
  10.6 19.7 %collective-permute-start.1 = (f32[33,1,512]{2,1,0:T(1,128)S(1)}, f32[33,1,512]{2,1,0:T(1,128)S(1)}, u32[]{:S(2)}, u32[]{:S(2)}) collective-permute-start(f32[33,1,512]{2,1,0:T(1,128)S(1)} %pad_maximum_fusion.13), channel_id=1, source_target_pairs={{0,4},{4,8},{8,12},{12,16},{16,20},{20,24},{24,28},{28,32},{32,36}... | collective-permute-start | bytes 202760 | tf_op jit(solution)/shard_map/ppermute | solution.py:14
  14.4 15.9 %collective-permute-start = (f32[33,1,512]{2,1,0:T(1,128)}, f32[33,1,512]{2,1,0:T(1,128)S(1)}, u32[]{:S(2)}, u32[]{:S(2)}) collective-permute-start(f32[33,1,512]{2,1,0:T(1,128)} %pad_maximum_fusion.12), channel_id=1, source_target_pairs={{4,0},{8,4},{12,8},{16,12},{20,16},{24,20},{28,24},{32,28},{36,32}... | collective-permute-start | bytes 202760 | tf_op jit(solution)/shard_map/ppermute | solution.py:15
  16.6 13.8 %copy-start.10 = (f32[1,16,512]{2,1,0:T(8,128)S(1)}, f32[1,16,512]{2,1,0:T(8,128)}, u32[]{:S(2)}) copy-start(f32[1,16,512]{2,1,0:T(8,128)} %param.14) | copy-start | bytes 98308
  16.6 8.5 %collective-permute-start.3 = (f32[33,16,1]{2,1,0:T(8,128)S(1)}, f32[33,16,1]{2,1,0:T(8,128)S(1)}, u32[]{:S(2)}, u32[]{:S(2)}) collective-permute-start(f32[33,16,1]{2,1,0:T(8,128)S(1)} %pad_maximum_fusion.9), channel_id=1, source_target_pairs={{0,1},{1,2},{2,3},{4,5},{5,6},{6,7},{8,9},{9,10},{10,11},{12,13},{... | collective-permute-start | bytes 6344 | tf_op jit(solution)/shard_map/ppermute | solution.py:14
  20.5 9.7 %collective-permute-start.2 = (f32[33,16,1]{2,1,0:T(8,128)}, f32[33,16,1]{2,1,0:T(8,128)S(1)}, u32[]{:S(2)}, u32[]{:S(2)}) collective-permute-start(f32[33,16,1]{2,1,0:T(8,128)} %pad_maximum_fusion.8), channel_id=1, source_target_pairs={{1,0},{2,1},{3,2},{5,4},{6,5},{7,6},{9,8},{10,9},{11,10},{13,12},{... | collective-permute-start | bytes 6344 | tf_op jit(solution)/shard_map/ppermute | solution.py:15
  37.4 13.1 %slice-start = ((f32[33,1,512]{2,1,0:T(1,128)}), f32[1,1,512]{2,1,0:T(1,128)S(1)}, s32[]{:S(2)}) async-start(f32[33,1,512]{2,1,0:T(1,128)} %copy-done.26), calls=%async_computation.2 | async-start | bytes 4096 | tf_op jit(solution)/shard_map/slice | solution.py:37
  37.5 13.1 %slice-start.1 = ((f32[33,1,512]{2,1,0:T(1,128)}), f32[1,1,512]{2,1,0:T(1,128)S(1)}, s32[]{:S(2)}) async-start(f32[33,1,512]{2,1,0:T(1,128)} %copy-done.27), calls=%async_computation.3 | async-start | bytes 4096 | tf_op jit(solution)/shard_map/slice | solution.py:37
  38.4 25.5 %collective-permute-start.5 = (f32[32,2,512]{2,1,0:T(2,128)}, f32[32,2,512]{2,1,0:T(2,128)}, u32[]{:S(2)}, u32[]{:S(2)}) collective-permute-start(f32[32,2,512]{2,1,0:T(2,128)} %get-tuple-element.29), channel_id=1, source_target_pairs={{0,4},{4,8},{8,12},{12,16},{16,20},{20,24},{24,28},{28,32},{32,36}... | collective-permute-start | bytes 393224 | tf_op jit(solution)/shard_map/ppermute | solution.py:14
  44.0 20.0 %collective-permute-start.4 = (f32[32,2,512]{2,1,0:T(2,128)}, f32[32,2,512]{2,1,0:T(2,128)}, u32[]{:S(2)}, u32[]{:S(2)}) collective-permute-start(f32[32,2,512]{2,1,0:T(2,128)} %get-tuple-element.30), channel_id=1, source_target_pairs={{4,0},{8,4},{12,8},{16,12},{20,16},{24,20},{28,24},{32,28},{36,32}... | collective-permute-start | bytes 393224 | tf_op jit(solution)/shard_map/ppermute | solution.py:15
  45.9 6.6 %collective-permute-start.7 = (f32[32,16,2]{2,1,0:T(8,128)S(1)}, f32[32,16,2]{2,1,0:T(8,128)S(1)}, u32[]{:S(2)}, u32[]{:S(2)}) collective-permute-start(f32[32,16,2]{2,1,0:T(8,128)S(1)} %get-tuple-element.31), channel_id=1, source_target_pairs={{0,1},{1,2},{2,3},{4,5},{5,6},{6,7},{8,9},{9,10},{10,11},{12,13},{... | collective-permute-start | bytes 12296 | tf_op jit(solution)/shard_map/ppermute | solution.py:14
  49.0 7.6 %collective-permute-start.6 = (f32[32,16,2]{2,1,0:T(8,128)S(1)}, f32[32,16,2]{2,1,0:T(8,128)S(1)}, u32[]{:S(2)}, u32[]{:S(2)}) collective-permute-start(f32[32,16,2]{2,1,0:T(8,128)S(1)} %get-tuple-element.32), channel_id=1, source_target_pairs={{1,0},{2,1},{3,2},{5,4},{6,5},{7,6},{9,8},{10,9},{11,10},{13,12},{... | collective-permute-start | bytes 12296 | tf_op jit(solution)/shard_map/ppermute | solution.py:15
  51.2 6.3 %copy-start.20 = (f32[1,1,16,512]{3,1,2,0:T(1,128)S(1)}, f32[1,1,16,512]{3,1,2,0:T(1,128)}, u32[]{:S(2)}) copy-start(f32[1,1,16,512]{3,1,2,0:T(1,128)} %copy-done.19) | copy-start | bytes 98308
  72.3 15.5 %copy-start.32 = (f32[32,1,128]{2,0,1:T(8,128)S(1)}, f32[32,1,128]{2,0,1:T(8,128)}, u32[]{:S(2)}) copy-start(f32[32,1,128]{2,0,1:T(8,128)} %scatter.4) | copy-start | bytes 49156
  72.5 27.5 %copy-start.2 = (f32[32,18,512]{2,1,0:T(8,128)S(1)}, f32[32,18,512]{2,1,0:T(8,128)}, u32[]{:S(2)}) copy-start(f32[32,18,512]{2,1,0:T(8,128)} %copy-done.1) | copy-start | bytes 3538948
  72.5 27.5 %copy-start.12 = (f32[16,512]{1,0:T(8,128)S(1)}, f32[16,512]{1,0:T(8,128)}, u32[]{:S(2)}) copy-start(f32[16,512]{1,0:T(8,128)} %get-tuple-element.40) | copy-start | bytes 98308
  74.4 24.3 %collective-permute-start.8 = (f32[32,1,512]{2,1,0:T(1,128)}, f32[32,1,512]{2,1,0:T(1,128)S(1)}, u32[]{:S(2)}, u32[]{:S(2)}) collective-permute-start(f32[32,1,512]{2,1,0:T(1,128)} %get-tuple-element.25), channel_id=1, source_target_pairs={{4,0},{8,4},{12,8},{16,12},{20,16},{24,20},{28,24},{32,28},{36,32}... | collective-permute-start | bytes 196616 | tf_op jit(solution)/shard_map/ppermute | solution.py:15
  76.3 22.4 %collective-permute-start.9 = (f32[32,1,512]{2,1,0:T(1,128)}, f32[32,1,512]{2,1,0:T(1,128)S(1)}, u32[]{:S(2)}, u32[]{:S(2)}) collective-permute-start(f32[32,1,512]{2,1,0:T(1,128)} %get-tuple-element.26), channel_id=1, source_target_pairs={{0,4},{4,8},{8,12},{12,16},{16,20},{20,24},{24,28},{28,32},{32,36}... | collective-permute-start | bytes 196616 | tf_op jit(solution)/shard_map/ppermute | solution.py:14
  81.8 17.0 %collective-permute-start.10 = (f32[32,16,1]{2,1,0:T(8,128)}, f32[32,16,1]{2,1,0:T(8,128)S(1)}, u32[]{:S(2)}, u32[]{:S(2)}) collective-permute-start(f32[32,16,1]{2,1,0:T(8,128)} %get-tuple-element.27), channel_id=1, source_target_pairs={{1,0},{2,1},{3,2},{5,4},{6,5},{7,6},{9,8},{10,9},{11,10},{13,12},{... | collective-permute-start | bytes 6152 | tf_op jit(solution)/shard_map/ppermute | solution.py:15
  83.1 15.7 %collective-permute-start.11 = (f32[32,16,1]{2,1,0:T(8,128)}, f32[32,16,1]{2,1,0:T(8,128)}, u32[]{:S(2)}, u32[]{:S(2)}) collective-permute-start(f32[32,16,1]{2,1,0:T(8,128)} %get-tuple-element.28), channel_id=1, source_target_pairs={{0,1},{1,2},{2,3},{4,5},{5,6},{6,7},{8,9},{9,10},{10,11},{12,13},{... | collective-permute-start | bytes 6152 | tf_op jit(solution)/shard_map/ppermute | solution.py:14
  88.5 19.5 %all-to-all-start = ((f32[32,5,128]{2,1,0:T(8,128)}), f32[32,5,128]{2,1,0:T(8,128)S(1)}, u32[]{:S(2)}, u32[]{:S(2)}) async-start(f32[32,5,128]{2,1,0:T(8,128)} %pad_maximum_fusion.11), calls=%async_computation | async-start | bytes 262144 | tf_op jit(solution)/shard_map/all_to_all | solution.py:138
  100.0 8.3 %copy-start.22 = (f32[64,128]{1,0:T(8,128)S(1)}, f32[64,128]{1,0:T(8,128)}, u32[]{:S(2)}) copy-start(f32[64,128]{1,0:T(8,128)} %reshape_squeeze.4) | copy-start | bytes 98308
  100.0 8.3 %copy-start.23 = (f32[64,128]{1,0:T(8,128)S(1)}, f32[64,128]{1,0:T(8,128)}, u32[]{:S(2)}) copy-start(f32[64,128]{1,0:T(8,128)} %convert_element_type.80) | copy-start | bytes 98308
  100.0 8.4 %copy-start.24 = (f32[1,8192]{1,0:T(1,128)S(1)}, f32[1,8192]{1,0:T(1,128)}, u32[]{:S(2)}) copy-start(f32[1,8192]{1,0:T(1,128)} %get-tuple-element.37) | copy-start | bytes 98308
  100.0 8.4 %copy-start.25 = (f32[1,8192]{1,0:T(1,128)S(1)}, f32[1,8192]{1,0:T(1,128)}, u32[]{:S(2)}) copy-start(f32[1,8192]{1,0:T(1,128)} %get-tuple-element.38) | copy-start | bytes 98308
  109.2 14.0 %all-to-all-start.1 = ((bf16[32,4,128]{2,1,0:T(4,128)(2,1)}), bf16[32,4,128]{2,1,0:T(4,128)(2,1)S(1)}, u32[]{:S(2)}, u32[]{:S(2)}) async-start(bf16[32,4,128]{2,1,0:T(4,128)(2,1)} %bitcast.29), calls=%async_computation.1 | async-start | bytes 65536 | tf_op jit(solution)/shard_map/all_to_all | solution.py:153
  (22 other events, 63.2 us)

commit v4 on v2

--- a/solution.py
+++ b/solution.py
@@ -14,6 +14,18 @@
     lo = lax.ppermute(tail, axis, [(i, i + 1) for i in range(count - 1)])
     hi = lax.ppermute(head, axis, [(i + 1, i) for i in range(count - 1)])
     return lo, hi
+
+
+def staged_all_to_all(values, inner=4):
+    count = lax.axis_size("gx")
+    outer = count // inner
+    near = [[o * inner + i for i in range(inner)] for o in range(outer)]
+    far = [[o * inner + i for o in range(outer)] for i in range(inner)]
+    rest = values.shape[1:]
+    values = values.reshape(outer, inner, *rest)
+    values = lax.all_to_all(values, "gx", 1, 1, axis_index_groups=near, tiled=True)
+    values = lax.all_to_all(values, "gx", 0, 0, axis_index_groups=far, tiled=True)
+    return values.reshape(count, *rest)
 
 
 def vertical_mix(matrix, right_side):
@@ -135,7 +147,7 @@
         offsets.reshape(tile_count, capacity).astype(jnp.float32)
     )
     packet = jnp.concatenate([outgoing.reshape(tile_count, capacity, out_width), offset_row], axis=1)
-    arrived = lax.all_to_all(packet, "gx", split_axis=0, concat_axis=0, tiled=True)
+    arrived = staged_all_to_all(packet)
     arrived_at = arrived[:, capacity, :capacity].reshape(slot_count).astype(jnp.int32)
     landing = jnp.arange(out_blocks)[:, None] == arrived_at[None, :]
     heating = jnp.dot(
@@ -150,9 +162,7 @@
         ocean_temp.astype(jnp.bfloat16).reshape(out_blocks, out_width),
         preferred_element_type=jnp.float32,
     ).astype(jnp.bfloat16)
-    delivered = lax.all_to_all(
-        returning.reshape(tile_count, capacity, out_width), "gx", split_axis=0, concat_axis=0, tiled=True
-    )
+    delivered = staged_all_to_all(returning.reshape(tile_count, capacity, out_width))
     per_pair = jnp.dot(
         placing.T.astype(jnp.bfloat16),
         delivered.reshape(slot_count, out_width),

time: 114 us -> 126 us (1.11)
  the two profiles are of different devices: /device:TPU:1 before, /device:TPU:6 now
where the time goes in v4:
time: 126 us; the launch traced here: 125 us
  starting transfers between devices  60.8 us (48%)
  local copies, waits for them, and re-layouts  25 us (20%)
  matrix products  14.3 us (11%)
  other arithmetic  12.9 us (10%)
  waiting for transfers between devices  10.7 us (8%)
  between operations  1.36 us (1%)
    all_to_all x2, starting transfers between devices, staged_all_to_all(): lax.all_to_all(values, 'gx', 0, 0, axis_index_groups=far, tiled=True)  19.2 us
    ppermute x6, starting transfers between devices, neighbours(): hi = lax.ppermute(head, axis, [(i + 1, i) for i in range(count - 1)])  15.7 us
    ppermute x6, starting transfers between devices, neighbours(): lo = lax.ppermute(tail, axis, [(i, i + 1) for i in range(count - 1)])  12.2 us
    all_to_all x2, starting transfers between devices, staged_all_to_all(): lax.all_to_all(values, 'gx', 1, 1, axis_index_groups=near, tiled=True)  10.4 us
    unnamed x72, local copies, waits for them, and re-layouts  10.4 us
    dot_general x2, matrix products, vertical_mix(): jnp.einsum('lm,mxy->lxy', matrix, right_side, precision=HIGHEST_PRECISION)  6.19 us
    ppermute x6, waiting for transfers between devices, neighbours(): lo = lax.ppermute(tail, axis, [(i, i + 1) for i in range(count - 1)])  4.03 us
    another operation x1, other arithmetic, local(): final_state = jnp.stack([p2, u2, v2])[None]  3.42 us
  transfers between devices with their start and end apart: 17, of which 4 were waited for; matrix products, arithmetic and copies ran while one was open for 33% of the time, Pallas kernels for 0%

profile of v4, /device:TPU:6, one launch (start us, length us, event | category | flops | bytes accessed | tf_op | source)
XLA Modules:
  0.0 125.1 jit_solution(3257852442935334691)
XLA Ops:
  4.1 3.2 %collective-permute-start.12 = (f32[4,8192]{1,0:T(4,128)}, f32[4,8192]{1,0:T(4,128)}, u32[]{:S(2)}, u32[]{:S(2)}) collective-permute-start(f32[4,8192]{1,0:T(4,128)} %maximum_select_fusion), channel_id=1, source_target_pairs={{0,128},{128,0},{1,129},{129,1},{2,130},{130,2},{3,131},{131,3},{4... | collective-permute-start | bytes 393224 | tf_op jit(solution)/shard_map/ppermute | solution.py:120
  7.4 3.2 %fusion.73 = (f32[1,1,32,16,512]{4,3,2,1,0:T(8,128)}, f32[1,1,32,16,512]{4,3,2,1,0:T(8,128)S(1)}, f32[1,1,32,16,512]{4,3,2,1,0:T(8,128)S(1)}) fusion(f32[1,3,32,16,512]{4,3,2,1,0:T(8,128)} %param.13), kind=kLoop, calls=%fused_computation.126 | loop fusion | bytes 6291456 | tf_op jit(solution)/shard_map/slice | solution.py:90
  11.4 1.3 %collective-permute-start.3 = (f32[33,16,1]{2,0,1:T(8,128)S(1)}, f32[33,16,1]{2,0,1:T(8,128)S(1)}, u32[]{:S(2)}, u32[]{:S(2)}) collective-permute-start(f32[33,16,1]{2,0,1:T(8,128)S(1)} %pad_maximum_fusion.11), channel_id=1, source_target_pairs={{0,1},{1,2},{2,3},{4,5},{5,6},{6,7},{8,9},{9,10},{10,11},{12,13},{... | collective-permute-start | bytes 6344 | tf_op jit(solution)/shard_map/ppermute | solution.py:14
  12.8 5.3 %collective-permute-start.2 = (f32[33,16,1]{2,0,1:T(8,128)S(1)}, f32[33,16,1]{2,0,1:T(8,128)}, u32[]{:S(2)}, u32[]{:S(2)}) collective-permute-start(f32[33,16,1]{2,0,1:T(8,128)S(1)} %pad_maximum_fusion.10), channel_id=1, source_target_pairs={{1,0},{2,1},{3,2},{5,4},{6,5},{7,6},{9,8},{10,9},{11,10},{13,12},{... | collective-permute-start | bytes 6344 | tf_op jit(solution)/shard_map/ppermute | solution.py:15
  18.7 1.9 %collective-permute-start.1 = (f32[33,1,512]{2,0,1:T(8,128)S(1)}, f32[33,1,512]{2,0,1:T(8,128)}, u32[]{:S(2)}, u32[]{:S(2)}) collective-permute-start(f32[33,1,512]{2,0,1:T(8,128)S(1)} %pad_maximum_fusion.14), channel_id=1, source_target_pairs={{0,4},{4,8},{8,12},{12,16},{16,20},{20,24},{24,28},{28,32},{32,36}... | collective-permute-start | bytes 202760 | tf_op jit(solution)/shard_map/ppermute | solution.py:14
  21.3 1.3 %collective-permute-start = (f32[33,1,512]{2,0,1:T(8,128)}, f32[33,1,512]{2,0,1:T(8,128)S(1)}, u32[]{:S(2)}, u32[]{:S(2)}) collective-permute-start(f32[33,1,512]{2,0,1:T(8,128)} %pad_maximum_fusion.13), channel_id=1, source_target_pairs={{4,0},{8,4},{12,8},{16,12},{20,16},{24,20},{28,24},{32,28},{36,32}... | collective-permute-start | bytes 202760 | tf_op jit(solution)/shard_map/ppermute | solution.py:15
  26.4 1.0 slice.241
  28.9 4.4 %fusion.6 = f32[32,16,512]{2,0,1:T(8,128)S(1)} fusion(f32[32,16,512]{2,0,1:T(8,128)S(1)} %bitcast.114, f32[32,16,1]{2,0,1:T(8,128)S(1)} %slice.244, f32[32,16,1]{2,0,1:T(8,128)S(1)} %slice.241, f32[32,16,512]{2,0,1:T(8,128)S(1)} %bitcast.117, f32[32,1,512]{2,0,1:T(8,128)S(1)} %slice.238, f32[32,1,512]{2,0,1:T(8,128)S(1)} %slice.235, ...), kind=kOutput, calls=%fused_computation.11 | convolution fusion | flops 105644032 | bytes 4366336 | tf_op jit(solution)/shard_map/lm,mxy->lxy/dot_general | solution.py:32
  34.1 1.3 %collective-permute-start.7 = (f32[32,16,2]{2,0,1:T(8,128)S(1)}, f32[32,16,2]{2,0,1:T(8,128)S(1)}, u32[]{:S(2)}, u32[]{:S(2)}) collective-permute-start(f32[32,16,2]{2,0,1:T(8,128)S(1)} %get-tuple-element.40), channel_id=1, source_target_pairs={{0,1},{1,2},{2,3},{4,5},{5,6},{6,7},{8,9},{9,10},{10,11},{12,13},{... | collective-permute-start | bytes 12296 | tf_op jit(solution)/shard_map/ppermute | solution.py:14
  35.5 4.6 %collective-permute-start.6 = (f32[32,16,2]{2,0,1:T(8,128)S(1)}, f32[32,16,2]{2,0,1:T(8,128)S(1)}, u32[]{:S(2)}, u32[]{:S(2)}) collective-permute-start(f32[32,16,2]{2,0,1:T(8,128)S(1)} %get-tuple-element.41), channel_id=1, source_target_pairs={{1,0},{2,1},{3,2},{5,4},{6,5},{7,6},{9,8},{10,9},{11,10},{13,12},{... | collective-permute-start | bytes 12296 | tf_op jit(solution)/shard_map/ppermute | solution.py:15
  42.1 3.4 %collective-permute-start.5 = (f32[32,2,512]{2,0,1:T(8,128)}, f32[32,2,512]{2,0,1:T(8,128)}, u32[]{:S(2)}, u32[]{:S(2)}) collective-permute-start(f32[32,2,512]{2,0,1:T(8,128)} %get-tuple-element.38), channel_id=1, source_target_pairs={{0,4},{4,8},{8,12},{12,16},{16,20},{20,24},{24,28},{28,32},{32,36}... | collective-permute-start | bytes 393224 | tf_op jit(solution)/shard_map/ppermute | solution.py:14
  45.5 1.3 %collective-permute-start.4 = (f32[32,2,512]{2,0,1:T(8,128)}, f32[32,2,512]{2,0,1:T(8,128)}, u32[]{:S(2)}, u32[]{:S(2)}) collective-permute-start(f32[32,2,512]{2,0,1:T(8,128)} %get-tuple-element.39), channel_id=1, source_target_pairs={{4,0},{8,4},{12,8},{16,12},{20,16},{24,20},{28,24},{32,28},{36,32}... | collective-permute-start | bytes 393224 | tf_op jit(solution)/shard_map/ppermute | solution.py:15
  46.9 1.9 %fusion.7 = f32[32,16,514]{2,0,1:T(8,128)} fusion(f32[32,16,1]{2,0,1:T(8,128)S(1)} %slice.241, f32[32,16,512]{2,0,1:T(8,128)S(1)} %bitcast.115, f32[32,16,1]{2,0,1:T(8,128)S(1)} %slice.244, f32[32,16,2]{2,0,1:T(8,128)S(1)} %collective-permute-done.6, f32[32,16,512]{2,0,1:T(8,128)S(1)} %fusion.6, f32[32,16,2]{2,0,1:T(8,128)S(1)} %collective-permute-done.7, ...), kind=kLoop, calls=%fused_computation.13 | loop fusion | flops 2105344 | bytes 3195008 | tf_op jit(solution)/shard_map/mul | solution.py:61
  50.1 2.9 %fusion.11 = bf16[64,8,128]{2,1,0:T(8,128)(2,1)S(1)} fusion(bf16[1,1,64,256,128]{4,3,2,1,0:T(8,128)(2,1)} %param.23, bf16[64,8,256]{2,1,0:T(8,128)(2,1)S(1)} %gather_fusion, pred[64]{0:T(512)(128)(4,1)S(1)} %copy-done.25), kind=kOutput, calls=%fused_computation.20 | convolution fusion | flops 33751040 | bytes 4587584 | tf_op jit(solution)/shard_map/fpi,pio->pfo/dot_general | solution.py:129
  54.3 6.8 %all-to-all-start = ((f32[8,4,5,128]{3,0,2,1:T(8,128)}), f32[8,4,5,128]{3,0,2,1:T(8,128)S(1)}, u32[]{:S(2)}, u32[]{:S(2)}) async-start(f32[8,4,5,128]{3,0,2,1:T(8,128)} %pad_maximum_fusion.15), calls=%async_computation | async-start | bytes 163840 | tf_op jit(solution)/shard_map/all_to_all | solution.py:26
  61.0 1.0 fusion.80
  62.1 3.3 %all-to-all-done = f32[8,4,5,128]{3,0,2,1:T(8,128)S(1)} async-done(((f32[8,4,5,128]{3,0,2,1:T(8,128)}), f32[8,4,5,128]{3,0,2,1:T(8,128)S(1)}, u32[]{:S(2)}, u32[]{:S(2)}) %all-to-all-start) | async-done | bytes 81952 | tf_op jit(solution)/shard_map/all_to_all | solution.py:26
  66.0 12.3 %all-to-all-start.1 = ((f32[8,4,5,128]{3,1,2,0:T(4,128)}), f32[8,4,5,128]{3,1,2,0:T(4,128)S(1)}, u32[]{:S(2)}, u32[]{:S(2)}) async-start(f32[8,4,5,128]{3,1,2,0:T(4,128)} %copy.93), calls=%async_computation.1 | async-start | bytes 163840 | tf_op jit(solution)/shard_map/all_to_all | solution.py:27
  78.4 1.4 %fusion.9 = f32[32,18,512]{2,0,1:T(8,128)S(1)} fusion(f32[32,1,512]{2,0,1:T(8,128)S(1)} %slice.235, f32[32,16,512]{2,0,1:T(8,128)S(1)} %bitcast.118, f32[32,1,512]{2,0,1:T(8,128)S(1)} %slice.238, f32[32,2,512]{2,0,1:T(8,128)} %collective-permute-done.4, f32[32,16,512]{2,0,1:T(8,128)S(1)} %fusion.6, f32[32,2,512]{2,0,1:T(8,128)} %collective-permute-done.5, ...), kind=kLoop, calls=%fused_computation.17 | loop fusion | flops 2359296 | bytes 3706880 | tf_op jit(solution)/shard_map/mul | solution.py:60
  79.8 1.8 %fusion.5 = f32[32,16,512]{2,0,1:T(8,128)S(1)} fusion(f32[32,16,512]{2,0,1:T(8,128)S(1)} %fusion.6, f32[32,16,514]{2,0,1:T(8,128)S(1)} %copy-done.1, f32[32,18,512]{2,0,1:T(8,128)S(1)} %fusion.9, f32[16,512]{1,0:T(8,128)S(1)} %bitcast.149, f32[1,32,32]{2,1,0:T(8,128)S(1)} %copy-done), kind=kOutput, calls=%fused_computation.9 | convolution fusion | flops 103546880 | bytes 11616256 | tf_op jit(solution)/shard_map/lm,mxy->lxy/dot_general | solution.py:32
  82.3 1.3 %collective-permute-start.8 = (f32[32,1,512]{2,0,1:T(8,128)}, f32[32,1,512]{2,0,1:T(8,128)S(1)}, u32[]{:S(2)}, u32[]{:S(2)}) collective-permute-start(f32[32,1,512]{2,0,1:T(8,128)} %get-tuple-element.34), channel_id=1, source_target_pairs={{4,0},{8,4},{12,8},{16,12},{20,16},{24,20},{28,24},{32,28},{36,32}... | collective-permute-start | bytes 196616 | tf_op jit(solution)/shard_map/ppermute | solution.py:15
  83.6 3.0 %collective-permute-start.9 = (f32[32,1,512]{2,0,1:T(8,128)}, f32[32,1,512]{2,0,1:T(8,128)S(1)}, u32[]{:S(2)}, u32[]{:S(2)}) collective-permute-start(f32[32,1,512]{2,0,1:T(8,128)} %get-tuple-element.35), channel_id=1, source_target_pairs={{0,4},{4,8},{8,12},{12,16},{16,20},{20,24},{24,28},{28,32},{32,36}... | collective-permute-start | bytes 196616 | tf_op jit(solution)/shard_map/ppermute | solution.py:14
  87.5 2.0 %collective-permute-start.10 = (f32[32,16,1]{2,0,1:T(8,128)}, f32[32,16,1]{2,0,1:T(8,128)S(1)}, u32[]{:S(2)}, u32[]{:S(2)}) collective-permute-start(f32[32,16,1]{2,0,1:T(8,128)} %get-tuple-element.36), channel_id=1, source_target_pairs={{1,0},{2,1},{3,2},{5,4},{6,5},{7,6},{9,8},{10,9},{11,10},{13,12},{... | collective-permute-start | bytes 6152 | tf_op jit(solution)/shard_map/ppermute | solution.py:15
  89.6 1.3 %collective-permute-start.11 = (f32[32,16,1]{2,0,1:T(8,128)}, f32[32,16,1]{2,0,1:T(8,128)S(1)}, u32[]{:S(2)}, u32[]{:S(2)}) collective-permute-start(f32[32,16,1]{2,0,1:T(8,128)} %get-tuple-element.37), channel_id=1, source_target_pairs={{0,1},{1,2},{2,3},{4,5},{5,6},{6,7},{8,9},{9,10},{10,11},{12,13},{... | collective-permute-start | bytes 6152 | tf_op jit(solution)/shard_map/ppermute | solution.py:14
  92.1 3.7 %all-to-all-start.2 = ((bf16[8,4,4,128]{3,2,0,1:T(4,128)(2,1)}), bf16[8,4,4,128]{3,2,0,1:T(4,128)(2,1)S(1)}, u32[]{:S(2)}, u32[]{:S(2)}) async-start(bf16[8,4,4,128]{3,2,0,1:T(4,128)(2,1)} %copy.96), calls=%async_computation.2 | async-start | bytes 65536 | tf_op jit(solution)/shard_map/all_to_all | solution.py:26
  96.1 4.0 %collective-permute-done.11 = f32[32,16,1]{2,0,1:T(8,128)S(1)} collective-permute-done((f32[32,16,1]{2,0,1:T(8,128)}, f32[32,16,1]{2,0,1:T(8,128)S(1)}, u32[]{:S(2)}, u32[]{:S(2)}) %collective-permute-start.11) | collective-permute-done | bytes 2080 | tf_op jit(solution)/shard_map/ppermute | solution.py:14
  101.5 3.4 %fusion.24 = (f32[1,32,16,512]{3,1,2,0:T(8,128)S(1)}, f32[1,32,16,512]{3,1,2,0:T(8,128)}) fusion(f32[32,16,512]{2,0,1:T(8,128)S(1)} %fusion.5, f32[32,1,512]{2,0,1:T(8,128)} %copy-done.17, f32[32,1,512]{2,0,1:T(8,128)} %copy-done.16, f32[32,18,512]{2,0,1:T(8,128)} %copy-done.3, f32[16,512]{1,0:T(8,128)} %bitcast.134, f32[32,16,1]{2,0,1:T(8,128)} %copy-done.8, ...), kind=kLoop, calls=%fused_computation.36 | loop fusion | flops 3145728 | bytes 5410816 | tf_op jit(solution)/shard_map/stack | solution.py:98
  105.6 6.9 %all-to-all-start.3 = ((bf16[8,4,4,128]{3,2,1,0:T(4,128)(2,1)}), bf16[8,4,4,128]{3,2,1,0:T(4,128)(2,1)S(1)}, u32[]{:S(2)}, u32[]{:S(2)}) async-start(bf16[8,4,4,128]{3,2,1,0:T(4,128)(2,1)} %copy.97), calls=%async_computation.3 | async-start | bytes 65536 | tf_op jit(solution)/shard_map/all_to_all | solution.py:27
  112.5 1.5 %maximum_bitcast_fusion = f32[1,3,32,16,512]{4,2,3,1,0:T(8,128)S(1)} fusion(f32[1,32,16,512]{3,1,2,0:T(8,128)} %get-tuple-element.33, f32[1,32,16,512]{3,1,2,0:T(8,128)S(1)} %get-tuple-element.32, f32[1,32,16,512]{3,1,2,0:T(8,128)S(1)} %bitcast.112), kind=kLoop, calls=%fused_computation.7 | loop fusion | flops 1572864 | bytes 6291456 | tf_op jit(solution)/shard_map/broadcast_in_dim | solution.py:98
  114.0 3.5 %copy.99 = f32[1,3,32,16,512]{4,3,2,1,0:T(8,128)} copy(f32[1,3,32,16,512]{4,2,3,1,0:T(8,128)S(1)} %maximum_bitcast_fusion) | data formatting | bytes 6291456
  117.5 3.0 %all-to-all-done.3 = bf16[8,4,4,128]{3,2,1,0:T(4,128)(2,1)S(1)} async-done(((bf16[8,4,4,128]{3,2,1,0:T(4,128)(2,1)}), bf16[8,4,4,128]{3,2,1,0:T(4,128)(2,1)S(1)}, u32[]{:S(2)}, u32[]{:S(2)}) %all-to-all-start.3) | async-done | bytes 32800 | tf_op jit(solution)/shard_map/all_to_all | solution.py:27
  120.7 3.4 %fusion.1 = f32[64,1,256]{2,1,0:T(1,128)S(1)} fusion(bf16[1,1,64,256,128]{4,3,2,1,0:T(8,128)(2,1)} %param.23, bf16[64,128,1]{1,0,2:T(8,128)(2,1)S(1)} %fusion.14), kind=kOutput, calls=%fused_computation.3 | convolution fusion | flops 4194304 | bytes 4276224 | tf_op jit(solution)/shard_map/pio,po->pi/dot_general | solution.py:171
  (142 shorter events, 23.2 us)
Async XLA Ops:
  0.6 28.3 %copy-start = (f32[1,32,32]{2,1,0:T(8,128)S(1)}, f32[1,32,32]{2,1,0:T(8,128)}, u32[]{:S(2)}) copy-start(f32[1,32,32]{2,1,0:T(8,128)} %param.16) | copy-start | bytes 12292
  3.1 4.2 %copy-start.11 = (f32[1,1,16,512]{3,1,2,0:T(1,128)}, f32[1,1,16,512]{3,1,2,0:T(1,128)S(1)}, u32[]{:S(2)}) copy-start(f32[1,1,16,512]{3,1,2,0:T(1,128)S(1)} %copy.112) | copy-start | bytes 98308
  3.2 4.1 %copy-start.13 = (f32[1,1,16,512]{3,1,2,0:T(1,128)}, f32[1,1,16,512]{3,1,2,0:T(1,128)S(1)}, u32[]{:S(2)}) copy-start(f32[1,1,16,512]{3,1,2,0:T(1,128)S(1)} %copy.111) | copy-start | bytes 98308
  4.1 44.7 %collective-permute-start.12 = (f32[4,8192]{1,0:T(4,128)}, f32[4,8192]{1,0:T(4,128)}, u32[]{:S(2)}, u32[]{:S(2)}) collective-permute-start(f32[4,8192]{1,0:T(4,128)} %maximum_select_fusion), channel_id=1, source_target_pairs={{0,128},{128,0},{1,129},{129,1},{2,130},{130,2},{3,131},{131,3},{4... | collective-permute-start | bytes 393224 | tf_op jit(solution)/shard_map/ppermute | solution.py:120
  11.4 13.9 %collective-permute-start.3 = (f32[33,16,1]{2,0,1:T(8,128)S(1)}, f32[33,16,1]{2,0,1:T(8,128)S(1)}, u32[]{:S(2)}, u32[]{:S(2)}) collective-permute-start(f32[33,16,1]{2,0,1:T(8,128)S(1)} %pad_maximum_fusion.11), channel_id=1, source_target_pairs={{0,1},{1,2},{2,3},{4,5},{5,6},{6,7},{8,9},{9,10},{10,11},{12,13},{... | collective-permute-start | bytes 6344 | tf_op jit(solution)/shard_map/ppermute | solution.py:14
  12.8 12.6 %collective-permute-start.2 = (f32[33,16,1]{2,0,1:T(8,128)S(1)}, f32[33,16,1]{2,0,1:T(8,128)}, u32[]{:S(2)}, u32[]{:S(2)}) collective-permute-start(f32[33,16,1]{2,0,1:T(8,128)S(1)} %pad_maximum_fusion.10), channel_id=1, source_target_pairs={{1,0},{2,1},{3,2},{5,4},{6,5},{7,6},{9,8},{10,9},{11,10},{13,12},{... | collective-permute-start | bytes 6344 | tf_op jit(solution)/shard_map/ppermute | solution.py:15
  18.0 4.5 %copy-start.20 = (s32[1,1,64]{2,1,0:T(1,128)S(1)}, s32[1,1,64]{2,1,0:T(1,128)}, u32[]{:S(2)}) copy-start(s32[1,1,64]{2,1,0:T(1,128)} %param.21) | copy-start | bytes 772
  18.0 5.0 %copy-start.28 = (s32[1,1,64]{2,1,0:T(1,128)S(1)}, s32[1,1,64]{2,1,0:T(1,128)}, u32[]{:S(2)}) copy-start(s32[1,1,64]{2,1,0:T(1,128)} %param.22) | copy-start | bytes 772
  18.0 5.0 %copy-start.29 = (s32[1,1,64,1]{2,3,1,0:T(1,128)S(1)}, s32[1,1,64,1]{2,3,1,0:T(1,128)}, u32[]{:S(2)}) copy-start(s32[1,1,64,1]{2,3,1,0:T(1,128)} %param.20) | copy-start | bytes 772
  18.0 6.6 %copy-start.4 = (f32[1,16,512]{2,1,0:T(8,128)S(1)}, f32[1,16,512]{2,1,0:T(8,128)}, u32[]{:S(2)}) copy-start(f32[1,16,512]{2,1,0:T(8,128)} %param.17) | copy-start | bytes 98308
  18.7 8.7 %collective-permute-start.1 = (f32[33,1,512]{2,0,1:T(8,128)S(1)}, f32[33,1,512]{2,0,1:T(8,128)}, u32[]{:S(2)}, u32[]{:S(2)}) collective-permute-start(f32[33,1,512]{2,0,1:T(8,128)S(1)} %pad_maximum_fusion.14), channel_id=1, source_target_pairs={{0,4},{4,8},{8,12},{12,16},{16,20},{20,24},{24,28},{28,32},{32,36}... | collective-permute-start | bytes 202760 | tf_op jit(solution)/shard_map/ppermute | solution.py:14
  21.3 7.0 %collective-permute-start = (f32[33,1,512]{2,0,1:T(8,128)}, f32[33,1,512]{2,0,1:T(8,128)S(1)}, u32[]{:S(2)}, u32[]{:S(2)}) collective-permute-start(f32[33,1,512]{2,0,1:T(8,128)} %pad_maximum_fusion.13), channel_id=1, source_target_pairs={{4,0},{8,4},{12,8},{16,12},{20,16},{24,20},{28,24},{32,28},{36,32}... | collective-permute-start | bytes 202760 | tf_op jit(solution)/shard_map/ppermute | solution.py:15
  34.1 12.7 %collective-permute-start.7 = (f32[32,16,2]{2,0,1:T(8,128)S(1)}, f32[32,16,2]{2,0,1:T(8,128)S(1)}, u32[]{:S(2)}, u32[]{:S(2)}) collective-permute-start(f32[32,16,2]{2,0,1:T(8,128)S(1)} %get-tuple-element.40), channel_id=1, source_target_pairs={{0,1},{1,2},{2,3},{4,5},{5,6},{6,7},{8,9},{9,10},{10,11},{12,13},{... | collective-permute-start | bytes 12296 | tf_op jit(solution)/shard_map/ppermute | solution.py:14
  35.5 11.4 %collective-permute-start.6 = (f32[32,16,2]{2,0,1:T(8,128)S(1)}, f32[32,16,2]{2,0,1:T(8,128)S(1)}, u32[]{:S(2)}, u32[]{:S(2)}) collective-permute-start(f32[32,16,2]{2,0,1:T(8,128)S(1)} %get-tuple-element.41), channel_id=1, source_target_pairs={{1,0},{2,1},{3,2},{5,4},{6,5},{7,6},{9,8},{10,9},{11,10},{13,12},{... | collective-permute-start | bytes 12296 | tf_op jit(solution)/shard_map/ppermute | solution.py:15
  42.1 36.2 %collective-permute-start.5 = (f32[32,2,512]{2,0,1:T(8,128)}, f32[32,2,512]{2,0,1:T(8,128)}, u32[]{:S(2)}, u32[]{:S(2)}) collective-permute-start(f32[32,2,512]{2,0,1:T(8,128)} %get-tuple-element.38), channel_id=1, source_target_pairs={{0,4},{4,8},{8,12},{12,16},{16,20},{20,24},{24,28},{28,32},{32,36}... | collective-permute-start | bytes 393224 | tf_op jit(solution)/shard_map/ppermute | solution.py:14
  45.5 32.8 %collective-permute-start.4 = (f32[32,2,512]{2,0,1:T(8,128)}, f32[32,2,512]{2,0,1:T(8,128)}, u32[]{:S(2)}, u32[]{:S(2)}) collective-permute-start(f32[32,2,512]{2,0,1:T(8,128)} %get-tuple-element.39), channel_id=1, source_target_pairs={{4,0},{8,4},{12,8},{16,12},{20,16},{24,20},{28,24},{32,28},{36,32}... | collective-permute-start | bytes 393224 | tf_op jit(solution)/shard_map/ppermute | solution.py:15
  50.1 28.3 %copy-start.9 = (f32[1,18,512]{2,1,0:T(8,128)S(1)}, f32[1,18,512]{2,1,0:T(8,128)}, u32[]{:S(2)}) copy-start(f32[1,18,512]{2,1,0:T(8,128)} %copy.138) | copy-start | bytes 110596
  54.3 11.1 %all-to-all-start = ((f32[8,4,5,128]{3,0,2,1:T(8,128)}), f32[8,4,5,128]{3,0,2,1:T(8,128)S(1)}, u32[]{:S(2)}, u32[]{:S(2)}) async-start(f32[8,4,5,128]{3,0,2,1:T(8,128)} %pad_maximum_fusion.15), calls=%async_computation | async-start | bytes 163840 | tf_op jit(solution)/shard_map/all_to_all | solution.py:26
  62.1 29.2 %copy-start.5 = (f32[1,8192]{1,0:T(1,128)}, f32[1,8192]{1,0:T(1,128)S(1)}, u32[]{:S(2)}) copy-start(f32[1,8192]{1,0:T(1,128)S(1)} %get-tuple-element.47) | copy-start | bytes 98308
  66.0 24.9 %all-to-all-start.1 = ((f32[8,4,5,128]{3,1,2,0:T(4,128)}), f32[8,4,5,128]{3,1,2,0:T(4,128)S(1)}, u32[]{:S(2)}, u32[]{:S(2)}) async-start(f32[8,4,5,128]{3,1,2,0:T(4,128)} %copy.93), calls=%async_computation.1 | async-start | bytes 163840 | tf_op jit(solution)/shard_map/all_to_all | solution.py:27
  81.6 9.6 %copy-start.15 = (f32[64,128]{1,0:T(8,128)S(1)}, f32[64,128]{1,0:T(8,128)}, u32[]{:S(2)}) copy-start(f32[64,128]{1,0:T(8,128)} %reshape_squeeze.4) | copy-start | bytes 98308
  81.6 19.9 %copy-start.2 = (f32[32,16,514]{2,0,1:T(8,128)S(1)}, f32[32,16,514]{2,0,1:T(8,128)}, u32[]{:S(2)}) copy-start(f32[32,16,514]{2,0,1:T(8,128)} %fusion.7) | copy-start | bytes 3158020
  82.3 17.8 %collective-permute-start.8 = (f32[32,1,512]{2,0,1:T(8,128)}, f32[32,1,512]{2,0,1:T(8,128)S(1)}, u32[]{:S(2)}, u32[]{:S(2)}) collective-permute-start(f32[32,1,512]{2,0,1:T(8,128)} %get-tuple-element.34), channel_id=1, source_target_pairs={{4,0},{8,4},{12,8},{16,12},{20,16},{24,20},{28,24},{32,28},{36,32}... | collective-permute-start | bytes 196616 | tf_op jit(solution)/shard_map/ppermute | solution.py:15
  83.6 16.6 %collective-permute-start.9 = (f32[32,1,512]{2,0,1:T(8,128)}, f32[32,1,512]{2,0,1:T(8,128)S(1)}, u32[]{:S(2)}, u32[]{:S(2)}) collective-permute-start(f32[32,1,512]{2,0,1:T(8,128)} %get-tuple-element.35), channel_id=1, source_target_pairs={{0,4},{4,8},{8,12},{12,16},{16,20},{20,24},{24,28},{28,32},{32,36}... | collective-permute-start | bytes 196616 | tf_op jit(solution)/shard_map/ppermute | solution.py:14
  87.5 8.6 %collective-permute-start.10 = (f32[32,16,1]{2,0,1:T(8,128)}, f32[32,16,1]{2,0,1:T(8,128)S(1)}, u32[]{:S(2)}, u32[]{:S(2)}) collective-permute-start(f32[32,16,1]{2,0,1:T(8,128)} %get-tuple-element.36), channel_id=1, source_target_pairs={{1,0},{2,1},{3,2},{5,4},{6,5},{7,6},{9,8},{10,9},{11,10},{13,12},{... | collective-permute-start | bytes 6152 | tf_op jit(solution)/shard_map/ppermute | solution.py:15
  89.6 10.6 %collective-permute-start.11 = (f32[32,16,1]{2,0,1:T(8,128)}, f32[32,16,1]{2,0,1:T(8,128)S(1)}, u32[]{:S(2)}, u32[]{:S(2)}) collective-permute-start(f32[32,16,1]{2,0,1:T(8,128)} %get-tuple-element.37), channel_id=1, source_target_pairs={{0,1},{1,2},{2,3},{4,5},{5,6},{6,7},{8,9},{9,10},{10,11},{12,13},{... | collective-permute-start | bytes 6152 | tf_op jit(solution)/shard_map/ppermute | solution.py:14
  92.1 12.8 %all-to-all-start.2 = ((bf16[8,4,4,128]{3,2,0,1:T(4,128)(2,1)}), bf16[8,4,4,128]{3,2,0,1:T(4,128)(2,1)S(1)}, u32[]{:S(2)}, u32[]{:S(2)}) async-start(bf16[8,4,4,128]{3,2,0,1:T(4,128)(2,1)} %copy.96), calls=%async_computation.2 | async-start | bytes 65536 | tf_op jit(solution)/shard_map/all_to_all | solution.py:26
  96.1 4.0 %copy-start.7 = (f32[32,16,1]{2,0,1:T(8,128)}, f32[32,16,1]{2,0,1:T(8,128)S(1)}, u32[]{:S(2)}) copy-start(f32[32,16,1]{2,0,1:T(8,128)S(1)} %collective-permute-done.10) | copy-start | bytes 6148
  105.6 14.9 %all-to-all-start.3 = ((bf16[8,4,4,128]{3,2,1,0:T(4,128)(2,1)}), bf16[8,4,4,128]{3,2,1,0:T(4,128)(2,1)S(1)}, u32[]{:S(2)}, u32[]{:S(2)}) async-start(bf16[8,4,4,128]{3,2,1,0:T(4,128)(2,1)} %copy.97), calls=%async_computation.3 | async-start | bytes 65536 | tf_op jit(solution)/shard_map/all_to_all | solution.py:27
  114.0 6.5 %copy-start.24 = (s32[64]{0:T(128)S(1)}, s32[64]{0:T(128)}, u32[]{:S(2)}) copy-start(s32[64]{0:T(128)} %copy-done.22) | copy-start | bytes 772
  120.7 3.6 %copy-start.6 = (f32[1,8192]{1,0:T(1,128)S(1)}, f32[1,8192]{1,0:T(1,128)}, u32[]{:S(2)}) copy-start(f32[1,8192]{1,0:T(1,128)} %copy-done.5) | copy-start | bytes 98308
  120.7 3.6 %copy-start.10 = (s32[1,16,512]{2,1,0:T(8,128)S(1)}, s32[1,16,512]{2,1,0:T(8,128)}, u32[]{:S(2)}) copy-start(s32[1,16,512]{2,1,0:T(8,128)} %param.15) | copy-start | bytes 98308
  (15 other events, 27.3 us)

commit v5 on v1

--- a/solution.py
+++ b/solution.py
@@ -62,41 +62,13 @@
     return p2, u2, v2
 
 
-def local(
-    model_state,
-    wave_speed,
-    wet_mask,
-    vertical,
-    surface_temp,
-    flux_coef,
-    heat_gain,
-    pair_tile,
-    pair_source,
-    pair_target,
-    intersection_weights,
-):
-    pressure = model_state[0, 0]
-    eastward = model_state[0, 1]
-    northward = model_state[0, 2]
-    sound_speed = wave_speed[0]
-    wetness = wet_mask[0].astype(jnp.float32)
-    matrix = vertical[0]
-    assert SUBSTEPS == 2
-    p2, u2, v2 = stencil(pressure, eastward, northward, sound_speed, wetness, matrix)
-    final_state = jnp.stack([p2, u2, v2])[None]
-
-    weights = intersection_weights[0, 0]
+def coupling_head(model_state, wetness, surface_temp, flux_coef, heat_gain, sources, targets, target_tile, weights):
     pair_count, in_width, out_width = weights.shape
-    tile_count = lax.axis_size("gx")
     grid_shape = surface_temp.shape[1:]
     cell_count = grid_shape[0] * grid_shape[1]
     in_blocks = cell_count // in_width
     out_blocks = cell_count // out_width
-    sources = pair_source[0, 0]
-    targets = pair_target[0, 0]
-    target_tile = pair_tile[0, 0, :, 0]
     is_atmos = lax.axis_index("sec") == 0
-    me = lax.axis_index("gx")
 
     own_st = surface_temp[0].reshape(cell_count)
     own_wet = wetness.reshape(cell_count)
@@ -111,21 +83,6 @@
     ocean_st = jnp.where(is_atmos, got[0], own_st)
     ocean_wet = jnp.where(is_atmos, got[1], own_wet)
 
-    pad = jnp.zeros((out_width - pair_count,), jnp.float32)
-    table = jnp.concatenate(
-        [
-            ocean_st.reshape(out_blocks, out_width),
-            ocean_wet.reshape(out_blocks, out_width),
-            jnp.concatenate([target_tile.astype(jnp.float32), pad])[None],
-            jnp.concatenate([targets.astype(jnp.float32), pad])[None],
-        ]
-    )
-    tables = lax.all_gather(table, "gx")
-    st_blocks = tables[:, :out_blocks].reshape(tile_count * out_blocks, out_width)
-    wet_blocks = tables[:, out_blocks:2 * out_blocks].reshape(tile_count * out_blocks, out_width)
-    all_tiles = tables[:, 2 * out_blocks, :pair_count].reshape(tile_count * pair_count).astype(jnp.int32)
-    all_targets = tables[:, 2 * out_blocks + 1, :pair_count].reshape(tile_count * pair_count).astype(jnp.int32)
-
     fluxes = jnp.tanh(jnp.dot(flux_coef, atmos_drivers, precision=HIGHEST_PRECISION)).astype(jnp.bfloat16)
     flux_count = fluxes.shape[0]
     blocks = fluxes.reshape(flux_count, in_blocks, in_width)
@@ -136,22 +93,80 @@
     heat = jnp.einsum(
         "f,pfo->po", heat_gain, regridded.astype(jnp.float32), precision=HIGHEST_PRECISION
     )
-    heats = lax.all_gather(heat, "gx").reshape(tile_count * pair_count, out_width)
+
+    index_row = jnp.zeros((1, out_width), jnp.float32)
+    index_row = index_row.at[0, :pair_count].set(target_tile.astype(jnp.float32))
+    index_row = index_row.at[0, out_width - pair_count:].set(targets.astype(jnp.float32))
+    return jnp.concatenate(
+        [heat, ocean_st.reshape(out_blocks, out_width), ocean_wet.reshape(out_blocks, out_width), index_row]
+    )
+
+
+def coupling_tail(tables, surface_temp, wetness, sources, targets, target_tile, weights):
+    tile_count, rows, out_width = tables.shape
+    pair_count, in_width, _ = weights.shape
+    grid_shape = surface_temp.shape[1:]
+    cell_count = grid_shape[0] * grid_shape[1]
+    in_blocks = cell_count // in_width
+    out_blocks = cell_count // out_width
+    me = lax.axis_index("gx")
+    heats = tables[:, :pair_count].reshape(tile_count * pair_count, out_width)
+    st_blocks = tables[:, pair_count:pair_count + out_blocks].reshape(tile_count * out_blocks, out_width)
+    wet_blocks = tables[:, pair_count + out_blocks:pair_count + 2 * out_blocks].reshape(
+        tile_count * out_blocks, out_width
+    )
+    index_rows = tables[:, pair_count + 2 * out_blocks]
+    all_tiles = index_rows[:, :pair_count].reshape(tile_count * pair_count).astype(jnp.int32)
+    all_targets = index_rows[:, out_width - pair_count:].reshape(tile_count * pair_count).astype(jnp.int32)
 
     own_match = (all_tiles[None, :] == me) & (all_targets[None, :] == jnp.arange(out_blocks)[:, None])
     heating = jnp.dot(own_match.astype(jnp.float32), heats, precision=HIGHEST_PRECISION)
-    ocean_temp = own_st + own_wet * heating.reshape(cell_count)
+    ocean_temp = surface_temp[0] + wetness * heating.reshape(grid_shape)
 
     pair_match = (all_tiles[None, :] == target_tile[:, None]) & (all_targets[None, :] == targets[:, None])
     pair_heating = jnp.dot(pair_match.astype(jnp.float32), heats, precision=HIGHEST_PRECISION)
-    rows = target_tile * out_blocks + targets
-    pair_temp = jnp.take(st_blocks, rows, axis=0) + jnp.take(wet_blocks, rows, axis=0) * pair_heating
+    picks = target_tile * out_blocks + targets
+    pair_temp = jnp.take(st_blocks, picks, axis=0) + jnp.take(wet_blocks, picks, axis=0) * pair_heating
     returned = pair_temp.astype(jnp.bfloat16)
     pieces = jnp.einsum("pio,po->pi", weights, returned, preferred_element_type=jnp.float32)
     owning = (jnp.arange(in_blocks)[:, None] == sources[None, :]).astype(jnp.float32)
-    atmos_temp = jnp.dot(owning, pieces, precision=HIGHEST_PRECISION)
+    atmos_temp = jnp.dot(owning, pieces, precision=HIGHEST_PRECISION).reshape(grid_shape)
+    is_atmos = lax.axis_index("sec") == 0
+    return jnp.where(is_atmos, atmos_temp, ocean_temp)[None]
 
-    surface_temps = jnp.where(is_atmos, atmos_temp.reshape(grid_shape), ocean_temp.reshape(grid_shape))[None]
+
+def local(
+    model_state,
+    wave_speed,
+    wet_mask,
+    vertical,
+    surface_temp,
+    flux_coef,
+    heat_gain,
+    pair_tile,
+    pair_source,
+    pair_target,
+    intersection_weights,
+):
+    weights = intersection_weights[0, 0]
+    sources = pair_source[0, 0]
+    targets = pair_target[0, 0]
+    target_tile = pair_tile[0, 0, :, 0]
+    wetness = wet_mask[0].astype(jnp.float32)
+    table = coupling_head(
+        model_state, wetness, surface_temp, flux_coef, heat_gain, sources, targets, target_tile, weights
+    )
+    table, pressure = lax.optimization_barrier((table, model_state[0, 0]))
+    tables = lax.all_gather(table, "gx")
+
+    eastward = model_state[0, 1]
+    northward = model_state[0, 2]
+    sound_speed = wave_speed[0]
+    matrix = vertical[0]
+    assert SUBSTEPS == 2
+    p2, u2, v2 = stencil(pressure, eastward, northward, sound_speed, wetness, matrix)
+    final_state = jnp.stack([p2, u2, v2])[None]
+    surface_temps = coupling_tail(tables, surface_temp, wetness, sources, targets, target_tile, weights)
     return (final_state, surface_temps)
 
 

time: 168 us -> 117 us (0.70)
  waiting for transfers between devices: 70.1 us -> 17.4 us
  matrix products: 15.8 us -> 12.3 us
  local copies, waits for them, and re-layouts: 18.9 us -> 21.4 us
  other arithmetic: 9.72 us -> 11.5 us
    all_gather x1 -> x0, waiting for transfers between devices: 61.2 us -> none  [local(): lax.all_gather(heat, 'gx').reshape(tile_count * pair_count, out_width)]
    all_gather x1, waiting for transfers between devices: 0.01 us -> 4.35 us  [local(): tables = lax.all_gather(table, 'gx')]
    another operation x0 -> x5, other arithmetic: none -> 3.29 us
    ppermute x6, waiting for transfers between devices: 1.43 us -> 4.14 us  [neighbours(): lo = lax.ppermute(tail, axis, [(i, i + 1) for i in range(count - 1)])]
    dot_general x7, matrix products: 11 us -> 8.37 us  [the longest x1 3.38 us: coupling_tail(): jnp.einsum('pio,po->pi', weights, returned, preferred_element_type=jnp.fl...]
    ppermute x6, starting transfers between devices: 22.9 us -> 24.8 us  [neighbours(): lo = lax.ppermute(tail, axis, [(i, i + 1) for i in range(count - 1)])]
    slice x3 -> x4, local copies, waits for them, and re-layouts: 5 us -> 6.27 us  [the longest x1 2.2 us: local(): eastward = model_state[0, 1]]
    unnamed x70 -> x45, local copies, waits for them, and re-layouts: 8.18 us -> 9.34 us
  transfers between devices with their start and end apart: 15 -> 14, of which waited for: 5 -> 7; matrix products, arithmetic and copies ran while one was open for 20% -> 23% of each run, Pallas kernels for 0% -> 0%
where the time goes in v5:
time: 117 us; the launch traced here: 116 us
  starting transfers between devices  38.5 us (33%)
  local copies, waits for them, and re-layouts  21.4 us (18%)
  waiting for transfers between devices  17.4 us (15%)
  between operations  14.7 us (13%)
  matrix products  12.3 us (11%)
  other arithmetic  11.5 us (10%)
    ppermute x6, starting transfers between devices, neighbours(): lo = lax.ppermute(tail, axis, [(i, i + 1) for i in range(count - 1)])  24.8 us
    ppermute x6, starting transfers between devices, neighbours(): hi = lax.ppermute(head, axis, [(i + 1, i) for i in range(count - 1)])  9.81 us
    unnamed x45, local copies, waits for them, and re-layouts  9.34 us
    ppermute x6, waiting for transfers between devices, neighbours(): hi = lax.ppermute(head, axis, [(i + 1, i) for i in range(count - 1)])  8.9 us
    all_gather x1, waiting for transfers between devices, local(): tables = lax.all_gather(table, 'gx')  4.35 us
    ppermute x6, waiting for transfers between devices, neighbours(): lo = lax.ppermute(tail, axis, [(i, i + 1) for i in range(count - 1)])  4.14 us
    dot_general x2, matrix products, vertical_mix(): jnp.einsum('lm,mxy->lxy', matrix, right_side, precision=HIGHEST_PRECISION)  3.89 us
    ppermute x1, starting transfers between devices, coupling_head(): got = lax.ppermute(sent, 'sec', [(0, 1), (1, 0)])  3.83 us
  transfers between devices with their start and end apart: 14, of which 7 were waited for; matrix products, arithmetic and copies ran while one was open for 23% of the time, Pallas kernels for 0%

profile of v5, /device:TPU:1, one launch (start us, length us, event | category | flops | bytes accessed | tf_op | source)
XLA Modules:
  0.0 115.7 jit_solution(5078017742290907067)
XLA Ops:
  10.0 3.8 %collective-permute-start = (f32[4,8192]{1,0:T(4,128)S(1)}, f32[4,8192]{1,0:T(4,128)}, u32[]{:S(2)}, u32[]{:S(2)}) collective-permute-start(f32[4,8192]{1,0:T(4,128)S(1)} %maximum_select_fusion), channel_id=1, source_target_pairs={{0,128},{128,0},{1,129},{129,1},{2,130},{130,2},{3,131},{131,3},{4... | collective-permute-start | bytes 393224 | tf_op jit(solution)/shard_map/ppermute | solution.py:81
  16.5 2.2 %fusion.79 = (f32[1,1,32,16,512]{4,3,2,1,0:T(8,128)S(1)}, f32[1,1,32,16,512]{4,3,2,1,0:T(8,128)S(1)}, f32[1,1,32,16,512]{4,3,2,1,0:T(8,128)S(1)}) fusion(f32[1,3,32,16,512]{4,3,2,1,0:T(8,128)} %param.17), kind=kLoop, calls=%fused_computation.135 | loop fusion | bytes 6291456 | tf_op jit(solution)/shard_map/slice | solution.py:162
  20.1 1.3 %broadcast_select_fusion.3 = f32[1,64]{1,0:T(1,128)S(1)} fusion(pred[]{:T(512)} %compare_reduce_fusion, s32[]{:T(128)} %bitcast.16, s32[1,1,64]{2,1,0:T(1,128)S(1)} %copy-done.7, f32[1,64]{1,0:T(1,128)S(1)} %fusion.71), kind=kLoop, calls=%fused_computation.124 | loop fusion | flops 128 | bytes 773 | tf_op jit(solution)/shard_map/select.3
  21.4 1.6 %copy.71 = f32[1,1,32,16,512]{4,2,3,1,0:T(8,128)} copy(f32[1,1,32,16,512]{4,3,2,1,0:T(8,128)S(1)} %get-tuple-element.44) | data formatting | bytes 2097152
  23.0 0.9 scatter.9
  23.9 1.0 fusion.86
  26.1 2.9 %fusion.11 = bf16[64,8,128]{2,1,0:T(8,128)(2,1)S(1)} fusion(bf16[1,1,64,256,128]{4,3,2,1,0:T(8,128)(2,1)} %param.27, bf16[64,8,256]{2,1,0:T(8,128)(2,1)S(1)} %gather_fusion, pred[64]{0:T(512)(128)(4,1)S(1)} %compare_and_fusion.1), kind=kOutput, calls=%fused_computation.22 | convolution fusion | flops 33751040 | bytes 4587584 | tf_op jit(solution)/shard_map/fpi,pio->pfo/dot_general | solution.py:90
  30.8 3.1 %collective-permute-start.4 = (f32[33,16,1]{2,0,1:T(8,128)S(1)}, f32[33,16,1]{2,0,1:T(8,128)S(1)}, u32[]{:S(2)}, u32[]{:S(2)}) collective-permute-start(f32[33,16,1]{2,0,1:T(8,128)S(1)} %pad_maximum_fusion.11), channel_id=1, source_target_pairs={{0,1},{1,2},{2,3},{4,5},{5,6},{6,7},{8,9},{9,10},{10,11},{12,13},{... | collective-permute-start | bytes 6344 | tf_op jit(solution)/shard_map/ppermute | solution.py:14
  34.0 1.3 %collective-permute-start.3 = (f32[33,16,1]{2,0,1:T(8,128)S(1)}, f32[33,16,1]{2,0,1:T(8,128)S(1)}, u32[]{:S(2)}, u32[]{:S(2)}) collective-permute-start(f32[33,16,1]{2,0,1:T(8,128)S(1)} %pad_maximum_fusion.10), channel_id=1, source_target_pairs={{1,0},{2,1},{3,2},{5,4},{6,5},{7,6},{9,8},{10,9},{11,10},{13,12},{... | collective-permute-start | bytes 6344 | tf_op jit(solution)/shard_map/ppermute | solution.py:15
  36.0 3.6 %collective-permute-start.2 = (f32[33,1,512]{2,0,1:T(8,128)S(1)}, f32[33,1,512]{2,0,1:T(8,128)S(1)}, u32[]{:S(2)}, u32[]{:S(2)}) collective-permute-start(f32[33,1,512]{2,0,1:T(8,128)S(1)} %pad_maximum_fusion.15), channel_id=1, source_target_pairs={{0,4},{4,8},{8,12},{12,16},{16,20},{20,24},{24,28},{28,32},{32,36}... | collective-permute-start | bytes 202760 | tf_op jit(solution)/shard_map/ppermute | solution.py:14
  39.6 1.9 %collective-permute-start.1 = (f32[33,1,512]{2,0,1:T(8,128)S(1)}, f32[33,1,512]{2,0,1:T(8,128)S(1)}, u32[]{:S(2)}, u32[]{:S(2)}) collective-permute-start(f32[33,1,512]{2,0,1:T(8,128)S(1)} %pad_maximum_fusion.14), channel_id=1, source_target_pairs={{4,0},{8,4},{12,8},{16,12},{20,16},{24,20},{28,24},{32,28},{36,32}... | collective-permute-start | bytes 202760 | tf_op jit(solution)/shard_map/ppermute | solution.py:15
  42.1 1.8 %collective-permute-done.3 = f32[33,16,1]{2,0,1:T(8,128)S(1)} collective-permute-done((f32[33,16,1]{2,0,1:T(8,128)S(1)}, f32[33,16,1]{2,0,1:T(8,128)S(1)}, u32[]{:S(2)}, u32[]{:S(2)}) %collective-permute-start.3) | collective-permute-done | bytes 2144 | tf_op jit(solution)/shard_map/ppermute | solution.py:15
  44.1 1.5 %collective-permute-done.1 = f32[33,1,512]{2,0,1:T(8,128)S(1)} collective-permute-done((f32[33,1,512]{2,0,1:T(8,128)S(1)}, f32[33,1,512]{2,0,1:T(8,128)S(1)}, u32[]{:S(2)}, u32[]{:S(2)}) %collective-permute-start.1) | collective-permute-done | bytes 67616 | tf_op jit(solution)/shard_map/ppermute | solution.py:15
  45.8 2.1 %fusion.6 = f32[32,16,512]{2,0,1:T(8,128)S(1)} fusion(f32[32,16,512]{2,0,1:T(8,128)S(1)} %bitcast.121, f32[32,16,512]{2,0,1:T(8,128)S(1)} %bitcast.112, f32[32,16,1]{2,0,1:T(8,128)S(1)} %slice.280, f32[32,16,1]{2,0,1:T(8,128)S(1)} %slice.277, f32[32,16,512]{2,0,1:T(8,128)S(1)} %bitcast.115, f32[32,1,512]{2,0,1:T(8,128)S(1)} %slice.274, ...), kind=kOutput, calls=%fused_computation.13 | convolution fusion | flops 105644032 | bytes 4366336 | tf_op jit(solution)/shard_map/lm,mxy->lxy/dot_general | solution.py:20
  48.1 1.3 %collective-permute-start.7 = (f32[32,16,2]{2,0,1:T(8,128)S(1)}, f32[32,16,2]{2,0,1:T(8,128)S(1)}, u32[]{:S(2)}, u32[]{:S(2)}) collective-permute-start(f32[32,16,2]{2,0,1:T(8,128)S(1)} %get-tuple-element.57), channel_id=1, source_target_pairs={{1,0},{2,1},{3,2},{5,4},{6,5},{7,6},{9,8},{10,9},{11,10},{13,12},{... | collective-permute-start | bytes 12296 | tf_op jit(solution)/shard_map/ppermute | solution.py:15
  49.4 6.0 %collective-permute-start.8 = (f32[32,16,2]{2,0,1:T(8,128)S(1)}, f32[32,16,2]{2,0,1:T(8,128)S(1)}, u32[]{:S(2)}, u32[]{:S(2)}) collective-permute-start(f32[32,16,2]{2,0,1:T(8,128)S(1)} %get-tuple-element.56), channel_id=1, source_target_pairs={{0,1},{1,2},{2,3},{4,5},{5,6},{6,7},{8,9},{9,10},{10,11},{12,13},{... | collective-permute-start | bytes 12296 | tf_op jit(solution)/shard_map/ppermute | solution.py:14
  55.4 1.9 %collective-permute-start.5 = (f32[32,2,512]{2,0,1:T(8,128)S(1)}, f32[32,2,512]{2,0,1:T(8,128)S(1)}, u32[]{:S(2)}, u32[]{:S(2)}) collective-permute-start(f32[32,2,512]{2,0,1:T(8,128)S(1)} %get-tuple-element.55), channel_id=1, source_target_pairs={{4,0},{8,4},{12,8},{16,12},{20,16},{24,20},{28,24},{32,28},{36,32}... | collective-permute-start | bytes 393224 | tf_op jit(solution)/shard_map/ppermute | solution.py:15
  57.3 3.6 %collective-permute-start.6 = (f32[32,2,512]{2,0,1:T(8,128)S(1)}, f32[32,2,512]{2,0,1:T(8,128)S(1)}, u32[]{:S(2)}, u32[]{:S(2)}) collective-permute-start(f32[32,2,512]{2,0,1:T(8,128)S(1)} %get-tuple-element.54), channel_id=1, source_target_pairs={{0,4},{4,8},{8,12},{12,16},{16,20},{20,24},{24,28},{28,32},{32,36}... | collective-permute-start | bytes 393224 | tf_op jit(solution)/shard_map/ppermute | solution.py:14
  62.5 2.7 %collective-permute-done.6 = f32[32,2,512]{2,0,1:T(8,128)S(1)} collective-permute-done((f32[32,2,512]{2,0,1:T(8,128)S(1)}, f32[32,2,512]{2,0,1:T(8,128)S(1)}, u32[]{:S(2)}, u32[]{:S(2)}) %collective-permute-start.6) | collective-permute-done | bytes 131104 | tf_op jit(solution)/shard_map/ppermute | solution.py:14
  65.5 1.8 %fusion.5 = f32[32,16,512]{2,0,1:T(8,128)S(1)} fusion(f32[32,16,512]{2,0,1:T(8,128)S(1)} %fusion.6, f32[32,16,514]{2,0,1:T(8,128)S(1)} %fusion.7, f32[32,18,512]{2,0,1:T(8,128)S(1)} %fusion.9, f32[16,512]{1,0:T(8,128)S(1)} %bitcast.145, f32[1,32,32]{2,1,0:T(8,128)S(1)} %copy-done), kind=kOutput, calls=%fused_computation.11 | convolution fusion | flops 103546880 | bytes 11616256 | tf_op jit(solution)/shard_map/lm,mxy->lxy/dot_general | solution.py:20
  67.9 4.4 %collective-permute-start.10 = (f32[32,1,512]{2,0,1:T(8,128)}, f32[32,1,512]{2,0,1:T(8,128)}, u32[]{:S(2)}, u32[]{:S(2)}) collective-permute-start(f32[32,1,512]{2,0,1:T(8,128)} %get-tuple-element.51), channel_id=1, source_target_pairs={{0,4},{4,8},{8,12},{12,16},{16,20},{20,24},{24,28},{28,32},{32,36}... | collective-permute-start | bytes 196616 | tf_op jit(solution)/shard_map/ppermute | solution.py:14
  72.3 1.9 %collective-permute-start.9 = (f32[32,1,512]{2,0,1:T(8,128)}, f32[32,1,512]{2,0,1:T(8,128)}, u32[]{:S(2)}, u32[]{:S(2)}) collective-permute-start(f32[32,1,512]{2,0,1:T(8,128)} %get-tuple-element.50), channel_id=1, source_target_pairs={{4,0},{8,4},{12,8},{16,12},{20,16},{24,20},{28,24},{32,28},{36,32}... | collective-permute-start | bytes 196616 | tf_op jit(solution)/shard_map/ppermute | solution.py:15
  75.1 4.1 %collective-permute-start.12 = (f32[32,16,1]{2,0,1:T(8,128)}, f32[32,16,1]{2,0,1:T(8,128)}, u32[]{:S(2)}, u32[]{:S(2)}) collective-permute-start(f32[32,16,1]{2,0,1:T(8,128)} %get-tuple-element.53), channel_id=1, source_target_pairs={{0,1},{1,2},{2,3},{4,5},{5,6},{6,7},{8,9},{9,10},{10,11},{12,13},{... | collective-permute-start | bytes 6152 | tf_op jit(solution)/shard_map/ppermute | solution.py:14
  79.2 1.5 %collective-permute-start.11 = (f32[32,16,1]{2,0,1:T(8,128)}, f32[32,16,1]{2,0,1:T(8,128)}, u32[]{:S(2)}, u32[]{:S(2)}) collective-permute-start(f32[32,16,1]{2,0,1:T(8,128)} %get-tuple-element.52), channel_id=1, source_target_pairs={{1,0},{2,1},{3,2},{5,4},{6,5},{7,6},{9,8},{10,9},{11,10},{13,12},{... | collective-permute-start | bytes 6152 | tf_op jit(solution)/shard_map/ppermute | solution.py:15
  81.9 1.4 %collective-permute-done.12 = f32[32,16,1]{2,0,1:T(8,128)} collective-permute-done((f32[32,16,1]{2,0,1:T(8,128)}, f32[32,16,1]{2,0,1:T(8,128)}, u32[]{:S(2)}, u32[]{:S(2)}) %collective-permute-start.12) | collective-permute-done | bytes 2080 | tf_op jit(solution)/shard_map/ppermute | solution.py:14
  83.3 4.9 %collective-permute-done.11 = f32[32,16,1]{2,0,1:T(8,128)} collective-permute-done((f32[32,16,1]{2,0,1:T(8,128)}, f32[32,16,1]{2,0,1:T(8,128)}, u32[]{:S(2)}, u32[]{:S(2)}) %collective-permute-start.11) | collective-permute-done | bytes 2080 | tf_op jit(solution)/shard_map/ppermute | solution.py:15
  88.3 2.1 %fusion.26 = (f32[1,32,16,512]{3,1,2,0:T(8,128)S(1)}, f32[1,32,16,512]{3,1,2,0:T(8,128)S(1)}) fusion(f32[32,16,512]{2,0,1:T(8,128)S(1)} %fusion.5, f32[32,1,512]{2,0,1:T(8,128)} %collective-permute-done.10, f32[32,1,512]{2,0,1:T(8,128)} %collective-permute-done.9, f32[32,18,512]{2,0,1:T(8,128)S(1)} %fusion.9, f32[16,512]{1,0:T(8,128)} %bitcast.128, ...), kind=kLoop, calls=%fused_computation.39 | loop fusion | flops 3145728 | bytes 5410816 | tf_op jit(solution)/shard_map/stack | solution.py:168
  90.8 3.5 %copy.38 = f32[1,3,32,16,512]{4,3,2,1,0:T(8,128)} copy(f32[1,3,32,16,512]{4,2,3,1,0:T(8,128)S(1)} %maximum_bitcast_fusion) | data formatting | bytes 6291456
  94.2 4.3 %all-gather.4.cloned.1.call-done = f32[32,193,128]{2,1,0:T(8,128)} async-done(((f32[1,193,128]{2,1,0:T(8,128)}), f32[32,193,128]{2,1,0:T(8,128)}) %all-gather.4.cloned.1.call-update) | async-done | bytes 3162128 | tf_op jit(solution)/shard_map/all_gather | solution.py:160
  98.6 0.9 slice.301
  99.7 2.1 %fusion.78 = (f32[32,64,128]{2,1,0:T(8,128)S(1)}, f32[32,64,128]{2,1,0:T(8,128)S(1)}, f32[32,64,128]{2,1,0:T(8,128)S(1)}) fusion(f32[32,193,128]{2,1,0:T(8,128)} %all-gather.4.cloned.1.call-done), kind=kLoop, calls=%fused_computation.134 | loop fusion | bytes 6291456 | tf_op jit(solution)/shard_map/slice | solution.py:114
  103.9 3.4 %fusion.1 = f32[64,1,256]{2,1,0:T(1,128)S(1)} fusion(bf16[1,1,64,256,128]{4,3,2,1,0:T(8,128)(2,1)} %param.27, bf16[64,128,1]{1,0,2:T(8,128)(2,1)S(1)} %fusion.16), kind=kOutput, calls=%fused_computation.5 | convolution fusion | flops 4194304 | bytes 4276224 | tf_op jit(solution)/shard_map/pio,po->pi/dot_general | solution.py:131
  (111 shorter events, 20.1 us)
Async XLA Ops:
  7.2 38.6 %copy-start = (f32[1,32,32]{2,1,0:T(8,128)S(1)}, f32[1,32,32]{2,1,0:T(8,128)}, u32[]{:S(2)}) copy-start(f32[1,32,32]{2,1,0:T(8,128)} %param.20) | copy-start | bytes 12292
  7.2 91.4 %all-gather.4.cloned.1.call-start = ((), (), s32[]{:S(2)}) async-start(), calls=%async_computation | async-start | bytes 3379200 | tf_op jit(solution)/shard_map/all_gather | solution.py:160
  8.0 37.6 %copy-start.1 = (f32[1,16,512]{2,0,1:T(1,128)}, f32[1,16,512]{2,0,1:T(1,128)S(1)}, u32[]{:S(2)}) copy-start(f32[1,16,512]{2,0,1:T(1,128)S(1)} %copy_convert_fusion) | copy-start | bytes 98308
  10.0 13.8 %collective-permute-start = (f32[4,8192]{1,0:T(4,128)S(1)}, f32[4,8192]{1,0:T(4,128)}, u32[]{:S(2)}, u32[]{:S(2)}) collective-permute-start(f32[4,8192]{1,0:T(4,128)S(1)} %maximum_select_fusion), channel_id=1, source_target_pairs={{0,128},{128,0},{1,129},{129,1},{2,130},{130,2},{3,131},{131,3},{4... | collective-permute-start | bytes 393224 | tf_op jit(solution)/shard_map/ppermute | solution.py:81
  16.5 2.9 %copy-start.9 = (s32[1,1,64,1]{2,3,1,0:T(1,128)S(1)}, s32[1,1,64,1]{2,3,1,0:T(1,128)}, u32[]{:S(2)}) copy-start(s32[1,1,64,1]{2,3,1,0:T(1,128)} %param.24) | copy-start | bytes 772
  16.5 3.5 %copy-start.7 = (s32[1,1,64]{2,1,0:T(1,128)S(1)}, s32[1,1,64]{2,1,0:T(1,128)}, u32[]{:S(2)}) copy-start(s32[1,1,64]{2,1,0:T(1,128)} %param.26) | copy-start | bytes 772
  16.5 4.9 %copy-start.4 = (f32[1,16,512]{2,1,0:T(8,128)S(1)}, f32[1,16,512]{2,1,0:T(8,128)}, u32[]{:S(2)}) copy-start(f32[1,16,512]{2,1,0:T(8,128)} %param.21) | copy-start | bytes 98308
  18.7 6.2 %copy-start.15 = (f32[8,4]{0,1:T(4,128)S(1)}, f32[8,4]{0,1:T(4,128)}, u32[]{:S(2)}) copy-start(f32[8,4]{0,1:T(4,128)} %param.22) | copy-start | bytes 388
  26.1 2.9 %copy-start.12 = (f32[8]{0:T(128)S(1)}, f32[8]{0:T(128)}, u32[]{:S(2)}) copy-start(f32[8]{0:T(128)} %param.23) | copy-start | bytes 100
  30.8 13.1 %collective-permute-start.4 = (f32[33,16,1]{2,0,1:T(8,128)S(1)}, f32[33,16,1]{2,0,1:T(8,128)S(1)}, u32[]{:S(2)}, u32[]{:S(2)}) collective-permute-start(f32[33,16,1]{2,0,1:T(8,128)S(1)} %pad_maximum_fusion.11), channel_id=1, source_target_pairs={{0,1},{1,2},{2,3},{4,5},{5,6},{6,7},{8,9},{9,10},{10,11},{12,13},{... | collective-permute-start | bytes 6344 | tf_op jit(solution)/shard_map/ppermute | solution.py:14
  34.0 9.9 %collective-permute-start.3 = (f32[33,16,1]{2,0,1:T(8,128)S(1)}, f32[33,16,1]{2,0,1:T(8,128)S(1)}, u32[]{:S(2)}, u32[]{:S(2)}) collective-permute-start(f32[33,16,1]{2,0,1:T(8,128)S(1)} %pad_maximum_fusion.10), channel_id=1, source_target_pairs={{1,0},{2,1},{3,2},{5,4},{6,5},{7,6},{9,8},{10,9},{11,10},{13,12},{... | collective-permute-start | bytes 6344 | tf_op jit(solution)/shard_map/ppermute | solution.py:15
  35.9 9.8 %copy-start.3 = (f32[1,1,32,16,512]{4,2,3,1,0:T(8,128)S(1)}, f32[1,1,32,16,512]{4,2,3,1,0:T(8,128)}, u32[]{:S(2)}) copy-start(f32[1,1,32,16,512]{4,2,3,1,0:T(8,128)} %copy.71) | copy-start | bytes 3145732
  35.9 9.8 %copy-start.14 = (f32[1,16,512]{2,1,0:T(8,128)S(1)}, f32[1,16,512]{2,1,0:T(8,128)}, u32[]{:S(2)}) copy-start(f32[1,16,512]{2,1,0:T(8,128)} %param.18) | copy-start | bytes 98308
  36.0 9.6 %collective-permute-start.2 = (f32[33,1,512]{2,0,1:T(8,128)S(1)}, f32[33,1,512]{2,0,1:T(8,128)S(1)}, u32[]{:S(2)}, u32[]{:S(2)}) collective-permute-start(f32[33,1,512]{2,0,1:T(8,128)S(1)} %pad_maximum_fusion.15), channel_id=1, source_target_pairs={{0,4},{4,8},{8,12},{12,16},{16,20},{20,24},{24,28},{28,32},{32,36}... | collective-permute-start | bytes 202760 | tf_op jit(solution)/shard_map/ppermute | solution.py:14
  39.6 6.1 %collective-permute-start.1 = (f32[33,1,512]{2,0,1:T(8,128)S(1)}, f32[33,1,512]{2,0,1:T(8,128)S(1)}, u32[]{:S(2)}, u32[]{:S(2)}) collective-permute-start(f32[33,1,512]{2,0,1:T(8,128)S(1)} %pad_maximum_fusion.14), channel_id=1, source_target_pairs={{4,0},{8,4},{12,8},{16,12},{20,16},{24,20},{28,24},{32,28},{36,32}... | collective-permute-start | bytes 202760 | tf_op jit(solution)/shard_map/ppermute | solution.py:15
  48.1 12.9 %collective-permute-start.7 = (f32[32,16,2]{2,0,1:T(8,128)S(1)}, f32[32,16,2]{2,0,1:T(8,128)S(1)}, u32[]{:S(2)}, u32[]{:S(2)}) collective-permute-start(f32[32,16,2]{2,0,1:T(8,128)S(1)} %get-tuple-element.57), channel_id=1, source_target_pairs={{1,0},{2,1},{3,2},{5,4},{6,5},{7,6},{9,8},{10,9},{11,10},{13,12},{... | collective-permute-start | bytes 12296 | tf_op jit(solution)/shard_map/ppermute | solution.py:15
  49.4 11.6 %collective-permute-start.8 = (f32[32,16,2]{2,0,1:T(8,128)S(1)}, f32[32,16,2]{2,0,1:T(8,128)S(1)}, u32[]{:S(2)}, u32[]{:S(2)}) collective-permute-start(f32[32,16,2]{2,0,1:T(8,128)S(1)} %get-tuple-element.56), channel_id=1, source_target_pairs={{0,1},{1,2},{2,3},{4,5},{5,6},{6,7},{8,9},{9,10},{10,11},{12,13},{... | collective-permute-start | bytes 12296 | tf_op jit(solution)/shard_map/ppermute | solution.py:14
  55.4 7.1 %collective-permute-start.5 = (f32[32,2,512]{2,0,1:T(8,128)S(1)}, f32[32,2,512]{2,0,1:T(8,128)S(1)}, u32[]{:S(2)}, u32[]{:S(2)}) collective-permute-start(f32[32,2,512]{2,0,1:T(8,128)S(1)} %get-tuple-element.55), channel_id=1, source_target_pairs={{4,0},{8,4},{12,8},{16,12},{20,16},{24,20},{28,24},{32,28},{36,32}... | collective-permute-start | bytes 393224 | tf_op jit(solution)/shard_map/ppermute | solution.py:15
  57.3 7.9 %collective-permute-start.6 = (f32[32,2,512]{2,0,1:T(8,128)S(1)}, f32[32,2,512]{2,0,1:T(8,128)S(1)}, u32[]{:S(2)}, u32[]{:S(2)}) collective-permute-start(f32[32,2,512]{2,0,1:T(8,128)S(1)} %get-tuple-element.54), channel_id=1, source_target_pairs={{0,4},{4,8},{8,12},{12,16},{16,20},{20,24},{24,28},{28,32},{32,36}... | collective-permute-start | bytes 393224 | tf_op jit(solution)/shard_map/ppermute | solution.py:14
  67.3 14.0 %copy-start.2 = (f32[1,16,512]{2,0,1:T(1,128)S(1)}, f32[1,16,512]{2,0,1:T(1,128)}, u32[]{:S(2)}) copy-start(f32[1,16,512]{2,0,1:T(1,128)} %copy-done.1) | copy-start | bytes 98308
  67.9 20.3 %collective-permute-start.10 = (f32[32,1,512]{2,0,1:T(8,128)}, f32[32,1,512]{2,0,1:T(8,128)}, u32[]{:S(2)}, u32[]{:S(2)}) collective-permute-start(f32[32,1,512]{2,0,1:T(8,128)} %get-tuple-element.51), channel_id=1, source_target_pairs={{0,4},{4,8},{8,12},{12,16},{16,20},{20,24},{24,28},{28,32},{32,36}... | collective-permute-start | bytes 196616 | tf_op jit(solution)/shard_map/ppermute | solution.py:14
  72.3 16.0 %collective-permute-start.9 = (f32[32,1,512]{2,0,1:T(8,128)}, f32[32,1,512]{2,0,1:T(8,128)}, u32[]{:S(2)}, u32[]{:S(2)}) collective-permute-start(f32[32,1,512]{2,0,1:T(8,128)} %get-tuple-element.50), channel_id=1, source_target_pairs={{4,0},{8,4},{12,8},{16,12},{20,16},{24,20},{28,24},{32,28},{36,32}... | collective-permute-start | bytes 196616 | tf_op jit(solution)/shard_map/ppermute | solution.py:15
  75.1 8.2 %collective-permute-start.12 = (f32[32,16,1]{2,0,1:T(8,128)}, f32[32,16,1]{2,0,1:T(8,128)}, u32[]{:S(2)}, u32[]{:S(2)}) collective-permute-start(f32[32,16,1]{2,0,1:T(8,128)} %get-tuple-element.53), channel_id=1, source_target_pairs={{0,1},{1,2},{2,3},{4,5},{5,6},{6,7},{8,9},{9,10},{10,11},{12,13},{... | collective-permute-start | bytes 6152 | tf_op jit(solution)/shard_map/ppermute | solution.py:14
  79.2 9.0 %collective-permute-start.11 = (f32[32,16,1]{2,0,1:T(8,128)}, f32[32,16,1]{2,0,1:T(8,128)}, u32[]{:S(2)}, u32[]{:S(2)}) collective-permute-start(f32[32,16,1]{2,0,1:T(8,128)} %get-tuple-element.52), channel_id=1, source_target_pairs={{1,0},{2,1},{3,2},{5,4},{6,5},{7,6},{9,8},{10,9},{11,10},{13,12},{... | collective-permute-start | bytes 6152 | tf_op jit(solution)/shard_map/ppermute | solution.py:15
  99.7 3.6 %copy-start.8 = (s32[1,1,64]{2,1,0:T(1,128)S(1)}, s32[1,1,64]{2,1,0:T(1,128)}, u32[]{:S(2)}) copy-start(s32[1,1,64]{2,1,0:T(1,128)} %param.26) | copy-start | bytes 772
  99.7 3.6 %copy-start.10 = (s32[1,1,64,1]{2,3,1,0:T(1,128)S(1)}, s32[1,1,64,1]{2,3,1,0:T(1,128)}, u32[]{:S(2)}) copy-start(s32[1,1,64,1]{2,3,1,0:T(1,128)} %param.24) | copy-start | bytes 772
  99.7 3.6 %copy-start.11 = (pred[64]{0:T(512)(128)(4,1)S(1)}, pred[64]{0:T(512)(128)(4,1)}, u32[]{:S(2)}) copy-start(pred[64]{0:T(512)(128)(4,1)} %get-tuple-element.37) | copy-start | bytes 196
  103.9 3.4 %copy-start.13 = (s32[1,1,64]{2,1,0:T(1,128)S(1)}, s32[1,1,64]{2,1,0:T(1,128)}, u32[]{:S(2)}) copy-start(s32[1,1,64]{2,1,0:T(1,128)} %param.25) | copy-start | bytes 772
  103.9 4.2 %copy-start.5 = (f32[1,16,512]{2,1,0:T(8,128)S(1)}, f32[1,16,512]{2,1,0:T(8,128)}, u32[]{:S(2)}) copy-start(f32[1,16,512]{2,1,0:T(8,128)} %param.21) | copy-start | bytes 98308
  103.9 4.2 %copy-start.6 = (s32[1,16,512]{2,1,0:T(8,128)S(1)}, s32[1,16,512]{2,1,0:T(8,128)}, u32[]{:S(2)}) copy-start(s32[1,16,512]{2,1,0:T(8,128)} %param.19) | copy-start | bytes 98308
Sparse Core Ops, SparseCore 0:
  30.1 68.4 all-gather.3

commit v6 on v2

--- a/solution.py
+++ b/solution.py
@@ -20,7 +20,7 @@
     return right_side + jnp.einsum("lm,mxy->lxy", matrix, right_side, precision=HIGHEST_PRECISION)
 
 
-def stencil(pressure, eastward, northward, sound_speed, wetness, matrix):
+def stencil(pressure, eastward, northward, sound_speed, wetness, matrix, stages):
     wet3 = wetness[None]
     lo_x, hi_x = neighbours(
         jnp.concatenate([eastward[:, :1], wet3[:, :1]], axis=0),
@@ -32,6 +32,7 @@
         jnp.concatenate([northward[:, :, -1:], wet3[:, :, -1:]], axis=0),
         "gy",
     )
+    lo_x, hi_x, lo_y, hi_y = stages[0]((lo_x, hi_x, lo_y, hi_y))
     levels = eastward.shape[0]
     u_ext = jnp.concatenate([lo_x[:levels], eastward, hi_x[:levels]], axis=1)
     wet_x = jnp.concatenate([lo_x[levels:], wet3, hi_x[levels:]], axis=1)
@@ -43,6 +44,7 @@
 
     lo2x, hi2x = neighbours(p1[:, :2], p1[:, -2:], "gx")
     lo2y, hi2y = neighbours(p1[:, :, :2], p1[:, :, -2:], "gy")
+    lo2x, hi2x, lo2y, hi2y = stages[1]((lo2x, hi2x, lo2y, hi2y))
     p1_x = jnp.concatenate([lo2x, p1, hi2x], axis=1)
     p1_y = jnp.concatenate([lo2y, p1, hi2y], axis=2)
     u1_ext = wet_x * (u_ext - 0.5 * (p1_x[:, 2:] - p1_x[:, :-2]))
@@ -53,6 +55,7 @@
 
     lo3x, hi3x = neighbours(p2[:, :1], p2[:, -1:], "gx")
     lo3y, hi3y = neighbours(p2[:, :, :1], p2[:, :, -1:], "gy")
+    lo3x, hi3x, lo3y, hi3y = stages[2]((lo3x, hi3x, lo3y, hi3y))
     p2_x = jnp.concatenate([lo3x, p2, hi3x], axis=1)
     p2_y = jnp.concatenate([lo3y, p2, hi3y], axis=2)
     u1 = u1_ext[:, 1:-1]
@@ -81,9 +84,6 @@
     sound_speed = wave_speed[0]
     wetness = wet_mask[0].astype(jnp.float32)
     matrix = vertical[0]
-    assert SUBSTEPS == 2
-    p2, u2, v2 = stencil(pressure, eastward, northward, sound_speed, wetness, matrix)
-    final_state = jnp.stack([p2, u2, v2])[None]
 
     weights = intersection_weights[0, 0]
     pair_count, in_width, out_width = weights.shape
@@ -129,33 +129,56 @@
     earlier = jnp.sum(same_tile & is_before, axis=1)
     slot_of = target_tile * capacity + earlier
     placing = jnp.arange(slot_count)[:, None] == slot_of[None, :]
-    outgoing = jnp.dot(placing.astype(jnp.float32), heat, precision=HIGHEST_PRECISION)
-    offsets = jnp.sum(jnp.where(placing, targets[None, :] + 1, 0), axis=1) - 1
-    offset_row = jnp.zeros((tile_count, 1, out_width), jnp.float32).at[:, 0, :capacity].set(
-        offsets.reshape(tile_count, capacity).astype(jnp.float32)
-    )
-    packet = jnp.concatenate([outgoing.reshape(tile_count, capacity, out_width), offset_row], axis=1)
-    arrived = lax.all_to_all(packet, "gx", split_axis=0, concat_axis=0, tiled=True)
-    arrived_at = arrived[:, capacity, :capacity].reshape(slot_count).astype(jnp.int32)
-    landing = jnp.arange(out_blocks)[:, None] == arrived_at[None, :]
-    heating = jnp.dot(
-        landing.astype(jnp.float32),
-        arrived[:, :capacity].reshape(slot_count, out_width),
-        precision=HIGHEST_PRECISION,
-    )
-    ocean_temp = ocean_st + ocean_wet * heating.reshape(cell_count)
-
-    returning = jnp.dot(
-        landing.T.astype(jnp.bfloat16),
-        ocean_temp.astype(jnp.bfloat16).reshape(out_blocks, out_width),
-        preferred_element_type=jnp.float32,
-    ).astype(jnp.bfloat16)
-    delivered = lax.all_to_all(
-        returning.reshape(tile_count, capacity, out_width), "gx", split_axis=0, concat_axis=0, tiled=True
-    )
+    carried = {}
+
+    def send_heat(halos):
+        outgoing = jnp.dot(placing.astype(jnp.float32), heat, precision=HIGHEST_PRECISION)
+        offsets = jnp.sum(jnp.where(placing, targets[None, :] + 1, 0), axis=1) - 1
+        offset_row = jnp.zeros((tile_count, 1, out_width), jnp.float32).at[:, 0, :capacity].set(
+            offsets.reshape(tile_count, capacity).astype(jnp.float32)
+        )
+        packet = jnp.concatenate([outgoing.reshape(tile_count, capacity, out_width), offset_row], axis=1)
+        carried["packet"], halos = lax.optimization_barrier((packet, halos))
+        return halos
+
+    def warm_ocean(halos):
+        arrived = lax.all_to_all(carried["packet"], "gx", split_axis=0, concat_axis=0, tiled=True)
+        arrived_at = arrived[:, capacity, :capacity].reshape(slot_count).astype(jnp.int32)
+        landing = jnp.arange(out_blocks)[:, None] == arrived_at[None, :]
+        heating = jnp.dot(
+            landing.astype(jnp.float32),
+            arrived[:, :capacity].reshape(slot_count, out_width),
+            precision=HIGHEST_PRECISION,
+        )
+        ocean_temp = ocean_st + ocean_wet * heating.reshape(cell_count)
+        returning = jnp.dot(
+            landing.T.astype(jnp.bfloat16),
+            ocean_temp.astype(jnp.bfloat16).reshape(out_blocks, out_width),
+            preferred_element_type=jnp.float32,
+        ).astype(jnp.bfloat16)
+        (carried["ocean"], carried["returning"]), halos = lax.optimization_barrier(
+            ((ocean_temp, returning), halos)
+        )
+        return halos
+
+    def return_temps(halos):
+        delivered = lax.all_to_all(
+            carried["returning"].reshape(tile_count, capacity, out_width), "gx", split_axis=0, concat_axis=0,
+            tiled=True,
+        )
+        carried["delivered"], halos = lax.optimization_barrier((delivered, halos))
+        return halos
+
+    assert SUBSTEPS == 2
+    p2, u2, v2 = stencil(
+        pressure, eastward, northward, sound_speed, wetness, matrix, (send_heat, warm_ocean, return_temps)
+    )
+    final_state = jnp.stack([p2, u2, v2])[None]
+
+    ocean_temp = carried["ocean"]
     per_pair = jnp.dot(
         placing.T.astype(jnp.bfloat16),
-        delivered.reshape(slot_count, out_width),
+        carried["delivered"].reshape(slot_count, out_width),
         preferred_element_type=jnp.float32,
     ).astype(jnp.bfloat16)
     pieces = jnp.einsum("pio,po->pi", weights, per_pair, preferred_element_type=jnp.float32)

time: 114 us -> 122 us (1.070)
  local copies, waits for them, and re-layouts: 19.6 us -> 27.5 us
  other arithmetic: 7.7 us -> 13.3 us
  waiting for transfers between devices: 9.67 us -> 6.55 us
  starting transfers between devices: 58.5 us -> 57.1 us
    all_to_all x2, waiting for transfers between devices: 4.32 us -> 0.01 us  [the longest x1 0.01 us: warm_ocean(): lax.all_to_all(carried['packet'], 'gx', split_axis=0, concat_axis=0, tile...]
    dot_general x1, matrix products: 3.38 us -> 1.18 us  [local(): jnp.einsum('pio,po->pi', weights, per_pair, preferred_element_type=jnp.fl...]
    dot_general x4, matrix products: 1.5 us -> 3.59 us  [the longest x1 1.5 us: warm_ocean(): jnp.dot(landing.T.astype(jnp.bfloat16), ocean_temp.astype(jnp.bfloat16).r...]
    ppermute x6, waiting for transfers between devices: 3.57 us -> 5.6 us  [neighbours(): hi = lax.ppermute(head, axis, [(i + 1, i) for i in range(count - 1)])]
    dot_general x2, matrix products: 6.42 us -> 4.74 us  [vertical_mix(): jnp.einsum('lm,mxy->lxy', matrix, right_side, precision=HIGHEST_PRECISION)]
    all_to_all x2, starting transfers between devices: 22.1 us -> 20.5 us  [the longest x1 11.5 us: warm_ocean(): lax.all_to_all(carried['packet'], 'gx', split_axis=0, concat_axis=0, tile...]
    convert_element_type x2, other arithmetic: 0.07 us -> 1.58 us  [the longest x1 1.57 us: warm_ocean(): arrived[:, capacity, :capacity].reshape(slot_count).astype(jnp.int32)]
    another operation x1, other arithmetic: 1.07 us -> 2.43 us  [local(): final_state = jnp.stack([p2, u2, v2])[None]]
  transfers between devices with their start and end apart: 15 -> 15, of which waited for: 4 -> 3; matrix products, arithmetic and copies ran while one was open for 29% -> 25% of each run, Pallas kernels for 0% -> 0%
where the time goes in v6:
time: 122 us; the launch traced here: 120 us
  starting transfers between devices  57.1 us (47%)
  local copies, waits for them, and re-layouts  27.5 us (23%)
  matrix products  14 us (11%)
  other arithmetic  13.3 us (11%)
  waiting for transfers between devices  6.55 us (5%)
  between operations  1.41 us (1%)
    ppermute x6, starting transfers between devices, neighbours(): lo = lax.ppermute(tail, axis, [(i, i + 1) for i in range(count - 1)])  22.4 us
    all_to_all x1, starting transfers between devices, warm_ocean(): lax.all_to_all(carried['packet'], 'gx', split_axis=0, concat_axis=0, tile...  11.5 us
    ppermute x6, starting transfers between devices, neighbours(): hi = lax.ppermute(head, axis, [(i + 1, i) for i in range(count - 1)])  10.4 us
    all_to_all x1, starting transfers between devices, return_temps(): lax.all_to_all(carried['returning'].reshape(tile_count, capacity, out_wid...  9 us
    unnamed x70, local copies, waits for them, and re-layouts  8.3 us
    ppermute x6, waiting for transfers between devices, neighbours(): hi = lax.ppermute(head, axis, [(i + 1, i) for i in range(count - 1)])  5.6 us
    dot_general x2, matrix products, vertical_mix(): jnp.einsum('lm,mxy->lxy', matrix, right_side, precision=HIGHEST_PRECISION)  4.74 us
    ppermute x1, starting transfers between devices, local(): got = lax.ppermute(sent, 'sec', [(0, 1), (1, 0)])  3.83 us
  transfers between devices with their start and end apart: 15, of which 3 were waited for; matrix products, arithmetic and copies ran while one was open for 25% of the time, Pallas kernels for 0%

profile of v6, /device:TPU:1, one launch (start us, length us, event | category | flops | bytes accessed | tf_op | source)
XLA Modules:
  0.0 119.9 jit_solution(11714615288319119936)
XLA Ops:
  3.4 3.8 %collective-permute-start = (f32[4,8192]{1,0:T(4,128)S(1)}, f32[4,8192]{1,0:T(4,128)}, u32[]{:S(2)}, u32[]{:S(2)}) collective-permute-start(f32[4,8192]{1,0:T(4,128)S(1)} %maximum_select_fusion), channel_id=1, source_target_pairs={{0,128},{128,0},{1,129},{129,1},{2,130},{130,2},{3,131},{131,3},{4... | collective-permute-start | bytes 393224 | tf_op jit(solution)/shard_map/ppermute | solution.py:108
  7.3 3.2 %fusion.73 = (f32[1,1,32,16,512]{4,3,2,1,0:T(8,128)}, f32[1,1,32,16,512]{4,3,2,1,0:T(8,128)S(1)}, f32[1,1,32,16,512]{4,3,2,1,0:T(8,128)S(1)}) fusion(f32[1,3,32,16,512]{4,3,2,1,0:T(8,128)} %param.13), kind=kLoop, calls=%fused_computation.125 | loop fusion | bytes 6291456 | tf_op jit(solution)/shard_map/slice | solution.py:81
  10.5 1.2 %copy_bitcast_fusion.2 = (f32[32,16,512]{2,0,1:T(8,128)S(1)}, f32[32,16,512]{2,0,1:T(8,128)S(1)}) fusion(f32[1,1,32,16,512]{4,3,2,1,0:T(8,128)S(1)} %get-tuple-element.55, f32[1,1,32,16,512]{4,3,2,1,0:T(8,128)S(1)} %get-tuple-element.56), kind=kLoop, calls=%fused_computation.59 | loop fusion | bytes 4194304 | tf_op jit(solution)/shard_map/squeeze | solution.py:83
  12.4 3.1 %collective-permute-start.1 = (f32[33,1,512]{2,0,1:T(8,128)}, f32[33,1,512]{2,0,1:T(8,128)}, u32[]{:S(2)}, u32[]{:S(2)}) collective-permute-start(f32[33,1,512]{2,0,1:T(8,128)} %pad_maximum_fusion.14), channel_id=1, source_target_pairs={{0,4},{4,8},{8,12},{12,16},{16,20},{20,24},{24,28},{28,32},{32,36}... | collective-permute-start | bytes 202760 | tf_op jit(solution)/shard_map/ppermute | solution.py:14
  16.2 1.9 %collective-permute-start.2 = (f32[33,1,512]{2,0,1:T(8,128)}, f32[33,1,512]{2,0,1:T(8,128)}, u32[]{:S(2)}, u32[]{:S(2)}) collective-permute-start(f32[33,1,512]{2,0,1:T(8,128)} %pad_maximum_fusion.15), channel_id=1, source_target_pairs={{4,0},{8,4},{12,8},{16,12},{20,16},{24,20},{28,24},{32,28},{36,32}... | collective-permute-start | bytes 202760 | tf_op jit(solution)/shard_map/ppermute | solution.py:15
  18.4 3.1 %collective-permute-start.3 = (f32[33,16,1]{2,0,1:T(8,128)S(1)}, f32[33,16,1]{2,0,1:T(8,128)S(1)}, u32[]{:S(2)}, u32[]{:S(2)}) collective-permute-start(f32[33,16,1]{2,0,1:T(8,128)S(1)} %pad_maximum_fusion.10), channel_id=1, source_target_pairs={{0,1},{1,2},{2,3},{4,5},{5,6},{6,7},{8,9},{9,10},{10,11},{12,13},{... | collective-permute-start | bytes 6344 | tf_op jit(solution)/shard_map/ppermute | solution.py:14
  21.5 1.3 %collective-permute-start.4 = (f32[33,16,1]{2,0,1:T(8,128)S(1)}, f32[33,16,1]{2,0,1:T(8,128)}, u32[]{:S(2)}, u32[]{:S(2)}) collective-permute-start(f32[33,16,1]{2,0,1:T(8,128)S(1)} %pad_maximum_fusion.11), channel_id=1, source_target_pairs={{1,0},{2,1},{3,2},{5,4},{6,5},{7,6},{9,8},{10,9},{11,10},{13,12},{... | collective-permute-start | bytes 6344 | tf_op jit(solution)/shard_map/ppermute | solution.py:15
  26.1 1.2 fusion
  28.0 2.9 %fusion.11 = bf16[64,8,128]{2,1,0:T(8,128)(2,1)S(1)} fusion(bf16[1,1,64,256,128]{4,3,2,1,0:T(8,128)(2,1)} %param.23, bf16[64,8,256]{2,1,0:T(8,128)(2,1)S(1)} %gather_fusion, pred[64]{0:T(512)(128)(4,1)} %compare_and_fusion), kind=kOutput, calls=%fused_computation.20 | convolution fusion | flops 33751040 | bytes 4587584 | tf_op jit(solution)/shard_map/fpi,pio->pfo/dot_general | solution.py:117
  33.3 1.3 %slice.206 = f32[1,1,512]{2,0,1:T(1,128)} slice(f32[33,1,512]{2,0,1:T(8,128)} %collective-permute-done.2), slice={[32:33], [0:1], [0:512]} | slice | bytes 4096 | tf_op jit(solution)/shard_map/slice | solution.py:38
  35.4 1.3 %slice.205 = f32[1,1,512]{2,0,1:T(1,128)} slice(f32[33,1,512]{2,0,1:T(8,128)} %collective-permute-done.1), slice={[32:33], [0:1], [0:512]} | slice | bytes 4096 | tf_op jit(solution)/shard_map/slice | solution.py:38
  37.6 1.5 %slice.218 = f32[1,16,1]{2,0,1:T(1,128)} slice(f32[33,16,1]{2,0,1:T(8,128)} %collective-permute-done.4), slice={[32:33], [0:16], [0:1]} | slice | bytes 128 | tf_op jit(solution)/shard_map/slice | solution.py:40
  40.7 2.9 %fusion.6 = f32[32,16,512]{2,0,1:T(8,128)S(1)} fusion(f32[32,16,512]{2,0,1:T(8,128)S(1)} %get-tuple-element.80, f32[32,16,1]{2,0,1:T(8,128)S(1)} %slice.203, f32[32,16,1]{2,0,1:T(8,128)S(1)} %slice.201, f32[32,16,512]{2,0,1:T(8,128)S(1)} %get-tuple-element.81, f32[32,1,512]{2,0,1:T(8,128)S(1)} %slice.199, f32[32,1,512]{2,0,1:T(8,128)S(1)} %slice.197, ...), kind=kOutput, calls=%fused_computation.11 | convolution fusion | flops 105644032 | bytes 4366336 | tf_op jit(solution)/shard_map/lm,mxy->lxy/dot_general | solution.py:20
  45.2 11.5 %all-to-all-start = ((f32[32,5,128]{2,1,0:T(8,128)}), f32[32,5,128]{2,1,0:T(8,128)}, u32[]{:S(2)}, u32[]{:S(2)}) async-start(f32[32,5,128]{2,1,0:T(8,128)} %pad_maximum_fusion.13), calls=%async_computation | async-start | bytes 262144 | tf_op jit(solution)/shard_map/all_to_all | solution.py:145
  58.2 2.2 %collective-permute-start.6 = (f32[32,2,512]{2,0,1:T(8,128)}, f32[32,2,512]{2,0,1:T(8,128)}, u32[]{:S(2)}, u32[]{:S(2)}) collective-permute-start(f32[32,2,512]{2,0,1:T(8,128)} %get-tuple-element.68), channel_id=1, source_target_pairs={{4,0},{8,4},{12,8},{16,12},{20,16},{24,20},{28,24},{32,28},{36,32}... | collective-permute-start | bytes 393224 | tf_op jit(solution)/shard_map/ppermute | solution.py:15
  60.4 3.3 %collective-permute-start.5 = (f32[32,2,512]{2,0,1:T(8,128)}, f32[32,2,512]{2,0,1:T(8,128)}, u32[]{:S(2)}, u32[]{:S(2)}) collective-permute-start(f32[32,2,512]{2,0,1:T(8,128)} %get-tuple-element.69), channel_id=1, source_target_pairs={{0,4},{4,8},{8,12},{12,16},{16,20},{20,24},{24,28},{28,32},{32,36}... | collective-permute-start | bytes 393224 | tf_op jit(solution)/shard_map/ppermute | solution.py:14
  63.8 1.3 %collective-permute-start.8 = (f32[32,16,2]{2,0,1:T(8,128)}, f32[32,16,2]{2,0,1:T(8,128)}, u32[]{:S(2)}, u32[]{:S(2)}) collective-permute-start(f32[32,16,2]{2,0,1:T(8,128)} %get-tuple-element.66), channel_id=1, source_target_pairs={{1,0},{2,1},{3,2},{5,4},{6,5},{7,6},{9,8},{10,9},{11,10},{13,12},{... | collective-permute-start | bytes 12296 | tf_op jit(solution)/shard_map/ppermute | solution.py:15
  65.1 5.6 %collective-permute-start.7 = (f32[32,16,2]{2,0,1:T(8,128)}, f32[32,16,2]{2,0,1:T(8,128)}, u32[]{:S(2)}, u32[]{:S(2)}) collective-permute-start(f32[32,16,2]{2,0,1:T(8,128)} %get-tuple-element.67), channel_id=1, source_target_pairs={{0,1},{1,2},{2,3},{4,5},{5,6},{6,7},{8,9},{9,10},{10,11},{12,13},{... | collective-permute-start | bytes 12296 | tf_op jit(solution)/shard_map/ppermute | solution.py:14
  71.8 1.6 %fusion.58 = s32[32,4]{1,0:T(8,128)} fusion(f32[32,5,128]{2,1,0:T(8,128)} %all-to-all-done), kind=kLoop, calls=%fused_computation.101 | loop fusion | flops 128 | bytes 1024 | tf_op jit(solution)/shard_map/convert_element_type | solution.py:146
  73.3 1.4 %convert_element_type.81 = s32[128]{0:T(128)} reshape(s32[32,4]{1,0:T(8,128)} %fusion.58) | data formatting | bytes 1024 | tf_op jit(solution)/shard_map/convert_element_type | solution.py:146
  76.5 1.5 %convolution_convert_fusion = bf16[128,128]{1,0:T(8,128)(2,1)} fusion(f32[64,128]{1,0:T(8,128)S(1)} %fusion.55, f32[64,128]{1,0:T(8,128)S(1)} %bitcast.122, f32[64,128]{1,0:T(8,128)S(1)} %bitcast.115, f32[64,128]{1,0:T(8,128)S(1)} %bitcast.120, f32[64,128]{1,0:T(8,128)S(1)} %reshape_squeeze.7, s32[128]{0:T(128)} %convert_element_type.81, pred[]{:T(512)S(6)} %eq.61), kind=kOutput, calls=%fused_computation.21 | convolution fusion | flops 2162688 | bytes 197121 | tf_op jit(solution)/shard_map/dot_general | solution.py:154
  78.0 9.0 %all-to-all-start.1 = ((bf16[32,4,128]{2,1,0:T(4,128)(2,1)}), bf16[32,4,128]{2,1,0:T(4,128)(2,1)}, u32[]{:S(2)}, u32[]{:S(2)}) async-start(bf16[32,4,128]{2,1,0:T(4,128)(2,1)} %bitcast.139), calls=%async_computation.1 | async-start | bytes 65536 | tf_op jit(solution)/shard_map/all_to_all | solution.py:165
  87.1 2.0 %fusion.7 = f32[32,16,514]{2,0,1:T(8,128)S(1)} fusion(f32[32,16,1]{2,0,1:T(8,128)S(1)} %slice.201, f32[32,16,512]{2,0,1:T(8,128)S(1)} %get-tuple-element.80, f32[32,16,1]{2,0,1:T(8,128)} %copy-done.5, f32[32,16,2]{2,0,1:T(8,128)} %collective-permute-done.8, f32[32,16,512]{2,0,1:T(8,128)S(1)} %fusion.6, f32[32,16,2]{2,0,1:T(8,128)} %collective-permute-done.7, ...), kind=kLoop, calls=%fused_computation.13 | loop fusion | flops 2105344 | bytes 3195008 | tf_op jit(solution)/shard_map/mul | solution.py:51
  89.1 1.6 %fusion.9 = f32[32,18,512]{2,0,1:T(8,128)S(1)} fusion(f32[32,1,512]{2,0,1:T(8,128)S(1)} %copy-done.9, f32[32,16,512]{2,0,1:T(8,128)S(1)} %get-tuple-element.81, f32[32,1,512]{2,0,1:T(8,128)S(1)} %copy-done.11, f32[32,2,512]{2,0,1:T(8,128)} %collective-permute-done.6, f32[32,16,512]{2,0,1:T(8,128)S(1)} %fusion.6, f32[32,2,512]{2,0,1:T(8,128)} %collective-permute-done.5, ...), kind=kLoop, calls=%fused_computation.17 | loop fusion | flops 2359296 | bytes 3706880 | tf_op jit(solution)/shard_map/mul | solution.py:50
  90.8 1.8 %fusion.5 = f32[32,16,512]{2,0,1:T(8,128)S(1)} fusion(f32[32,16,512]{2,0,1:T(8,128)S(1)} %fusion.6, f32[32,16,514]{2,0,1:T(8,128)S(1)} %fusion.7, f32[32,18,512]{2,0,1:T(8,128)S(1)} %fusion.9, f32[16,512]{1,0:T(8,128)S(1)} %bitcast.143, f32[1,32,32]{2,1,0:T(8,128)S(1)} %copy-done), kind=kOutput, calls=%fused_computation.9 | convolution fusion | flops 103546880 | bytes 11616256 | tf_op jit(solution)/shard_map/lm,mxy->lxy/dot_general | solution.py:20
  93.3 2.4 %collective-permute-start.10 = (f32[32,1,512]{2,0,1:T(8,128)}, f32[32,1,512]{2,0,1:T(8,128)}, u32[]{:S(2)}, u32[]{:S(2)}) collective-permute-start(f32[32,1,512]{2,0,1:T(8,128)} %get-tuple-element.64), channel_id=1, source_target_pairs={{4,0},{8,4},{12,8},{16,12},{20,16},{24,20},{28,24},{32,28},{36,32}... | collective-permute-start | bytes 196616 | tf_op jit(solution)/shard_map/ppermute | solution.py:15
  95.6 3.2 %collective-permute-start.9 = (f32[32,1,512]{2,0,1:T(8,128)}, f32[32,1,512]{2,0,1:T(8,128)}, u32[]{:S(2)}, u32[]{:S(2)}) collective-permute-start(f32[32,1,512]{2,0,1:T(8,128)} %get-tuple-element.65), channel_id=1, source_target_pairs={{0,4},{4,8},{8,12},{12,16},{16,20},{20,24},{24,28},{28,32},{32,36}... | collective-permute-start | bytes 196616 | tf_op jit(solution)/shard_map/ppermute | solution.py:14
  99.0 1.3 %collective-permute-start.12 = (f32[32,16,1]{2,0,1:T(8,128)S(1)}, f32[32,16,1]{2,0,1:T(8,128)S(1)}, u32[]{:S(2)}, u32[]{:S(2)}) collective-permute-start(f32[32,16,1]{2,0,1:T(8,128)S(1)} %get-tuple-element.62), channel_id=1, source_target_pairs={{1,0},{2,1},{3,2},{5,4},{6,5},{7,6},{9,8},{10,9},{11,10},{13,12},{... | collective-permute-start | bytes 6152 | tf_op jit(solution)/shard_map/ppermute | solution.py:15
  100.3 4.0 %collective-permute-start.11 = (f32[32,16,1]{2,0,1:T(8,128)S(1)}, f32[32,16,1]{2,0,1:T(8,128)S(1)}, u32[]{:S(2)}, u32[]{:S(2)}) collective-permute-start(f32[32,16,1]{2,0,1:T(8,128)S(1)} %get-tuple-element.63), channel_id=1, source_target_pairs={{0,1},{1,2},{2,3},{4,5},{5,6},{6,7},{8,9},{9,10},{10,11},{12,13},{... | collective-permute-start | bytes 6152 | tf_op jit(solution)/shard_map/ppermute | solution.py:14
  104.3 4.6 %collective-permute-done.12 = f32[32,16,1]{2,0,1:T(8,128)S(1)} collective-permute-done((f32[32,16,1]{2,0,1:T(8,128)S(1)}, f32[32,16,1]{2,0,1:T(8,128)S(1)}, u32[]{:S(2)}, u32[]{:S(2)}) %collective-permute-start.12) | collective-permute-done | bytes 2080 | tf_op jit(solution)/shard_map/ppermute | solution.py:15
  110.5 2.4 %fusion.24 = (f32[1,32,16,512]{3,1,2,0:T(8,128)S(1)}, f32[1,32,16,512]{3,1,2,0:T(8,128)S(1)}) fusion(f32[32,16,512]{2,0,1:T(8,128)S(1)} %fusion.5, f32[32,1,512]{2,0,1:T(8,128)} %collective-permute-done.9, f32[32,1,512]{2,0,1:T(8,128)} %collective-permute-done.10, f32[32,18,512]{2,0,1:T(8,128)} %copy-done.4, f32[16,512]{1,0:T(8,128)S(1)} %bitcast.128, ...), kind=kLoop, calls=%fused_computation.36 | loop fusion | flops 3145728 | bytes 5410816 | tf_op jit(solution)/shard_map/stack | solution.py:176
  113.4 3.5 %copy.42 = f32[1,3,32,16,512]{4,3,2,1,0:T(8,128)} copy(f32[1,3,32,16,512]{4,2,3,1,0:T(8,128)S(1)} %maximum_bitcast_fusion) | data formatting | bytes 6291456
  (132 shorter events, 25.5 us)
Async XLA Ops:
  0.6 40.0 %copy-start = (f32[1,32,32]{2,1,0:T(8,128)S(1)}, f32[1,32,32]{2,1,0:T(8,128)}, u32[]{:S(2)}) copy-start(f32[1,32,32]{2,1,0:T(8,128)} %param.16) | copy-start | bytes 12292
  3.4 22.6 %collective-permute-start = (f32[4,8192]{1,0:T(4,128)S(1)}, f32[4,8192]{1,0:T(4,128)}, u32[]{:S(2)}, u32[]{:S(2)}) collective-permute-start(f32[4,8192]{1,0:T(4,128)S(1)} %maximum_select_fusion), channel_id=1, source_target_pairs={{0,128},{128,0},{1,129},{129,1},{2,130},{130,2},{3,131},{131,3},{4... | collective-permute-start | bytes 393224 | tf_op jit(solution)/shard_map/ppermute | solution.py:108
  11.7 11.1 %copy-start.21 = (s32[1,1,64]{2,1,0:T(1,128)S(1)}, s32[1,1,64]{2,1,0:T(1,128)}, u32[]{:S(2)}) copy-start(s32[1,1,64]{2,1,0:T(1,128)} %param.21) | copy-start | bytes 772
  11.7 11.7 %copy-start.28 = (s32[1,1,64]{2,1,0:T(1,128)S(1)}, s32[1,1,64]{2,1,0:T(1,128)}, u32[]{:S(2)}) copy-start(s32[1,1,64]{2,1,0:T(1,128)} %param.22) | copy-start | bytes 772
  11.7 11.7 %copy-start.29 = (s32[1,1,64,1]{2,3,1,0:T(1,128)S(1)}, s32[1,1,64,1]{2,3,1,0:T(1,128)}, u32[]{:S(2)}) copy-start(s32[1,1,64,1]{2,3,1,0:T(1,128)} %param.20) | copy-start | bytes 772
  11.7 12.4 %copy-start.7 = (f32[1,16,512]{2,1,0:T(8,128)S(1)}, f32[1,16,512]{2,1,0:T(8,128)}, u32[]{:S(2)}) copy-start(f32[1,16,512]{2,1,0:T(8,128)} %param.17) | copy-start | bytes 98308
  12.4 20.9 %collective-permute-start.1 = (f32[33,1,512]{2,0,1:T(8,128)}, f32[33,1,512]{2,0,1:T(8,128)}, u32[]{:S(2)}, u32[]{:S(2)}) collective-permute-start(f32[33,1,512]{2,0,1:T(8,128)} %pad_maximum_fusion.14), channel_id=1, source_target_pairs={{0,4},{4,8},{8,12},{12,16},{16,20},{20,24},{24,28},{28,32},{32,36}... | collective-permute-start | bytes 202760 | tf_op jit(solution)/shard_map/ppermute | solution.py:14
  16.2 17.1 %collective-permute-start.2 = (f32[33,1,512]{2,0,1:T(8,128)}, f32[33,1,512]{2,0,1:T(8,128)}, u32[]{:S(2)}, u32[]{:S(2)}) collective-permute-start(f32[33,1,512]{2,0,1:T(8,128)} %pad_maximum_fusion.15), channel_id=1, source_target_pairs={{4,0},{8,4},{12,8},{16,12},{20,16},{24,20},{28,24},{32,28},{36,32}... | collective-permute-start | bytes 202760 | tf_op jit(solution)/shard_map/ppermute | solution.py:15
  18.4 13.9 %collective-permute-start.3 = (f32[33,16,1]{2,0,1:T(8,128)S(1)}, f32[33,16,1]{2,0,1:T(8,128)S(1)}, u32[]{:S(2)}, u32[]{:S(2)}) collective-permute-start(f32[33,16,1]{2,0,1:T(8,128)S(1)} %pad_maximum_fusion.10), channel_id=1, source_target_pairs={{0,1},{1,2},{2,3},{4,5},{5,6},{6,7},{8,9},{9,10},{10,11},{12,13},{... | collective-permute-start | bytes 6344 | tf_op jit(solution)/shard_map/ppermute | solution.py:14
  21.5 11.7 %collective-permute-start.4 = (f32[33,16,1]{2,0,1:T(8,128)S(1)}, f32[33,16,1]{2,0,1:T(8,128)}, u32[]{:S(2)}, u32[]{:S(2)}) collective-permute-start(f32[33,16,1]{2,0,1:T(8,128)S(1)} %pad_maximum_fusion.11), channel_id=1, source_target_pairs={{1,0},{2,1},{3,2},{5,4},{6,5},{7,6},{9,8},{10,9},{11,10},{13,12},{... | collective-permute-start | bytes 6344 | tf_op jit(solution)/shard_map/ppermute | solution.py:15
  28.0 3.5 %copy-start.15 = (f32[32,1,128]{2,0,1:T(8,128)S(1)}, f32[32,1,128]{2,0,1:T(8,128)}, u32[]{:S(2)}) copy-start(f32[32,1,128]{2,0,1:T(8,128)} %scatter.4) | copy-start | bytes 49156
  30.9 9.7 %copy-start.6 = (f32[1,1,32,16,512]{4,3,2,1,0:T(8,128)S(1)}, f32[1,1,32,16,512]{4,3,2,1,0:T(8,128)}, u32[]{:S(2)}) copy-start(f32[1,1,32,16,512]{4,3,2,1,0:T(8,128)} %get-tuple-element.54) | copy-start | bytes 3145732
  30.9 9.7 %copy-start.26 = (f32[1,16,512]{2,1,0:T(8,128)S(1)}, f32[1,16,512]{2,1,0:T(8,128)}, u32[]{:S(2)}) copy-start(f32[1,16,512]{2,1,0:T(8,128)} %param.14) | copy-start | bytes 98308
  35.4 8.2 %copy-start.8 = (f32[32,1,512]{2,0,1:T(8,128)}, f32[32,1,512]{2,0,1:T(8,128)S(1)}, u32[]{:S(2)}) copy-start(f32[32,1,512]{2,0,1:T(8,128)S(1)} %slice.197) | copy-start | bytes 196612
  37.6 6.0 %copy-start.10 = (f32[32,1,512]{2,0,1:T(8,128)}, f32[32,1,512]{2,0,1:T(8,128)S(1)}, u32[]{:S(2)}) copy-start(f32[32,1,512]{2,0,1:T(8,128)S(1)} %slice.199) | copy-start | bytes 196612
  43.6 13.1 %copy-start.16 = (f32[1,16,1]{2,0,1:T(1,128)S(1)}, f32[1,16,1]{2,0,1:T(1,128)}, u32[]{:S(2)}) copy-start(f32[1,16,1]{2,0,1:T(1,128)} %slice.218) | copy-start | bytes 196
  43.6 13.1 %copy-start.17 = (f32[1,16,1]{2,0,1:T(1,128)S(1)}, f32[1,16,1]{2,0,1:T(1,128)}, u32[]{:S(2)}) copy-start(f32[1,16,1]{2,0,1:T(1,128)} %slice.217) | copy-start | bytes 196
  43.6 13.9 %copy-start.18 = (f32[1,1,512]{2,0,1:T(1,128)S(1)}, f32[1,1,512]{2,0,1:T(1,128)}, u32[]{:S(2)}) copy-start(f32[1,1,512]{2,0,1:T(1,128)} %slice.206) | copy-start | bytes 6148
  43.6 13.9 %copy-start.19 = (f32[1,1,512]{2,0,1:T(1,128)S(1)}, f32[1,1,512]{2,0,1:T(1,128)}, u32[]{:S(2)}) copy-start(f32[1,1,512]{2,0,1:T(1,128)} %slice.205) | copy-start | bytes 6148
  45.2 26.5 %all-to-all-start = ((f32[32,5,128]{2,1,0:T(8,128)}), f32[32,5,128]{2,1,0:T(8,128)}, u32[]{:S(2)}, u32[]{:S(2)}) async-start(f32[32,5,128]{2,1,0:T(8,128)} %pad_maximum_fusion.13), calls=%async_computation | async-start | bytes 262144 | tf_op jit(solution)/shard_map/all_to_all | solution.py:145
  58.2 19.8 %collective-permute-start.6 = (f32[32,2,512]{2,0,1:T(8,128)}, f32[32,2,512]{2,0,1:T(8,128)}, u32[]{:S(2)}, u32[]{:S(2)}) collective-permute-start(f32[32,2,512]{2,0,1:T(8,128)} %get-tuple-element.68), channel_id=1, source_target_pairs={{4,0},{8,4},{12,8},{16,12},{20,16},{24,20},{28,24},{32,28},{36,32}... | collective-permute-start | bytes 393224 | tf_op jit(solution)/shard_map/ppermute | solution.py:15
  60.4 17.6 %collective-permute-start.5 = (f32[32,2,512]{2,0,1:T(8,128)}, f32[32,2,512]{2,0,1:T(8,128)}, u32[]{:S(2)}, u32[]{:S(2)}) collective-permute-start(f32[32,2,512]{2,0,1:T(8,128)} %get-tuple-element.69), channel_id=1, source_target_pairs={{0,4},{4,8},{8,12},{12,16},{16,20},{20,24},{24,28},{28,32},{32,36}... | collective-permute-start | bytes 393224 | tf_op jit(solution)/shard_map/ppermute | solution.py:14
  63.8 14.2 %collective-permute-start.8 = (f32[32,16,2]{2,0,1:T(8,128)}, f32[32,16,2]{2,0,1:T(8,128)}, u32[]{:S(2)}, u32[]{:S(2)}) collective-permute-start(f32[32,16,2]{2,0,1:T(8,128)} %get-tuple-element.66), channel_id=1, source_target_pairs={{1,0},{2,1},{3,2},{5,4},{6,5},{7,6},{9,8},{10,9},{11,10},{13,12},{... | collective-permute-start | bytes 12296 | tf_op jit(solution)/shard_map/ppermute | solution.py:15
  65.1 12.9 %collective-permute-start.7 = (f32[32,16,2]{2,0,1:T(8,128)}, f32[32,16,2]{2,0,1:T(8,128)}, u32[]{:S(2)}, u32[]{:S(2)}) collective-permute-start(f32[32,16,2]{2,0,1:T(8,128)} %get-tuple-element.67), channel_id=1, source_target_pairs={{0,1},{1,2},{2,3},{4,5},{5,6},{6,7},{8,9},{9,10},{10,11},{12,13},{... | collective-permute-start | bytes 12296 | tf_op jit(solution)/shard_map/ppermute | solution.py:14
  78.0 31.8 %all-to-all-start.1 = ((bf16[32,4,128]{2,1,0:T(4,128)(2,1)}), bf16[32,4,128]{2,1,0:T(4,128)(2,1)}, u32[]{:S(2)}, u32[]{:S(2)}) async-start(bf16[32,4,128]{2,1,0:T(4,128)(2,1)} %bitcast.139), calls=%async_computation.1 | async-start | bytes 65536 | tf_op jit(solution)/shard_map/all_to_all | solution.py:165
  92.6 17.9 %copy-start.3 = (f32[32,16,514]{2,0,1:T(8,128)S(1)}, f32[32,16,514]{2,0,1:T(8,128)}, u32[]{:S(2)}) copy-start(f32[32,16,514]{2,0,1:T(8,128)} %copy-done.2) | copy-start | bytes 3158020
  93.3 16.6 %collective-permute-start.10 = (f32[32,1,512]{2,0,1:T(8,128)}, f32[32,1,512]{2,0,1:T(8,128)}, u32[]{:S(2)}, u32[]{:S(2)}) collective-permute-start(f32[32,1,512]{2,0,1:T(8,128)} %get-tuple-element.64), channel_id=1, source_target_pairs={{4,0},{8,4},{12,8},{16,12},{20,16},{24,20},{28,24},{32,28},{36,32}... | collective-permute-start | bytes 196616 | tf_op jit(solution)/shard_map/ppermute | solution.py:15
  95.6 14.2 %collective-permute-start.9 = (f32[32,1,512]{2,0,1:T(8,128)}, f32[32,1,512]{2,0,1:T(8,128)}, u32[]{:S(2)}, u32[]{:S(2)}) collective-permute-start(f32[32,1,512]{2,0,1:T(8,128)} %get-tuple-element.65), channel_id=1, source_target_pairs={{0,4},{4,8},{8,12},{12,16},{16,20},{20,24},{24,28},{28,32},{32,36}... | collective-permute-start | bytes 196616 | tf_op jit(solution)/shard_map/ppermute | solution.py:14
  99.0 9.9 %collective-permute-start.12 = (f32[32,16,1]{2,0,1:T(8,128)S(1)}, f32[32,16,1]{2,0,1:T(8,128)S(1)}, u32[]{:S(2)}, u32[]{:S(2)}) collective-permute-start(f32[32,16,1]{2,0,1:T(8,128)S(1)} %get-tuple-element.62), channel_id=1, source_target_pairs={{1,0},{2,1},{3,2},{5,4},{6,5},{7,6},{9,8},{10,9},{11,10},{13,12},{... | collective-permute-start | bytes 6152 | tf_op jit(solution)/shard_map/ppermute | solution.py:15
  100.3 9.5 %collective-permute-start.11 = (f32[32,16,1]{2,0,1:T(8,128)S(1)}, f32[32,16,1]{2,0,1:T(8,128)S(1)}, u32[]{:S(2)}, u32[]{:S(2)}) collective-permute-start(f32[32,16,1]{2,0,1:T(8,128)S(1)} %get-tuple-element.63), channel_id=1, source_target_pairs={{0,1},{1,2},{2,3},{4,5},{5,6},{6,7},{8,9},{9,10},{10,11},{12,13},{... | collective-permute-start | bytes 6152 | tf_op jit(solution)/shard_map/ppermute | solution.py:14
  113.4 3.5 %copy-start.25 = (s32[64]{0:T(128)S(1)}, s32[64]{0:T(128)}, u32[]{:S(2)}) copy-start(s32[64]{0:T(128)} %copy-done.23) | copy-start | bytes 772
  113.4 4.4 %copy-start.1 = (bf16[1,1,64,256,128]{4,3,2,1,0:T(8,128)(2,1)S(1)}, bf16[1,1,64,256,128]{4,3,2,1,0:T(8,128)(2,1)}, u32[]{:S(2)}) copy-start(bf16[1,1,64,256,128]{4,3,2,1,0:T(8,128)(2,1)} %param.23) | copy-start | bytes 12582916
  (13 other events, 23.7 us)

commit v7 on v2

--- a/solution.py
+++ b/solution.py
@@ -16,6 +16,17 @@
     return lo, hi
 
 
+def neighbours_exchanged(head, tail, axis):
+    count = lax.axis_size(axis)
+    me = lax.axis_index(axis)
+    ranks = jnp.arange(count).reshape((count,) + (1,) * head.ndim)
+    sent = jnp.where(ranks == me - 1, head[None], jnp.where(ranks == me + 1, tail[None], 0.0))
+    got = lax.all_to_all(sent, axis, 0, 0, tiled=True)
+    lo = jnp.sum(jnp.where(ranks == me - 1, got, 0.0), axis=0)
+    hi = jnp.sum(jnp.where(ranks == me + 1, got, 0.0), axis=0)
+    return lo, hi
+
+
 def vertical_mix(matrix, right_side):
     return right_side + jnp.einsum("lm,mxy->lxy", matrix, right_side, precision=HIGHEST_PRECISION)
 
@@ -27,7 +38,7 @@
         jnp.concatenate([eastward[:, -1:], wet3[:, -1:]], axis=0),
         "gx",
     )
-    lo_y, hi_y = neighbours(
+    lo_y, hi_y = neighbours_exchanged(
         jnp.concatenate([northward[:, :, :1], wet3[:, :, :1]], axis=0),
         jnp.concatenate([northward[:, :, -1:], wet3[:, :, -1:]], axis=0),
         "gy",
@@ -42,7 +53,7 @@
     p1 = vertical_mix(matrix, pressure - sound_speed * divergence)
 
     lo2x, hi2x = neighbours(p1[:, :2], p1[:, -2:], "gx")
-    lo2y, hi2y = neighbours(p1[:, :, :2], p1[:, :, -2:], "gy")
+    lo2y, hi2y = neighbours_exchanged(p1[:, :, :2], p1[:, :, -2:], "gy")
     p1_x = jnp.concatenate([lo2x, p1, hi2x], axis=1)
     p1_y = jnp.concatenate([lo2y, p1, hi2y], axis=2)
     u1_ext = wet_x * (u_ext - 0.5 * (p1_x[:, 2:] - p1_x[:, :-2]))
@@ -52,7 +63,7 @@
     p2 = vertical_mix(matrix, p1 - sound_speed * divergence)
 
     lo3x, hi3x = neighbours(p2[:, :1], p2[:, -1:], "gx")
-    lo3y, hi3y = neighbours(p2[:, :, :1], p2[:, :, -1:], "gy")
+    lo3y, hi3y = neighbours_exchanged(p2[:, :, :1], p2[:, :, -1:], "gy")
     p2_x = jnp.concatenate([lo3x, p2, hi3x], axis=1)
     p2_y = jnp.concatenate([lo3y, p2, hi3y], axis=2)
     u1 = u1_ext[:, 1:-1]

time: 114 us -> 132 us (1.16)
  local copies, waits for them, and re-layouts: 19.6 us -> 35.5 us
  other arithmetic: 7.7 us -> 19.5 us
  waiting for transfers between devices: 9.67 us -> 5.17 us
  starting transfers between devices: 58.5 us -> 54.2 us
    all_to_all x0 -> x3, starting transfers between devices: none -> 13 us  [neighbours_exchanged(): got = lax.all_to_all(sent, axis, 0, 0, tiled=True)]
    ppermute x6 -> x3, starting transfers between devices: 22.8 us -> 11.3 us  [neighbours(): lo = lax.ppermute(tail, axis, [(i, i + 1) for i in range(count - 1)])]
    unnamed x54 -> x98, local copies, waits for them, and re-layouts: 8.46 us -> 14 us
    reduce_sum x0 -> x4, local copies, waits for them, and re-layouts: none -> 4.94 us  [the longest x2 2.48 us: neighbours_exchanged(): hi = jnp.sum(jnp.where(ranks == me + 1, got, 0.0), axis=0)]
    slice x2 -> x5, local copies, waits for them, and re-layouts: 0.28 us -> 4.76 us  [the longest x3 4.29 us: stencil(): lo2y, hi2y = neighbours_exchanged(p1[:, :, :2], p1[:, :, -2:], 'gy')]
    ppermute x6 -> x3, starting transfers between devices: 9.86 us -> 5.94 us  [neighbours(): hi = lax.ppermute(head, axis, [(i + 1, i) for i in range(count - 1)])]
    ppermute x6 -> x3, waiting for transfers between devices: 3.57 us -> 0.01 us  [neighbours(): hi = lax.ppermute(head, axis, [(i + 1, i) for i in range(count - 1)])]
    all_to_all x0 -> x3, other arithmetic: none -> 2.54 us  [neighbours_exchanged(): got = lax.all_to_all(sent, axis, 0, 0, tiled=True)]
  transfers between devices with their start and end apart: 15 -> 12, of which waited for: 4 -> 2; matrix products, arithmetic and copies ran while one was open for 29% -> 40% of each run, Pallas kernels for 0% -> 0%
where the time goes in v7:
time: 132 us; the launch traced here: 131 us
  starting transfers between devices  54.2 us (41%)
  local copies, waits for them, and re-layouts  35.5 us (27%)
  other arithmetic  19.5 us (15%)
  matrix products  15.1 us (11%)
  waiting for transfers between devices  5.17 us (4%)
  between operations  1.42 us (1%)
    all_to_all x1, starting transfers between devices, local(): lax.all_to_all(packet, 'gx', split_axis=0, concat_axis=0, tiled=True)  14 us
    unnamed x98, local copies, waits for them, and re-layouts  14 us
    all_to_all x3, starting transfers between devices, neighbours_exchanged(): got = lax.all_to_all(sent, axis, 0, 0, tiled=True)  13 us
    ppermute x3, starting transfers between devices, neighbours(): lo = lax.ppermute(tail, axis, [(i, i + 1) for i in range(count - 1)])  11.3 us
    dot_general x2, matrix products, vertical_mix(): jnp.einsum('lm,mxy->lxy', matrix, right_side, precision=HIGHEST_PRECISION)  6.32 us
    all_to_all x1, starting transfers between devices, local(): lax.all_to_all(returning.reshape(tile_count, capacity, out_width), 'gx',...  6.22 us
    ppermute x3, starting transfers between devices, neighbours(): hi = lax.ppermute(head, axis, [(i + 1, i) for i in range(count - 1)])  5.94 us
    slice x3, local copies, waits for them, and re-layouts, stencil(): lo2y, hi2y = neighbours_exchanged(p1[:, :, :2], p1[:, :, -2:], 'gy')  4.29 us
  transfers between devices with their start and end apart: 12, of which 2 were waited for; matrix products, arithmetic and copies ran while one was open for 40% of the time, Pallas kernels for 0%

profile of v7, /device:TPU:1, one launch (start us, length us, event | category | flops | bytes accessed | tf_op | source)
XLA Modules:
  0.0 130.9 jit_solution(3905161728013096580)
XLA Ops:
  4.2 3.7 %collective-permute-start.6 = (f32[4,8192]{1,0:T(4,128)}, f32[4,8192]{1,0:T(4,128)}, u32[]{:S(2)}, u32[]{:S(2)}) collective-permute-start(f32[4,8192]{1,0:T(4,128)} %maximum_select_fusion), channel_id=1, source_target_pairs={{0,128},{128,0},{1,129},{129,1},{2,130},{130,2},{3,131},{131,3},{4... | collective-permute-start | bytes 393224 | tf_op jit(solution)/shard_map/ppermute | solution.py:119
  8.0 3.2 %fusion.74 = (f32[1,1,32,16,512]{4,3,2,1,0:T(8,128)}, f32[1,1,32,16,512]{4,3,2,1,0:T(8,128)S(1)}, f32[1,1,32,16,512]{4,3,2,1,0:T(8,128)S(1)}) fusion(f32[1,3,32,16,512]{4,3,2,1,0:T(8,128)} %param.13), kind=kLoop, calls=%fused_computation.142 | loop fusion | bytes 6291456 | tf_op jit(solution)/shard_map/slice | solution.py:89
  13.2 4.0 %all-to-all-start = ((f32[4,1,528]{2,1,0:T(1,128)}), f32[4,1,528]{2,1,0:T(1,128)S(1)}, u32[]{:S(2)}, u32[]{:S(2)}) async-start(f32[4,1,528]{2,1,0:T(1,128)} %reshape.252), calls=%async_computation | async-start | bytes 20480 | tf_op jit(solution)/shard_map/all_to_all | solution.py:24
  17.9 3.4 %collective-permute-start.1 = (f32[33,1,512]{2,0,1:T(8,128)S(1)}, f32[33,1,512]{2,0,1:T(8,128)S(1)}, u32[]{:S(2)}, u32[]{:S(2)}) collective-permute-start(f32[33,1,512]{2,0,1:T(8,128)S(1)} %pad_maximum_fusion.13), channel_id=1, source_target_pairs={{0,4},{4,8},{8,12},{12,16},{16,20},{20,24},{24,28},{28,32},{32,36}... | collective-permute-start | bytes 202760 | tf_op jit(solution)/shard_map/ppermute | solution.py:14
  21.4 1.9 %collective-permute-start = (f32[33,1,512]{2,0,1:T(8,128)S(1)}, f32[33,1,512]{2,0,1:T(8,128)S(1)}, u32[]{:S(2)}, u32[]{:S(2)}) collective-permute-start(f32[33,1,512]{2,0,1:T(8,128)S(1)} %pad_maximum_fusion.12), channel_id=1, source_target_pairs={{4,0},{8,4},{12,8},{16,12},{20,16},{24,20},{28,24},{32,28},{36,32}... | collective-permute-start | bytes 202760 | tf_op jit(solution)/shard_map/ppermute | solution.py:15
  30.8 4.5 %fusion.6 = f32[32,16,512]{2,0,1:T(8,128)S(1)} fusion(f32[32,16,512]{2,0,1:T(8,128)S(1)} %bitcast.137, f32[32,16,1]{2,0,1:T(8,128)S(1)} %copy.106, f32[32,16,1]{2,0,1:T(8,128)} %copy.105, f32[32,16,512]{2,0,1:T(8,128)S(1)} %bitcast.140, f32[32,1,512]{2,0,1:T(8,128)S(1)} %slice.254, f32[32,1,512]{2,0,1:T(8,128)S(1)} %slice.251, ...), kind=kOutput, calls=%fused_computation.11 | convolution fusion | flops 105644032 | bytes 4366336 | tf_op jit(solution)/shard_map/lm,mxy->lxy/dot_general | solution.py:31
  36.9 1.7 %copy.111 = f32[32,16,2]{0,1,2:T(8,128)} copy(f32[32,16,2]{2,0,1:T(8,128)} %get-tuple-element.44) | data formatting | bytes 8192 | tf_op jit(solution)/shard_map/slice | solution.py:56
  38.6 1.7 %copy.112 = f32[32,16,2]{0,1,2:T(8,128)} copy(f32[32,16,2]{2,0,1:T(8,128)} %get-tuple-element.45) | data formatting | bytes 8192 | tf_op jit(solution)/shard_map/slice | solution.py:56
  41.9 4.5 %all-to-all-start.1 = ((f32[4,1,1024]{2,1,0:T(1,128)}), f32[4,1,1024]{2,1,0:T(1,128)S(1)}, u32[]{:S(2)}, u32[]{:S(2)}) async-start(f32[4,1,1024]{2,1,0:T(1,128)} %reshape.254), calls=%async_computation.1 | async-start | bytes 32768 | tf_op jit(solution)/shard_map/all_to_all | solution.py:24
  48.5 3.9 %collective-permute-start.3 = (f32[32,2,512]{2,0,1:T(8,128)}, f32[32,2,512]{2,0,1:T(8,128)}, u32[]{:S(2)}, u32[]{:S(2)}) collective-permute-start(f32[32,2,512]{2,0,1:T(8,128)} %get-tuple-element.42), channel_id=1, source_target_pairs={{0,4},{4,8},{8,12},{12,16},{16,20},{20,24},{24,28},{28,32},{32,36}... | collective-permute-start | bytes 393224 | tf_op jit(solution)/shard_map/ppermute | solution.py:14
  52.4 2.1 %collective-permute-start.2 = (f32[32,2,512]{2,0,1:T(8,128)}, f32[32,2,512]{2,0,1:T(8,128)}, u32[]{:S(2)}, u32[]{:S(2)}) collective-permute-start(f32[32,2,512]{2,0,1:T(8,128)} %get-tuple-element.43), channel_id=1, source_target_pairs={{4,0},{8,4},{12,8},{16,12},{20,16},{24,20},{28,24},{32,28},{36,32}... | collective-permute-start | bytes 393224 | tf_op jit(solution)/shard_map/ppermute | solution.py:15
  54.5 1.3 reduce.15
  56.6 1.3 %select_reduce_fusion = (f32[32,16,2]{0,1,2:T(8,128)}, f32[32,16,2]{0,1,2:T(8,128)}) fusion(pred[4]{0:T(512)(128)(4,1)} %copy-done.24, pred[4]{0:T(512)(128)(4,1)} %copy-done.26, f32[4,2,16,32]{3,2,1,0:T(8,128)S(1)} %reshape.255), kind=kLoop, calls=%fused_computation.78 | loop fusion | flops 14336 | bytes 24584 | tf_op jit(solution)/shard_map/reduce_sum | solution.py:25
  57.9 1.6 %copy.114 = f32[32,16,2]{2,0,1:T(8,128)} copy(f32[32,16,2]{0,1,2:T(8,128)} %get-tuple-element.26) | data formatting | bytes 8192 | tf_op jit(solution)/shard_map/reduce_sum | solution.py:25
  59.5 1.6 %copy.113 = f32[32,16,2]{2,0,1:T(8,128)} copy(f32[32,16,2]{0,1,2:T(8,128)} %get-tuple-element.27) | data formatting | bytes 8192 | tf_op jit(solution)/shard_map/reduce_sum | solution.py:26
  61.1 3.0 %fusion.7 = f32[32,16,514]{2,0,1:T(8,128)} fusion(f32[32,16,1]{2,0,1:T(8,128)} %copy.105, f32[32,16,512]{2,0,1:T(8,128)S(1)} %bitcast.138, f32[32,16,1]{2,0,1:T(8,128)S(1)} %copy.106, f32[32,16,2]{2,0,1:T(8,128)} %copy.113, f32[32,16,512]{2,0,1:T(8,128)S(1)} %fusion.6, f32[32,16,2]{2,0,1:T(8,128)} %copy.114, f32[16,514]{1,0:T(8,128)} %bitcast.154), kind=kLoop, calls=%fused_computation.13 | loop fusion | flops 2105344 | bytes 3195008 | tf_op jit(solution)/shard_map/mul | solution.py:60
  65.5 2.9 %fusion.11 = bf16[64,8,128]{2,1,0:T(8,128)(2,1)S(1)} fusion(bf16[1,1,64,256,128]{4,3,2,1,0:T(8,128)(2,1)} %param.23, bf16[64,8,256]{2,1,0:T(8,128)(2,1)S(1)} %gather_fusion, pred[64]{0:T(512)(128)(4,1)S(1)} %copy-done.34), kind=kOutput, calls=%fused_computation.20 | convolution fusion | flops 33751040 | bytes 4587584 | tf_op jit(solution)/shard_map/fpi,pio->pfo/dot_general | solution.py:128
  68.7 1.0 fusion.80
  70.9 1.4 %fusion.9 = f32[32,18,512]{2,0,1:T(8,128)S(1)} fusion(f32[32,1,512]{2,0,1:T(8,128)S(1)} %copy-done.8, f32[32,16,512]{2,0,1:T(8,128)S(1)} %bitcast.141, f32[32,1,512]{2,0,1:T(8,128)S(1)} %copy-done.6, f32[32,2,512]{2,0,1:T(8,128)} %collective-permute-done.2, f32[32,16,512]{2,0,1:T(8,128)S(1)} %fusion.6, f32[32,2,512]{2,0,1:T(8,128)} %collective-permute-done.3, ...), kind=kLoop, calls=%fused_computation.17 | loop fusion | flops 2359296 | bytes 3706880 | tf_op jit(solution)/shard_map/mul | solution.py:59
  72.3 1.8 %fusion.5 = f32[32,16,512]{2,0,1:T(8,128)S(1)} fusion(f32[32,16,512]{2,0,1:T(8,128)S(1)} %fusion.6, f32[32,16,514]{2,0,1:T(8,128)S(1)} %copy-done.1, f32[32,18,512]{2,0,1:T(8,128)S(1)} %fusion.9, f32[16,512]{1,0:T(8,128)S(1)} %bitcast.175, f32[1,32,32]{2,1,0:T(8,128)S(1)} %copy-done), kind=kOutput, calls=%fused_computation.9 | convolution fusion | flops 103546880 | bytes 11616256 | tf_op jit(solution)/shard_map/lm,mxy->lxy/dot_general | solution.py:31
  75.2 4.5 %all-to-all-start.2 = ((f32[4,1,512]{2,1,0:T(1,128)}), f32[4,1,512]{2,1,0:T(1,128)S(1)}, u32[]{:S(2)}, u32[]{:S(2)}) async-start(f32[4,1,512]{2,1,0:T(1,128)} %reshape.256), calls=%async_computation.2 | async-start | bytes 16384 | tf_op jit(solution)/shard_map/all_to_all | solution.py:24
  79.7 1.9 %collective-permute-start.4 = (f32[32,1,512]{2,0,1:T(8,128)S(1)}, f32[32,1,512]{2,0,1:T(8,128)S(1)}, u32[]{:S(2)}, u32[]{:S(2)}) collective-permute-start(f32[32,1,512]{2,0,1:T(8,128)S(1)} %get-tuple-element.40), channel_id=1, source_target_pairs={{4,0},{8,4},{12,8},{16,12},{20,16},{24,20},{28,24},{32,28},{36,32}... | collective-permute-start | bytes 196616 | tf_op jit(solution)/shard_map/ppermute | solution.py:15
  81.7 3.9 %collective-permute-start.5 = (f32[32,1,512]{2,0,1:T(8,128)S(1)}, f32[32,1,512]{2,0,1:T(8,128)S(1)}, u32[]{:S(2)}, u32[]{:S(2)}) collective-permute-start(f32[32,1,512]{2,0,1:T(8,128)S(1)} %get-tuple-element.41), channel_id=1, source_target_pairs={{0,4},{4,8},{8,12},{12,16},{16,20},{20,24},{24,28},{28,32},{32,36}... | collective-permute-start | bytes 196616 | tf_op jit(solution)/shard_map/ppermute | solution.py:14
  85.6 14.0 %all-to-all-start.3 = ((f32[32,5,128]{2,1,0:T(8,128)}), f32[32,5,128]{2,1,0:T(8,128)}, u32[]{:S(2)}, u32[]{:S(2)}) async-start(f32[32,5,128]{2,1,0:T(8,128)} %pad_maximum_fusion.11), calls=%async_computation.3 | async-start | bytes 262144 | tf_op jit(solution)/shard_map/all_to_all | solution.py:149
  103.5 3.4 %fusion.24 = (f32[1,32,16,512]{3,1,2,0:T(8,128)S(1)}, f32[1,32,16,512]{3,1,2,0:T(8,128)}) fusion(f32[32,16,512]{2,0,1:T(8,128)S(1)} %fusion.5, f32[32,1,512]{2,0,1:T(8,128)} %copy-done.20, f32[32,1,512]{2,0,1:T(8,128)} %copy-done.19, f32[32,18,512]{2,0,1:T(8,128)} %copy-done.3, f32[16,512]{1,0:T(8,128)} %bitcast.155, f32[32,16,1]{2,0,1:T(8,128)} %copy.116, ...), kind=kLoop, calls=%fused_computation.36 | loop fusion | flops 3145728 | bytes 5410816 | tf_op jit(solution)/shard_map/stack | solution.py:97
  106.9 2.1 %all-to-all-done.3 = f32[32,5,128]{2,1,0:T(8,128)} async-done(((f32[32,5,128]{2,1,0:T(8,128)}), f32[32,5,128]{2,1,0:T(8,128)}, u32[]{:S(2)}, u32[]{:S(2)}) %all-to-all-start.3) | async-done | bytes 81952 | tf_op jit(solution)/shard_map/all_to_all | solution.py:149
  109.0 1.0 fusion.59
  112.0 6.2 %all-to-all-start.4 = ((bf16[32,4,128]{2,1,0:T(4,128)(2,1)}), bf16[32,4,128]{2,1,0:T(4,128)(2,1)S(1)}, u32[]{:S(2)}, u32[]{:S(2)}) async-start(bf16[32,4,128]{2,1,0:T(4,128)(2,1)} %bitcast.41), calls=%async_computation.4 | async-start | bytes 65536 | tf_op jit(solution)/shard_map/all_to_all | solution.py:164
  118.2 1.5 %maximum_bitcast_fusion = f32[1,3,32,16,512]{4,2,3,1,0:T(8,128)S(1)} fusion(f32[1,32,16,512]{3,1,2,0:T(8,128)} %get-tuple-element.39, f32[1,32,16,512]{3,1,2,0:T(8,128)S(1)} %get-tuple-element.38, f32[1,32,16,512]{3,1,2,0:T(8,128)S(1)} %bitcast.135), kind=kLoop, calls=%fused_computation.7 | loop fusion | flops 1572864 | bytes 6291456 | tf_op jit(solution)/shard_map/broadcast_in_dim | solution.py:97
  119.8 3.5 %copy.119 = f32[1,3,32,16,512]{4,3,2,1,0:T(8,128)} copy(f32[1,3,32,16,512]{4,2,3,1,0:T(8,128)S(1)} %maximum_bitcast_fusion) | data formatting | bytes 6291456
  123.2 3.1 %all-to-all-done.4 = bf16[32,4,128]{2,1,0:T(4,128)(2,1)S(1)} async-done(((bf16[32,4,128]{2,1,0:T(4,128)(2,1)}), bf16[32,4,128]{2,1,0:T(4,128)(2,1)S(1)}, u32[]{:S(2)}, u32[]{:S(2)}) %all-to-all-start.4) | async-done | bytes 32800 | tf_op jit(solution)/shard_map/all_to_all | solution.py:164
  126.5 3.4 %fusion.1 = f32[64,1,256]{2,1,0:T(1,128)S(1)} fusion(bf16[1,1,64,256,128]{4,3,2,1,0:T(8,128)(2,1)} %param.23, bf16[64,128,1]{1,0,2:T(8,128)(2,1)S(1)} %fusion.14), kind=kOutput, calls=%fused_computation.3 | convolution fusion | flops 4194304 | bytes 4276224 | tf_op jit(solution)/shard_map/pio,po->pi/dot_general | solution.py:172
  (171 shorter events, 30.1 us)
Async XLA Ops:
  0.6 30.2 %copy-start = (f32[1,32,32]{2,1,0:T(8,128)S(1)}, f32[1,32,32]{2,1,0:T(8,128)}, u32[]{:S(2)}) copy-start(f32[1,32,32]{2,1,0:T(8,128)} %param.16) | copy-start | bytes 12292
  2.2 9.0 %copy-start.11 = (f32[1,1,16,512]{3,1,2,0:T(1,128)}, f32[1,1,16,512]{3,1,2,0:T(1,128)S(1)}, u32[]{:S(2)}) copy-start(f32[1,1,16,512]{3,1,2,0:T(1,128)S(1)} %copy.133) | copy-start | bytes 98308
  3.1 8.1 %copy-start.13 = (f32[1,1,16,512]{3,1,2,0:T(1,128)}, f32[1,1,16,512]{3,1,2,0:T(1,128)S(1)}, u32[]{:S(2)}) copy-start(f32[1,1,16,512]{3,1,2,0:T(1,128)S(1)} %copy.130) | copy-start | bytes 98308
  3.2 8.1 %copy-start.15 = (f32[1,1,16,512]{3,1,2,0:T(1,128)}, f32[1,1,16,512]{3,1,2,0:T(1,128)S(1)}, u32[]{:S(2)}) copy-start(f32[1,1,16,512]{3,1,2,0:T(1,128)S(1)} %copy.132) | copy-start | bytes 98308
  3.2 8.0 %copy-start.17 = (f32[1,1,16,512]{3,1,2,0:T(1,128)}, f32[1,1,16,512]{3,1,2,0:T(1,128)S(1)}, u32[]{:S(2)}) copy-start(f32[1,1,16,512]{3,1,2,0:T(1,128)S(1)} %copy.131) | copy-start | bytes 98308
  4.2 60.0 %collective-permute-start.6 = (f32[4,8192]{1,0:T(4,128)}, f32[4,8192]{1,0:T(4,128)}, u32[]{:S(2)}, u32[]{:S(2)}) collective-permute-start(f32[4,8192]{1,0:T(4,128)} %maximum_select_fusion), channel_id=1, source_target_pairs={{0,128},{128,0},{1,129},{129,1},{2,130},{130,2},{3,131},{131,3},{4... | collective-permute-start | bytes 393224 | tf_op jit(solution)/shard_map/ppermute | solution.py:119
  12.3 15.7 %copy-start.24 = (pred[4]{0:T(512)(128)(4,1)}, pred[4]{0:T(512)(128)(4,1)S(1)}, u32[]{:S(2)}) copy-start(pred[4]{0:T(512)(128)(4,1)S(1)} %get-tuple-element.58) | copy-start | bytes 16
  12.4 15.7 %copy-start.26 = (pred[4]{0:T(512)(128)(4,1)}, pred[4]{0:T(512)(128)(4,1)S(1)}, u32[]{:S(2)}) copy-start(pred[4]{0:T(512)(128)(4,1)S(1)} %get-tuple-element.59) | copy-start | bytes 16
  13.2 13.5 %all-to-all-start = ((f32[4,1,528]{2,1,0:T(1,128)}), f32[4,1,528]{2,1,0:T(1,128)S(1)}, u32[]{:S(2)}, u32[]{:S(2)}) async-start(f32[4,1,528]{2,1,0:T(1,128)} %reshape.252), calls=%async_computation | async-start | bytes 20480 | tf_op jit(solution)/shard_map/all_to_all | solution.py:24
  17.2 6.1 %copy-start.29 = (s32[1,1,64]{2,1,0:T(1,128)S(1)}, s32[1,1,64]{2,1,0:T(1,128)}, u32[]{:S(2)}) copy-start(s32[1,1,64]{2,1,0:T(1,128)} %param.21) | copy-start | bytes 772
  17.2 6.6 %copy-start.38 = (s32[1,1,64]{2,1,0:T(1,128)S(1)}, s32[1,1,64]{2,1,0:T(1,128)}, u32[]{:S(2)}) copy-start(s32[1,1,64]{2,1,0:T(1,128)} %param.22) | copy-start | bytes 772
  17.2 6.6 %copy-start.39 = (s32[1,1,64,1]{2,3,1,0:T(1,128)S(1)}, s32[1,1,64,1]{2,3,1,0:T(1,128)}, u32[]{:S(2)}) copy-start(s32[1,1,64,1]{2,3,1,0:T(1,128)} %param.20) | copy-start | bytes 772
  17.2 8.1 %copy-start.4 = (f32[1,16,512]{2,1,0:T(8,128)S(1)}, f32[1,16,512]{2,1,0:T(8,128)}, u32[]{:S(2)}) copy-start(f32[1,16,512]{2,1,0:T(8,128)} %param.17) | copy-start | bytes 98308
  17.9 12.9 %copy-start.35 = (f32[1,16,512]{2,1,0:T(8,128)S(1)}, f32[1,16,512]{2,1,0:T(8,128)}, u32[]{:S(2)}) copy-start(f32[1,16,512]{2,1,0:T(8,128)} %param.14) | copy-start | bytes 98308
  17.9 12.2 %collective-permute-start.1 = (f32[33,1,512]{2,0,1:T(8,128)S(1)}, f32[33,1,512]{2,0,1:T(8,128)S(1)}, u32[]{:S(2)}, u32[]{:S(2)}) collective-permute-start(f32[33,1,512]{2,0,1:T(8,128)S(1)} %pad_maximum_fusion.13), channel_id=1, source_target_pairs={{0,4},{4,8},{8,12},{12,16},{16,20},{20,24},{24,28},{28,32},{32,36}... | collective-permute-start | bytes 202760 | tf_op jit(solution)/shard_map/ppermute | solution.py:14
  21.4 8.8 %collective-permute-start = (f32[33,1,512]{2,0,1:T(8,128)S(1)}, f32[33,1,512]{2,0,1:T(8,128)S(1)}, u32[]{:S(2)}, u32[]{:S(2)}) collective-permute-start(f32[33,1,512]{2,0,1:T(8,128)S(1)} %pad_maximum_fusion.12), channel_id=1, source_target_pairs={{4,0},{8,4},{12,8},{16,12},{20,16},{24,20},{28,24},{32,28},{36,32}... | collective-permute-start | bytes 202760 | tf_op jit(solution)/shard_map/ppermute | solution.py:15
  30.1 5.2 %copy-start.5 = (f32[32,1,512]{2,0,1:T(8,128)}, f32[32,1,512]{2,0,1:T(8,128)S(1)}, u32[]{:S(2)}) copy-start(f32[32,1,512]{2,0,1:T(8,128)S(1)} %slice.254) | copy-start | bytes 196612
  30.2 5.2 %copy-start.7 = (f32[32,1,512]{2,0,1:T(8,128)}, f32[32,1,512]{2,0,1:T(8,128)S(1)}, u32[]{:S(2)}) copy-start(f32[32,1,512]{2,0,1:T(8,128)S(1)} %slice.251) | copy-start | bytes 196612
  41.9 12.6 %all-to-all-start.1 = ((f32[4,1,1024]{2,1,0:T(1,128)}), f32[4,1,1024]{2,1,0:T(1,128)S(1)}, u32[]{:S(2)}, u32[]{:S(2)}) async-start(f32[4,1,1024]{2,1,0:T(1,128)} %reshape.254), calls=%async_computation.1 | async-start | bytes 32768 | tf_op jit(solution)/shard_map/all_to_all | solution.py:24
  48.5 22.3 %collective-permute-start.3 = (f32[32,2,512]{2,0,1:T(8,128)}, f32[32,2,512]{2,0,1:T(8,128)}, u32[]{:S(2)}, u32[]{:S(2)}) collective-permute-start(f32[32,2,512]{2,0,1:T(8,128)} %get-tuple-element.42), channel_id=1, source_target_pairs={{0,4},{4,8},{8,12},{12,16},{16,20},{20,24},{24,28},{28,32},{32,36}... | collective-permute-start | bytes 393224 | tf_op jit(solution)/shard_map/ppermute | solution.py:14
  52.4 18.4 %collective-permute-start.2 = (f32[32,2,512]{2,0,1:T(8,128)}, f32[32,2,512]{2,0,1:T(8,128)}, u32[]{:S(2)}, u32[]{:S(2)}) collective-permute-start(f32[32,2,512]{2,0,1:T(8,128)} %get-tuple-element.43), channel_id=1, source_target_pairs={{4,0},{8,4},{12,8},{16,12},{20,16},{24,20},{28,24},{32,28},{36,32}... | collective-permute-start | bytes 393224 | tf_op jit(solution)/shard_map/ppermute | solution.py:15
  65.5 4.6 %copy-start.21 = (f32[32,1,128]{2,0,1:T(8,128)S(1)}, f32[32,1,128]{2,0,1:T(8,128)}, u32[]{:S(2)}) copy-start(f32[32,1,128]{2,0,1:T(8,128)} %scatter.4) | copy-start | bytes 49156
  65.5 5.3 %copy-start.6 = (f32[32,1,512]{2,0,1:T(8,128)S(1)}, f32[32,1,512]{2,0,1:T(8,128)}, u32[]{:S(2)}) copy-start(f32[32,1,512]{2,0,1:T(8,128)} %copy-done.5) | copy-start | bytes 196612
  65.5 5.3 %copy-start.8 = (f32[32,1,512]{2,0,1:T(8,128)S(1)}, f32[32,1,512]{2,0,1:T(8,128)}, u32[]{:S(2)}) copy-start(f32[32,1,512]{2,0,1:T(8,128)} %copy-done.7) | copy-start | bytes 196612
  65.5 5.3 %copy-start.9 = (f32[1,18,512]{2,1,0:T(8,128)S(1)}, f32[1,18,512]{2,1,0:T(8,128)}, u32[]{:S(2)}) copy-start(f32[1,18,512]{2,1,0:T(8,128)} %copy.158) | copy-start | bytes 110596
  74.1 29.4 %copy-start.2 = (f32[32,16,514]{2,0,1:T(8,128)S(1)}, f32[32,16,514]{2,0,1:T(8,128)}, u32[]{:S(2)}) copy-start(f32[32,16,514]{2,0,1:T(8,128)} %fusion.7) | copy-start | bytes 3158020
  75.2 10.4 %all-to-all-start.2 = ((f32[4,1,512]{2,1,0:T(1,128)}), f32[4,1,512]{2,1,0:T(1,128)S(1)}, u32[]{:S(2)}, u32[]{:S(2)}) async-start(f32[4,1,512]{2,1,0:T(1,128)} %reshape.256), calls=%async_computation.2 | async-start | bytes 16384 | tf_op jit(solution)/shard_map/all_to_all | solution.py:24
  79.7 22.5 %collective-permute-start.4 = (f32[32,1,512]{2,0,1:T(8,128)S(1)}, f32[32,1,512]{2,0,1:T(8,128)S(1)}, u32[]{:S(2)}, u32[]{:S(2)}) collective-permute-start(f32[32,1,512]{2,0,1:T(8,128)S(1)} %get-tuple-element.40), channel_id=1, source_target_pairs={{4,0},{8,4},{12,8},{16,12},{20,16},{24,20},{28,24},{32,28},{36,32}... | collective-permute-start | bytes 196616 | tf_op jit(solution)/shard_map/ppermute | solution.py:15
  81.7 20.6 %collective-permute-start.5 = (f32[32,1,512]{2,0,1:T(8,128)S(1)}, f32[32,1,512]{2,0,1:T(8,128)S(1)}, u32[]{:S(2)}, u32[]{:S(2)}) collective-permute-start(f32[32,1,512]{2,0,1:T(8,128)S(1)} %get-tuple-element.41), channel_id=1, source_target_pairs={{0,4},{4,8},{8,12},{12,16},{16,20},{20,24},{24,28},{28,32},{32,36}... | collective-permute-start | bytes 196616 | tf_op jit(solution)/shard_map/ppermute | solution.py:14
  85.6 23.4 %all-to-all-start.3 = ((f32[32,5,128]{2,1,0:T(8,128)}), f32[32,5,128]{2,1,0:T(8,128)}, u32[]{:S(2)}, u32[]{:S(2)}) async-start(f32[32,5,128]{2,1,0:T(8,128)} %pad_maximum_fusion.11), calls=%async_computation.3 | async-start | bytes 262144 | tf_op jit(solution)/shard_map/all_to_all | solution.py:149
  112.0 14.3 %all-to-all-start.4 = ((bf16[32,4,128]{2,1,0:T(4,128)(2,1)}), bf16[32,4,128]{2,1,0:T(4,128)(2,1)S(1)}, u32[]{:S(2)}, u32[]{:S(2)}) async-start(bf16[32,4,128]{2,1,0:T(4,128)(2,1)} %bitcast.41), calls=%async_computation.4 | async-start | bytes 65536 | tf_op jit(solution)/shard_map/all_to_all | solution.py:164
  119.7 6.6 %copy-start.33 = (s32[64]{0:T(128)S(1)}, s32[64]{0:T(128)}, u32[]{:S(2)}) copy-start(s32[64]{0:T(128)} %copy-done.31) | copy-start | bytes 772
  (20 other events, 50.0 us)

commit v8 on v2

--- a/solution.py
+++ b/solution.py
@@ -81,9 +81,6 @@
     sound_speed = wave_speed[0]
     wetness = wet_mask[0].astype(jnp.float32)
     matrix = vertical[0]
-    assert SUBSTEPS == 2
-    p2, u2, v2 = stencil(pressure, eastward, northward, sound_speed, wetness, matrix)
-    final_state = jnp.stack([p2, u2, v2])[None]
 
     weights = intersection_weights[0, 0]
     pair_count, in_width, out_width = weights.shape
@@ -99,16 +96,13 @@
 
     own_st = surface_temp[0].reshape(cell_count)
     own_wet = wetness.reshape(cell_count)
-    drivers = jnp.stack(
+    got = lax.ppermute(jnp.stack([own_st, own_wet]), "sec", [(1, 0)])
+    ocean_st = got[0]
+    ocean_wet = got[1]
+    atmos_drivers = jnp.stack(
         [model_state[0, 0, 0].reshape(cell_count), model_state[0, 1, 0].reshape(cell_count),
          model_state[0, 2, 0].reshape(cell_count), own_st]
     )
-    zeros = jnp.zeros_like(own_st)
-    sent = jnp.where(is_atmos, drivers, jnp.stack([own_st, own_wet, zeros, zeros]))
-    got = lax.ppermute(sent, "sec", [(0, 1), (1, 0)])
-    atmos_drivers = jnp.where(is_atmos, drivers, got)
-    ocean_st = jnp.where(is_atmos, got[0], own_st)
-    ocean_wet = jnp.where(is_atmos, got[1], own_wet)
 
     fluxes = jnp.tanh(jnp.dot(flux_coef, atmos_drivers, precision=HIGHEST_PRECISION)).astype(jnp.bfloat16)
     flux_count = fluxes.shape[0]
@@ -136,6 +130,10 @@
     )
     packet = jnp.concatenate([outgoing.reshape(tile_count, capacity, out_width), offset_row], axis=1)
     arrived = lax.all_to_all(packet, "gx", split_axis=0, concat_axis=0, tiled=True)
+    arrived, pressure, eastward, northward = lax.optimization_barrier((arrived, pressure, eastward, northward))
+    assert SUBSTEPS == 2
+    p2, u2, v2 = stencil(pressure, eastward, northward, sound_speed, wetness, matrix)
+    final_state = jnp.stack([p2, u2, v2])[None]
     arrived_at = arrived[:, capacity, :capacity].reshape(slot_count).astype(jnp.int32)
     landing = jnp.arange(out_blocks)[:, None] == arrived_at[None, :]
     heating = jnp.dot(
@@ -162,7 +160,8 @@
     owning = (jnp.arange(in_blocks)[:, None] == sources[None, :]).astype(jnp.float32)
     atmos_temp = jnp.dot(owning, pieces, precision=HIGHEST_PRECISION)
 
-    surface_temps = jnp.where(is_atmos, atmos_temp.reshape(grid_shape), ocean_temp.reshape(grid_shape))[None]
+    ocean_back = lax.ppermute(ocean_temp, "sec", [(0, 1)])
+    surface_temps = jnp.where(is_atmos, atmos_temp.reshape(grid_shape), ocean_back.reshape(grid_shape))[None]
     return (final_state, surface_temps)
 
 

time: 114 us -> 118 us (1.035)
  the two profiles are of different devices: /device:TPU:1 before, /device:TPU:111 now
where the time goes in v8:
time: 118 us; the launch traced here: 117 us
  starting transfers between devices  62.2 us (53%)
  local copies, waits for them, and re-layouts  15.4 us (13%)
  waiting for transfers between devices  15 us (13%)
  matrix products  14.8 us (13%)
  other arithmetic  8.74 us (7%)
  between operations  1.18 us (1%)
    ppermute x6, starting transfers between devices, neighbours(): lo = lax.ppermute(tail, axis, [(i, i + 1) for i in range(count - 1)])  20.5 us
    ppermute x6, starting transfers between devices, neighbours(): hi = lax.ppermute(head, axis, [(i + 1, i) for i in range(count - 1)])  18 us
    all_to_all x1, starting transfers between devices, local(): lax.all_to_all(packet, 'gx', split_axis=0, concat_axis=0, tiled=True)  9.04 us
    ppermute x6, waiting for transfers between devices, neighbours(): hi = lax.ppermute(head, axis, [(i + 1, i) for i in range(count - 1)])  8.53 us
    all_to_all x1, starting transfers between devices, local(): lax.all_to_all(returning.reshape(tile_count, capacity, out_width), 'gx',...  7.54 us
    unnamed x20, local copies, waits for them, and re-layouts  6.82 us
    ppermute x1, starting transfers between devices, local(): ocean_back = lax.ppermute(ocean_temp, 'sec', [(0, 1)])  5.77 us
    ppermute x6, waiting for transfers between devices, neighbours(): lo = lax.ppermute(tail, axis, [(i, i + 1) for i in range(count - 1)])  5.67 us
  transfers between devices with their start and end apart: 16, of which 6 were waited for; matrix products, arithmetic and copies ran while one was open for 21% of the time, Pallas kernels for 0%

profile of v8, /device:TPU:111, one launch (start us, length us, event | category | flops | bytes accessed | tf_op | source)
XLA Modules:
  0.0 117.3 jit_solution(11138653464360987135)
XLA Ops:
  2.3 1.3 %collective-permute-start.12 = (f32[2,8192]{1,0:T(2,128)S(1)}, f32[2,8192]{1,0:T(2,128)S(1)}, u32[]{:S(2)}, u32[]{:S(2)}) collective-permute-start(f32[2,8192]{1,0:T(2,128)S(1)} %pad_maximum_fusion.15), channel_id=1, source_target_pairs={{128,0},{129,1},{130,2},{131,3},{132,4},{133,5},{134,6},{135,7},{1... | collective-permute-start | bytes 196616 | tf_op jit(solution)/shard_map/ppermute | solution.py:99
  5.6 0.9 convert_reduce_fusion
  8.3 1.2 fusion
  10.1 2.9 %fusion.11 = bf16[64,8,128]{2,1,0:T(8,128)(2,1)S(1)} fusion(bf16[1,1,64,256,128]{4,3,2,1,0:T(8,128)(2,1)} %param.23, bf16[64,8,256]{2,1,0:T(8,128)(2,1)S(1)} %gather_fusion, pred[64]{0:T(512)(128)(4,1)S(1)} %compare_and_fusion), kind=kOutput, calls=%fused_computation.20 | convolution fusion | flops 33751040 | bytes 4587584 | tf_op jit(solution)/shard_map/fpi,pio->pfo/dot_general | solution.py:111
  14.3 9.0 %all-to-all-start = ((f32[32,5,128]{2,1,0:T(8,128)}), f32[32,5,128]{2,1,0:T(8,128)S(1)}, u32[]{:S(2)}, u32[]{:S(2)}) async-start(f32[32,5,128]{2,1,0:T(8,128)} %pad_maximum_fusion.12), calls=%async_computation | async-start | bytes 262144 | tf_op jit(solution)/shard_map/all_to_all | solution.py:132
  23.4 2.2 %fusion.76 = (f32[1,1,32,16,512]{4,3,2,1,0:T(8,128)S(1)}, f32[1,1,32,16,512]{4,3,2,1,0:T(8,128)S(1)}, f32[1,1,32,16,512]{4,3,2,1,0:T(8,128)S(1)}) fusion(f32[1,3,32,16,512]{4,3,2,1,0:T(8,128)} %param.13), kind=kLoop, calls=%fused_computation.127 | loop fusion | bytes 6291456 | tf_op jit(solution)/shard_map/slice | solution.py:80
  25.6 1.2 %copy_bitcast_fusion = (f32[32,16,512]{2,0,1:T(8,128)S(1)}, f32[32,16,512]{2,0,1:T(8,128)S(1)}) fusion(f32[1,1,32,16,512]{4,3,2,1,0:T(8,128)S(1)} %get-tuple-element.30, f32[1,1,32,16,512]{4,3,2,1,0:T(8,128)S(1)} %get-tuple-element.31), kind=kLoop, calls=%fused_computation.58 | loop fusion | bytes 4194304 | tf_op jit(solution)/shard_map/squeeze | solution.py:80
  27.4 1.6 %copy.69 = f32[1,1,32,16,512]{4,2,3,1,0:T(8,128)} copy(f32[1,1,32,16,512]{4,3,2,1,0:T(8,128)S(1)} %get-tuple-element.32) | data formatting | bytes 2097152
  31.0 7.5 %all-to-all-start.1 = ((bf16[32,4,128]{2,1,0:T(4,128)(2,1)}), bf16[32,4,128]{2,1,0:T(4,128)(2,1)S(1)}, u32[]{:S(2)}, u32[]{:S(2)}) async-start(bf16[32,4,128]{2,1,0:T(4,128)(2,1)} %bitcast.30), calls=%async_computation.1 | async-start | bytes 65536 | tf_op jit(solution)/shard_map/all_to_all | solution.py:151
  38.6 5.8 %collective-permute-start.13 = (f32[8192]{0:T(1024)S(1)}, f32[8192]{0:T(1024)S(1)}, u32[]{:S(2)}, u32[]{:S(2)}) collective-permute-start(f32[8192]{0:T(1024)S(1)} %fusion.58), channel_id=1, source_target_pairs={{0,128},{1,129},{2,130},{3,131},{4,132},{5,133},{6,134},{7,135},{8... | collective-permute-start | bytes 98312 | tf_op jit(solution)/shard_map/ppermute | solution.py:163
  44.4 5.4 %collective-permute-start.1 = (f32[33,1,512]{2,0,1:T(8,128)S(1)}, f32[33,1,512]{2,0,1:T(8,128)}, u32[]{:S(2)}, u32[]{:S(2)}) collective-permute-start(f32[33,1,512]{2,0,1:T(8,128)S(1)} %pad_maximum_fusion.14), channel_id=1, source_target_pairs={{0,4},{4,8},{8,12},{12,16},{16,20},{20,24},{24,28},{28,32},{32,36}... | collective-permute-start | bytes 202760 | tf_op jit(solution)/shard_map/ppermute | solution.py:14
  50.0 1.3 %collective-permute-start.3 = (f32[33,16,1]{2,0,1:T(8,128)S(1)}, f32[33,16,1]{2,0,1:T(8,128)S(1)}, u32[]{:S(2)}, u32[]{:S(2)}) collective-permute-start(f32[33,16,1]{2,0,1:T(8,128)S(1)} %pad_maximum_fusion.11), channel_id=1, source_target_pairs={{0,1},{1,2},{2,3},{4,5},{5,6},{6,7},{8,9},{9,10},{10,11},{12,13},{... | collective-permute-start | bytes 6344 | tf_op jit(solution)/shard_map/ppermute | solution.py:14
  51.4 4.0 %collective-permute-start.2 = (f32[33,16,1]{2,0,1:T(8,128)S(1)}, f32[33,16,1]{2,0,1:T(8,128)S(1)}, u32[]{:S(2)}, u32[]{:S(2)}) collective-permute-start(f32[33,16,1]{2,0,1:T(8,128)S(1)} %pad_maximum_fusion.10), channel_id=1, source_target_pairs={{1,0},{2,1},{3,2},{5,4},{6,5},{7,6},{9,8},{10,9},{11,10},{13,12},{... | collective-permute-start | bytes 6344 | tf_op jit(solution)/shard_map/ppermute | solution.py:15
  55.4 1.9 %collective-permute-start = (f32[33,1,512]{2,0,1:T(8,128)S(1)}, f32[33,1,512]{2,0,1:T(8,128)}, u32[]{:S(2)}, u32[]{:S(2)}) collective-permute-start(f32[33,1,512]{2,0,1:T(8,128)S(1)} %pad_maximum_fusion.13), channel_id=1, source_target_pairs={{4,0},{8,4},{12,8},{16,12},{20,16},{24,20},{28,24},{32,28},{36,32}... | collective-permute-start | bytes 202760 | tf_op jit(solution)/shard_map/ppermute | solution.py:15
  57.3 1.6 %collective-permute-done.3 = f32[33,16,1]{2,0,1:T(8,128)S(1)} collective-permute-done((f32[33,16,1]{2,0,1:T(8,128)S(1)}, f32[33,16,1]{2,0,1:T(8,128)S(1)}, u32[]{:S(2)}, u32[]{:S(2)}) %collective-permute-start.3) | collective-permute-done | bytes 2144 | tf_op jit(solution)/shard_map/ppermute | solution.py:14
  59.0 1.8 %collective-permute-done.2 = f32[33,16,1]{2,0,1:T(8,128)S(1)} collective-permute-done((f32[33,16,1]{2,0,1:T(8,128)S(1)}, f32[33,16,1]{2,0,1:T(8,128)S(1)}, u32[]{:S(2)}, u32[]{:S(2)}) %collective-permute-start.2) | collective-permute-done | bytes 2144 | tf_op jit(solution)/shard_map/ppermute | solution.py:15
  61.2 3.4 %fusion.1 = f32[64,1,256]{2,1,0:T(1,128)S(1)} fusion(bf16[1,1,64,256,128]{4,3,2,1,0:T(8,128)(2,1)} %param.23, bf16[64,128,1]{1,0,2:T(8,128)(2,1)S(1)} %fusion.14), kind=kOutput, calls=%fused_computation.3 | convolution fusion | flops 4194304 | bytes 4276224 | tf_op jit(solution)/shard_map/pio,po->pi/dot_general | solution.py:159
  66.5 3.6 %fusion.6 = f32[32,16,512]{2,0,1:T(8,128)S(1)} fusion(f32[32,16,512]{2,0,1:T(8,128)} %bitcast.105, f32[32,16,512]{2,0,1:T(8,128)S(1)} %get-tuple-element.20, f32[32,16,1]{2,0,1:T(8,128)S(1)} %slice.240, f32[32,16,1]{2,0,1:T(8,128)S(1)} %slice.238, f32[32,16,512]{2,0,1:T(8,128)S(1)} %get-tuple-element.19, f32[32,1,512]{2,0,1:T(8,128)S(1)} %slice.236, ...), kind=kOutput, calls=%fused_computation.11 | convolution fusion | flops 105644032 | bytes 4366336 | tf_op jit(solution)/shard_map/lm,mxy->lxy/dot_general | solution.py:20
  70.3 1.3 %collective-permute-start.7 = (f32[32,16,2]{2,0,1:T(8,128)S(1)}, f32[32,16,2]{2,0,1:T(8,128)S(1)}, u32[]{:S(2)}, u32[]{:S(2)}) collective-permute-start(f32[32,16,2]{2,0,1:T(8,128)S(1)} %get-tuple-element.44), channel_id=1, source_target_pairs={{0,1},{1,2},{2,3},{4,5},{5,6},{6,7},{8,9},{9,10},{10,11},{12,13},{... | collective-permute-start | bytes 12296 | tf_op jit(solution)/shard_map/ppermute | solution.py:14
  71.6 4.5 %collective-permute-start.6 = (f32[32,16,2]{2,0,1:T(8,128)S(1)}, f32[32,16,2]{2,0,1:T(8,128)S(1)}, u32[]{:S(2)}, u32[]{:S(2)}) collective-permute-start(f32[32,16,2]{2,0,1:T(8,128)S(1)} %get-tuple-element.45), channel_id=1, source_target_pairs={{1,0},{2,1},{3,2},{5,4},{6,5},{7,6},{9,8},{10,9},{11,10},{13,12},{... | collective-permute-start | bytes 12296 | tf_op jit(solution)/shard_map/ppermute | solution.py:15
  77.5 5.5 %collective-permute-start.5 = (f32[32,2,512]{2,0,1:T(8,128)S(1)}, f32[32,2,512]{2,0,1:T(8,128)S(1)}, u32[]{:S(2)}, u32[]{:S(2)}) collective-permute-start(f32[32,2,512]{2,0,1:T(8,128)S(1)} %get-tuple-element.42), channel_id=1, source_target_pairs={{0,4},{4,8},{8,12},{12,16},{16,20},{20,24},{24,28},{28,32},{32,36}... | collective-permute-start | bytes 393224 | tf_op jit(solution)/shard_map/ppermute | solution.py:14
  83.0 2.1 %collective-permute-start.4 = (f32[32,2,512]{2,0,1:T(8,128)S(1)}, f32[32,2,512]{2,0,1:T(8,128)S(1)}, u32[]{:S(2)}, u32[]{:S(2)}) collective-permute-start(f32[32,2,512]{2,0,1:T(8,128)S(1)} %get-tuple-element.43), channel_id=1, source_target_pairs={{4,0},{8,4},{12,8},{16,12},{20,16},{24,20},{28,24},{32,28},{36,32}... | collective-permute-start | bytes 393224 | tf_op jit(solution)/shard_map/ppermute | solution.py:15
  86.0 5.4 %collective-permute-done.4 = f32[32,2,512]{2,0,1:T(8,128)S(1)} collective-permute-done((f32[32,2,512]{2,0,1:T(8,128)S(1)}, f32[32,2,512]{2,0,1:T(8,128)S(1)}, u32[]{:S(2)}, u32[]{:S(2)}) %collective-permute-start.4) | collective-permute-done | bytes 131104 | tf_op jit(solution)/shard_map/ppermute | solution.py:15
  91.7 1.9 %fusion.5 = f32[32,16,512]{2,0,1:T(8,128)S(1)} fusion(f32[32,16,512]{2,0,1:T(8,128)S(1)} %fusion.6, f32[32,16,514]{2,0,1:T(8,128)S(1)} %fusion.7, f32[32,18,512]{2,0,1:T(8,128)S(1)} %fusion.9, f32[16,512]{1,0:T(8,128)S(1)} %bitcast.128, f32[1,32,32]{2,1,0:T(8,128)S(1)} %copy-done), kind=kOutput, calls=%fused_computation.9 | convolution fusion | flops 103546880 | bytes 11616256 | tf_op jit(solution)/shard_map/lm,mxy->lxy/dot_general | solution.py:20
  93.8 1.9 %collective-permute-start.8 = (f32[32,1,512]{2,0,1:T(8,128)S(1)}, f32[32,1,512]{2,0,1:T(8,128)S(1)}, u32[]{:S(2)}, u32[]{:S(2)}) collective-permute-start(f32[32,1,512]{2,0,1:T(8,128)S(1)} %get-tuple-element.38), channel_id=1, source_target_pairs={{4,0},{8,4},{12,8},{16,12},{20,16},{24,20},{28,24},{32,28},{36,32}... | collective-permute-start | bytes 196616 | tf_op jit(solution)/shard_map/ppermute | solution.py:15
  95.7 5.8 %collective-permute-start.9 = (f32[32,1,512]{2,0,1:T(8,128)S(1)}, f32[32,1,512]{2,0,1:T(8,128)S(1)}, u32[]{:S(2)}, u32[]{:S(2)}) collective-permute-start(f32[32,1,512]{2,0,1:T(8,128)S(1)} %get-tuple-element.39), channel_id=1, source_target_pairs={{0,4},{4,8},{8,12},{12,16},{16,20},{20,24},{24,28},{28,32},{32,36}... | collective-permute-start | bytes 196616 | tf_op jit(solution)/shard_map/ppermute | solution.py:14
  101.4 3.6 %collective-permute-start.10 = (f32[32,16,1]{2,0,1:T(8,128)S(1)}, f32[32,16,1]{2,0,1:T(8,128)S(1)}, u32[]{:S(2)}, u32[]{:S(2)}) collective-permute-start(f32[32,16,1]{2,0,1:T(8,128)S(1)} %get-tuple-element.40), channel_id=1, source_target_pairs={{1,0},{2,1},{3,2},{5,4},{6,5},{7,6},{9,8},{10,9},{11,10},{13,12},{... | collective-permute-start | bytes 6152 | tf_op jit(solution)/shard_map/ppermute | solution.py:15
  105.1 1.3 %collective-permute-start.11 = (f32[32,16,1]{2,0,1:T(8,128)S(1)}, f32[32,16,1]{2,0,1:T(8,128)S(1)}, u32[]{:S(2)}, u32[]{:S(2)}) collective-permute-start(f32[32,16,1]{2,0,1:T(8,128)S(1)} %get-tuple-element.41), channel_id=1, source_target_pairs={{0,1},{1,2},{2,3},{4,5},{5,6},{6,7},{8,9},{9,10},{10,11},{12,13},{... | collective-permute-start | bytes 6152 | tf_op jit(solution)/shard_map/ppermute | solution.py:14
  107.0 1.4 %collective-permute-done.10 = f32[32,16,1]{2,0,1:T(8,128)S(1)} collective-permute-done((f32[32,16,1]{2,0,1:T(8,128)S(1)}, f32[32,16,1]{2,0,1:T(8,128)S(1)}, u32[]{:S(2)}, u32[]{:S(2)}) %collective-permute-start.10) | collective-permute-done | bytes 2080 | tf_op jit(solution)/shard_map/ppermute | solution.py:15
  108.4 4.0 %collective-permute-done.11 = f32[32,16,1]{2,0,1:T(8,128)S(1)} collective-permute-done((f32[32,16,1]{2,0,1:T(8,128)S(1)}, f32[32,16,1]{2,0,1:T(8,128)S(1)}, u32[]{:S(2)}, u32[]{:S(2)}) %collective-permute-start.11) | collective-permute-done | bytes 2080 | tf_op jit(solution)/shard_map/ppermute | solution.py:14
  112.4 1.1 fusion.24
  113.8 3.5 %copy.42 = f32[1,3,32,16,512]{4,3,2,1,0:T(8,128)} copy(f32[1,3,32,16,512]{4,2,3,1,0:T(8,128)S(1)} %maximum_bitcast_fusion) | data formatting | bytes 6291456
  (81 shorter events, 16.4 us)
Async XLA Ops:
  0.6 65.9 %copy-start = (f32[1,32,32]{2,1,0:T(8,128)S(1)}, f32[1,32,32]{2,1,0:T(8,128)}, u32[]{:S(2)}) copy-start(f32[1,32,32]{2,1,0:T(8,128)} %param.16) | copy-start | bytes 12292
  2.3 26.7 %collective-permute-start.12 = (f32[2,8192]{1,0:T(2,128)S(1)}, f32[2,8192]{1,0:T(2,128)S(1)}, u32[]{:S(2)}, u32[]{:S(2)}) collective-permute-start(f32[2,8192]{1,0:T(2,128)S(1)} %pad_maximum_fusion.15), channel_id=1, source_target_pairs={{128,0},{129,1},{130,2},{131,3},{132,4},{133,5},{134,6},{135,7},{1... | collective-permute-start | bytes 196616 | tf_op jit(solution)/shard_map/ppermute | solution.py:99
  10.1 2.9 %copy-start.2 = (f32[8]{0:T(128)S(1)}, f32[8]{0:T(128)}, u32[]{:S(2)}) copy-start(f32[8]{0:T(128)} %param.19) | copy-start | bytes 100
  14.3 15.5 %all-to-all-start = ((f32[32,5,128]{2,1,0:T(8,128)}), f32[32,5,128]{2,1,0:T(8,128)S(1)}, u32[]{:S(2)}, u32[]{:S(2)}) async-start(f32[32,5,128]{2,1,0:T(8,128)} %pad_maximum_fusion.12), calls=%async_computation | async-start | bytes 262144 | tf_op jit(solution)/shard_map/all_to_all | solution.py:132
  31.0 30.0 %all-to-all-start.1 = ((bf16[32,4,128]{2,1,0:T(4,128)(2,1)}), bf16[32,4,128]{2,1,0:T(4,128)(2,1)S(1)}, u32[]{:S(2)}, u32[]{:S(2)}) async-start(bf16[32,4,128]{2,1,0:T(4,128)(2,1)} %bitcast.30), calls=%async_computation.1 | async-start | bytes 65536 | tf_op jit(solution)/shard_map/all_to_all | solution.py:151
  38.6 16.8 %copy-start.1 = (f32[1,1,512]{2,0,1:T(1,128)S(1)}, f32[1,1,512]{2,0,1:T(1,128)}, u32[]{:S(2)}) copy-start(f32[1,1,512]{2,0,1:T(1,128)} %get-tuple-element.52) | copy-start | bytes 6148
  38.6 22.4 %collective-permute-start.13 = (f32[8192]{0:T(1024)S(1)}, f32[8192]{0:T(1024)S(1)}, u32[]{:S(2)}, u32[]{:S(2)}) collective-permute-start(f32[8192]{0:T(1024)S(1)} %fusion.58), channel_id=1, source_target_pairs={{0,128},{1,129},{2,130},{3,131},{4,132},{5,133},{6,134},{7,135},{8... | collective-permute-start | bytes 98312 | tf_op jit(solution)/shard_map/ppermute | solution.py:163
  44.4 20.4 %collective-permute-start.1 = (f32[33,1,512]{2,0,1:T(8,128)S(1)}, f32[33,1,512]{2,0,1:T(8,128)}, u32[]{:S(2)}, u32[]{:S(2)}) collective-permute-start(f32[33,1,512]{2,0,1:T(8,128)S(1)} %pad_maximum_fusion.14), channel_id=1, source_target_pairs={{0,4},{4,8},{8,12},{12,16},{16,20},{20,24},{24,28},{28,32},{32,36}... | collective-permute-start | bytes 202760 | tf_op jit(solution)/shard_map/ppermute | solution.py:14
  50.0 8.9 %collective-permute-start.3 = (f32[33,16,1]{2,0,1:T(8,128)S(1)}, f32[33,16,1]{2,0,1:T(8,128)S(1)}, u32[]{:S(2)}, u32[]{:S(2)}) collective-permute-start(f32[33,16,1]{2,0,1:T(8,128)S(1)} %pad_maximum_fusion.11), channel_id=1, source_target_pairs={{0,1},{1,2},{2,3},{4,5},{5,6},{6,7},{8,9},{9,10},{10,11},{12,13},{... | collective-permute-start | bytes 6344 | tf_op jit(solution)/shard_map/ppermute | solution.py:14
  51.4 9.4 %collective-permute-start.2 = (f32[33,16,1]{2,0,1:T(8,128)S(1)}, f32[33,16,1]{2,0,1:T(8,128)S(1)}, u32[]{:S(2)}, u32[]{:S(2)}) collective-permute-start(f32[33,16,1]{2,0,1:T(8,128)S(1)} %pad_maximum_fusion.10), channel_id=1, source_target_pairs={{1,0},{2,1},{3,2},{5,4},{6,5},{7,6},{9,8},{10,9},{11,10},{13,12},{... | collective-permute-start | bytes 6344 | tf_op jit(solution)/shard_map/ppermute | solution.py:15
  55.4 10.2 %collective-permute-start = (f32[33,1,512]{2,0,1:T(8,128)S(1)}, f32[33,1,512]{2,0,1:T(8,128)}, u32[]{:S(2)}, u32[]{:S(2)}) collective-permute-start(f32[33,1,512]{2,0,1:T(8,128)S(1)} %pad_maximum_fusion.13), channel_id=1, source_target_pairs={{4,0},{8,4},{12,8},{16,12},{20,16},{24,20},{28,24},{32,28},{36,32}... | collective-permute-start | bytes 202760 | tf_op jit(solution)/shard_map/ppermute | solution.py:15
  61.2 3.4 %copy-start.3 = (s32[1,1,64]{2,1,0:T(1,128)S(1)}, s32[1,1,64]{2,1,0:T(1,128)}, u32[]{:S(2)}) copy-start(s32[1,1,64]{2,1,0:T(1,128)} %param.21) | copy-start | bytes 772
  61.2 5.3 %copy-start.4 = (f32[1,16,512]{2,1,0:T(8,128)S(1)}, f32[1,16,512]{2,1,0:T(8,128)}, u32[]{:S(2)}) copy-start(f32[1,16,512]{2,1,0:T(8,128)} %param.14) | copy-start | bytes 98308
  70.3 14.9 %collective-permute-start.7 = (f32[32,16,2]{2,0,1:T(8,128)S(1)}, f32[32,16,2]{2,0,1:T(8,128)S(1)}, u32[]{:S(2)}, u32[]{:S(2)}) collective-permute-start(f32[32,16,2]{2,0,1:T(8,128)S(1)} %get-tuple-element.44), channel_id=1, source_target_pairs={{0,1},{1,2},{2,3},{4,5},{5,6},{6,7},{8,9},{9,10},{10,11},{12,13},{... | collective-permute-start | bytes 12296 | tf_op jit(solution)/shard_map/ppermute | solution.py:14
  71.6 13.6 %collective-permute-start.6 = (f32[32,16,2]{2,0,1:T(8,128)S(1)}, f32[32,16,2]{2,0,1:T(8,128)S(1)}, u32[]{:S(2)}, u32[]{:S(2)}) collective-permute-start(f32[32,16,2]{2,0,1:T(8,128)S(1)} %get-tuple-element.45), channel_id=1, source_target_pairs={{1,0},{2,1},{3,2},{5,4},{6,5},{7,6},{9,8},{10,9},{11,10},{13,12},{... | collective-permute-start | bytes 12296 | tf_op jit(solution)/shard_map/ppermute | solution.py:15
  77.5 8.5 %collective-permute-start.5 = (f32[32,2,512]{2,0,1:T(8,128)S(1)}, f32[32,2,512]{2,0,1:T(8,128)S(1)}, u32[]{:S(2)}, u32[]{:S(2)}) collective-permute-start(f32[32,2,512]{2,0,1:T(8,128)S(1)} %get-tuple-element.42), channel_id=1, source_target_pairs={{0,4},{4,8},{8,12},{12,16},{16,20},{20,24},{24,28},{28,32},{32,36}... | collective-permute-start | bytes 393224 | tf_op jit(solution)/shard_map/ppermute | solution.py:14
  83.0 8.4 %collective-permute-start.4 = (f32[32,2,512]{2,0,1:T(8,128)S(1)}, f32[32,2,512]{2,0,1:T(8,128)S(1)}, u32[]{:S(2)}, u32[]{:S(2)}) collective-permute-start(f32[32,2,512]{2,0,1:T(8,128)S(1)} %get-tuple-element.43), channel_id=1, source_target_pairs={{4,0},{8,4},{12,8},{16,12},{20,16},{24,20},{28,24},{32,28},{36,32}... | collective-permute-start | bytes 393224 | tf_op jit(solution)/shard_map/ppermute | solution.py:15
  93.8 18.7 %collective-permute-start.8 = (f32[32,1,512]{2,0,1:T(8,128)S(1)}, f32[32,1,512]{2,0,1:T(8,128)S(1)}, u32[]{:S(2)}, u32[]{:S(2)}) collective-permute-start(f32[32,1,512]{2,0,1:T(8,128)S(1)} %get-tuple-element.38), channel_id=1, source_target_pairs={{4,0},{8,4},{12,8},{16,12},{20,16},{24,20},{28,24},{32,28},{36,32}... | collective-permute-start | bytes 196616 | tf_op jit(solution)/shard_map/ppermute | solution.py:15
  95.7 16.7 %collective-permute-start.9 = (f32[32,1,512]{2,0,1:T(8,128)S(1)}, f32[32,1,512]{2,0,1:T(8,128)S(1)}, u32[]{:S(2)}, u32[]{:S(2)}) collective-permute-start(f32[32,1,512]{2,0,1:T(8,128)S(1)} %get-tuple-element.39), channel_id=1, source_target_pairs={{0,4},{4,8},{8,12},{12,16},{16,20},{20,24},{24,28},{28,32},{32,36}... | collective-permute-start | bytes 196616 | tf_op jit(solution)/shard_map/ppermute | solution.py:14
  101.4 6.9 %collective-permute-start.10 = (f32[32,16,1]{2,0,1:T(8,128)S(1)}, f32[32,16,1]{2,0,1:T(8,128)S(1)}, u32[]{:S(2)}, u32[]{:S(2)}) collective-permute-start(f32[32,16,1]{2,0,1:T(8,128)S(1)} %get-tuple-element.40), channel_id=1, source_target_pairs={{1,0},{2,1},{3,2},{5,4},{6,5},{7,6},{9,8},{10,9},{11,10},{13,12},{... | collective-permute-start | bytes 6152 | tf_op jit(solution)/shard_map/ppermute | solution.py:15
  105.1 7.3 %collective-permute-start.11 = (f32[32,16,1]{2,0,1:T(8,128)S(1)}, f32[32,16,1]{2,0,1:T(8,128)S(1)}, u32[]{:S(2)}, u32[]{:S(2)}) collective-permute-start(f32[32,16,1]{2,0,1:T(8,128)S(1)} %get-tuple-element.41), channel_id=1, source_target_pairs={{0,1},{1,2},{2,3},{4,5},{5,6},{6,7},{8,9},{9,10},{10,11},{12,13},{... | collective-permute-start | bytes 6152 | tf_op jit(solution)/shard_map/ppermute | solution.py:14

commit v9 on v8

--- a/solution.py
+++ b/solution.py
@@ -130,7 +130,7 @@
     )
     packet = jnp.concatenate([outgoing.reshape(tile_count, capacity, out_width), offset_row], axis=1)
     arrived = lax.all_to_all(packet, "gx", split_axis=0, concat_axis=0, tiled=True)
-    arrived, pressure, eastward, northward = lax.optimization_barrier((arrived, pressure, eastward, northward))
+    arrived, pressure = lax.optimization_barrier((arrived, pressure))
     assert SUBSTEPS == 2
     p2, u2, v2 = stencil(pressure, eastward, northward, sound_speed, wetness, matrix)
     final_state = jnp.stack([p2, u2, v2])[None]

time: 118 us -> 128 us (1.085)
  the two profiles are of different devices: /device:TPU:111 before, /device:TPU:1 now
where the time goes in v9:
time: 128 us; the launch traced here: 126 us
  starting transfers between devices  58.6 us (46%)
  local copies, waits for them, and re-layouts  25.1 us (20%)
  matrix products  17.2 us (13%)
  other arithmetic  13.9 us (11%)
  waiting for transfers between devices  10.1 us (8%)
    ppermute x6, starting transfers between devices, neighbours(): lo = lax.ppermute(tail, axis, [(i, i + 1) for i in range(count - 1)])  21.8 us
    all_to_all x1, starting transfers between devices, local(): lax.all_to_all(packet, 'gx', split_axis=0, concat_axis=0, tiled=True)  11.1 us
    ppermute x6, starting transfers between devices, neighbours(): hi = lax.ppermute(head, axis, [(i + 1, i) for i in range(count - 1)])  9.8 us
    unnamed x32, local copies, waits for them, and re-layouts  9.33 us
    all_to_all x1, starting transfers between devices, local(): lax.all_to_all(returning.reshape(tile_count, capacity, out_width), 'gx',...  7.5 us
    ppermute x6, waiting for transfers between devices, neighbours(): hi = lax.ppermute(head, axis, [(i + 1, i) for i in range(count - 1)])  7.46 us
    ppermute x1, starting transfers between devices, local(): ocean_back = lax.ppermute(ocean_temp, 'sec', [(0, 1)])  7 us
    dot_general x2, matrix products, vertical_mix(): jnp.einsum('lm,mxy->lxy', matrix, right_side, precision=HIGHEST_PRECISION)  5.57 us
  transfers between devices with their start and end apart: 16, of which 4 were waited for; matrix products, arithmetic and copies ran while one was open for 29% of the time, Pallas kernels for 0%

profile of v9, /device:TPU:1, one launch (start us, length us, event | category | flops | bytes accessed | tf_op | source)
XLA Modules:
  0.0 126.1 jit_solution(15693050325637934343)
XLA Ops:
  2.3 1.3 %collective-permute-start.12 = (f32[2,8192]{1,0:T(2,128)S(1)}, f32[2,8192]{1,0:T(2,128)}, u32[]{:S(2)}, u32[]{:S(2)}) collective-permute-start(f32[2,8192]{1,0:T(2,128)S(1)} %pad_maximum_fusion.15), channel_id=1, source_target_pairs={{128,0},{129,1},{130,2},{131,3},{132,4},{133,5},{134,6},{135,7},{1... | collective-permute-start | bytes 196616 | tf_op jit(solution)/shard_map/ppermute | solution.py:99
  10.1 2.9 %fusion.11 = bf16[64,8,128]{2,1,0:T(8,128)(2,1)S(1)} fusion(bf16[1,1,64,256,128]{4,3,2,1,0:T(8,128)(2,1)} %param.23, bf16[64,8,256]{2,1,0:T(8,128)(2,1)S(1)} %gather_fusion, pred[64]{0:T(512)(128)(4,1)S(1)} %compare_and_fusion), kind=kOutput, calls=%fused_computation.20 | convolution fusion | flops 33751040 | bytes 4587584 | tf_op jit(solution)/shard_map/fpi,pio->pfo/dot_general | solution.py:111
  14.3 11.1 %all-to-all-start = ((f32[32,5,128]{2,1,0:T(8,128)}), f32[32,5,128]{2,1,0:T(8,128)S(1)}, u32[]{:S(2)}, u32[]{:S(2)}) async-start(f32[32,5,128]{2,1,0:T(8,128)} %pad_maximum_fusion.12), calls=%async_computation | async-start | bytes 262144 | tf_op jit(solution)/shard_map/all_to_all | solution.py:132
  25.5 2.2 %fusion.76 = (f32[1,1,32,16,512]{4,3,2,1,0:T(8,128)S(1)}, f32[1,1,32,16,512]{4,3,2,1,0:T(8,128)S(1)}, f32[1,1,32,16,512]{4,3,2,1,0:T(8,128)S(1)}) fusion(f32[1,3,32,16,512]{4,3,2,1,0:T(8,128)} %param.13), kind=kLoop, calls=%fused_computation.127 | loop fusion | bytes 6291456 | tf_op jit(solution)/shard_map/slice | solution.py:79
  28.3 3.5 %collective-permute-start.1 = (f32[33,1,512]{2,0,1:T(8,128)S(1)}, f32[33,1,512]{2,0,1:T(8,128)}, u32[]{:S(2)}, u32[]{:S(2)}) collective-permute-start(f32[33,1,512]{2,0,1:T(8,128)S(1)} %pad_maximum_fusion.14), channel_id=1, source_target_pairs={{0,4},{4,8},{8,12},{12,16},{16,20},{20,24},{24,28},{28,32},{32,36}... | collective-permute-start | bytes 202760 | tf_op jit(solution)/shard_map/ppermute | solution.py:14
  33.5 3.8 %collective-permute-start.3 = (f32[33,16,1]{2,0,1:T(8,128)}, f32[33,16,1]{2,0,1:T(8,128)}, u32[]{:S(2)}, u32[]{:S(2)}) collective-permute-start(f32[33,16,1]{2,0,1:T(8,128)} %pad_maximum_fusion.11), channel_id=1, source_target_pairs={{0,1},{1,2},{2,3},{4,5},{5,6},{6,7},{8,9},{9,10},{10,11},{12,13},{... | collective-permute-start | bytes 6344 | tf_op jit(solution)/shard_map/ppermute | solution.py:14
  38.0 1.3 %collective-permute-start.2 = (f32[33,16,1]{2,0,1:T(8,128)}, f32[33,16,1]{2,0,1:T(8,128)}, u32[]{:S(2)}, u32[]{:S(2)}) collective-permute-start(f32[33,16,1]{2,0,1:T(8,128)} %pad_maximum_fusion.10), channel_id=1, source_target_pairs={{1,0},{2,1},{3,2},{5,4},{6,5},{7,6},{9,8},{10,9},{11,10},{13,12},{... | collective-permute-start | bytes 6344 | tf_op jit(solution)/shard_map/ppermute | solution.py:15
  40.0 1.9 %collective-permute-start = (f32[33,1,512]{2,0,1:T(8,128)}, f32[33,1,512]{2,0,1:T(8,128)}, u32[]{:S(2)}, u32[]{:S(2)}) collective-permute-start(f32[33,1,512]{2,0,1:T(8,128)} %pad_maximum_fusion.13), channel_id=1, source_target_pairs={{4,0},{8,4},{12,8},{16,12},{20,16},{24,20},{28,24},{32,28},{36,32}... | collective-permute-start | bytes 202760 | tf_op jit(solution)/shard_map/ppermute | solution.py:15
  41.9 1.6 %copy.69 = f32[1,1,32,16,512]{4,2,3,1,0:T(8,128)} copy(f32[1,1,32,16,512]{4,3,2,1,0:T(8,128)S(1)} %get-tuple-element.28) | data formatting | bytes 2097152
  45.2 4.5 %collective-permute-done.2 = f32[33,16,1]{2,0,1:T(8,128)} collective-permute-done((f32[33,16,1]{2,0,1:T(8,128)}, f32[33,16,1]{2,0,1:T(8,128)}, u32[]{:S(2)}, u32[]{:S(2)}) %collective-permute-start.2) | collective-permute-done | bytes 2144 | tf_op jit(solution)/shard_map/ppermute | solution.py:15
  52.3 1.7 %slice.241 = f32[32,16,1]{2,0,1:T(8,128)} slice(f32[33,16,1]{2,0,1:T(8,128)} %collective-permute-done.2), slice={[0:32], [0:16], [0:1]} | slice | bytes 4096 | tf_op jit(solution)/shard_map/slice | solution.py:38
  57.1 1.5 %slice.238 = f32[32,1,512]{2,0,1:T(8,128)} slice(f32[33,1,512]{2,0,1:T(8,128)} %collective-permute-done.1), slice={[0:32], [0:1], [0:512]} | slice | bytes 131072 | tf_op jit(solution)/shard_map/slice | solution.py:36
  58.6 1.5 %slice.235 = f32[32,1,512]{2,0,1:T(8,128)} slice(f32[33,1,512]{2,0,1:T(8,128)} %collective-permute-done), slice={[0:32], [0:1], [0:512]} | slice | bytes 131072 | tf_op jit(solution)/shard_map/slice | solution.py:36
  60.7 3.7 %fusion.6 = f32[32,16,512]{2,0,1:T(8,128)S(1)} fusion(f32[32,16,512]{2,0,1:T(8,128)} %bitcast.113, f32[32,16,512]{2,0,1:T(8,128)S(1)} %bitcast.108, f32[32,16,1]{2,0,1:T(8,128)S(1)} %slice.244, f32[32,16,1]{2,0,1:T(8,128)} %slice.241, f32[32,16,512]{2,0,1:T(8,128)S(1)} %bitcast.111, f32[32,1,512]{2,0,1:T(8,128)} %slice.238, f32[32,1,512]{2,0,1:T(8,128)} %slice.235, ...), kind=kOutput, calls=%fused_computation.11 | convolution fusion | flops 105644032 | bytes 4366336 | tf_op jit(solution)/shard_map/lm,mxy->lxy/dot_general | solution.py:20
  67.7 1.5 %convolution_convert_fusion = bf16[128,128]{1,0:T(8,128)(2,1)} fusion(f32[64,128]{1,0:T(8,128)S(1)} %bitcast.118, f32[64,128]{1,0:T(8,128)S(1)} %bitcast.116, f32[64,128]{1,0:T(8,128)S(1)} %fusion.60, s32[128]{0:T(128)} %convert_element_type.71), kind=kOutput, calls=%fused_computation.21 | convolution fusion | flops 2146304 | bytes 131584 | tf_op jit(solution)/shard_map/dot_general | solution.py:146
  69.2 7.5 %all-to-all-start.1 = ((bf16[32,4,128]{2,1,0:T(4,128)(2,1)}), bf16[32,4,128]{2,1,0:T(4,128)(2,1)}, u32[]{:S(2)}, u32[]{:S(2)}) async-start(bf16[32,4,128]{2,1,0:T(4,128)(2,1)} %bitcast.126), calls=%async_computation.1 | async-start | bytes 65536 | tf_op jit(solution)/shard_map/all_to_all | solution.py:151
  76.7 2.4 %collective-permute-start.7 = (f32[32,16,2]{2,0,1:T(8,128)}, f32[32,16,2]{2,0,1:T(8,128)S(1)}, u32[]{:S(2)}, u32[]{:S(2)}) collective-permute-start(f32[32,16,2]{2,0,1:T(8,128)} %get-tuple-element.40), channel_id=1, source_target_pairs={{0,1},{1,2},{2,3},{4,5},{5,6},{6,7},{8,9},{9,10},{10,11},{12,13},{... | collective-permute-start | bytes 12296 | tf_op jit(solution)/shard_map/ppermute | solution.py:14
  79.1 1.3 %collective-permute-start.6 = (f32[32,16,2]{2,0,1:T(8,128)}, f32[32,16,2]{2,0,1:T(8,128)S(1)}, u32[]{:S(2)}, u32[]{:S(2)}) collective-permute-start(f32[32,16,2]{2,0,1:T(8,128)} %get-tuple-element.41), channel_id=1, source_target_pairs={{1,0},{2,1},{3,2},{5,4},{6,5},{7,6},{9,8},{10,9},{11,10},{13,12},{... | collective-permute-start | bytes 12296 | tf_op jit(solution)/shard_map/ppermute | solution.py:15
  80.4 7.0 %collective-permute-start.13 = (f32[8192]{0:T(1024)S(1)}, f32[8192]{0:T(1024)S(1)}, u32[]{:S(2)}, u32[]{:S(2)}) collective-permute-start(f32[8192]{0:T(1024)S(1)} %fusion.58), channel_id=1, source_target_pairs={{0,128},{1,129},{2,130},{3,131},{4,132},{5,133},{6,134},{7,135},{8... | collective-permute-start | bytes 98312 | tf_op jit(solution)/shard_map/ppermute | solution.py:163
  87.4 3.5 %collective-permute-start.5 = (f32[32,2,512]{2,0,1:T(8,128)}, f32[32,2,512]{2,0,1:T(8,128)}, u32[]{:S(2)}, u32[]{:S(2)}) collective-permute-start(f32[32,2,512]{2,0,1:T(8,128)} %get-tuple-element.38), channel_id=1, source_target_pairs={{0,4},{4,8},{8,12},{12,16},{16,20},{20,24},{24,28},{28,32},{32,36}... | collective-permute-start | bytes 393224 | tf_op jit(solution)/shard_map/ppermute | solution.py:14
  90.9 2.1 %collective-permute-start.4 = (f32[32,2,512]{2,0,1:T(8,128)}, f32[32,2,512]{2,0,1:T(8,128)}, u32[]{:S(2)}, u32[]{:S(2)}) collective-permute-start(f32[32,2,512]{2,0,1:T(8,128)} %get-tuple-element.39), channel_id=1, source_target_pairs={{4,0},{8,4},{12,8},{16,12},{20,16},{24,20},{28,24},{32,28},{36,32}... | collective-permute-start | bytes 393224 | tf_op jit(solution)/shard_map/ppermute | solution.py:15
  93.1 2.8 %fusion.7 = f32[32,16,514]{2,0,1:T(8,128)} fusion(f32[32,16,1]{2,0,1:T(8,128)} %slice.241, f32[32,16,512]{2,0,1:T(8,128)S(1)} %bitcast.109, f32[32,16,1]{2,0,1:T(8,128)S(1)} %slice.244, f32[32,16,2]{2,0,1:T(8,128)S(1)} %collective-permute-done.6, f32[32,16,512]{2,0,1:T(8,128)S(1)} %fusion.6, f32[32,16,2]{2,0,1:T(8,128)S(1)} %collective-permute-done.7, ...), kind=kLoop, calls=%fused_computation.13 | loop fusion | flops 2105344 | bytes 3195008 | tf_op jit(solution)/shard_map/mul | solution.py:49
  96.9 3.4 %fusion.1 = f32[64,1,256]{2,1,0:T(1,128)S(1)} fusion(bf16[1,1,64,256,128]{4,3,2,1,0:T(8,128)(2,1)} %param.23, bf16[64,128,1]{1,0,2:T(8,128)(2,1)S(1)} %fusion.14), kind=kOutput, calls=%fused_computation.3 | convolution fusion | flops 4194304 | bytes 4276224 | tf_op jit(solution)/shard_map/pio,po->pi/dot_general | solution.py:159
  100.6 1.4 %fusion.9 = f32[32,18,512]{2,0,1:T(8,128)S(1)} fusion(f32[32,1,512]{2,0,1:T(8,128)S(1)} %copy-done.3, f32[32,16,512]{2,0,1:T(8,128)S(1)} %bitcast.112, f32[32,1,512]{2,0,1:T(8,128)S(1)} %copy-done.2, f32[32,2,512]{2,0,1:T(8,128)} %collective-permute-done.4, f32[32,16,512]{2,0,1:T(8,128)S(1)} %fusion.6, f32[32,2,512]{2,0,1:T(8,128)} %collective-permute-done.5, ...), kind=kLoop, calls=%fused_computation.17 | loop fusion | flops 2359296 | bytes 3706880 | tf_op jit(solution)/shard_map/mul | solution.py:48
  102.0 1.9 %fusion.5 = f32[32,16,512]{2,0,1:T(8,128)S(1)} fusion(f32[32,16,512]{2,0,1:T(8,128)S(1)} %fusion.6, f32[32,16,514]{2,0,1:T(8,128)S(1)} %copy-done.1, f32[32,18,512]{2,0,1:T(8,128)S(1)} %fusion.9, f32[16,512]{1,0:T(8,128)S(1)} %bitcast.136, f32[1,32,32]{2,1,0:T(8,128)S(1)} %copy-done), kind=kOutput, calls=%fused_computation.9 | convolution fusion | flops 103546880 | bytes 11616256 | tf_op jit(solution)/shard_map/lm,mxy->lxy/dot_general | solution.py:20
  104.1 1.9 %collective-permute-start.8 = (f32[32,1,512]{2,0,1:T(8,128)S(1)}, f32[32,1,512]{2,0,1:T(8,128)S(1)}, u32[]{:S(2)}, u32[]{:S(2)}) collective-permute-start(f32[32,1,512]{2,0,1:T(8,128)S(1)} %get-tuple-element.34), channel_id=1, source_target_pairs={{4,0},{8,4},{12,8},{16,12},{20,16},{24,20},{28,24},{32,28},{36,32}... | collective-permute-start | bytes 196616 | tf_op jit(solution)/shard_map/ppermute | solution.py:15
  106.0 3.6 %collective-permute-start.9 = (f32[32,1,512]{2,0,1:T(8,128)S(1)}, f32[32,1,512]{2,0,1:T(8,128)S(1)}, u32[]{:S(2)}, u32[]{:S(2)}) collective-permute-start(f32[32,1,512]{2,0,1:T(8,128)S(1)} %get-tuple-element.35), channel_id=1, source_target_pairs={{0,4},{4,8},{8,12},{12,16},{16,20},{20,24},{24,28},{28,32},{32,36}... | collective-permute-start | bytes 196616 | tf_op jit(solution)/shard_map/ppermute | solution.py:14
  109.6 1.3 %collective-permute-start.10 = (f32[32,16,1]{2,0,1:T(8,128)S(1)}, f32[32,16,1]{2,0,1:T(8,128)S(1)}, u32[]{:S(2)}, u32[]{:S(2)}) collective-permute-start(f32[32,16,1]{2,0,1:T(8,128)S(1)} %get-tuple-element.36), channel_id=1, source_target_pairs={{1,0},{2,1},{3,2},{5,4},{6,5},{7,6},{9,8},{10,9},{11,10},{13,12},{... | collective-permute-start | bytes 6152 | tf_op jit(solution)/shard_map/ppermute | solution.py:15
  110.9 4.9 %collective-permute-start.11 = (f32[32,16,1]{2,0,1:T(8,128)S(1)}, f32[32,16,1]{2,0,1:T(8,128)S(1)}, u32[]{:S(2)}, u32[]{:S(2)}) collective-permute-start(f32[32,16,1]{2,0,1:T(8,128)S(1)} %get-tuple-element.37), channel_id=1, source_target_pairs={{0,1},{1,2},{2,3},{4,5},{5,6},{6,7},{8,9},{9,10},{10,11},{12,13},{... | collective-permute-start | bytes 6152 | tf_op jit(solution)/shard_map/ppermute | solution.py:14
  116.5 2.9 %collective-permute-done.10 = f32[32,16,1]{2,0,1:T(8,128)S(1)} collective-permute-done((f32[32,16,1]{2,0,1:T(8,128)S(1)}, f32[32,16,1]{2,0,1:T(8,128)S(1)}, u32[]{:S(2)}, u32[]{:S(2)}) %collective-permute-start.10) | collective-permute-done | bytes 2080 | tf_op jit(solution)/shard_map/ppermute | solution.py:15
  119.4 1.8 %collective-permute-done.11 = f32[32,16,1]{2,0,1:T(8,128)S(1)} collective-permute-done((f32[32,16,1]{2,0,1:T(8,128)S(1)}, f32[32,16,1]{2,0,1:T(8,128)S(1)}, u32[]{:S(2)}, u32[]{:S(2)}) %collective-permute-start.11) | collective-permute-done | bytes 2080 | tf_op jit(solution)/shard_map/ppermute | solution.py:14
  122.6 3.5 %copy.42 = f32[1,3,32,16,512]{4,3,2,1,0:T(8,128)} copy(f32[1,3,32,16,512]{4,2,3,1,0:T(8,128)S(1)} %maximum_bitcast_fusion) | data formatting | bytes 6291456
  (92 shorter events, 27.7 us)
Async XLA Ops:
  0.6 60.1 %copy-start = (f32[1,32,32]{2,1,0:T(8,128)S(1)}, f32[1,32,32]{2,1,0:T(8,128)}, u32[]{:S(2)}) copy-start(f32[1,32,32]{2,1,0:T(8,128)} %param.16) | copy-start | bytes 12292
  2.3 51.7 %collective-permute-start.12 = (f32[2,8192]{1,0:T(2,128)S(1)}, f32[2,8192]{1,0:T(2,128)}, u32[]{:S(2)}, u32[]{:S(2)}) collective-permute-start(f32[2,8192]{1,0:T(2,128)S(1)} %pad_maximum_fusion.15), channel_id=1, source_target_pairs={{128,0},{129,1},{130,2},{131,3},{132,4},{133,5},{134,6},{135,7},{1... | collective-permute-start | bytes 196616 | tf_op jit(solution)/shard_map/ppermute | solution.py:99
  7.2 6.1 %copy-start.7 = (s32[64]{0:T(128)}, s32[64]{0:T(128)S(1)}, u32[]{:S(2)}) copy-start(s32[64]{0:T(128)S(1)} %multiply_add_fusion) | copy-start | bytes 772
  10.1 2.9 %copy-start.5 = (f32[8]{0:T(128)S(1)}, f32[8]{0:T(128)}, u32[]{:S(2)}) copy-start(f32[8]{0:T(128)} %param.19) | copy-start | bytes 100
  14.3 45.7 %all-to-all-start = ((f32[32,5,128]{2,1,0:T(8,128)}), f32[32,5,128]{2,1,0:T(8,128)S(1)}, u32[]{:S(2)}, u32[]{:S(2)}) async-start(f32[32,5,128]{2,1,0:T(8,128)} %pad_maximum_fusion.12), calls=%async_computation | async-start | bytes 262144 | tf_op jit(solution)/shard_map/all_to_all | solution.py:132
  28.3 26.7 %collective-permute-start.1 = (f32[33,1,512]{2,0,1:T(8,128)S(1)}, f32[33,1,512]{2,0,1:T(8,128)}, u32[]{:S(2)}, u32[]{:S(2)}) collective-permute-start(f32[33,1,512]{2,0,1:T(8,128)S(1)} %pad_maximum_fusion.14), channel_id=1, source_target_pairs={{0,4},{4,8},{8,12},{12,16},{16,20},{20,24},{24,28},{28,32},{32,36}... | collective-permute-start | bytes 202760 | tf_op jit(solution)/shard_map/ppermute | solution.py:14
  33.5 10.9 %collective-permute-start.3 = (f32[33,16,1]{2,0,1:T(8,128)}, f32[33,16,1]{2,0,1:T(8,128)}, u32[]{:S(2)}, u32[]{:S(2)}) collective-permute-start(f32[33,16,1]{2,0,1:T(8,128)} %pad_maximum_fusion.11), channel_id=1, source_target_pairs={{0,1},{1,2},{2,3},{4,5},{5,6},{6,7},{8,9},{9,10},{10,11},{12,13},{... | collective-permute-start | bytes 6344 | tf_op jit(solution)/shard_map/ppermute | solution.py:14
  38.0 11.7 %collective-permute-start.2 = (f32[33,16,1]{2,0,1:T(8,128)}, f32[33,16,1]{2,0,1:T(8,128)}, u32[]{:S(2)}, u32[]{:S(2)}) collective-permute-start(f32[33,16,1]{2,0,1:T(8,128)} %pad_maximum_fusion.10), channel_id=1, source_target_pairs={{1,0},{2,1},{3,2},{5,4},{6,5},{7,6},{9,8},{10,9},{11,10},{13,12},{... | collective-permute-start | bytes 6344 | tf_op jit(solution)/shard_map/ppermute | solution.py:15
  40.0 15.7 %collective-permute-start = (f32[33,1,512]{2,0,1:T(8,128)}, f32[33,1,512]{2,0,1:T(8,128)}, u32[]{:S(2)}, u32[]{:S(2)}) collective-permute-start(f32[33,1,512]{2,0,1:T(8,128)} %pad_maximum_fusion.13), channel_id=1, source_target_pairs={{4,0},{8,4},{12,8},{16,12},{20,16},{24,20},{28,24},{32,28},{36,32}... | collective-permute-start | bytes 202760 | tf_op jit(solution)/shard_map/ppermute | solution.py:15
  69.2 26.8 %all-to-all-start.1 = ((bf16[32,4,128]{2,1,0:T(4,128)(2,1)}), bf16[32,4,128]{2,1,0:T(4,128)(2,1)}, u32[]{:S(2)}, u32[]{:S(2)}) async-start(bf16[32,4,128]{2,1,0:T(4,128)(2,1)} %bitcast.126), calls=%async_computation.1 | async-start | bytes 65536 | tf_op jit(solution)/shard_map/all_to_all | solution.py:151
  76.7 16.4 %collective-permute-start.7 = (f32[32,16,2]{2,0,1:T(8,128)}, f32[32,16,2]{2,0,1:T(8,128)S(1)}, u32[]{:S(2)}, u32[]{:S(2)}) collective-permute-start(f32[32,16,2]{2,0,1:T(8,128)} %get-tuple-element.40), channel_id=1, source_target_pairs={{0,1},{1,2},{2,3},{4,5},{5,6},{6,7},{8,9},{9,10},{10,11},{12,13},{... | collective-permute-start | bytes 12296 | tf_op jit(solution)/shard_map/ppermute | solution.py:14
  79.1 14.0 %collective-permute-start.6 = (f32[32,16,2]{2,0,1:T(8,128)}, f32[32,16,2]{2,0,1:T(8,128)S(1)}, u32[]{:S(2)}, u32[]{:S(2)}) collective-permute-start(f32[32,16,2]{2,0,1:T(8,128)} %get-tuple-element.41), channel_id=1, source_target_pairs={{1,0},{2,1},{3,2},{5,4},{6,5},{7,6},{9,8},{10,9},{11,10},{13,12},{... | collective-permute-start | bytes 12296 | tf_op jit(solution)/shard_map/ppermute | solution.py:15
  80.4 15.5 %collective-permute-start.13 = (f32[8192]{0:T(1024)S(1)}, f32[8192]{0:T(1024)S(1)}, u32[]{:S(2)}, u32[]{:S(2)}) collective-permute-start(f32[8192]{0:T(1024)S(1)} %fusion.58), channel_id=1, source_target_pairs={{0,128},{1,129},{2,130},{3,131},{4,132},{5,133},{6,134},{7,135},{8... | collective-permute-start | bytes 98312 | tf_op jit(solution)/shard_map/ppermute | solution.py:163
  87.4 13.1 %collective-permute-start.5 = (f32[32,2,512]{2,0,1:T(8,128)}, f32[32,2,512]{2,0,1:T(8,128)}, u32[]{:S(2)}, u32[]{:S(2)}) collective-permute-start(f32[32,2,512]{2,0,1:T(8,128)} %get-tuple-element.38), channel_id=1, source_target_pairs={{0,4},{4,8},{8,12},{12,16},{16,20},{20,24},{24,28},{28,32},{32,36}... | collective-permute-start | bytes 393224 | tf_op jit(solution)/shard_map/ppermute | solution.py:14
  90.9 9.6 %collective-permute-start.4 = (f32[32,2,512]{2,0,1:T(8,128)}, f32[32,2,512]{2,0,1:T(8,128)}, u32[]{:S(2)}, u32[]{:S(2)}) collective-permute-start(f32[32,2,512]{2,0,1:T(8,128)} %get-tuple-element.39), channel_id=1, source_target_pairs={{4,0},{8,4},{12,8},{16,12},{20,16},{24,20},{28,24},{32,28},{36,32}... | collective-permute-start | bytes 393224 | tf_op jit(solution)/shard_map/ppermute | solution.py:15
  93.0 2.9 %copy-start.8 = (s32[64]{0:T(128)S(1)}, s32[64]{0:T(128)}, u32[]{:S(2)}) copy-start(s32[64]{0:T(128)} %copy-done.7) | copy-start | bytes 772
  96.9 3.5 %copy-start.6 = (s32[1,1,64]{2,1,0:T(1,128)S(1)}, s32[1,1,64]{2,1,0:T(1,128)}, u32[]{:S(2)}) copy-start(s32[1,1,64]{2,1,0:T(1,128)} %param.21) | copy-start | bytes 772
  96.9 3.7 %copy-start.2 = (f32[32,1,512]{2,0,1:T(8,128)S(1)}, f32[32,1,512]{2,0,1:T(8,128)}, u32[]{:S(2)}) copy-start(f32[32,1,512]{2,0,1:T(8,128)} %slice.238) | copy-start | bytes 196612
  96.9 3.7 %copy-start.3 = (f32[32,1,512]{2,0,1:T(8,128)S(1)}, f32[32,1,512]{2,0,1:T(8,128)}, u32[]{:S(2)}) copy-start(f32[32,1,512]{2,0,1:T(8,128)} %slice.235) | copy-start | bytes 196612
  96.9 3.7 %copy-start.4 = (f32[1,18,512]{2,1,0:T(8,128)S(1)}, f32[1,18,512]{2,1,0:T(8,128)}, u32[]{:S(2)}) copy-start(f32[1,18,512]{2,1,0:T(8,128)} %copy.72) | copy-start | bytes 110596
  100.6 1.4 %copy-start.1 = (f32[32,16,514]{2,0,1:T(8,128)S(1)}, f32[32,16,514]{2,0,1:T(8,128)}, u32[]{:S(2)}) copy-start(f32[32,16,514]{2,0,1:T(8,128)} %fusion.7) | copy-start | bytes 3158020
  100.6 1.4 %copy-start.9 = (f32[1,16,512]{2,1,0:T(8,128)S(1)}, f32[1,16,512]{2,1,0:T(8,128)}, u32[]{:S(2)}) copy-start(f32[1,16,512]{2,1,0:T(8,128)} %param.14) | copy-start | bytes 98308
  104.1 17.1 %collective-permute-start.8 = (f32[32,1,512]{2,0,1:T(8,128)S(1)}, f32[32,1,512]{2,0,1:T(8,128)S(1)}, u32[]{:S(2)}, u32[]{:S(2)}) collective-permute-start(f32[32,1,512]{2,0,1:T(8,128)S(1)} %get-tuple-element.34), channel_id=1, source_target_pairs={{4,0},{8,4},{12,8},{16,12},{20,16},{24,20},{28,24},{32,28},{36,32}... | collective-permute-start | bytes 196616 | tf_op jit(solution)/shard_map/ppermute | solution.py:15
  106.0 15.2 %collective-permute-start.9 = (f32[32,1,512]{2,0,1:T(8,128)S(1)}, f32[32,1,512]{2,0,1:T(8,128)S(1)}, u32[]{:S(2)}, u32[]{:S(2)}) collective-permute-start(f32[32,1,512]{2,0,1:T(8,128)S(1)} %get-tuple-element.35), channel_id=1, source_target_pairs={{0,4},{4,8},{8,12},{12,16},{16,20},{20,24},{24,28},{28,32},{32,36}... | collective-permute-start | bytes 196616 | tf_op jit(solution)/shard_map/ppermute | solution.py:14
  109.6 9.8 %collective-permute-start.10 = (f32[32,16,1]{2,0,1:T(8,128)S(1)}, f32[32,16,1]{2,0,1:T(8,128)S(1)}, u32[]{:S(2)}, u32[]{:S(2)}) collective-permute-start(f32[32,16,1]{2,0,1:T(8,128)S(1)} %get-tuple-element.36), channel_id=1, source_target_pairs={{1,0},{2,1},{3,2},{5,4},{6,5},{7,6},{9,8},{10,9},{11,10},{13,12},{... | collective-permute-start | bytes 6152 | tf_op jit(solution)/shard_map/ppermute | solution.py:15
  110.9 10.2 %collective-permute-start.11 = (f32[32,16,1]{2,0,1:T(8,128)S(1)}, f32[32,16,1]{2,0,1:T(8,128)S(1)}, u32[]{:S(2)}, u32[]{:S(2)}) collective-permute-start(f32[32,16,1]{2,0,1:T(8,128)S(1)} %get-tuple-element.37), channel_id=1, source_target_pairs={{0,1},{1,2},{2,3},{4,5},{5,6},{6,7},{8,9},{9,10},{10,11},{12,13},{... | collective-permute-start | bytes 6152 | tf_op jit(solution)/shard_map/ppermute | solution.py:14

commit v10 on v2

--- a/solution.py
+++ b/solution.py
@@ -81,9 +81,6 @@
     sound_speed = wave_speed[0]
     wetness = wet_mask[0].astype(jnp.float32)
     matrix = vertical[0]
-    assert SUBSTEPS == 2
-    p2, u2, v2 = stencil(pressure, eastward, northward, sound_speed, wetness, matrix)
-    final_state = jnp.stack([p2, u2, v2])[None]
 
     weights = intersection_weights[0, 0]
     pair_count, in_width, out_width = weights.shape
@@ -136,6 +133,10 @@
     )
     packet = jnp.concatenate([outgoing.reshape(tile_count, capacity, out_width), offset_row], axis=1)
     arrived = lax.all_to_all(packet, "gx", split_axis=0, concat_axis=0, tiled=True)
+    arrived, pressure, eastward, northward = lax.optimization_barrier((arrived, pressure, eastward, northward))
+    assert SUBSTEPS == 2
+    p2, u2, v2 = stencil(pressure, eastward, northward, sound_speed, wetness, matrix)
+    final_state = jnp.stack([p2, u2, v2])[None]
     arrived_at = arrived[:, capacity, :capacity].reshape(slot_count).astype(jnp.int32)
     landing = jnp.arange(out_blocks)[:, None] == arrived_at[None, :]
     heating = jnp.dot(

time: 114 us -> 118 us (1.035)
  the two profiles are of different devices: /device:TPU:1 before, /device:TPU:111 now
where the time goes in v10:
time: 118 us; the launch traced here: 117 us
  starting transfers between devices  55.6 us (47%)
  waiting for transfers between devices  20.2 us (17%)
  local copies, waits for them, and re-layouts  17.5 us (15%)
  matrix products  14.2 us (12%)
  other arithmetic  7.84 us (7%)
  between operations  1.35 us (1%)
    ppermute x6, starting transfers between devices, neighbours(): lo = lax.ppermute(tail, axis, [(i, i + 1) for i in range(count - 1)])  19.2 us
    ppermute x6, starting transfers between devices, neighbours(): hi = lax.ppermute(head, axis, [(i + 1, i) for i in range(count - 1)])  18.1 us
    all_to_all x1, starting transfers between devices, local(): lax.all_to_all(packet, 'gx', split_axis=0, concat_axis=0, tiled=True)  9.32 us
    ppermute x6, waiting for transfers between devices, neighbours(): hi = lax.ppermute(head, axis, [(i + 1, i) for i in range(count - 1)])  8.41 us
    unnamed x45, local copies, waits for them, and re-layouts  7.49 us
    all_to_all x1, starting transfers between devices, local(): lax.all_to_all(returning.reshape(tile_count, capacity, out_width), 'gx',...  6.97 us
    ppermute x6, waiting for transfers between devices, neighbours(): lo = lax.ppermute(tail, axis, [(i, i + 1) for i in range(count - 1)])  6.4 us
    dot_general x2, matrix products, vertical_mix(): jnp.einsum('lm,mxy->lxy', matrix, right_side, precision=HIGHEST_PRECISION)  5.45 us
  transfers between devices with their start and end apart: 15, of which 6 were waited for; matrix products, arithmetic and copies ran while one was open for 16% of the time, Pallas kernels for 0%

profile of v10, /device:TPU:111, one launch (start us, length us, event | category | flops | bytes accessed | tf_op | source)
XLA Modules:
  0.0 116.7 jit_solution(17069033113725106223)
XLA Ops:
  3.4 2.1 %collective-permute-start = (f32[4,8192]{1,0:T(4,128)S(1)}, f32[4,8192]{1,0:T(4,128)}, u32[]{:S(2)}, u32[]{:S(2)}) collective-permute-start(f32[4,8192]{1,0:T(4,128)S(1)} %maximum_select_fusion), channel_id=1, source_target_pairs={{0,128},{128,0},{1,129},{129,1},{2,130},{130,2},{3,131},{131,3},{4... | collective-permute-start | bytes 393224 | tf_op jit(solution)/shard_map/ppermute | solution.py:105
  5.5 1.2 %compare_and_fusion = pred[64]{0:T(512)(128)(4,1)} fusion(s32[1,1,64]{2,1,0:T(1,128)} %param.21), kind=kLoop, calls=%fused_computation.116 | loop fusion | flops 384 | bytes 320 | tf_op jit(solution)/shard_map/jit(_take)/and | solution.py:113
  6.8 1.1 fusion.67
  8.6 2.2 %fusion.73 = (f32[1,1,32,16,512]{4,3,2,1,0:T(8,128)S(1)}, f32[1,1,32,16,512]{4,3,2,1,0:T(8,128)S(1)}, f32[1,1,32,16,512]{4,3,2,1,0:T(8,128)S(1)}) fusion(f32[1,3,32,16,512]{4,3,2,1,0:T(8,128)} %param.13), kind=kLoop, calls=%fused_computation.126 | loop fusion | bytes 6291456 | tf_op jit(solution)/shard_map/slice | solution.py:80
  11.2 1.2 %copy_bitcast_fusion = (f32[32,16,512]{2,0,1:T(8,128)S(1)}, f32[32,16,512]{2,0,1:T(8,128)S(1)}) fusion(f32[1,1,32,16,512]{4,3,2,1,0:T(8,128)S(1)} %get-tuple-element.30, f32[1,1,32,16,512]{4,3,2,1,0:T(8,128)S(1)} %get-tuple-element.31), kind=kLoop, calls=%fused_computation.58 | loop fusion | bytes 4194304 | tf_op jit(solution)/shard_map/squeeze | solution.py:80
  15.0 1.6 %copy.80 = f32[1,1,32,16,512]{4,2,3,1,0:T(8,128)} copy(f32[1,1,32,16,512]{4,3,2,1,0:T(8,128)S(1)} %get-tuple-element.32) | data formatting | bytes 2097152
  17.7 2.9 %fusion.11 = bf16[64,8,128]{2,1,0:T(8,128)(2,1)S(1)} fusion(bf16[1,1,64,256,128]{4,3,2,1,0:T(8,128)(2,1)} %param.23, bf16[64,8,256]{2,1,0:T(8,128)(2,1)S(1)} %gather_fusion, pred[64]{0:T(512)(128)(4,1)S(1)} %copy-done.11), kind=kOutput, calls=%fused_computation.20 | convolution fusion | flops 33751040 | bytes 4587584 | tf_op jit(solution)/shard_map/fpi,pio->pfo/dot_general | solution.py:114
  22.0 9.3 %all-to-all-start = ((f32[32,5,128]{2,1,0:T(8,128)}), f32[32,5,128]{2,1,0:T(8,128)S(1)}, u32[]{:S(2)}, u32[]{:S(2)}) async-start(f32[32,5,128]{2,1,0:T(8,128)} %pad_maximum_fusion.13), calls=%async_computation | async-start | bytes 262144 | tf_op jit(solution)/shard_map/all_to_all | solution.py:135
  32.3 5.4 %all-to-all-done = f32[32,5,128]{2,1,0:T(8,128)S(1)} async-done(((f32[32,5,128]{2,1,0:T(8,128)}), f32[32,5,128]{2,1,0:T(8,128)S(1)}, u32[]{:S(2)}, u32[]{:S(2)}) %all-to-all-start) | async-done | bytes 81952 | tf_op jit(solution)/shard_map/all_to_all | solution.py:135
  39.0 7.0 %all-to-all-start.1 = ((bf16[32,4,128]{2,1,0:T(4,128)(2,1)}), bf16[32,4,128]{2,1,0:T(4,128)(2,1)S(1)}, u32[]{:S(2)}, u32[]{:S(2)}) async-start(bf16[32,4,128]{2,1,0:T(4,128)(2,1)} %bitcast.31), calls=%async_computation.1 | async-start | bytes 65536 | tf_op jit(solution)/shard_map/all_to_all | solution.py:154
  46.0 4.6 %collective-permute-start.2 = (f32[33,1,512]{2,0,1:T(8,128)S(1)}, f32[33,1,512]{2,0,1:T(8,128)S(1)}, u32[]{:S(2)}, u32[]{:S(2)}) collective-permute-start(f32[33,1,512]{2,0,1:T(8,128)S(1)} %pad_maximum_fusion.15), channel_id=1, source_target_pairs={{0,4},{4,8},{8,12},{12,16},{16,20},{20,24},{24,28},{28,32},{32,36}... | collective-permute-start | bytes 202760 | tf_op jit(solution)/shard_map/ppermute | solution.py:14
  50.7 1.3 %collective-permute-start.4 = (f32[33,16,1]{2,0,1:T(8,128)S(1)}, f32[33,16,1]{2,0,1:T(8,128)S(1)}, u32[]{:S(2)}, u32[]{:S(2)}) collective-permute-start(f32[33,16,1]{2,0,1:T(8,128)S(1)} %pad_maximum_fusion.11), channel_id=1, source_target_pairs={{0,1},{1,2},{2,3},{4,5},{5,6},{6,7},{8,9},{9,10},{10,11},{12,13},{... | collective-permute-start | bytes 6344 | tf_op jit(solution)/shard_map/ppermute | solution.py:14
  52.1 4.0 %collective-permute-start.3 = (f32[33,16,1]{2,0,1:T(8,128)S(1)}, f32[33,16,1]{2,0,1:T(8,128)S(1)}, u32[]{:S(2)}, u32[]{:S(2)}) collective-permute-start(f32[33,16,1]{2,0,1:T(8,128)S(1)} %pad_maximum_fusion.10), channel_id=1, source_target_pairs={{1,0},{2,1},{3,2},{5,4},{6,5},{7,6},{9,8},{10,9},{11,10},{13,12},{... | collective-permute-start | bytes 6344 | tf_op jit(solution)/shard_map/ppermute | solution.py:15
  56.1 1.9 %collective-permute-start.1 = (f32[33,1,512]{2,0,1:T(8,128)S(1)}, f32[33,1,512]{2,0,1:T(8,128)}, u32[]{:S(2)}, u32[]{:S(2)}) collective-permute-start(f32[33,1,512]{2,0,1:T(8,128)S(1)} %pad_maximum_fusion.14), channel_id=1, source_target_pairs={{4,0},{8,4},{12,8},{16,12},{20,16},{24,20},{28,24},{32,28},{36,32}... | collective-permute-start | bytes 202760 | tf_op jit(solution)/shard_map/ppermute | solution.py:15
  58.0 2.3 %collective-permute-done.4 = f32[33,16,1]{2,0,1:T(8,128)S(1)} collective-permute-done((f32[33,16,1]{2,0,1:T(8,128)S(1)}, f32[33,16,1]{2,0,1:T(8,128)S(1)}, u32[]{:S(2)}, u32[]{:S(2)}) %collective-permute-start.4) | collective-permute-done | bytes 2144 | tf_op jit(solution)/shard_map/ppermute | solution.py:14
  60.4 1.8 %collective-permute-done.3 = f32[33,16,1]{2,0,1:T(8,128)S(1)} collective-permute-done((f32[33,16,1]{2,0,1:T(8,128)S(1)}, f32[33,16,1]{2,0,1:T(8,128)S(1)}, u32[]{:S(2)}, u32[]{:S(2)}) %collective-permute-start.3) | collective-permute-done | bytes 2144 | tf_op jit(solution)/shard_map/ppermute | solution.py:15
  62.6 3.4 %fusion.1 = f32[64,1,256]{2,1,0:T(1,128)S(1)} fusion(bf16[1,1,64,256,128]{4,3,2,1,0:T(8,128)(2,1)} %param.23, bf16[64,128,1]{1,0,2:T(8,128)(2,1)S(1)} %fusion.14), kind=kOutput, calls=%fused_computation.3 | convolution fusion | flops 4194304 | bytes 4276224 | tf_op jit(solution)/shard_map/pio,po->pi/dot_general | solution.py:162
  67.1 3.6 %fusion.6 = f32[32,16,512]{2,0,1:T(8,128)S(1)} fusion(f32[32,16,512]{2,0,1:T(8,128)} %bitcast.105, f32[32,16,512]{2,0,1:T(8,128)S(1)} %get-tuple-element.20, f32[32,16,1]{2,0,1:T(8,128)S(1)} %slice.240, f32[32,16,1]{2,0,1:T(8,128)S(1)} %slice.238, f32[32,16,512]{2,0,1:T(8,128)S(1)} %get-tuple-element.19, f32[32,1,512]{2,0,1:T(8,128)S(1)} %slice.236, ...), kind=kOutput, calls=%fused_computation.11 | convolution fusion | flops 105644032 | bytes 4366336 | tf_op jit(solution)/shard_map/lm,mxy->lxy/dot_general | solution.py:20
  70.9 1.3 %collective-permute-start.8 = (f32[32,16,2]{2,0,1:T(8,128)S(1)}, f32[32,16,2]{2,0,1:T(8,128)S(1)}, u32[]{:S(2)}, u32[]{:S(2)}) collective-permute-start(f32[32,16,2]{2,0,1:T(8,128)S(1)} %get-tuple-element.44), channel_id=1, source_target_pairs={{0,1},{1,2},{2,3},{4,5},{5,6},{6,7},{8,9},{9,10},{10,11},{12,13},{... | collective-permute-start | bytes 12296 | tf_op jit(solution)/shard_map/ppermute | solution.py:14
  72.2 4.5 %collective-permute-start.7 = (f32[32,16,2]{2,0,1:T(8,128)S(1)}, f32[32,16,2]{2,0,1:T(8,128)S(1)}, u32[]{:S(2)}, u32[]{:S(2)}) collective-permute-start(f32[32,16,2]{2,0,1:T(8,128)S(1)} %get-tuple-element.45), channel_id=1, source_target_pairs={{1,0},{2,1},{3,2},{5,4},{6,5},{7,6},{9,8},{10,9},{11,10},{13,12},{... | collective-permute-start | bytes 12296 | tf_op jit(solution)/shard_map/ppermute | solution.py:15
  77.4 5.0 %collective-permute-start.6 = (f32[32,2,512]{2,0,1:T(8,128)S(1)}, f32[32,2,512]{2,0,1:T(8,128)S(1)}, u32[]{:S(2)}, u32[]{:S(2)}) collective-permute-start(f32[32,2,512]{2,0,1:T(8,128)S(1)} %get-tuple-element.42), channel_id=1, source_target_pairs={{0,4},{4,8},{8,12},{12,16},{16,20},{20,24},{24,28},{28,32},{32,36}... | collective-permute-start | bytes 393224 | tf_op jit(solution)/shard_map/ppermute | solution.py:14
  82.4 2.1 %collective-permute-start.5 = (f32[32,2,512]{2,0,1:T(8,128)S(1)}, f32[32,2,512]{2,0,1:T(8,128)S(1)}, u32[]{:S(2)}, u32[]{:S(2)}) collective-permute-start(f32[32,2,512]{2,0,1:T(8,128)S(1)} %get-tuple-element.43), channel_id=1, source_target_pairs={{4,0},{8,4},{12,8},{16,12},{20,16},{24,20},{28,24},{32,28},{36,32}... | collective-permute-start | bytes 393224 | tf_op jit(solution)/shard_map/ppermute | solution.py:15
  85.4 5.4 %collective-permute-done.5 = f32[32,2,512]{2,0,1:T(8,128)S(1)} collective-permute-done((f32[32,2,512]{2,0,1:T(8,128)S(1)}, f32[32,2,512]{2,0,1:T(8,128)S(1)}, u32[]{:S(2)}, u32[]{:S(2)}) %collective-permute-start.5) | collective-permute-done | bytes 131104 | tf_op jit(solution)/shard_map/ppermute | solution.py:15
  91.1 1.9 %fusion.5 = f32[32,16,512]{2,0,1:T(8,128)S(1)} fusion(f32[32,16,512]{2,0,1:T(8,128)S(1)} %fusion.6, f32[32,16,514]{2,0,1:T(8,128)S(1)} %fusion.7, f32[32,18,512]{2,0,1:T(8,128)S(1)} %fusion.9, f32[16,512]{1,0:T(8,128)S(1)} %bitcast.131, f32[1,32,32]{2,1,0:T(8,128)S(1)} %copy-done), kind=kOutput, calls=%fused_computation.9 | convolution fusion | flops 103546880 | bytes 11616256 | tf_op jit(solution)/shard_map/lm,mxy->lxy/dot_general | solution.py:20
  93.2 1.9 %collective-permute-start.9 = (f32[32,1,512]{2,0,1:T(8,128)S(1)}, f32[32,1,512]{2,0,1:T(8,128)S(1)}, u32[]{:S(2)}, u32[]{:S(2)}) collective-permute-start(f32[32,1,512]{2,0,1:T(8,128)S(1)} %get-tuple-element.38), channel_id=1, source_target_pairs={{4,0},{8,4},{12,8},{16,12},{20,16},{24,20},{28,24},{32,28},{36,32}... | collective-permute-start | bytes 196616 | tf_op jit(solution)/shard_map/ppermute | solution.py:15
  95.1 5.8 %collective-permute-start.10 = (f32[32,1,512]{2,0,1:T(8,128)S(1)}, f32[32,1,512]{2,0,1:T(8,128)S(1)}, u32[]{:S(2)}, u32[]{:S(2)}) collective-permute-start(f32[32,1,512]{2,0,1:T(8,128)S(1)} %get-tuple-element.39), channel_id=1, source_target_pairs={{0,4},{4,8},{8,12},{12,16},{16,20},{20,24},{24,28},{28,32},{32,36}... | collective-permute-start | bytes 196616 | tf_op jit(solution)/shard_map/ppermute | solution.py:14
  100.9 3.6 %collective-permute-start.11 = (f32[32,16,1]{2,0,1:T(8,128)S(1)}, f32[32,16,1]{2,0,1:T(8,128)S(1)}, u32[]{:S(2)}, u32[]{:S(2)}) collective-permute-start(f32[32,16,1]{2,0,1:T(8,128)S(1)} %get-tuple-element.40), channel_id=1, source_target_pairs={{1,0},{2,1},{3,2},{5,4},{6,5},{7,6},{9,8},{10,9},{11,10},{13,12},{... | collective-permute-start | bytes 6152 | tf_op jit(solution)/shard_map/ppermute | solution.py:15
  104.5 1.3 %collective-permute-start.12 = (f32[32,16,1]{2,0,1:T(8,128)S(1)}, f32[32,16,1]{2,0,1:T(8,128)S(1)}, u32[]{:S(2)}, u32[]{:S(2)}) collective-permute-start(f32[32,16,1]{2,0,1:T(8,128)S(1)} %get-tuple-element.41), channel_id=1, source_target_pairs={{0,1},{1,2},{2,3},{4,5},{5,6},{6,7},{8,9},{9,10},{10,11},{12,13},{... | collective-permute-start | bytes 6152 | tf_op jit(solution)/shard_map/ppermute | solution.py:14
  106.6 1.2 %collective-permute-done.11 = f32[32,16,1]{2,0,1:T(8,128)S(1)} collective-permute-done((f32[32,16,1]{2,0,1:T(8,128)S(1)}, f32[32,16,1]{2,0,1:T(8,128)S(1)}, u32[]{:S(2)}, u32[]{:S(2)}) %collective-permute-start.11) | collective-permute-done | bytes 2080 | tf_op jit(solution)/shard_map/ppermute | solution.py:15
  107.8 4.0 %collective-permute-done.12 = f32[32,16,1]{2,0,1:T(8,128)S(1)} collective-permute-done((f32[32,16,1]{2,0,1:T(8,128)S(1)}, f32[32,16,1]{2,0,1:T(8,128)S(1)}, u32[]{:S(2)}, u32[]{:S(2)}) %collective-permute-start.12) | collective-permute-done | bytes 2080 | tf_op jit(solution)/shard_map/ppermute | solution.py:14
  111.9 1.1 fusion.24
  113.2 3.5 %copy.49 = f32[1,3,32,16,512]{4,3,2,1,0:T(8,128)} copy(f32[1,3,32,16,512]{4,2,3,1,0:T(8,128)S(1)} %maximum_bitcast_fusion) | data formatting | bytes 6291456
  (105 shorter events, 15.9 us)
Async XLA Ops:
  0.6 66.5 %copy-start = (f32[1,32,32]{2,1,0:T(8,128)S(1)}, f32[1,32,32]{2,1,0:T(8,128)}, u32[]{:S(2)}) copy-start(f32[1,32,32]{2,1,0:T(8,128)} %param.16) | copy-start | bytes 12292
  3.4 13.1 %collective-permute-start = (f32[4,8192]{1,0:T(4,128)S(1)}, f32[4,8192]{1,0:T(4,128)}, u32[]{:S(2)}, u32[]{:S(2)}) collective-permute-start(f32[4,8192]{1,0:T(4,128)S(1)} %maximum_select_fusion), channel_id=1, source_target_pairs={{0,128},{128,0},{1,129},{129,1},{2,130},{130,2},{3,131},{131,3},{4... | collective-permute-start | bytes 393224 | tf_op jit(solution)/shard_map/ppermute | solution.py:105
  8.6 2.3 %copy-start.15 = (s32[1,1,64]{2,1,0:T(1,128)S(1)}, s32[1,1,64]{2,1,0:T(1,128)}, u32[]{:S(2)}) copy-start(s32[1,1,64]{2,1,0:T(1,128)} %param.22) | copy-start | bytes 772
  8.6 2.3 %copy-start.16 = (s32[1,1,64,1]{2,3,1,0:T(1,128)S(1)}, s32[1,1,64,1]{2,3,1,0:T(1,128)}, u32[]{:S(2)}) copy-start(s32[1,1,64,1]{2,3,1,0:T(1,128)} %param.20) | copy-start | bytes 772
  11.1 1.3 %copy-start.9 = (s32[64]{0:T(128)}, s32[64]{0:T(128)S(1)}, u32[]{:S(2)}) copy-start(s32[64]{0:T(128)S(1)} %multiply_add_fusion) | copy-start | bytes 772
  11.2 1.8 %copy-start.1 = (f32[1,16,512]{2,1,0:T(8,128)S(1)}, f32[1,16,512]{2,1,0:T(8,128)}, u32[]{:S(2)}) copy-start(f32[1,16,512]{2,1,0:T(8,128)} %param.17) | copy-start | bytes 98308
  14.3 2.2 %copy-start.12 = (s32[64]{0:T(128)S(1)}, s32[64]{0:T(128)}, u32[]{:S(2)}) copy-start(s32[64]{0:T(128)} %fusion.67) | copy-start | bytes 772
  14.3 2.2 %copy-start.14 = (f32[8,4]{0,1:T(4,128)S(1)}, f32[8,4]{0,1:T(4,128)}, u32[]{:S(2)}) copy-start(f32[8,4]{0,1:T(4,128)} %param.18) | copy-start | bytes 388
  15.0 2.7 %copy-start.11 = (pred[64]{0:T(512)(128)(4,1)S(1)}, pred[64]{0:T(512)(128)(4,1)}, u32[]{:S(2)}) copy-start(pred[64]{0:T(512)(128)(4,1)} %compare_and_fusion) | copy-start | bytes 196
  17.7 2.9 %copy-start.7 = (f32[8]{0:T(128)S(1)}, f32[8]{0:T(128)}, u32[]{:S(2)}) copy-start(f32[8]{0:T(128)} %param.19) | copy-start | bytes 100
  17.7 3.2 %copy-start.10 = (s32[64]{0:T(128)S(1)}, s32[64]{0:T(128)}, u32[]{:S(2)}) copy-start(s32[64]{0:T(128)} %copy-done.9) | copy-start | bytes 772
  17.7 3.5 %copy-start.4 = (f32[32,1,128]{2,0,1:T(8,128)S(1)}, f32[32,1,128]{2,0,1:T(8,128)}, u32[]{:S(2)}) copy-start(f32[32,1,128]{2,0,1:T(8,128)} %scatter.4) | copy-start | bytes 49156
  17.7 20.4 %copy-start.3 = (f32[64,128]{1,0:T(8,128)S(1)}, f32[64,128]{1,0:T(8,128)}, u32[]{:S(2)}) copy-start(f32[64,128]{1,0:T(8,128)} %reshape_squeeze.4) | copy-start | bytes 98308
  20.7 25.3 %copy-start.6 = (f32[1,1,512]{2,0,1:T(1,128)S(1)}, f32[1,1,512]{2,0,1:T(1,128)}, u32[]{:S(2)}) copy-start(f32[1,1,512]{2,0,1:T(1,128)} %get-tuple-element.53) | copy-start | bytes 6148
  22.0 15.8 %all-to-all-start = ((f32[32,5,128]{2,1,0:T(8,128)}), f32[32,5,128]{2,1,0:T(8,128)S(1)}, u32[]{:S(2)}, u32[]{:S(2)}) async-start(f32[32,5,128]{2,1,0:T(8,128)} %pad_maximum_fusion.13), calls=%async_computation | async-start | bytes 262144 | tf_op jit(solution)/shard_map/all_to_all | solution.py:135
  39.0 23.5 %all-to-all-start.1 = ((bf16[32,4,128]{2,1,0:T(4,128)(2,1)}), bf16[32,4,128]{2,1,0:T(4,128)(2,1)S(1)}, u32[]{:S(2)}, u32[]{:S(2)}) async-start(bf16[32,4,128]{2,1,0:T(4,128)(2,1)} %bitcast.31), calls=%async_computation.1 | async-start | bytes 65536 | tf_op jit(solution)/shard_map/all_to_all | solution.py:154
  45.9 10.2 %copy-start.5 = (f32[1,1,512]{2,0,1:T(1,128)S(1)}, f32[1,1,512]{2,0,1:T(1,128)}, u32[]{:S(2)}) copy-start(f32[1,1,512]{2,0,1:T(1,128)} %get-tuple-element.52) | copy-start | bytes 6148
  46.0 20.2 %collective-permute-start.2 = (f32[33,1,512]{2,0,1:T(8,128)S(1)}, f32[33,1,512]{2,0,1:T(8,128)S(1)}, u32[]{:S(2)}, u32[]{:S(2)}) collective-permute-start(f32[33,1,512]{2,0,1:T(8,128)S(1)} %pad_maximum_fusion.15), channel_id=1, source_target_pairs={{0,4},{4,8},{8,12},{12,16},{16,20},{20,24},{24,28},{28,32},{32,36}... | collective-permute-start | bytes 202760 | tf_op jit(solution)/shard_map/ppermute | solution.py:14
  50.7 9.6 %collective-permute-start.4 = (f32[33,16,1]{2,0,1:T(8,128)S(1)}, f32[33,16,1]{2,0,1:T(8,128)S(1)}, u32[]{:S(2)}, u32[]{:S(2)}) collective-permute-start(f32[33,16,1]{2,0,1:T(8,128)S(1)} %pad_maximum_fusion.11), channel_id=1, source_target_pairs={{0,1},{1,2},{2,3},{4,5},{5,6},{6,7},{8,9},{9,10},{10,11},{12,13},{... | collective-permute-start | bytes 6344 | tf_op jit(solution)/shard_map/ppermute | solution.py:14
  52.1 10.1 %collective-permute-start.3 = (f32[33,16,1]{2,0,1:T(8,128)S(1)}, f32[33,16,1]{2,0,1:T(8,128)S(1)}, u32[]{:S(2)}, u32[]{:S(2)}) collective-permute-start(f32[33,16,1]{2,0,1:T(8,128)S(1)} %pad_maximum_fusion.10), channel_id=1, source_target_pairs={{1,0},{2,1},{3,2},{5,4},{6,5},{7,6},{9,8},{10,9},{11,10},{13,12},{... | collective-permute-start | bytes 6344 | tf_op jit(solution)/shard_map/ppermute | solution.py:15
  56.1 10.1 %collective-permute-start.1 = (f32[33,1,512]{2,0,1:T(8,128)S(1)}, f32[33,1,512]{2,0,1:T(8,128)}, u32[]{:S(2)}, u32[]{:S(2)}) collective-permute-start(f32[33,1,512]{2,0,1:T(8,128)S(1)} %pad_maximum_fusion.14), channel_id=1, source_target_pairs={{4,0},{8,4},{12,8},{16,12},{20,16},{24,20},{28,24},{32,28},{36,32}... | collective-permute-start | bytes 202760 | tf_op jit(solution)/shard_map/ppermute | solution.py:15
  62.6 3.4 %copy-start.8 = (s32[1,1,64]{2,1,0:T(1,128)S(1)}, s32[1,1,64]{2,1,0:T(1,128)}, u32[]{:S(2)}) copy-start(s32[1,1,64]{2,1,0:T(1,128)} %param.21) | copy-start | bytes 772
  62.6 4.5 %copy-start.13 = (f32[1,16,512]{2,1,0:T(8,128)S(1)}, f32[1,16,512]{2,1,0:T(8,128)}, u32[]{:S(2)}) copy-start(f32[1,16,512]{2,1,0:T(8,128)} %param.14) | copy-start | bytes 98308
  70.9 13.6 %collective-permute-start.8 = (f32[32,16,2]{2,0,1:T(8,128)S(1)}, f32[32,16,2]{2,0,1:T(8,128)S(1)}, u32[]{:S(2)}, u32[]{:S(2)}) collective-permute-start(f32[32,16,2]{2,0,1:T(8,128)S(1)} %get-tuple-element.44), channel_id=1, source_target_pairs={{0,1},{1,2},{2,3},{4,5},{5,6},{6,7},{8,9},{9,10},{10,11},{12,13},{... | collective-permute-start | bytes 12296 | tf_op jit(solution)/shard_map/ppermute | solution.py:14
  72.2 12.4 %collective-permute-start.7 = (f32[32,16,2]{2,0,1:T(8,128)S(1)}, f32[32,16,2]{2,0,1:T(8,128)S(1)}, u32[]{:S(2)}, u32[]{:S(2)}) collective-permute-start(f32[32,16,2]{2,0,1:T(8,128)S(1)} %get-tuple-element.45), channel_id=1, source_target_pairs={{1,0},{2,1},{3,2},{5,4},{6,5},{7,6},{9,8},{10,9},{11,10},{13,12},{... | collective-permute-start | bytes 12296 | tf_op jit(solution)/shard_map/ppermute | solution.py:15
  77.4 8.0 %collective-permute-start.6 = (f32[32,2,512]{2,0,1:T(8,128)S(1)}, f32[32,2,512]{2,0,1:T(8,128)S(1)}, u32[]{:S(2)}, u32[]{:S(2)}) collective-permute-start(f32[32,2,512]{2,0,1:T(8,128)S(1)} %get-tuple-element.42), channel_id=1, source_target_pairs={{0,4},{4,8},{8,12},{12,16},{16,20},{20,24},{24,28},{28,32},{32,36}... | collective-permute-start | bytes 393224 | tf_op jit(solution)/shard_map/ppermute | solution.py:14
  82.4 8.4 %collective-permute-start.5 = (f32[32,2,512]{2,0,1:T(8,128)S(1)}, f32[32,2,512]{2,0,1:T(8,128)S(1)}, u32[]{:S(2)}, u32[]{:S(2)}) collective-permute-start(f32[32,2,512]{2,0,1:T(8,128)S(1)} %get-tuple-element.43), channel_id=1, source_target_pairs={{4,0},{8,4},{12,8},{16,12},{20,16},{24,20},{28,24},{32,28},{36,32}... | collective-permute-start | bytes 393224 | tf_op jit(solution)/shard_map/ppermute | solution.py:15
  93.0 12.8 %copy-start.2 = (s32[1,16,512]{2,1,0:T(8,128)S(1)}, s32[1,16,512]{2,1,0:T(8,128)}, u32[]{:S(2)}) copy-start(s32[1,16,512]{2,1,0:T(8,128)} %param.15) | copy-start | bytes 98308
  93.2 18.7 %collective-permute-start.9 = (f32[32,1,512]{2,0,1:T(8,128)S(1)}, f32[32,1,512]{2,0,1:T(8,128)S(1)}, u32[]{:S(2)}, u32[]{:S(2)}) collective-permute-start(f32[32,1,512]{2,0,1:T(8,128)S(1)} %get-tuple-element.38), channel_id=1, source_target_pairs={{4,0},{8,4},{12,8},{16,12},{20,16},{24,20},{28,24},{32,28},{36,32}... | collective-permute-start | bytes 196616 | tf_op jit(solution)/shard_map/ppermute | solution.py:15
  95.1 16.7 %collective-permute-start.10 = (f32[32,1,512]{2,0,1:T(8,128)S(1)}, f32[32,1,512]{2,0,1:T(8,128)S(1)}, u32[]{:S(2)}, u32[]{:S(2)}) collective-permute-start(f32[32,1,512]{2,0,1:T(8,128)S(1)} %get-tuple-element.39), channel_id=1, source_target_pairs={{0,4},{4,8},{8,12},{12,16},{16,20},{20,24},{24,28},{28,32},{32,36}... | collective-permute-start | bytes 196616 | tf_op jit(solution)/shard_map/ppermute | solution.py:14
  100.9 6.9 %collective-permute-start.11 = (f32[32,16,1]{2,0,1:T(8,128)S(1)}, f32[32,16,1]{2,0,1:T(8,128)S(1)}, u32[]{:S(2)}, u32[]{:S(2)}) collective-permute-start(f32[32,16,1]{2,0,1:T(8,128)S(1)} %get-tuple-element.40), channel_id=1, source_target_pairs={{1,0},{2,1},{3,2},{5,4},{6,5},{7,6},{9,8},{10,9},{11,10},{13,12},{... | collective-permute-start | bytes 6152 | tf_op jit(solution)/shard_map/ppermute | solution.py:15
  104.5 7.3 %collective-permute-start.12 = (f32[32,16,1]{2,0,1:T(8,128)S(1)}, f32[32,16,1]{2,0,1:T(8,128)S(1)}, u32[]{:S(2)}, u32[]{:S(2)}) collective-permute-start(f32[32,16,1]{2,0,1:T(8,128)S(1)} %get-tuple-element.41), channel_id=1, source_target_pairs={{0,1},{1,2},{2,3},{4,5},{5,6},{6,7},{8,9},{9,10},{10,11},{12,13},{... | collective-permute-start | bytes 6152 | tf_op jit(solution)/shard_map/ppermute | solution.py:14

commit v11 on v2

--- a/solution.py
+++ b/solution.py
@@ -20,7 +20,7 @@
     return right_side + jnp.einsum("lm,mxy->lxy", matrix, right_side, precision=HIGHEST_PRECISION)
 
 
-def stencil(pressure, eastward, northward, sound_speed, wetness, matrix):
+def stencil(pressure, eastward, northward, sound_speed, wetness, matrix, tie):
     wet3 = wetness[None]
     lo_x, hi_x = neighbours(
         jnp.concatenate([eastward[:, :1], wet3[:, :1]], axis=0),
@@ -49,7 +49,7 @@
     v1_ext = wet_y * (v_ext - 0.5 * (p1_y[:, :, 2:] - p1_y[:, :, :-2]))
 
     divergence = (u1_ext[:, 2:] - u1_ext[:, :-2]) + (v1_ext[:, :, 2:] - v1_ext[:, :, :-2])
-    p2 = vertical_mix(matrix, p1 - sound_speed * divergence)
+    p2 = tie(vertical_mix(matrix, p1 - sound_speed * divergence))
 
     lo3x, hi3x = neighbours(p2[:, :1], p2[:, -1:], "gx")
     lo3y, hi3y = neighbours(p2[:, :, :1], p2[:, :, -1:], "gy")
@@ -81,9 +81,6 @@
     sound_speed = wave_speed[0]
     wetness = wet_mask[0].astype(jnp.float32)
     matrix = vertical[0]
-    assert SUBSTEPS == 2
-    p2, u2, v2 = stencil(pressure, eastward, northward, sound_speed, wetness, matrix)
-    final_state = jnp.stack([p2, u2, v2])[None]
 
     weights = intersection_weights[0, 0]
     pair_count, in_width, out_width = weights.shape
@@ -153,6 +150,16 @@
     delivered = lax.all_to_all(
         returning.reshape(tile_count, capacity, out_width), "gx", split_axis=0, concat_axis=0, tiled=True
     )
+    carried = {}
+
+    def tie(p2):
+        carried["delivered"], p2 = lax.optimization_barrier((delivered, p2))
+        return p2
+
+    assert SUBSTEPS == 2
+    p2, u2, v2 = stencil(pressure, eastward, northward, sound_speed, wetness, matrix, tie)
+    final_state = jnp.stack([p2, u2, v2])[None]
+    delivered = carried["delivered"]
     per_pair = jnp.dot(
         placing.T.astype(jnp.bfloat16),
         delivered.reshape(slot_count, out_width),

time: 114 us -> 126 us (1.11)
  matrix products: 15.1 us -> 19.7 us
  waiting for transfers between devices: 9.67 us -> 14 us
  starting transfers between devices: 58.5 us -> 54.6 us
  other arithmetic: 7.7 us -> 11.4 us
  local copies, waits for them, and re-layouts: 19.6 us -> 23.2 us
    all_to_all x1, waiting for transfers between devices: 0.01 us -> 5.86 us  [local(): lax.all_to_all(packet, 'gx', split_axis=0, concat_axis=0, tiled=True)]
    all_to_all x1, starting transfers between devices: 8.15 us -> 4.09 us  [local(): lax.all_to_all(returning.reshape(tile_count, capacity, out_width), 'gx',...]
    dot_general x2, matrix products: 6.42 us -> 10.2 us  [vertical_mix(): jnp.einsum('lm,mxy->lxy', matrix, right_side, precision=HIGHEST_PRECISION)]
    all_to_all x1, waiting for transfers between devices: 4.32 us -> 2.42 us  [local(): lax.all_to_all(returning.reshape(tile_count, capacity, out_width), 'gx',...]
    reshape x1, local copies, waits for them, and re-layouts: 0.03 us -> 1.39 us  [local(): atmos_temp.reshape(grid_shape)]
    unnamed x54 -> x62, local copies, waits for them, and re-layouts: 8.46 us -> 7.77 us
  transfers between devices with their start and end apart: 15 -> 15, of which waited for: 4 -> 5; matrix products, arithmetic and copies ran while one was open for 29% -> 29% of each run, Pallas kernels for 0% -> 0%
where the time goes in v11:
time: 126 us; the launch traced here: 124 us
  starting transfers between devices  54.6 us (43%)
  local copies, waits for them, and re-layouts  23.2 us (18%)
  matrix products  19.7 us (16%)
  waiting for transfers between devices  14 us (11%)
  other arithmetic  11.4 us (9%)
  between operations  1.31 us (1%)
    ppermute x6, starting transfers between devices, neighbours(): lo = lax.ppermute(tail, axis, [(i, i + 1) for i in range(count - 1)])  23.6 us
    all_to_all x1, starting transfers between devices, local(): lax.all_to_all(packet, 'gx', split_axis=0, concat_axis=0, tiled=True)  13.1 us
    dot_general x2, matrix products, vertical_mix(): jnp.einsum('lm,mxy->lxy', matrix, right_side, precision=HIGHEST_PRECISION)  10.2 us
    ppermute x6, starting transfers between devices, neighbours(): hi = lax.ppermute(head, axis, [(i + 1, i) for i in range(count - 1)])  10 us
    unnamed x62, local copies, waits for them, and re-layouts  7.77 us
    all_to_all x1, waiting for transfers between devices, local(): lax.all_to_all(packet, 'gx', split_axis=0, concat_axis=0, tiled=True)  5.86 us
    all_to_all x1, starting transfers between devices, local(): lax.all_to_all(returning.reshape(tile_count, capacity, out_width), 'gx',...  4.09 us
    ppermute x6, waiting for transfers between devices, neighbours(): hi = lax.ppermute(head, axis, [(i + 1, i) for i in range(count - 1)])  3.8 us
  transfers between devices with their start and end apart: 15, of which 5 were waited for; matrix products, arithmetic and copies ran while one was open for 29% of the time, Pallas kernels for 0%

profile of v11, /device:TPU:1, one launch (start us, length us, event | category | flops | bytes accessed | tf_op | source)
XLA Modules:
  0.0 124.1 jit_solution(3757874816638566668)
XLA Ops:
  4.1 3.7 %collective-permute-start = (f32[4,8192]{1,0:T(4,128)}, f32[4,8192]{1,0:T(4,128)}, u32[]{:S(2)}, u32[]{:S(2)}) collective-permute-start(f32[4,8192]{1,0:T(4,128)} %maximum_select_fusion), channel_id=1, source_target_pairs={{0,128},{128,0},{1,129},{129,1},{2,130},{130,2},{3,131},{131,3},{4... | collective-permute-start | bytes 393224 | tf_op jit(solution)/shard_map/ppermute | solution.py:105
  8.0 3.2 %fusion.74 = (f32[1,1,32,16,512]{4,3,2,1,0:T(8,128)}, f32[1,1,32,16,512]{4,3,2,1,0:T(8,128)S(1)}, f32[1,1,32,16,512]{4,3,2,1,0:T(8,128)S(1)}) fusion(f32[1,3,32,16,512]{4,3,2,1,0:T(8,128)} %param.13), kind=kLoop, calls=%fused_computation.127 | loop fusion | bytes 6291456 | tf_op jit(solution)/shard_map/slice | solution.py:78
  12.0 3.8 %collective-permute-start.4 = (f32[33,16,1]{2,0,1:T(8,128)S(1)}, f32[33,16,1]{2,0,1:T(8,128)}, u32[]{:S(2)}, u32[]{:S(2)}) collective-permute-start(f32[33,16,1]{2,0,1:T(8,128)S(1)} %pad_maximum_fusion.11), channel_id=1, source_target_pairs={{0,1},{1,2},{2,3},{4,5},{5,6},{6,7},{8,9},{9,10},{10,11},{12,13},{... | collective-permute-start | bytes 6344 | tf_op jit(solution)/shard_map/ppermute | solution.py:14
  15.8 1.3 %collective-permute-start.3 = (f32[33,16,1]{2,0,1:T(8,128)S(1)}, f32[33,16,1]{2,0,1:T(8,128)S(1)}, u32[]{:S(2)}, u32[]{:S(2)}) collective-permute-start(f32[33,16,1]{2,0,1:T(8,128)S(1)} %pad_maximum_fusion.10), channel_id=1, source_target_pairs={{1,0},{2,1},{3,2},{5,4},{6,5},{7,6},{9,8},{10,9},{11,10},{13,12},{... | collective-permute-start | bytes 6344 | tf_op jit(solution)/shard_map/ppermute | solution.py:15
  17.9 3.4 %collective-permute-start.2 = (f32[33,1,512]{2,0,1:T(8,128)S(1)}, f32[33,1,512]{2,0,1:T(8,128)}, u32[]{:S(2)}, u32[]{:S(2)}) collective-permute-start(f32[33,1,512]{2,0,1:T(8,128)S(1)} %pad_maximum_fusion.15), channel_id=1, source_target_pairs={{0,4},{4,8},{8,12},{12,16},{16,20},{20,24},{24,28},{28,32},{32,36}... | collective-permute-start | bytes 202760 | tf_op jit(solution)/shard_map/ppermute | solution.py:14
  21.3 1.9 %collective-permute-start.1 = (f32[33,1,512]{2,0,1:T(8,128)S(1)}, f32[33,1,512]{2,0,1:T(8,128)}, u32[]{:S(2)}, u32[]{:S(2)}) collective-permute-start(f32[33,1,512]{2,0,1:T(8,128)S(1)} %pad_maximum_fusion.14), channel_id=1, source_target_pairs={{4,0},{8,4},{12,8},{16,12},{20,16},{24,20},{28,24},{32,28},{36,32}... | collective-permute-start | bytes 202760 | tf_op jit(solution)/shard_map/ppermute | solution.py:15
  27.7 1.0 slice.248
  30.4 4.4 %fusion.6 = f32[32,16,512]{2,0,1:T(8,128)S(1)} fusion(f32[32,16,512]{2,0,1:T(8,128)S(1)} %bitcast.111, f32[32,16,1]{2,0,1:T(8,128)S(1)} %slice.248, f32[32,16,1]{2,0,1:T(8,128)S(1)} %slice.245, f32[32,16,512]{2,0,1:T(8,128)S(1)} %bitcast.114, f32[32,1,512]{2,0,1:T(8,128)S(1)} %slice.242, f32[32,1,512]{2,0,1:T(8,128)S(1)} %slice.239, ...), kind=kOutput, calls=%fused_computation.11 | convolution fusion | flops 105644032 | bytes 4366336 | tf_op jit(solution)/shard_map/lm,mxy->lxy/dot_general | solution.py:20
  35.7 4.3 %collective-permute-start.8 = (f32[32,16,2]{2,0,1:T(8,128)S(1)}, f32[32,16,2]{2,0,1:T(8,128)S(1)}, u32[]{:S(2)}, u32[]{:S(2)}) collective-permute-start(f32[32,16,2]{2,0,1:T(8,128)S(1)} %get-tuple-element.40), channel_id=1, source_target_pairs={{0,1},{1,2},{2,3},{4,5},{5,6},{6,7},{8,9},{9,10},{10,11},{12,13},{... | collective-permute-start | bytes 12296 | tf_op jit(solution)/shard_map/ppermute | solution.py:14
  40.0 1.3 %collective-permute-start.7 = (f32[32,16,2]{2,0,1:T(8,128)S(1)}, f32[32,16,2]{2,0,1:T(8,128)S(1)}, u32[]{:S(2)}, u32[]{:S(2)}) collective-permute-start(f32[32,16,2]{2,0,1:T(8,128)S(1)} %get-tuple-element.41), channel_id=1, source_target_pairs={{1,0},{2,1},{3,2},{5,4},{6,5},{7,6},{9,8},{10,9},{11,10},{13,12},{... | collective-permute-start | bytes 12296 | tf_op jit(solution)/shard_map/ppermute | solution.py:15
  42.8 3.9 %collective-permute-start.6 = (f32[32,2,512]{2,0,1:T(8,128)}, f32[32,2,512]{2,0,1:T(8,128)S(1)}, u32[]{:S(2)}, u32[]{:S(2)}) collective-permute-start(f32[32,2,512]{2,0,1:T(8,128)} %get-tuple-element.38), channel_id=1, source_target_pairs={{0,4},{4,8},{8,12},{12,16},{16,20},{20,24},{24,28},{28,32},{32,36}... | collective-permute-start | bytes 393224 | tf_op jit(solution)/shard_map/ppermute | solution.py:14
  46.7 1.9 %collective-permute-start.5 = (f32[32,2,512]{2,0,1:T(8,128)}, f32[32,2,512]{2,0,1:T(8,128)}, u32[]{:S(2)}, u32[]{:S(2)}) collective-permute-start(f32[32,2,512]{2,0,1:T(8,128)} %get-tuple-element.39), channel_id=1, source_target_pairs={{4,0},{8,4},{12,8},{16,12},{20,16},{24,20},{28,24},{32,28},{36,32}... | collective-permute-start | bytes 393224 | tf_op jit(solution)/shard_map/ppermute | solution.py:15
  48.6 1.2 collective-permute-done.7
  49.9 1.9 %fusion.7 = f32[32,16,514]{2,0,1:T(8,128)} fusion(f32[32,16,1]{2,0,1:T(8,128)S(1)} %slice.245, f32[32,16,512]{2,0,1:T(8,128)S(1)} %bitcast.112, f32[32,16,1]{2,0,1:T(8,128)S(1)} %slice.248, f32[32,16,2]{2,0,1:T(8,128)S(1)} %collective-permute-done.7, f32[32,16,512]{2,0,1:T(8,128)S(1)} %fusion.6, f32[32,16,2]{2,0,1:T(8,128)S(1)} %collective-permute-done.8, ...), kind=kLoop, calls=%fused_computation.13 | loop fusion | flops 2105344 | bytes 3195008 | tf_op jit(solution)/shard_map/mul | solution.py:49
  53.1 2.9 %fusion.11 = bf16[64,8,128]{2,1,0:T(8,128)(2,1)S(1)} fusion(bf16[1,1,64,256,128]{4,3,2,1,0:T(8,128)(2,1)} %param.23, bf16[64,8,256]{2,1,0:T(8,128)(2,1)S(1)} %gather_fusion, pred[64]{0:T(512)(128)(4,1)S(1)} %copy-done.20), kind=kOutput, calls=%fused_computation.20 | convolution fusion | flops 33751040 | bytes 4587584 | tf_op jit(solution)/shard_map/fpi,pio->pfo/dot_general | solution.py:114
  57.3 13.1 %all-to-all-start = ((f32[32,5,128]{2,1,0:T(8,128)}), f32[32,5,128]{2,1,0:T(8,128)S(1)}, u32[]{:S(2)}, u32[]{:S(2)}) async-start(f32[32,5,128]{2,1,0:T(8,128)} %pad_maximum_fusion.13), calls=%async_computation | async-start | bytes 262144 | tf_op jit(solution)/shard_map/all_to_all | solution.py:135
  70.4 1.0 fusion.81
  71.5 2.3 %fusion.9 = f32[32,18,512]{2,0,1:T(8,128)} fusion(f32[32,1,512]{2,0,1:T(8,128)S(1)} %slice.239, f32[32,16,512]{2,0,1:T(8,128)S(1)} %bitcast.115, f32[32,1,512]{2,0,1:T(8,128)S(1)} %slice.242, f32[32,2,512]{2,0,1:T(8,128)} %collective-permute-done.5, f32[32,16,512]{2,0,1:T(8,128)S(1)} %fusion.6, f32[32,2,512]{2,0,1:T(8,128)S(1)} %collective-permute-done.6, ...), kind=kLoop, calls=%fused_computation.17 | loop fusion | flops 2359296 | bytes 3706880 | tf_op jit(solution)/shard_map/mul | solution.py:48
  73.8 5.9 %all-to-all-done = f32[32,5,128]{2,1,0:T(8,128)S(1)} async-done(((f32[32,5,128]{2,1,0:T(8,128)}), f32[32,5,128]{2,1,0:T(8,128)S(1)}, u32[]{:S(2)}, u32[]{:S(2)}) %all-to-all-start) | async-done | bytes 81952 | tf_op jit(solution)/shard_map/all_to_all | solution.py:135
  80.9 4.1 %all-to-all-start.1 = ((bf16[32,4,128]{2,1,0:T(4,128)(2,1)}), bf16[32,4,128]{2,1,0:T(4,128)(2,1)S(1)}, u32[]{:S(2)}, u32[]{:S(2)}) async-start(bf16[32,4,128]{2,1,0:T(4,128)(2,1)} %bitcast.19), calls=%async_computation.1 | async-start | bytes 65536 | tf_op jit(solution)/shard_map/all_to_all | solution.py:150
  85.0 5.8 %fusion.5 = f32[32,16,512]{2,0,1:T(8,128)S(1)} fusion(f32[32,16,512]{2,0,1:T(8,128)S(1)} %fusion.6, f32[32,16,514]{2,0,1:T(8,128)} %fusion.7, f32[32,18,512]{2,0,1:T(8,128)} %fusion.9, f32[16,512]{1,0:T(8,128)S(1)} %bitcast.143, f32[1,32,32]{2,1,0:T(8,128)S(1)} %copy-done), kind=kOutput, calls=%fused_computation.9 | convolution fusion | flops 103546880 | bytes 11616256 | tf_op jit(solution)/shard_map/lm,mxy->lxy/dot_general | solution.py:20
  90.8 2.4 %all-to-all-done.1 = bf16[32,4,128]{2,1,0:T(4,128)(2,1)S(1)} async-done(((bf16[32,4,128]{2,1,0:T(4,128)(2,1)}), bf16[32,4,128]{2,1,0:T(4,128)(2,1)S(1)}, u32[]{:S(2)}, u32[]{:S(2)}) %all-to-all-start.1) | async-done | bytes 32800 | tf_op jit(solution)/shard_map/all_to_all | solution.py:150
  95.0 3.5 %fusion.1 = f32[64,1,256]{2,1,0:T(1,128)S(1)} fusion(bf16[1,1,64,256,128]{4,3,2,1,0:T(8,128)(2,1)} %param.23, bf16[64,128,1]{1,0,2:T(8,128)(2,1)S(1)} %fusion.14), kind=kOutput, calls=%fused_computation.3 | convolution fusion | flops 4194304 | bytes 4276224 | tf_op jit(solution)/shard_map/pio,po->pi/dot_general | solution.py:168
  99.3 1.4 %reshape.169 = f32[1,16,512]{2,0,1:T(1,128)} reshape(f32[32,256]{1,0:T(8,128)} %fusion.49) | data formatting | bytes 65536 | tf_op jit(solution)/shard_map/reshape | solution.py:172
  100.7 2.3 %collective-permute-start.9 = (f32[32,1,512]{2,0,1:T(8,128)}, f32[32,1,512]{2,0,1:T(8,128)S(1)}, u32[]{:S(2)}, u32[]{:S(2)}) collective-permute-start(f32[32,1,512]{2,0,1:T(8,128)} %get-tuple-element.34), channel_id=1, source_target_pairs={{4,0},{8,4},{12,8},{16,12},{20,16},{24,20},{28,24},{32,28},{36,32}... | collective-permute-start | bytes 196616 | tf_op jit(solution)/shard_map/ppermute | solution.py:15
  103.0 3.3 %collective-permute-start.10 = (f32[32,1,512]{2,0,1:T(8,128)}, f32[32,1,512]{2,0,1:T(8,128)S(1)}, u32[]{:S(2)}, u32[]{:S(2)}) collective-permute-start(f32[32,1,512]{2,0,1:T(8,128)} %get-tuple-element.35), channel_id=1, source_target_pairs={{0,4},{4,8},{8,12},{12,16},{16,20},{20,24},{24,28},{28,32},{32,36}... | collective-permute-start | bytes 196616 | tf_op jit(solution)/shard_map/ppermute | solution.py:14
  106.3 1.3 %collective-permute-start.11 = (f32[32,16,1]{2,0,1:T(8,128)}, f32[32,16,1]{2,0,1:T(8,128)S(1)}, u32[]{:S(2)}, u32[]{:S(2)}) collective-permute-start(f32[32,16,1]{2,0,1:T(8,128)} %get-tuple-element.36), channel_id=1, source_target_pairs={{1,0},{2,1},{3,2},{5,4},{6,5},{7,6},{9,8},{10,9},{11,10},{13,12},{... | collective-permute-start | bytes 6152 | tf_op jit(solution)/shard_map/ppermute | solution.py:15
  107.6 4.9 %collective-permute-start.12 = (f32[32,16,1]{2,0,1:T(8,128)}, f32[32,16,1]{2,0,1:T(8,128)S(1)}, u32[]{:S(2)}, u32[]{:S(2)}) collective-permute-start(f32[32,16,1]{2,0,1:T(8,128)} %get-tuple-element.37), channel_id=1, source_target_pairs={{0,1},{1,2},{2,3},{4,5},{5,6},{6,7},{8,9},{9,10},{10,11},{12,13},{... | collective-permute-start | bytes 6152 | tf_op jit(solution)/shard_map/ppermute | solution.py:14
  114.1 2.6 %collective-permute-done.11 = f32[32,16,1]{2,0,1:T(8,128)S(1)} collective-permute-done((f32[32,16,1]{2,0,1:T(8,128)}, f32[32,16,1]{2,0,1:T(8,128)S(1)}, u32[]{:S(2)}, u32[]{:S(2)}) %collective-permute-start.11) | collective-permute-done | bytes 2080 | tf_op jit(solution)/shard_map/ppermute | solution.py:15
  116.6 1.9 %collective-permute-done.12 = f32[32,16,1]{2,0,1:T(8,128)S(1)} collective-permute-done((f32[32,16,1]{2,0,1:T(8,128)}, f32[32,16,1]{2,0,1:T(8,128)S(1)}, u32[]{:S(2)}, u32[]{:S(2)}) %collective-permute-start.12) | collective-permute-done | bytes 2080 | tf_op jit(solution)/shard_map/ppermute | solution.py:14
  118.5 1.8 %fusion.24 = (f32[1,32,16,512]{3,1,2,0:T(8,128)S(1)}, f32[1,32,16,512]{3,1,2,0:T(8,128)S(1)}) fusion(f32[32,16,512]{2,0,1:T(8,128)S(1)} %fusion.5, f32[32,1,512]{2,0,1:T(8,128)S(1)} %collective-permute-done.10, f32[32,1,512]{2,0,1:T(8,128)S(1)} %collective-permute-done.9, f32[32,18,512]{2,0,1:T(8,128)S(1)} %copy-done.2, f32[16,512]{1,0:T(8,128)} %bitcast.129, ...), kind=kLoop, calls=%fused_computation.36 | loop fusion | flops 3145728 | bytes 5410816 | tf_op jit(solution)/shard_map/stack | solution.py:161
  120.7 3.5 %copy.53 = f32[1,3,32,16,512]{4,3,2,1,0:T(8,128)} copy(f32[1,3,32,16,512]{4,2,3,1,0:T(8,128)S(1)} %maximum_bitcast_fusion) | data formatting | bytes 6291456
  (121 shorter events, 21.6 us)
Async XLA Ops:
  0.6 29.8 %copy-start = (f32[1,32,32]{2,1,0:T(8,128)S(1)}, f32[1,32,32]{2,1,0:T(8,128)}, u32[]{:S(2)}) copy-start(f32[1,32,32]{2,1,0:T(8,128)} %param.16) | copy-start | bytes 12292
  3.1 8.1 %copy-start.7 = (f32[1,1,16,512]{3,1,2,0:T(1,128)}, f32[1,1,16,512]{3,1,2,0:T(1,128)S(1)}, u32[]{:S(2)}) copy-start(f32[1,1,16,512]{3,1,2,0:T(1,128)S(1)} %copy.64) | copy-start | bytes 98308
  3.1 8.0 %copy-start.9 = (f32[1,1,16,512]{3,1,2,0:T(1,128)}, f32[1,1,16,512]{3,1,2,0:T(1,128)S(1)}, u32[]{:S(2)}) copy-start(f32[1,1,16,512]{3,1,2,0:T(1,128)S(1)} %copy.65) | copy-start | bytes 98308
  3.2 8.0 %copy-start.11 = (f32[1,1,16,512]{3,1,2,0:T(1,128)}, f32[1,1,16,512]{3,1,2,0:T(1,128)S(1)}, u32[]{:S(2)}) copy-start(f32[1,1,16,512]{3,1,2,0:T(1,128)S(1)} %copy.66) | copy-start | bytes 98308
  4.1 47.6 %collective-permute-start = (f32[4,8192]{1,0:T(4,128)}, f32[4,8192]{1,0:T(4,128)}, u32[]{:S(2)}, u32[]{:S(2)}) collective-permute-start(f32[4,8192]{1,0:T(4,128)} %maximum_select_fusion), channel_id=1, source_target_pairs={{0,128},{128,0},{1,129},{129,1},{2,130},{130,2},{3,131},{131,3},{4... | collective-permute-start | bytes 393224 | tf_op jit(solution)/shard_map/ppermute | solution.py:105
  12.0 14.7 %collective-permute-start.4 = (f32[33,16,1]{2,0,1:T(8,128)S(1)}, f32[33,16,1]{2,0,1:T(8,128)}, u32[]{:S(2)}, u32[]{:S(2)}) collective-permute-start(f32[33,16,1]{2,0,1:T(8,128)S(1)} %pad_maximum_fusion.11), channel_id=1, source_target_pairs={{0,1},{1,2},{2,3},{4,5},{5,6},{6,7},{8,9},{9,10},{10,11},{12,13},{... | collective-permute-start | bytes 6344 | tf_op jit(solution)/shard_map/ppermute | solution.py:14
  15.8 11.7 %collective-permute-start.3 = (f32[33,16,1]{2,0,1:T(8,128)S(1)}, f32[33,16,1]{2,0,1:T(8,128)S(1)}, u32[]{:S(2)}, u32[]{:S(2)}) collective-permute-start(f32[33,16,1]{2,0,1:T(8,128)S(1)} %pad_maximum_fusion.10), channel_id=1, source_target_pairs={{1,0},{2,1},{3,2},{5,4},{6,5},{7,6},{9,8},{10,9},{11,10},{13,12},{... | collective-permute-start | bytes 6344 | tf_op jit(solution)/shard_map/ppermute | solution.py:15
  17.2 6.1 %copy-start.16 = (s32[1,1,64]{2,1,0:T(1,128)S(1)}, s32[1,1,64]{2,1,0:T(1,128)}, u32[]{:S(2)}) copy-start(s32[1,1,64]{2,1,0:T(1,128)} %param.21) | copy-start | bytes 772
  17.2 6.7 %copy-start.23 = (s32[1,1,64]{2,1,0:T(1,128)S(1)}, s32[1,1,64]{2,1,0:T(1,128)}, u32[]{:S(2)}) copy-start(s32[1,1,64]{2,1,0:T(1,128)} %param.22) | copy-start | bytes 772
  17.2 6.7 %copy-start.24 = (s32[1,1,64,1]{2,3,1,0:T(1,128)S(1)}, s32[1,1,64,1]{2,3,1,0:T(1,128)}, u32[]{:S(2)}) copy-start(s32[1,1,64,1]{2,3,1,0:T(1,128)} %param.20) | copy-start | bytes 772
  17.2 8.2 %copy-start.3 = (f32[1,16,512]{2,1,0:T(8,128)S(1)}, f32[1,16,512]{2,1,0:T(8,128)}, u32[]{:S(2)}) copy-start(f32[1,16,512]{2,1,0:T(8,128)} %param.17) | copy-start | bytes 98308
  17.9 10.9 %collective-permute-start.2 = (f32[33,1,512]{2,0,1:T(8,128)S(1)}, f32[33,1,512]{2,0,1:T(8,128)}, u32[]{:S(2)}, u32[]{:S(2)}) collective-permute-start(f32[33,1,512]{2,0,1:T(8,128)S(1)} %pad_maximum_fusion.15), channel_id=1, source_target_pairs={{0,4},{4,8},{8,12},{12,16},{16,20},{20,24},{24,28},{28,32},{32,36}... | collective-permute-start | bytes 202760 | tf_op jit(solution)/shard_map/ppermute | solution.py:14
  21.3 8.3 %collective-permute-start.1 = (f32[33,1,512]{2,0,1:T(8,128)S(1)}, f32[33,1,512]{2,0,1:T(8,128)}, u32[]{:S(2)}, u32[]{:S(2)}) collective-permute-start(f32[33,1,512]{2,0,1:T(8,128)S(1)} %pad_maximum_fusion.14), channel_id=1, source_target_pairs={{4,0},{8,4},{12,8},{16,12},{20,16},{24,20},{28,24},{32,28},{36,32}... | collective-permute-start | bytes 202760 | tf_op jit(solution)/shard_map/ppermute | solution.py:15
  35.7 12.9 %collective-permute-start.8 = (f32[32,16,2]{2,0,1:T(8,128)S(1)}, f32[32,16,2]{2,0,1:T(8,128)S(1)}, u32[]{:S(2)}, u32[]{:S(2)}) collective-permute-start(f32[32,16,2]{2,0,1:T(8,128)S(1)} %get-tuple-element.40), channel_id=1, source_target_pairs={{0,1},{1,2},{2,3},{4,5},{5,6},{6,7},{8,9},{9,10},{10,11},{12,13},{... | collective-permute-start | bytes 12296 | tf_op jit(solution)/shard_map/ppermute | solution.py:14
  40.0 9.9 %collective-permute-start.7 = (f32[32,16,2]{2,0,1:T(8,128)S(1)}, f32[32,16,2]{2,0,1:T(8,128)S(1)}, u32[]{:S(2)}, u32[]{:S(2)}) collective-permute-start(f32[32,16,2]{2,0,1:T(8,128)S(1)} %get-tuple-element.41), channel_id=1, source_target_pairs={{1,0},{2,1},{3,2},{5,4},{6,5},{7,6},{9,8},{10,9},{11,10},{13,12},{... | collective-permute-start | bytes 12296 | tf_op jit(solution)/shard_map/ppermute | solution.py:15
  42.8 28.7 %collective-permute-start.6 = (f32[32,2,512]{2,0,1:T(8,128)}, f32[32,2,512]{2,0,1:T(8,128)S(1)}, u32[]{:S(2)}, u32[]{:S(2)}) collective-permute-start(f32[32,2,512]{2,0,1:T(8,128)} %get-tuple-element.38), channel_id=1, source_target_pairs={{0,4},{4,8},{8,12},{12,16},{16,20},{20,24},{24,28},{28,32},{32,36}... | collective-permute-start | bytes 393224 | tf_op jit(solution)/shard_map/ppermute | solution.py:14
  46.7 24.8 %collective-permute-start.5 = (f32[32,2,512]{2,0,1:T(8,128)}, f32[32,2,512]{2,0,1:T(8,128)}, u32[]{:S(2)}, u32[]{:S(2)}) collective-permute-start(f32[32,2,512]{2,0,1:T(8,128)} %get-tuple-element.39), channel_id=1, source_target_pairs={{4,0},{8,4},{12,8},{16,12},{20,16},{24,20},{28,24},{32,28},{36,32}... | collective-permute-start | bytes 393224 | tf_op jit(solution)/shard_map/ppermute | solution.py:15
  53.1 3.2 %copy-start.19 = (s32[64]{0:T(128)S(1)}, s32[64]{0:T(128)}, u32[]{:S(2)}) copy-start(s32[64]{0:T(128)} %copy-done.18) | copy-start | bytes 772
  53.1 3.5 %copy-start.14 = (f32[32,1,128]{2,0,1:T(8,128)S(1)}, f32[32,1,128]{2,0,1:T(8,128)}, u32[]{:S(2)}) copy-start(f32[32,1,128]{2,0,1:T(8,128)} %scatter.4) | copy-start | bytes 49156
  57.3 22.4 %all-to-all-start = ((f32[32,5,128]{2,1,0:T(8,128)}), f32[32,5,128]{2,1,0:T(8,128)S(1)}, u32[]{:S(2)}, u32[]{:S(2)}) async-start(f32[32,5,128]{2,1,0:T(8,128)} %pad_maximum_fusion.13), calls=%async_computation | async-start | bytes 262144 | tf_op jit(solution)/shard_map/all_to_all | solution.py:135
  71.5 8.6 %copy-start.5 = (f32[1,8192]{1,0:T(1,128)}, f32[1,8192]{1,0:T(1,128)S(1)}, u32[]{:S(2)}) copy-start(f32[1,8192]{1,0:T(1,128)S(1)} %get-tuple-element.46) | copy-start | bytes 98308
  71.5 8.6 %copy-start.6 = (f32[1,8192]{1,0:T(1,128)}, f32[1,8192]{1,0:T(1,128)S(1)}, u32[]{:S(2)}) copy-start(f32[1,8192]{1,0:T(1,128)S(1)} %get-tuple-element.47) | copy-start | bytes 98308
  71.5 8.6 %copy-start.13 = (f32[64,128]{1,0:T(8,128)S(1)}, f32[64,128]{1,0:T(8,128)}, u32[]{:S(2)}) copy-start(f32[64,128]{1,0:T(8,128)} %reshape_squeeze.4) | copy-start | bytes 98308
  71.5 13.5 %copy-start.21 = (f32[1,16,512]{2,1,0:T(8,128)S(1)}, f32[1,16,512]{2,1,0:T(8,128)}, u32[]{:S(2)}) copy-start(f32[1,16,512]{2,1,0:T(8,128)} %param.14) | copy-start | bytes 98308
  80.9 12.3 %all-to-all-start.1 = ((bf16[32,4,128]{2,1,0:T(4,128)(2,1)}), bf16[32,4,128]{2,1,0:T(4,128)(2,1)S(1)}, u32[]{:S(2)}, u32[]{:S(2)}) async-start(bf16[32,4,128]{2,1,0:T(4,128)(2,1)} %bitcast.19), calls=%async_computation.1 | async-start | bytes 65536 | tf_op jit(solution)/shard_map/all_to_all | solution.py:150
  95.0 3.5 %copy-start.17 = (s32[1,1,64]{2,1,0:T(1,128)S(1)}, s32[1,1,64]{2,1,0:T(1,128)}, u32[]{:S(2)}) copy-start(s32[1,1,64]{2,1,0:T(1,128)} %param.21) | copy-start | bytes 772
  95.0 23.5 %copy-start.1 = (f32[32,16,514]{2,0,1:T(8,128)S(1)}, f32[32,16,514]{2,0,1:T(8,128)}, u32[]{:S(2)}) copy-start(f32[32,16,514]{2,0,1:T(8,128)} %fusion.7) | copy-start | bytes 3158020
  95.0 23.5 %copy-start.2 = (f32[32,18,512]{2,0,1:T(8,128)S(1)}, f32[32,18,512]{2,0,1:T(8,128)}, u32[]{:S(2)}) copy-start(f32[32,18,512]{2,0,1:T(8,128)} %fusion.9) | copy-start | bytes 3538948
  100.7 17.8 %collective-permute-start.9 = (f32[32,1,512]{2,0,1:T(8,128)}, f32[32,1,512]{2,0,1:T(8,128)S(1)}, u32[]{:S(2)}, u32[]{:S(2)}) collective-permute-start(f32[32,1,512]{2,0,1:T(8,128)} %get-tuple-element.34), channel_id=1, source_target_pairs={{4,0},{8,4},{12,8},{16,12},{20,16},{24,20},{28,24},{32,28},{36,32}... | collective-permute-start | bytes 196616 | tf_op jit(solution)/shard_map/ppermute | solution.py:15
  103.0 15.5 %collective-permute-start.10 = (f32[32,1,512]{2,0,1:T(8,128)}, f32[32,1,512]{2,0,1:T(8,128)S(1)}, u32[]{:S(2)}, u32[]{:S(2)}) collective-permute-start(f32[32,1,512]{2,0,1:T(8,128)} %get-tuple-element.35), channel_id=1, source_target_pairs={{0,4},{4,8},{8,12},{12,16},{16,20},{20,24},{24,28},{28,32},{32,36}... | collective-permute-start | bytes 196616 | tf_op jit(solution)/shard_map/ppermute | solution.py:14
  106.3 10.4 %collective-permute-start.11 = (f32[32,16,1]{2,0,1:T(8,128)}, f32[32,16,1]{2,0,1:T(8,128)S(1)}, u32[]{:S(2)}, u32[]{:S(2)}) collective-permute-start(f32[32,16,1]{2,0,1:T(8,128)} %get-tuple-element.36), channel_id=1, source_target_pairs={{1,0},{2,1},{3,2},{5,4},{6,5},{7,6},{9,8},{10,9},{11,10},{13,12},{... | collective-permute-start | bytes 6152 | tf_op jit(solution)/shard_map/ppermute | solution.py:15
  107.6 10.9 %collective-permute-start.12 = (f32[32,16,1]{2,0,1:T(8,128)}, f32[32,16,1]{2,0,1:T(8,128)S(1)}, u32[]{:S(2)}, u32[]{:S(2)}) collective-permute-start(f32[32,16,1]{2,0,1:T(8,128)} %get-tuple-element.37), channel_id=1, source_target_pairs={{0,1},{1,2},{2,3},{4,5},{5,6},{6,7},{8,9},{9,10},{10,11},{12,13},{... | collective-permute-start | bytes 6152 | tf_op jit(solution)/shard_map/ppermute | solution.py:14
  (8 other events, 16.1 us)

commit v12 on v2

--- a/solution.py
+++ b/solution.py
@@ -11,9 +11,10 @@
 
 def neighbours(head, tail, axis):
     count = lax.axis_size(axis)
-    lo = lax.ppermute(tail, axis, [(i, i + 1) for i in range(count - 1)])
-    hi = lax.ppermute(head, axis, [(i + 1, i) for i in range(count - 1)])
-    return lo, hi
+    me = lax.axis_index(axis)
+    lo = lax.ppermute(tail, axis, [(i, (i + 1) % count) for i in range(count)])
+    hi = lax.ppermute(head, axis, [((i + 1) % count, i) for i in range(count)])
+    return jnp.where(me > 0, lo, 0.0), jnp.where(me < count - 1, hi, 0.0)
 
 
 def vertical_mix(matrix, right_side):

time: 114 us -> 103 us (0.904)
  starting transfers between devices: 58.5 us -> 41.8 us
  waiting for transfers between devices: 9.67 us -> 16.6 us
  other arithmetic: 7.7 us -> 12.9 us
  local copies, waits for them, and re-layouts: 19.6 us -> 15.9 us
  matrix products: 15.1 us -> 13.4 us
    ppermute x12, starting transfers between devices: 32.7 us -> 15.9 us  [the longest x6 8.71 us: neighbours(): lo = lax.ppermute(tail, axis, [(i, (i + 1) % count) for i in range(count)])]
    ppermute x12, waiting for transfers between devices: 5.34 us -> 12.3 us  [the longest x6 7.31 us: neighbours(): hi = lax.ppermute(head, axis, [((i + 1) % count, i) for i in range(count)])]
    select_n x0 -> x12, other arithmetic: none -> 3.8 us  [neighbours(): return (jnp.where(me > 0, lo, 0.0), jnp.where(me < count - 1, hi, 0.0))]
    dot_general x2, matrix products: 6.42 us -> 4.73 us  [vertical_mix(): jnp.einsum('lm,mxy->lxy', matrix, right_side, precision=HIGHEST_PRECISION)]
    slice x2, local copies, waits for them, and re-layouts: 1.44 us -> 0.01 us  [stencil(): wet_x = jnp.concatenate([lo_x[levels:], wet3, hi_x[levels:]], axis=1)]
    unnamed x54 -> x64, local copies, waits for them, and re-layouts: 8.46 us -> 9.38 us
  transfers between devices with their start and end apart: 15 -> 15, of which waited for: 4 -> 7; matrix products, arithmetic and copies ran while one was open for 29% -> 31% of each run, Pallas kernels for 0% -> 0%
where the time goes in v12:
time: 103 us; the launch traced here: 102 us
  starting transfers between devices  41.8 us (41%)
  waiting for transfers between devices  16.6 us (16%)
  local copies, waits for them, and re-layouts  15.9 us (15%)
  matrix products  13.4 us (13%)
  other arithmetic  12.9 us (13%)
  between operations  1.39 us (1%)
    all_to_all x1, starting transfers between devices, local(): lax.all_to_all(packet, 'gx', split_axis=0, concat_axis=0, tiled=True)  13.2 us
    unnamed x64, local copies, waits for them, and re-layouts  9.38 us
    all_to_all x1, starting transfers between devices, local(): lax.all_to_all(returning.reshape(tile_count, capacity, out_width), 'gx',...  8.95 us
    ppermute x6, starting transfers between devices, neighbours(): lo = lax.ppermute(tail, axis, [(i, (i + 1) % count) for i in range(count)])  8.71 us
    ppermute x6, waiting for transfers between devices, neighbours(): hi = lax.ppermute(head, axis, [((i + 1) % count, i) for i in range(count)])  7.31 us
    ppermute x6, starting transfers between devices, neighbours(): hi = lax.ppermute(head, axis, [((i + 1) % count, i) for i in range(count)])  7.15 us
    ppermute x6, waiting for transfers between devices, neighbours(): lo = lax.ppermute(tail, axis, [(i, (i + 1) % count) for i in range(count)])  4.99 us
    dot_general x2, matrix products, vertical_mix(): jnp.einsum('lm,mxy->lxy', matrix, right_side, precision=HIGHEST_PRECISION)  4.73 us
  transfers between devices with their start and end apart: 15, of which 7 were waited for; matrix products, arithmetic and copies ran while one was open for 31% of the time, Pallas kernels for 0%

profile of v12, /device:TPU:1, one launch (start us, length us, event | category | flops | bytes accessed | tf_op | source)
XLA Modules:
  0.0 102.0 jit_solution(11509747935898987932)
XLA Ops:
  2.3 0.8 slice_bitcast_fusion.2
  3.3 0.8 maximum_select_fusion
  4.1 3.7 %collective-permute-start.12 = (f32[4,8192]{1,0:T(4,128)}, f32[4,8192]{1,0:T(4,128)}, u32[]{:S(2)}, u32[]{:S(2)}) collective-permute-start(f32[4,8192]{1,0:T(4,128)} %maximum_select_fusion), channel_id=1, source_target_pairs={{0,128},{128,0},{1,129},{129,1},{2,130},{130,2},{3,131},{131,3},{4... | collective-permute-start | bytes 393224 | tf_op jit(solution)/shard_map/ppermute | solution.py:109
  8.0 3.2 %fusion.74 = (f32[1,1,32,16,512]{4,3,2,1,0:T(8,128)}, f32[1,1,32,16,512]{4,3,2,1,0:T(8,128)S(1)}, f32[1,1,32,16,512]{4,3,2,1,0:T(8,128)S(1)}) fusion(f32[1,3,32,16,512]{4,3,2,1,0:T(8,128)} %param.13), kind=kLoop, calls=%fused_computation.139 | loop fusion | bytes 6291456 | tf_op jit(solution)/shard_map/slice | solution.py:79
  12.0 1.3 %collective-permute-start.3 = (f32[33,16,1]{2,0,1:T(8,128)S(1)}, f32[33,16,1]{2,0,1:T(8,128)S(1)}, u32[]{:S(2)}, u32[]{:S(2)}) collective-permute-start(f32[33,16,1]{2,0,1:T(8,128)S(1)} %pad_maximum_fusion.11), channel_id=1, source_target_pairs={{0,1},{1,2},{2,3},{3,0},{4,5},{5,6},{6,7},{7,4},{8,9},{9,10},{10,1... | collective-permute-start | bytes 6344 | tf_op jit(solution)/shard_map/ppermute | solution.py:15
  13.3 1.5 %collective-permute-start.2 = (f32[33,16,1]{2,0,1:T(8,128)S(1)}, f32[33,16,1]{2,0,1:T(8,128)S(1)}, u32[]{:S(2)}, u32[]{:S(2)}) collective-permute-start(f32[33,16,1]{2,0,1:T(8,128)S(1)} %pad_maximum_fusion.10), channel_id=1, source_target_pairs={{1,0},{2,1},{3,2},{0,3},{5,4},{6,5},{7,6},{4,7},{9,8},{10,9},{11,1... | collective-permute-start | bytes 6344 | tf_op jit(solution)/shard_map/ppermute | solution.py:16
  16.2 1.8 %collective-permute-start.1 = (f32[33,1,512]{2,0,1:T(8,128)}, f32[33,1,512]{2,0,1:T(8,128)}, u32[]{:S(2)}, u32[]{:S(2)}) collective-permute-start(f32[33,1,512]{2,0,1:T(8,128)} %pad_maximum_fusion.15), channel_id=1, source_target_pairs={{0,4},{4,8},{8,12},{12,16},{16,20},{20,24},{24,28},{28,32},{32,36}... | collective-permute-start | bytes 202760 | tf_op jit(solution)/shard_map/ppermute | solution.py:15
  21.9 0.9 broadcast_select_fusion.11
  23.0 0.9 broadcast_select_fusion.12
  23.9 2.9 %fusion.6 = f32[32,16,512]{2,0,1:T(8,128)S(1)} fusion(f32[32,16,512]{2,0,1:T(8,128)S(1)} %bitcast.111, f32[32,16,1]{2,0,1:T(8,128)S(1)} %slice.244, f32[32,16,1]{2,0,1:T(8,128)S(1)} %slice.241, f32[32,16,512]{2,0,1:T(8,128)S(1)} %bitcast.114, f32[32,1,512]{2,0,1:T(8,128)S(1)} %slice.238, f32[32,1,512]{2,0,1:T(8,128)S(1)} %slice.235, ...), kind=kOutput, calls=%fused_computation.11 | convolution fusion | flops 105644032 | bytes 4366336 | tf_op jit(solution)/shard_map/lm,mxy->lxy/dot_general | solution.py:21
  27.6 0.9 collective-permute-start.7
  29.2 2.7 %collective-permute-start.5 = (f32[32,2,512]{2,0,1:T(8,128)}, f32[32,2,512]{2,0,1:T(8,128)}, u32[]{:S(2)}, u32[]{:S(2)}) collective-permute-start(f32[32,2,512]{2,0,1:T(8,128)} %get-tuple-element.34), channel_id=1, source_target_pairs={{0,4},{4,8},{8,12},{12,16},{16,20},{20,24},{24,28},{28,32},{32,36}... | collective-permute-start | bytes 393224 | tf_op jit(solution)/shard_map/ppermute | solution.py:15
  31.9 2.0 %collective-permute-start.6 = (f32[32,16,2]{2,0,1:T(8,128)S(1)}, f32[32,16,2]{2,0,1:T(8,128)S(1)}, u32[]{:S(2)}, u32[]{:S(2)}) collective-permute-start(f32[32,16,2]{2,0,1:T(8,128)S(1)} %get-tuple-element.37), channel_id=1, source_target_pairs={{1,0},{2,1},{3,2},{0,3},{5,4},{6,5},{7,6},{4,7},{9,8},{10,9},{11,1... | collective-permute-start | bytes 12296 | tf_op jit(solution)/shard_map/ppermute | solution.py:16
  34.1 3.4 %collective-permute-done.6 = f32[32,16,2]{2,0,1:T(8,128)S(1)} collective-permute-done((f32[32,16,2]{2,0,1:T(8,128)S(1)}, f32[32,16,2]{2,0,1:T(8,128)S(1)}, u32[]{:S(2)}, u32[]{:S(2)}) %collective-permute-start.6) | collective-permute-done | bytes 4128 | tf_op jit(solution)/shard_map/ppermute | solution.py:16
  37.6 1.9 %fusion.7 = f32[32,16,514]{2,0,1:T(8,128)} fusion(f32[32,16,1]{2,0,1:T(8,128)S(1)} %slice.241, f32[32,16,512]{2,0,1:T(8,128)S(1)} %bitcast.112, f32[32,16,1]{2,0,1:T(8,128)S(1)} %slice.244, f32[32,16,2]{2,0,1:T(8,128)S(1)} %broadcast_select_fusion.5, f32[32,16,512]{2,0,1:T(8,128)S(1)} %fusion.6, f32[32,16,2]{2,0,1:T(8,128)S(1)} %broadcast_select_fusion.4, ...), kind=kLoop, calls=%fused_computation.13 | loop fusion | flops 2105344 | bytes 3195008 | tf_op jit(solution)/shard_map/mul | solution.py:50
  40.8 2.9 %fusion.11 = bf16[64,8,128]{2,1,0:T(8,128)(2,1)S(1)} fusion(bf16[1,1,64,256,128]{4,3,2,1,0:T(8,128)(2,1)} %param.23, bf16[64,8,256]{2,1,0:T(8,128)(2,1)S(1)} %gather_fusion, pred[64]{0:T(512)(128)(4,1)S(1)} %copy-done.20), kind=kOutput, calls=%fused_computation.20 | convolution fusion | flops 33751040 | bytes 4587584 | tf_op jit(solution)/shard_map/fpi,pio->pfo/dot_general | solution.py:118
  45.0 13.2 %all-to-all-start = ((f32[32,5,128]{2,1,0:T(8,128)}), f32[32,5,128]{2,1,0:T(8,128)S(1)}, u32[]{:S(2)}, u32[]{:S(2)}) async-start(f32[32,5,128]{2,1,0:T(8,128)} %pad_maximum_fusion.13), calls=%async_computation | async-start | bytes 262144 | tf_op jit(solution)/shard_map/all_to_all | solution.py:139
  58.2 1.0 %fusion.81 = (f32[1,8192]{1,0:T(1,128)S(1)}, f32[1,8192]{1,0:T(1,128)S(1)}) fusion(f32[4,8192]{1,0:T(4,128)} %collective-permute-done.12), kind=kLoop, calls=%fused_computation.146 | loop fusion | bytes 131072 | tf_op jit(solution)/shard_map/slice | solution.py:111
  59.3 0.9 broadcast_select_fusion.6
  60.2 0.9 broadcast_select_fusion.7
  61.5 1.0 copy-done.1
  62.5 1.9 %fusion.5 = f32[32,16,512]{2,0,1:T(8,128)S(1)} fusion(f32[32,16,512]{2,0,1:T(8,128)S(1)} %fusion.6, f32[32,16,514]{2,0,1:T(8,128)S(1)} %copy-done.1, f32[32,18,512]{2,0,1:T(8,128)S(1)} %fusion.9, f32[16,512]{1,0:T(8,128)S(1)} %bitcast.143, f32[1,32,32]{2,1,0:T(8,128)S(1)} %copy-done), kind=kOutput, calls=%fused_computation.9 | convolution fusion | flops 103546880 | bytes 11616256 | tf_op jit(solution)/shard_map/lm,mxy->lxy/dot_general | solution.py:21
  64.5 3.5 %collective-permute-start.10 = (f32[32,16,1]{2,0,1:T(8,128)S(1)}, f32[32,16,1]{2,0,1:T(8,128)S(1)}, u32[]{:S(2)}, u32[]{:S(2)}) collective-permute-start(f32[32,16,1]{2,0,1:T(8,128)S(1)} %get-tuple-element.32), channel_id=1, source_target_pairs={{1,0},{2,1},{3,2},{0,3},{5,4},{6,5},{7,6},{4,7},{9,8},{10,9},{11,1... | collective-permute-start | bytes 6152 | tf_op jit(solution)/shard_map/ppermute | solution.py:16
  68.1 2.0 %collective-permute-start.9 = (f32[32,1,512]{2,0,1:T(8,128)S(1)}, f32[32,1,512]{2,0,1:T(8,128)S(1)}, u32[]{:S(2)}, u32[]{:S(2)}) collective-permute-start(f32[32,1,512]{2,0,1:T(8,128)S(1)} %get-tuple-element.31), channel_id=1, source_target_pairs={{0,4},{4,8},{8,12},{12,16},{16,20},{20,24},{24,28},{28,32},{32,36}... | collective-permute-start | bytes 196616 | tf_op jit(solution)/shard_map/ppermute | solution.py:15
  70.1 3.8 %collective-permute-done.10 = f32[32,16,1]{2,0,1:T(8,128)S(1)} collective-permute-done((f32[32,16,1]{2,0,1:T(8,128)S(1)}, f32[32,16,1]{2,0,1:T(8,128)S(1)}, u32[]{:S(2)}, u32[]{:S(2)}) %collective-permute-start.10) | collective-permute-done | bytes 2080 | tf_op jit(solution)/shard_map/ppermute | solution.py:16
  73.9 4.1 %collective-permute-done.11 = f32[32,16,1]{2,0,1:T(8,128)S(1)} collective-permute-done((f32[32,16,1]{2,0,1:T(8,128)S(1)}, f32[32,16,1]{2,0,1:T(8,128)S(1)}, u32[]{:S(2)}, u32[]{:S(2)}) %collective-permute-start.11) | collective-permute-done | bytes 2080 | tf_op jit(solution)/shard_map/ppermute | solution.py:15
  78.1 1.1 %fusion.24 = (f32[1,32,16,512]{3,1,2,0:T(8,128)S(1)}, f32[1,32,16,512]{3,1,2,0:T(8,128)S(1)}) fusion(f32[32,16,512]{2,0,1:T(8,128)S(1)} %fusion.5, f32[32,1,512]{2,0,1:T(8,128)S(1)} %broadcast_select_fusion.13, f32[32,1,512]{2,0,1:T(8,128)S(1)} %broadcast_select_fusion.14, f32[32,18,512]{2,0,1:T(8,128)S(1)} %fusion.9, f32[16,512]{1,0:T(8,128)S(1)} %bitcast.129, ...), kind=kLoop, calls=%fused_computation.36 | loop fusion | flops 3145728 | bytes 5410816 | tf_op jit(solution)/shard_map/stack | solution.py:87
  79.5 0.8 convolution_convert_fusion
  80.4 8.9 %all-to-all-start.1 = ((bf16[32,4,128]{2,1,0:T(4,128)(2,1)}), bf16[32,4,128]{2,1,0:T(4,128)(2,1)S(1)}, u32[]{:S(2)}, u32[]{:S(2)}) async-start(bf16[32,4,128]{2,1,0:T(4,128)(2,1)} %bitcast.31), calls=%async_computation.1 | async-start | bytes 65536 | tf_op jit(solution)/shard_map/all_to_all | solution.py:154
  89.7 3.5 %copy.49 = f32[1,3,32,16,512]{4,3,2,1,0:T(8,128)} copy(f32[1,3,32,16,512]{4,2,3,1,0:T(8,128)S(1)} %maximum_bitcast_fusion) | data formatting | bytes 6291456
  93.1 4.3 %all-to-all-done.1 = bf16[32,4,128]{2,1,0:T(4,128)(2,1)S(1)} async-done(((bf16[32,4,128]{2,1,0:T(4,128)(2,1)}), bf16[32,4,128]{2,1,0:T(4,128)(2,1)S(1)}, u32[]{:S(2)}, u32[]{:S(2)}) %all-to-all-start.1) | async-done | bytes 32800 | tf_op jit(solution)/shard_map/all_to_all | solution.py:154
  97.7 3.4 %fusion.1 = f32[64,1,256]{2,1,0:T(1,128)S(1)} fusion(bf16[1,1,64,256,128]{4,3,2,1,0:T(8,128)(2,1)} %param.23, bf16[64,128,1]{1,0,2:T(8,128)(2,1)S(1)} %fusion.14), kind=kOutput, calls=%fused_computation.3 | convolution fusion | flops 4194304 | bytes 4276224 | tf_op jit(solution)/shard_map/pio,po->pi/dot_general | solution.py:162
  (135 shorter events, 14.5 us)
Async XLA Ops:
  0.6 23.2 %copy-start = (f32[1,32,32]{2,1,0:T(8,128)S(1)}, f32[1,32,32]{2,1,0:T(8,128)}, u32[]{:S(2)}) copy-start(f32[1,32,32]{2,1,0:T(8,128)} %param.16) | copy-start | bytes 12292
  2.2 8.9 %copy-start.7 = (f32[1,1,16,512]{3,1,2,0:T(1,128)}, f32[1,1,16,512]{3,1,2,0:T(1,128)S(1)}, u32[]{:S(2)}) copy-start(f32[1,1,16,512]{3,1,2,0:T(1,128)S(1)} %copy.63) | copy-start | bytes 98308
  3.1 8.1 %copy-start.9 = (f32[1,1,16,512]{3,1,2,0:T(1,128)}, f32[1,1,16,512]{3,1,2,0:T(1,128)S(1)}, u32[]{:S(2)}) copy-start(f32[1,1,16,512]{3,1,2,0:T(1,128)S(1)} %copy.60) | copy-start | bytes 98308
  3.2 8.0 %copy-start.11 = (f32[1,1,16,512]{3,1,2,0:T(1,128)}, f32[1,1,16,512]{3,1,2,0:T(1,128)S(1)}, u32[]{:S(2)}) copy-start(f32[1,1,16,512]{3,1,2,0:T(1,128)S(1)} %copy.62) | copy-start | bytes 98308
  3.2 8.0 %copy-start.13 = (f32[1,1,16,512]{3,1,2,0:T(1,128)}, f32[1,1,16,512]{3,1,2,0:T(1,128)S(1)}, u32[]{:S(2)}) copy-start(f32[1,1,16,512]{3,1,2,0:T(1,128)S(1)} %copy.61) | copy-start | bytes 98308
  4.1 35.4 %collective-permute-start.12 = (f32[4,8192]{1,0:T(4,128)}, f32[4,8192]{1,0:T(4,128)}, u32[]{:S(2)}, u32[]{:S(2)}) collective-permute-start(f32[4,8192]{1,0:T(4,128)} %maximum_select_fusion), channel_id=1, source_target_pairs={{0,128},{128,0},{1,129},{129,1},{2,130},{130,2},{3,131},{131,3},{4... | collective-permute-start | bytes 393224 | tf_op jit(solution)/shard_map/ppermute | solution.py:109
  12.0 9.5 %collective-permute-start.3 = (f32[33,16,1]{2,0,1:T(8,128)S(1)}, f32[33,16,1]{2,0,1:T(8,128)S(1)}, u32[]{:S(2)}, u32[]{:S(2)}) collective-permute-start(f32[33,16,1]{2,0,1:T(8,128)S(1)} %pad_maximum_fusion.11), channel_id=1, source_target_pairs={{0,1},{1,2},{2,3},{3,0},{4,5},{5,6},{6,7},{7,4},{8,9},{9,10},{10,1... | collective-permute-start | bytes 6344 | tf_op jit(solution)/shard_map/ppermute | solution.py:15
  13.3 8.3 %collective-permute-start.2 = (f32[33,16,1]{2,0,1:T(8,128)S(1)}, f32[33,16,1]{2,0,1:T(8,128)S(1)}, u32[]{:S(2)}, u32[]{:S(2)}) collective-permute-start(f32[33,16,1]{2,0,1:T(8,128)S(1)} %pad_maximum_fusion.10), channel_id=1, source_target_pairs={{1,0},{2,1},{3,2},{0,3},{5,4},{6,5},{7,6},{4,7},{9,8},{10,9},{11,1... | collective-permute-start | bytes 6344 | tf_op jit(solution)/shard_map/ppermute | solution.py:16
  14.9 3.7 %copy-start.16 = (s32[1,1,64]{2,1,0:T(1,128)S(1)}, s32[1,1,64]{2,1,0:T(1,128)}, u32[]{:S(2)}) copy-start(s32[1,1,64]{2,1,0:T(1,128)} %param.21) | copy-start | bytes 772
  14.9 4.3 %copy-start.24 = (s32[1,1,64]{2,1,0:T(1,128)S(1)}, s32[1,1,64]{2,1,0:T(1,128)}, u32[]{:S(2)}) copy-start(s32[1,1,64]{2,1,0:T(1,128)} %param.22) | copy-start | bytes 772
  14.9 4.3 %copy-start.25 = (s32[1,1,64,1]{2,3,1,0:T(1,128)S(1)}, s32[1,1,64,1]{2,3,1,0:T(1,128)}, u32[]{:S(2)}) copy-start(s32[1,1,64,1]{2,3,1,0:T(1,128)} %param.20) | copy-start | bytes 772
  14.9 5.8 %copy-start.3 = (f32[1,16,512]{2,1,0:T(8,128)S(1)}, f32[1,16,512]{2,1,0:T(8,128)}, u32[]{:S(2)}) copy-start(f32[1,16,512]{2,1,0:T(8,128)} %param.17) | copy-start | bytes 98308
  16.2 5.8 %collective-permute-start.1 = (f32[33,1,512]{2,0,1:T(8,128)}, f32[33,1,512]{2,0,1:T(8,128)}, u32[]{:S(2)}, u32[]{:S(2)}) collective-permute-start(f32[33,1,512]{2,0,1:T(8,128)} %pad_maximum_fusion.15), channel_id=1, source_target_pairs={{0,4},{4,8},{8,12},{12,16},{16,20},{20,24},{24,28},{28,32},{32,36}... | collective-permute-start | bytes 202760 | tf_op jit(solution)/shard_map/ppermute | solution.py:15
  18.6 4.4 %collective-permute-start = (f32[33,1,512]{2,0,1:T(8,128)}, f32[33,1,512]{2,0,1:T(8,128)}, u32[]{:S(2)}, u32[]{:S(2)}) collective-permute-start(f32[33,1,512]{2,0,1:T(8,128)} %pad_maximum_fusion.14), channel_id=1, source_target_pairs={{4,0},{8,4},{12,8},{16,12},{20,16},{24,20},{28,24},{32,28},{36,32}... | collective-permute-start | bytes 202760 | tf_op jit(solution)/shard_map/ppermute | solution.py:16
  21.6 2.3 %copy-start.2 = (f32[1,1,32,16,512]{4,3,2,1,0:T(8,128)S(1)}, f32[1,1,32,16,512]{4,3,2,1,0:T(8,128)}, u32[]{:S(2)}) copy-start(f32[1,1,32,16,512]{4,3,2,1,0:T(8,128)} %get-tuple-element.25) | copy-start | bytes 3145732
  27.6 6.5 %collective-permute-start.7 = (f32[32,16,2]{2,0,1:T(8,128)S(1)}, f32[32,16,2]{2,0,1:T(8,128)S(1)}, u32[]{:S(2)}, u32[]{:S(2)}) collective-permute-start(f32[32,16,2]{2,0,1:T(8,128)S(1)} %get-tuple-element.36), channel_id=1, source_target_pairs={{0,1},{1,2},{2,3},{3,0},{4,5},{5,6},{6,7},{7,4},{8,9},{9,10},{10,1... | collective-permute-start | bytes 12296 | tf_op jit(solution)/shard_map/ppermute | solution.py:15
  29.2 30.1 %collective-permute-start.5 = (f32[32,2,512]{2,0,1:T(8,128)}, f32[32,2,512]{2,0,1:T(8,128)}, u32[]{:S(2)}, u32[]{:S(2)}) collective-permute-start(f32[32,2,512]{2,0,1:T(8,128)} %get-tuple-element.34), channel_id=1, source_target_pairs={{0,4},{4,8},{8,12},{12,16},{16,20},{20,24},{24,28},{28,32},{32,36}... | collective-permute-start | bytes 393224 | tf_op jit(solution)/shard_map/ppermute | solution.py:15
  31.9 28.3 %collective-permute-start.4 = (f32[32,2,512]{2,0,1:T(8,128)S(1)}, f32[32,2,512]{2,0,1:T(8,128)}, u32[]{:S(2)}, u32[]{:S(2)}) collective-permute-start(f32[32,2,512]{2,0,1:T(8,128)S(1)} %get-tuple-element.35), channel_id=1, source_target_pairs={{4,0},{8,4},{12,8},{16,12},{20,16},{24,20},{28,24},{32,28},{36,32}... | collective-permute-start | bytes 393224 | tf_op jit(solution)/shard_map/ppermute | solution.py:16
  31.9 5.6 %collective-permute-start.6 = (f32[32,16,2]{2,0,1:T(8,128)S(1)}, f32[32,16,2]{2,0,1:T(8,128)S(1)}, u32[]{:S(2)}, u32[]{:S(2)}) collective-permute-start(f32[32,16,2]{2,0,1:T(8,128)S(1)} %get-tuple-element.37), channel_id=1, source_target_pairs={{1,0},{2,1},{3,2},{0,3},{5,4},{6,5},{7,6},{4,7},{9,8},{10,9},{11,1... | collective-permute-start | bytes 12296 | tf_op jit(solution)/shard_map/ppermute | solution.py:16
  37.6 3.2 %copy-start.20 = (pred[64]{0:T(512)(128)(4,1)S(1)}, pred[64]{0:T(512)(128)(4,1)}, u32[]{:S(2)}) copy-start(pred[64]{0:T(512)(128)(4,1)} %compare_and_fusion) | copy-start | bytes 196
  40.8 2.9 %copy-start.15 = (f32[8]{0:T(128)S(1)}, f32[8]{0:T(128)}, u32[]{:S(2)}) copy-start(f32[8]{0:T(128)} %param.19) | copy-start | bytes 100
  40.8 3.2 %copy-start.19 = (s32[64]{0:T(128)S(1)}, s32[64]{0:T(128)}, u32[]{:S(2)}) copy-start(s32[64]{0:T(128)} %copy-done.18) | copy-start | bytes 772
  43.7 17.4 %copy-start.4 = (f32[1,18,512]{2,1,0:T(8,128)S(1)}, f32[1,18,512]{2,1,0:T(8,128)}, u32[]{:S(2)}) copy-start(f32[1,18,512]{2,1,0:T(8,128)} %copy.88) | copy-start | bytes 110596
  45.0 34.2 %all-to-all-start = ((f32[32,5,128]{2,1,0:T(8,128)}), f32[32,5,128]{2,1,0:T(8,128)S(1)}, u32[]{:S(2)}, u32[]{:S(2)}) async-start(f32[32,5,128]{2,1,0:T(8,128)} %pad_maximum_fusion.13), calls=%async_computation | async-start | bytes 262144 | tf_op jit(solution)/shard_map/all_to_all | solution.py:139
  64.3 13.8 %copy-start.5 = (f32[1,16,512]{2,1,0:T(8,128)S(1)}, f32[1,16,512]{2,1,0:T(8,128)}, u32[]{:S(2)}) copy-start(f32[1,16,512]{2,1,0:T(8,128)} %copy.90) | copy-start | bytes 98308
  64.5 9.4 %collective-permute-start.10 = (f32[32,16,1]{2,0,1:T(8,128)S(1)}, f32[32,16,1]{2,0,1:T(8,128)S(1)}, u32[]{:S(2)}, u32[]{:S(2)}) collective-permute-start(f32[32,16,1]{2,0,1:T(8,128)S(1)} %get-tuple-element.32), channel_id=1, source_target_pairs={{1,0},{2,1},{3,2},{0,3},{5,4},{6,5},{7,6},{4,7},{9,8},{10,9},{11,1... | collective-permute-start | bytes 6152 | tf_op jit(solution)/shard_map/ppermute | solution.py:16
  68.0 10.0 %collective-permute-start.8 = (f32[32,1,512]{2,0,1:T(8,128)S(1)}, f32[32,1,512]{2,0,1:T(8,128)S(1)}, u32[]{:S(2)}, u32[]{:S(2)}) collective-permute-start(f32[32,1,512]{2,0,1:T(8,128)S(1)} %get-tuple-element.30), channel_id=1, source_target_pairs={{4,0},{8,4},{12,8},{16,12},{20,16},{24,20},{28,24},{32,28},{36,32}... | collective-permute-start | bytes 196616 | tf_op jit(solution)/shard_map/ppermute | solution.py:16
  68.1 10.0 %collective-permute-start.9 = (f32[32,1,512]{2,0,1:T(8,128)S(1)}, f32[32,1,512]{2,0,1:T(8,128)S(1)}, u32[]{:S(2)}, u32[]{:S(2)}) collective-permute-start(f32[32,1,512]{2,0,1:T(8,128)S(1)} %get-tuple-element.31), channel_id=1, source_target_pairs={{0,4},{4,8},{8,12},{12,16},{16,20},{20,24},{24,28},{28,32},{32,36}... | collective-permute-start | bytes 196616 | tf_op jit(solution)/shard_map/ppermute | solution.py:15
  70.1 7.9 %collective-permute-start.11 = (f32[32,16,1]{2,0,1:T(8,128)S(1)}, f32[32,16,1]{2,0,1:T(8,128)S(1)}, u32[]{:S(2)}, u32[]{:S(2)}) collective-permute-start(f32[32,16,1]{2,0,1:T(8,128)S(1)} %get-tuple-element.33), channel_id=1, source_target_pairs={{0,1},{1,2},{2,3},{3,0},{4,5},{5,6},{6,7},{7,4},{8,9},{9,10},{10,1... | collective-permute-start | bytes 6152 | tf_op jit(solution)/shard_map/ppermute | solution.py:15
  80.4 17.1 %all-to-all-start.1 = ((bf16[32,4,128]{2,1,0:T(4,128)(2,1)}), bf16[32,4,128]{2,1,0:T(4,128)(2,1)S(1)}, u32[]{:S(2)}, u32[]{:S(2)}) async-start(bf16[32,4,128]{2,1,0:T(4,128)(2,1)} %bitcast.31), calls=%async_computation.1 | async-start | bytes 65536 | tf_op jit(solution)/shard_map/all_to_all | solution.py:154
  97.6 3.4 %copy-start.17 = (s32[1,1,64]{2,1,0:T(1,128)S(1)}, s32[1,1,64]{2,1,0:T(1,128)}, u32[]{:S(2)}) copy-start(s32[1,1,64]{2,1,0:T(1,128)} %param.21) | copy-start | bytes 772
  97.6 3.6 %copy-start.6 = (s32[1,16,512]{2,1,0:T(8,128)S(1)}, s32[1,16,512]{2,1,0:T(8,128)}, u32[]{:S(2)}) copy-start(s32[1,16,512]{2,1,0:T(8,128)} %param.15) | copy-start | bytes 98308
  (9 other events, 15.5 us)

commit v13 on v12

--- a/solution.py
+++ b/solution.py
@@ -12,9 +12,11 @@
 def neighbours(head, tail, axis):
     count = lax.axis_size(axis)
     me = lax.axis_index(axis)
+    tail = jnp.where(me < count - 1, tail, 0.0)
+    head = jnp.where(me > 0, head, 0.0)
     lo = lax.ppermute(tail, axis, [(i, (i + 1) % count) for i in range(count)])
     hi = lax.ppermute(head, axis, [((i + 1) % count, i) for i in range(count)])
-    return jnp.where(me > 0, lo, 0.0), jnp.where(me < count - 1, hi, 0.0)
+    return lo, hi
 
 
 def vertical_mix(matrix, right_side):

time: 103 us -> 98 us (0.951)
  waiting for transfers between devices: 16.6 us -> 9.58 us
  local copies, waits for them, and re-layouts: 15.9 us -> 19.5 us
  other arithmetic: 12.9 us -> 10 us
  matrix products: 13.4 us -> 15.1 us
    ppermute x6, waiting for transfers between devices: 7.31 us -> 3.07 us  [neighbours(): hi = lax.ppermute(head, axis, [((i + 1) % count, i) for i in range(count)])]
    ppermute x6, waiting for transfers between devices: 4.99 us -> 2.2 us  [neighbours(): lo = lax.ppermute(tail, axis, [(i, (i + 1) % count) for i in range(count)])]
    select_n x12 -> x8, other arithmetic: 3.8 us -> 1.22 us  [the longest x4 0.97 us: neighbours(): tail = jnp.where(me < count - 1, tail, 0.0)]
    all_to_all x1, starting transfers between devices: 8.95 us -> 10.7 us  [local(): lax.all_to_all(returning.reshape(tile_count, capacity, out_width), 'gx',...]
    dot_general x2, matrix products: 4.73 us -> 6.34 us  [vertical_mix(): jnp.einsum('lm,mxy->lxy', matrix, right_side, precision=HIGHEST_PRECISION)]
    ppermute x6, starting transfers between devices: 8.71 us -> 7.15 us  [neighbours(): lo = lax.ppermute(tail, axis, [(i, (i + 1) % count) for i in range(count)])]
    all_to_all x1, starting transfers between devices: 13.2 us -> 11.7 us  [local(): lax.all_to_all(packet, 'gx', split_axis=0, concat_axis=0, tiled=True)]
    slice x2, local copies, waits for them, and re-layouts: 0.01 us -> 1.44 us  [stencil(): wet_x = jnp.concatenate([lo_x[levels:], wet3, hi_x[levels:]], axis=1)]
  transfers between devices with their start and end apart: 15 -> 15, of which waited for: 7 -> 3; matrix products, arithmetic and copies ran while one was open for 31% -> 36% of each run, Pallas kernels for 0% -> 0%
where the time goes in v13:
time: 98 us; the launch traced here: 97.3 us
  starting transfers between devices  41.8 us (43%)
  local copies, waits for them, and re-layouts  19.5 us (20%)
  matrix products  15.1 us (15%)
  other arithmetic  10 us (10%)
  waiting for transfers between devices  9.58 us (10%)
  between operations  1.33 us (1%)
    all_to_all x1, starting transfers between devices, local(): lax.all_to_all(packet, 'gx', split_axis=0, concat_axis=0, tiled=True)  11.7 us
    all_to_all x1, starting transfers between devices, local(): lax.all_to_all(returning.reshape(tile_count, capacity, out_width), 'gx',...  10.7 us
    unnamed x76, local copies, waits for them, and re-layouts  9.7 us
    ppermute x6, starting transfers between devices, neighbours(): hi = lax.ppermute(head, axis, [((i + 1) % count, i) for i in range(count)])  8.43 us
    ppermute x6, starting transfers between devices, neighbours(): lo = lax.ppermute(tail, axis, [(i, (i + 1) % count) for i in range(count)])  7.15 us
    dot_general x2, matrix products, vertical_mix(): jnp.einsum('lm,mxy->lxy', matrix, right_side, precision=HIGHEST_PRECISION)  6.34 us
    all_to_all x1, waiting for transfers between devices, local(): lax.all_to_all(returning.reshape(tile_count, capacity, out_width), 'gx',...  4.3 us
    ppermute x1, starting transfers between devices, local(): got = lax.ppermute(sent, 'sec', [(0, 1), (1, 0)])  3.74 us
  transfers between devices with their start and end apart: 15, of which 3 were waited for; matrix products, arithmetic and copies ran while one was open for 36% of the time, Pallas kernels for 0%

profile of v13, /device:TPU:1, one launch (start us, length us, event | category | flops | bytes accessed | tf_op | source)
XLA Modules:
  0.0 97.3 jit_solution(15381203731856201772)
XLA Ops:
  0.7 0.8 copy_convert_fusion
  1.4 0.8 copy.95
  2.3 0.8 slice_bitcast_fusion.2
  3.3 0.8 maximum_select_fusion
  4.1 3.7 %collective-permute-start.12 = (f32[4,8192]{1,0:T(4,128)}, f32[4,8192]{1,0:T(4,128)}, u32[]{:S(2)}, u32[]{:S(2)}) collective-permute-start(f32[4,8192]{1,0:T(4,128)} %maximum_select_fusion), channel_id=1, source_target_pairs={{0,128},{128,0},{1,129},{129,1},{2,130},{130,2},{3,131},{131,3},{4... | collective-permute-start | bytes 393224 | tf_op jit(solution)/shard_map/ppermute | solution.py:111
  8.0 3.3 %fusion.74 = (f32[1,1,32,16,512]{4,3,2,1,0:T(8,128)}, f32[1,1,32,16,512]{4,3,2,1,0:T(8,128)S(1)}, f32[1,1,32,16,512]{4,3,2,1,0:T(8,128)S(1)}) fusion(f32[1,3,32,16,512]{4,3,2,1,0:T(8,128)} %param.13), kind=kLoop, calls=%fused_computation.135 | loop fusion | bytes 6291456 | tf_op jit(solution)/shard_map/slice | solution.py:81
  12.3 1.2 %collective-permute-start.3 = (f32[33,16,1]{0,1,2:T(8,128)S(1)}, f32[33,16,1]{0,1,2:T(8,128)S(1)}, u32[]{:S(2)}, u32[]{:S(2)}) collective-permute-start(f32[33,16,1]{0,1,2:T(8,128)S(1)} %maximum_select_fusion.4), channel_id=1, source_target_pairs={{0,1},{1,2},{2,3},{3,0},{4,5},{5,6},{6,7},{7,4},{8,9},{9,10},{10,1... | collective-permute-start | bytes 6344 | tf_op jit(solution)/shard_map/ppermute | solution.py:17
  13.8 1.5 %collective-permute-start.2 = (f32[33,16,1]{0,1,2:T(8,128)S(1)}, f32[33,16,1]{0,1,2:T(8,128)S(1)}, u32[]{:S(2)}, u32[]{:S(2)}) collective-permute-start(f32[33,16,1]{0,1,2:T(8,128)S(1)} %maximum_select_fusion.3), channel_id=1, source_target_pairs={{1,0},{2,1},{3,2},{0,3},{5,4},{6,5},{7,6},{4,7},{9,8},{10,9},{11,1... | collective-permute-start | bytes 6344 | tf_op jit(solution)/shard_map/ppermute | solution.py:18
  15.9 1.9 %collective-permute-start.1 = (f32[33,1,512]{2,0,1:T(8,128)S(1)}, f32[33,1,512]{2,0,1:T(8,128)S(1)}, u32[]{:S(2)}, u32[]{:S(2)}) collective-permute-start(f32[33,1,512]{2,0,1:T(8,128)S(1)} %maximum_select_fusion.2), channel_id=1, source_target_pairs={{0,4},{4,8},{8,12},{12,16},{16,20},{20,24},{24,28},{28,32},{32,36}... | collective-permute-start | bytes 202760 | tf_op jit(solution)/shard_map/ppermute | solution.py:17
  22.5 0.9 copy.74
  24.1 4.5 %fusion.6 = f32[32,16,512]{2,0,1:T(8,128)S(1)} fusion(f32[32,16,512]{2,0,1:T(8,128)S(1)} %bitcast.117, f32[32,16,1]{2,0,1:T(8,128)} %copy.74, f32[32,16,1]{2,0,1:T(8,128)S(1)} %copy.71, f32[32,16,512]{2,0,1:T(8,128)S(1)} %bitcast.120, f32[32,1,512]{2,0,1:T(8,128)S(1)} %slice.238, f32[32,1,512]{2,0,1:T(8,128)S(1)} %slice.235, ...), kind=kOutput, calls=%fused_computation.11 | convolution fusion | flops 105644032 | bytes 4366336 | tf_op jit(solution)/shard_map/lm,mxy->lxy/dot_general | solution.py:23
  28.6 0.7 slice_select_fusion.4
  29.6 2.7 %collective-permute-start.6 = (f32[32,16,2]{2,0,1:T(8,128)S(1)}, f32[32,16,2]{2,0,1:T(8,128)S(1)}, u32[]{:S(2)}, u32[]{:S(2)}) collective-permute-start(f32[32,16,2]{2,0,1:T(8,128)S(1)} %get-tuple-element.39), channel_id=1, source_target_pairs={{1,0},{2,1},{3,2},{0,3},{5,4},{6,5},{7,6},{4,7},{9,8},{10,9},{11,1... | collective-permute-start | bytes 12296 | tf_op jit(solution)/shard_map/ppermute | solution.py:18
  32.2 0.7 slice.245
  34.3 2.3 %collective-permute-start.5 = (f32[32,2,512]{2,0,1:T(8,128)}, f32[32,2,512]{2,0,1:T(8,128)}, u32[]{:S(2)}, u32[]{:S(2)}) collective-permute-start(f32[32,2,512]{2,0,1:T(8,128)} %get-tuple-element.36), channel_id=1, source_target_pairs={{0,4},{4,8},{8,12},{12,16},{16,20},{20,24},{24,28},{28,32},{32,36}... | collective-permute-start | bytes 393224 | tf_op jit(solution)/shard_map/ppermute | solution.py:17
  36.6 2.6 %collective-permute-start.4 = (f32[32,2,512]{2,0,1:T(8,128)}, f32[32,2,512]{2,0,1:T(8,128)}, u32[]{:S(2)}, u32[]{:S(2)}) collective-permute-start(f32[32,2,512]{2,0,1:T(8,128)} %get-tuple-element.37), channel_id=1, source_target_pairs={{4,0},{8,4},{12,8},{16,12},{20,16},{24,20},{28,24},{32,28},{36,32}... | collective-permute-start | bytes 393224 | tf_op jit(solution)/shard_map/ppermute | solution.py:18
  39.3 1.9 %fusion.7 = f32[32,16,514]{2,0,1:T(8,128)} fusion(f32[32,16,1]{2,0,1:T(8,128)S(1)} %copy.71, f32[32,16,512]{2,0,1:T(8,128)S(1)} %bitcast.118, f32[32,16,1]{2,0,1:T(8,128)S(1)} %copy-done.2, f32[32,16,2]{2,0,1:T(8,128)S(1)} %collective-permute-done.6, f32[32,16,512]{2,0,1:T(8,128)S(1)} %fusion.6, f32[32,16,2]{2,0,1:T(8,128)S(1)} %collective-permute-done.7, ...), kind=kLoop, calls=%fused_computation.13 | loop fusion | flops 2105344 | bytes 3195008 | tf_op jit(solution)/shard_map/mul | solution.py:52
  42.5 2.9 %fusion.11 = bf16[64,8,128]{2,1,0:T(8,128)(2,1)S(1)} fusion(bf16[1,1,64,256,128]{4,3,2,1,0:T(8,128)(2,1)} %param.23, bf16[64,8,256]{2,1,0:T(8,128)(2,1)S(1)} %gather_fusion, pred[64]{0:T(512)(128)(4,1)} %compare_and_fusion), kind=kOutput, calls=%fused_computation.20 | convolution fusion | flops 33751040 | bytes 4587584 | tf_op jit(solution)/shard_map/fpi,pio->pfo/dot_general | solution.py:120
  46.7 11.7 %all-to-all-start = ((f32[32,5,128]{2,1,0:T(8,128)}), f32[32,5,128]{2,1,0:T(8,128)S(1)}, u32[]{:S(2)}, u32[]{:S(2)}) async-start(f32[32,5,128]{2,1,0:T(8,128)} %pad_maximum_fusion.11), calls=%async_computation | async-start | bytes 262144 | tf_op jit(solution)/shard_map/all_to_all | solution.py:141
  58.6 1.4 %fusion.9 = f32[32,18,512]{2,0,1:T(8,128)S(1)} fusion(f32[32,1,512]{2,0,1:T(8,128)S(1)} %copy-done.5, f32[32,16,512]{2,0,1:T(8,128)S(1)} %bitcast.121, f32[32,1,512]{2,0,1:T(8,128)S(1)} %slice.238, f32[32,2,512]{2,0,1:T(8,128)} %collective-permute-done.4, f32[32,16,512]{2,0,1:T(8,128)S(1)} %fusion.6, f32[32,2,512]{2,0,1:T(8,128)} %collective-permute-done.5, ...), kind=kLoop, calls=%fused_computation.17 | loop fusion | flops 2359296 | bytes 3706880 | tf_op jit(solution)/shard_map/mul | solution.py:51
  60.0 1.9 %fusion.5 = f32[32,16,512]{2,0,1:T(8,128)S(1)} fusion(f32[32,16,512]{2,0,1:T(8,128)S(1)} %fusion.6, f32[32,16,514]{2,0,1:T(8,128)S(1)} %copy-done.1, f32[32,18,512]{2,0,1:T(8,128)S(1)} %fusion.9, f32[16,512]{1,0:T(8,128)S(1)} %bitcast.155, f32[1,32,32]{2,1,0:T(8,128)S(1)} %copy-done), kind=kOutput, calls=%fused_computation.9 | convolution fusion | flops 103546880 | bytes 11616256 | tf_op jit(solution)/shard_map/lm,mxy->lxy/dot_general | solution.py:23
  62.3 1.5 %collective-permute-start.9 = (f32[32,1,512]{2,0,1:T(8,128)S(1)}, f32[32,1,512]{2,0,1:T(8,128)S(1)}, u32[]{:S(2)}, u32[]{:S(2)}) collective-permute-start(f32[32,1,512]{2,0,1:T(8,128)S(1)} %get-tuple-element.33), channel_id=1, source_target_pairs={{0,4},{4,8},{8,12},{12,16},{16,20},{20,24},{24,28},{28,32},{32,36}... | collective-permute-start | bytes 196616 | tf_op jit(solution)/shard_map/ppermute | solution.py:17
  63.9 1.3 %collective-permute-start.10 = (f32[32,16,1]{2,0,1:T(8,128)S(1)}, f32[32,16,1]{2,0,1:T(8,128)S(1)}, u32[]{:S(2)}, u32[]{:S(2)}) collective-permute-start(f32[32,16,1]{2,0,1:T(8,128)S(1)} %get-tuple-element.34), channel_id=1, source_target_pairs={{1,0},{2,1},{3,2},{0,3},{5,4},{6,5},{7,6},{4,7},{9,8},{10,9},{11,1... | collective-permute-start | bytes 6152 | tf_op jit(solution)/shard_map/ppermute | solution.py:18
  65.3 1.0 %fusion.77 = (f32[1,8192]{1,0:T(1,128)S(1)}, f32[1,8192]{1,0:T(1,128)S(1)}) fusion(f32[4,8192]{1,0:T(4,128)} %collective-permute-done.12), kind=kLoop, calls=%fused_computation.138 | loop fusion | bytes 131072 | tf_op jit(solution)/shard_map/slice | solution.py:113
  66.4 3.1 %collective-permute-done.10 = f32[32,16,1]{2,0,1:T(8,128)S(1)} collective-permute-done((f32[32,16,1]{2,0,1:T(8,128)S(1)}, f32[32,16,1]{2,0,1:T(8,128)S(1)}, u32[]{:S(2)}, u32[]{:S(2)}) %collective-permute-start.10) | collective-permute-done | bytes 2080 | tf_op jit(solution)/shard_map/ppermute | solution.py:18
  69.4 2.2 %collective-permute-done.11 = f32[32,16,1]{2,0,1:T(8,128)S(1)} collective-permute-done((f32[32,16,1]{2,0,1:T(8,128)S(1)}, f32[32,16,1]{2,0,1:T(8,128)S(1)}, u32[]{:S(2)}, u32[]{:S(2)}) %collective-permute-start.11) | collective-permute-done | bytes 2080 | tf_op jit(solution)/shard_map/ppermute | solution.py:17
  71.6 1.1 %fusion.24 = (f32[1,32,16,512]{3,1,2,0:T(8,128)S(1)}, f32[1,32,16,512]{3,1,2,0:T(8,128)S(1)}) fusion(f32[32,16,512]{2,0,1:T(8,128)S(1)} %fusion.5, f32[32,1,512]{2,0,1:T(8,128)S(1)} %collective-permute-done.9, f32[32,1,512]{2,0,1:T(8,128)S(1)} %collective-permute-done.8, f32[32,18,512]{2,0,1:T(8,128)S(1)} %fusion.9, f32[16,512]{1,0:T(8,128)S(1)} %bitcast.135, ...), kind=kLoop, calls=%fused_computation.36 | loop fusion | flops 3145728 | bytes 5410816 | tf_op jit(solution)/shard_map/stack | solution.py:89
  73.1 0.8 convolution_convert_fusion
  73.9 10.7 %all-to-all-start.1 = ((bf16[32,4,128]{2,1,0:T(4,128)(2,1)}), bf16[32,4,128]{2,1,0:T(4,128)(2,1)S(1)}, u32[]{:S(2)}, u32[]{:S(2)}) async-start(bf16[32,4,128]{2,1,0:T(4,128)(2,1)} %bitcast.35), calls=%async_computation.1 | async-start | bytes 65536 | tf_op jit(solution)/shard_map/all_to_all | solution.py:156
  85.0 3.5 %copy.81 = f32[1,3,32,16,512]{4,3,2,1,0:T(8,128)} copy(f32[1,3,32,16,512]{4,2,3,1,0:T(8,128)S(1)} %maximum_bitcast_fusion) | data formatting | bytes 6291456
  88.5 4.3 %all-to-all-done.1 = bf16[32,4,128]{2,1,0:T(4,128)(2,1)S(1)} async-done(((bf16[32,4,128]{2,1,0:T(4,128)(2,1)}), bf16[32,4,128]{2,1,0:T(4,128)(2,1)S(1)}, u32[]{:S(2)}, u32[]{:S(2)}) %all-to-all-start.1) | async-done | bytes 32800 | tf_op jit(solution)/shard_map/all_to_all | solution.py:156
  93.0 3.4 %fusion.1 = f32[64,1,256]{2,1,0:T(1,128)S(1)} fusion(bf16[1,1,64,256,128]{4,3,2,1,0:T(8,128)(2,1)} %param.23, bf16[64,128,1]{1,0,2:T(8,128)(2,1)S(1)} %fusion.14), kind=kOutput, calls=%fused_computation.3 | convolution fusion | flops 4194304 | bytes 4276224 | tf_op jit(solution)/shard_map/pio,po->pi/dot_general | solution.py:164
  (137 shorter events, 14.0 us)
Async XLA Ops:
  0.6 23.4 %copy-start = (f32[1,32,32]{2,1,0:T(8,128)S(1)}, f32[1,32,32]{2,1,0:T(8,128)}, u32[]{:S(2)}) copy-start(f32[1,32,32]{2,1,0:T(8,128)} %param.16) | copy-start | bytes 12292
  2.2 9.0 %copy-start.10 = (f32[1,1,16,512]{3,1,2,0:T(1,128)}, f32[1,1,16,512]{3,1,2,0:T(1,128)S(1)}, u32[]{:S(2)}) copy-start(f32[1,1,16,512]{3,1,2,0:T(1,128)S(1)} %copy.95) | copy-start | bytes 98308
  3.1 8.2 %copy-start.12 = (f32[1,1,16,512]{3,1,2,0:T(1,128)}, f32[1,1,16,512]{3,1,2,0:T(1,128)S(1)}, u32[]{:S(2)}) copy-start(f32[1,1,16,512]{3,1,2,0:T(1,128)S(1)} %copy.92) | copy-start | bytes 98308
  3.2 8.1 %copy-start.14 = (f32[1,1,16,512]{3,1,2,0:T(1,128)}, f32[1,1,16,512]{3,1,2,0:T(1,128)S(1)}, u32[]{:S(2)}) copy-start(f32[1,1,16,512]{3,1,2,0:T(1,128)S(1)} %copy.94) | copy-start | bytes 98308
  3.2 8.1 %copy-start.16 = (f32[1,1,16,512]{3,1,2,0:T(1,128)}, f32[1,1,16,512]{3,1,2,0:T(1,128)S(1)}, u32[]{:S(2)}) copy-start(f32[1,1,16,512]{3,1,2,0:T(1,128)S(1)} %copy.93) | copy-start | bytes 98308
  4.1 37.0 %collective-permute-start.12 = (f32[4,8192]{1,0:T(4,128)}, f32[4,8192]{1,0:T(4,128)}, u32[]{:S(2)}, u32[]{:S(2)}) collective-permute-start(f32[4,8192]{1,0:T(4,128)} %maximum_select_fusion), channel_id=1, source_target_pairs={{0,128},{128,0},{1,129},{129,1},{2,130},{130,2},{3,131},{131,3},{4... | collective-permute-start | bytes 393224 | tf_op jit(solution)/shard_map/ppermute | solution.py:111
  12.3 9.1 %collective-permute-start.3 = (f32[33,16,1]{0,1,2:T(8,128)S(1)}, f32[33,16,1]{0,1,2:T(8,128)S(1)}, u32[]{:S(2)}, u32[]{:S(2)}) collective-permute-start(f32[33,16,1]{0,1,2:T(8,128)S(1)} %maximum_select_fusion.4), channel_id=1, source_target_pairs={{0,1},{1,2},{2,3},{3,0},{4,5},{5,6},{6,7},{7,4},{8,9},{9,10},{10,1... | collective-permute-start | bytes 6344 | tf_op jit(solution)/shard_map/ppermute | solution.py:17
  13.8 7.7 %collective-permute-start.2 = (f32[33,16,1]{0,1,2:T(8,128)S(1)}, f32[33,16,1]{0,1,2:T(8,128)S(1)}, u32[]{:S(2)}, u32[]{:S(2)}) collective-permute-start(f32[33,16,1]{0,1,2:T(8,128)S(1)} %maximum_select_fusion.3), channel_id=1, source_target_pairs={{1,0},{2,1},{3,2},{0,3},{5,4},{6,5},{7,6},{4,7},{9,8},{10,9},{11,1... | collective-permute-start | bytes 6344 | tf_op jit(solution)/shard_map/ppermute | solution.py:18
  15.3 3.3 %copy-start.31 = (s32[1,1,64,1]{2,3,1,0:T(1,128)S(1)}, s32[1,1,64,1]{2,3,1,0:T(1,128)}, u32[]{:S(2)}) copy-start(s32[1,1,64,1]{2,3,1,0:T(1,128)} %param.20) | copy-start | bytes 772
  15.3 4.8 %copy-start.3 = (f32[1,16,512]{2,1,0:T(8,128)S(1)}, f32[1,16,512]{2,1,0:T(8,128)}, u32[]{:S(2)}) copy-start(f32[1,16,512]{2,1,0:T(8,128)} %param.17) | copy-start | bytes 98308
  15.9 7.5 %collective-permute-start.1 = (f32[33,1,512]{2,0,1:T(8,128)S(1)}, f32[33,1,512]{2,0,1:T(8,128)S(1)}, u32[]{:S(2)}, u32[]{:S(2)}) collective-permute-start(f32[33,1,512]{2,0,1:T(8,128)S(1)} %maximum_select_fusion.2), channel_id=1, source_target_pairs={{0,4},{4,8},{8,12},{12,16},{16,20},{20,24},{24,28},{28,32},{32,36}... | collective-permute-start | bytes 202760 | tf_op jit(solution)/shard_map/ppermute | solution.py:17
  17.8 5.6 %collective-permute-start = (f32[33,1,512]{2,0,1:T(8,128)S(1)}, f32[33,1,512]{2,0,1:T(8,128)S(1)}, u32[]{:S(2)}, u32[]{:S(2)}) collective-permute-start(f32[33,1,512]{2,0,1:T(8,128)S(1)} %maximum_select_fusion.1), channel_id=1, source_target_pairs={{4,0},{8,4},{12,8},{16,12},{20,16},{24,20},{28,24},{32,28},{36,32}... | collective-permute-start | bytes 202760 | tf_op jit(solution)/shard_map/ppermute | solution.py:18
  23.4 5.1 %copy-start.4 = (f32[32,1,512]{2,0,1:T(8,128)}, f32[32,1,512]{2,0,1:T(8,128)S(1)}, u32[]{:S(2)}) copy-start(f32[32,1,512]{2,0,1:T(8,128)S(1)} %slice.235) | copy-start | bytes 196612
  28.6 10.6 %copy-start.2 = (f32[32,16,1]{2,0,1:T(8,128)S(1)}, f32[32,16,1]{2,0,1:T(8,128)}, u32[]{:S(2)}) copy-start(f32[32,16,1]{2,0,1:T(8,128)} %copy.74) | copy-start | bytes 6148
  28.6 10.6 %copy-start.7 = (f32[1,16,514]{2,1,0:T(8,128)S(1)}, f32[1,16,514]{2,1,0:T(8,128)}, u32[]{:S(2)}) copy-start(f32[1,16,514]{2,1,0:T(8,128)} %copy.121) | copy-start | bytes 98692
  29.5 9.7 %collective-permute-start.7 = (f32[32,16,2]{2,0,1:T(8,128)S(1)}, f32[32,16,2]{2,0,1:T(8,128)S(1)}, u32[]{:S(2)}, u32[]{:S(2)}) collective-permute-start(f32[32,16,2]{2,0,1:T(8,128)S(1)} %get-tuple-element.38), channel_id=1, source_target_pairs={{0,1},{1,2},{2,3},{3,0},{4,5},{5,6},{6,7},{7,4},{8,9},{9,10},{10,1... | collective-permute-start | bytes 12296 | tf_op jit(solution)/shard_map/ppermute | solution.py:17
  29.6 9.6 %collective-permute-start.6 = (f32[32,16,2]{2,0,1:T(8,128)S(1)}, f32[32,16,2]{2,0,1:T(8,128)S(1)}, u32[]{:S(2)}, u32[]{:S(2)}) collective-permute-start(f32[32,16,2]{2,0,1:T(8,128)S(1)} %get-tuple-element.39), channel_id=1, source_target_pairs={{1,0},{2,1},{3,2},{0,3},{5,4},{6,5},{7,6},{4,7},{9,8},{10,9},{11,1... | collective-permute-start | bytes 12296 | tf_op jit(solution)/shard_map/ppermute | solution.py:18
  34.3 24.2 %collective-permute-start.5 = (f32[32,2,512]{2,0,1:T(8,128)}, f32[32,2,512]{2,0,1:T(8,128)}, u32[]{:S(2)}, u32[]{:S(2)}) collective-permute-start(f32[32,2,512]{2,0,1:T(8,128)} %get-tuple-element.36), channel_id=1, source_target_pairs={{0,4},{4,8},{8,12},{12,16},{16,20},{20,24},{24,28},{28,32},{32,36}... | collective-permute-start | bytes 393224 | tf_op jit(solution)/shard_map/ppermute | solution.py:17
  36.6 21.9 %collective-permute-start.4 = (f32[32,2,512]{2,0,1:T(8,128)}, f32[32,2,512]{2,0,1:T(8,128)}, u32[]{:S(2)}, u32[]{:S(2)}) collective-permute-start(f32[32,2,512]{2,0,1:T(8,128)} %get-tuple-element.37), channel_id=1, source_target_pairs={{4,0},{8,4},{12,8},{16,12},{20,16},{24,20},{28,24},{32,28},{36,32}... | collective-permute-start | bytes 393224 | tf_op jit(solution)/shard_map/ppermute | solution.py:18
  42.5 3.6 %copy-start.19 = (f32[32,1,128]{2,0,1:T(8,128)S(1)}, f32[32,1,128]{2,0,1:T(8,128)}, u32[]{:S(2)}) copy-start(f32[32,1,128]{2,0,1:T(8,128)} %scatter.4) | copy-start | bytes 49156
  42.5 16.0 %copy-start.5 = (f32[32,1,512]{2,0,1:T(8,128)S(1)}, f32[32,1,512]{2,0,1:T(8,128)}, u32[]{:S(2)}) copy-start(f32[32,1,512]{2,0,1:T(8,128)} %copy-done.4) | copy-start | bytes 196612
  42.5 16.0 %copy-start.6 = (f32[1,18,512]{2,1,0:T(8,128)S(1)}, f32[1,18,512]{2,1,0:T(8,128)}, u32[]{:S(2)}) copy-start(f32[1,18,512]{2,1,0:T(8,128)} %copy.120) | copy-start | bytes 110596
  46.7 26.0 %all-to-all-start = ((f32[32,5,128]{2,1,0:T(8,128)}), f32[32,5,128]{2,1,0:T(8,128)S(1)}, u32[]{:S(2)}, u32[]{:S(2)}) async-start(f32[32,5,128]{2,1,0:T(8,128)} %pad_maximum_fusion.11), calls=%async_computation | async-start | bytes 262144 | tf_op jit(solution)/shard_map/all_to_all | solution.py:141
  61.8 9.8 %copy-start.8 = (f32[1,16,512]{2,1,0:T(8,128)S(1)}, f32[1,16,512]{2,1,0:T(8,128)}, u32[]{:S(2)}) copy-start(f32[1,16,512]{2,1,0:T(8,128)} %copy.122) | copy-start | bytes 98308
  62.0 9.6 %collective-permute-start.8 = (f32[32,1,512]{2,0,1:T(8,128)S(1)}, f32[32,1,512]{2,0,1:T(8,128)S(1)}, u32[]{:S(2)}, u32[]{:S(2)}) collective-permute-start(f32[32,1,512]{2,0,1:T(8,128)S(1)} %get-tuple-element.32), channel_id=1, source_target_pairs={{4,0},{8,4},{12,8},{16,12},{20,16},{24,20},{28,24},{32,28},{36,32}... | collective-permute-start | bytes 196616 | tf_op jit(solution)/shard_map/ppermute | solution.py:18
  62.3 9.3 %collective-permute-start.9 = (f32[32,1,512]{2,0,1:T(8,128)S(1)}, f32[32,1,512]{2,0,1:T(8,128)S(1)}, u32[]{:S(2)}, u32[]{:S(2)}) collective-permute-start(f32[32,1,512]{2,0,1:T(8,128)S(1)} %get-tuple-element.33), channel_id=1, source_target_pairs={{0,4},{4,8},{8,12},{12,16},{16,20},{20,24},{24,28},{28,32},{32,36}... | collective-permute-start | bytes 196616 | tf_op jit(solution)/shard_map/ppermute | solution.py:17
  63.9 5.6 %collective-permute-start.10 = (f32[32,16,1]{2,0,1:T(8,128)S(1)}, f32[32,16,1]{2,0,1:T(8,128)S(1)}, u32[]{:S(2)}, u32[]{:S(2)}) collective-permute-start(f32[32,16,1]{2,0,1:T(8,128)S(1)} %get-tuple-element.34), channel_id=1, source_target_pairs={{1,0},{2,1},{3,2},{0,3},{5,4},{6,5},{7,6},{4,7},{9,8},{10,9},{11,1... | collective-permute-start | bytes 6152 | tf_op jit(solution)/shard_map/ppermute | solution.py:18
  65.2 6.4 %collective-permute-start.11 = (f32[32,16,1]{2,0,1:T(8,128)S(1)}, f32[32,16,1]{2,0,1:T(8,128)S(1)}, u32[]{:S(2)}, u32[]{:S(2)}) collective-permute-start(f32[32,16,1]{2,0,1:T(8,128)S(1)} %get-tuple-element.35), channel_id=1, source_target_pairs={{0,1},{1,2},{2,3},{3,0},{4,5},{5,6},{6,7},{7,4},{8,9},{9,10},{10,1... | collective-permute-start | bytes 6152 | tf_op jit(solution)/shard_map/ppermute | solution.py:17
  73.9 18.8 %all-to-all-start.1 = ((bf16[32,4,128]{2,1,0:T(4,128)(2,1)}), bf16[32,4,128]{2,1,0:T(4,128)(2,1)S(1)}, u32[]{:S(2)}, u32[]{:S(2)}) async-start(bf16[32,4,128]{2,1,0:T(4,128)(2,1)} %bitcast.35), calls=%async_computation.1 | async-start | bytes 65536 | tf_op jit(solution)/shard_map/all_to_all | solution.py:156
  85.0 7.8 %copy-start.27 = (s32[64]{0:T(128)S(1)}, s32[64]{0:T(128)}, u32[]{:S(2)}) copy-start(s32[64]{0:T(128)} %copy-done.25) | copy-start | bytes 772
  93.0 3.4 %copy-start.24 = (s32[1,1,64]{2,1,0:T(1,128)S(1)}, s32[1,1,64]{2,1,0:T(1,128)}, u32[]{:S(2)}) copy-start(s32[1,1,64]{2,1,0:T(1,128)} %param.21) | copy-start | bytes 772
  93.0 3.6 %copy-start.9 = (s32[1,16,512]{2,1,0:T(8,128)S(1)}, s32[1,16,512]{2,1,0:T(8,128)}, u32[]{:S(2)}) copy-start(s32[1,16,512]{2,1,0:T(8,128)} %param.15) | copy-start | bytes 98308
  (15 other events, 30.2 us)

commit v14 on v13

--- a/solution.py
+++ b/solution.py
@@ -106,12 +106,10 @@
         [model_state[0, 0, 0].reshape(cell_count), model_state[0, 1, 0].reshape(cell_count),
          model_state[0, 2, 0].reshape(cell_count), own_st]
     )
-    zeros = jnp.zeros_like(own_st)
-    sent = jnp.where(is_atmos, drivers, jnp.stack([own_st, own_wet, zeros, zeros]))
-    got = lax.ppermute(sent, "sec", [(0, 1), (1, 0)])
-    atmos_drivers = jnp.where(is_atmos, drivers, got)
-    ocean_st = jnp.where(is_atmos, got[0], own_st)
-    ocean_wet = jnp.where(is_atmos, got[1], own_wet)
+    got = lax.ppermute(jnp.concatenate([drivers, own_wet[None]]), "sec", [(0, 1), (1, 0)])
+    atmos_drivers = jnp.where(is_atmos, drivers, got[:4])
+    ocean_st = jnp.where(is_atmos, got[3], own_st)
+    ocean_wet = jnp.where(is_atmos, got[4], own_wet)
 
     fluxes = jnp.tanh(jnp.dot(flux_coef, atmos_drivers, precision=HIGHEST_PRECISION)).astype(jnp.bfloat16)
     flux_count = fluxes.shape[0]

time: 98 us -> 98.8 us (level)
  no operation moved by 1% of the time
where the time goes in v14:
time: 98.8 us; the launch traced here: 98.1 us
  starting transfers between devices  41.8 us (42%)
  local copies, waits for them, and re-layouts  20.3 us (21%)
  matrix products  16 us (16%)
  waiting for transfers between devices  9.52 us (10%)
  other arithmetic  9.14 us (9%)
  between operations  1.31 us (1%)
    all_to_all x1, starting transfers between devices, local(): lax.all_to_all(packet, 'gx', split_axis=0, concat_axis=0, tiled=True)  11.7 us
    all_to_all x1, starting transfers between devices, local(): lax.all_to_all(returning.reshape(tile_count, capacity, out_width), 'gx',...  10.7 us
    unnamed x76, local copies, waits for them, and re-layouts  9.69 us
    ppermute x6, starting transfers between devices, neighbours(): hi = lax.ppermute(head, axis, [((i + 1) % count, i) for i in range(count)])  8.44 us
    ppermute x6, starting transfers between devices, neighbours(): lo = lax.ppermute(tail, axis, [(i, (i + 1) % count) for i in range(count)])  7.14 us
    dot_general x2, matrix products, vertical_mix(): jnp.einsum('lm,mxy->lxy', matrix, right_side, precision=HIGHEST_PRECISION)  6.34 us
    all_to_all x1, waiting for transfers between devices, local(): lax.all_to_all(returning.reshape(tile_count, capacity, out_width), 'gx',...  4.3 us
    ppermute x1, starting transfers between devices, local(): lax.ppermute(jnp.concatenate([drivers, own_wet[None]]), 'sec', [(0, 1), (...  3.74 us
  transfers between devices with their start and end apart: 15, of which 3 were waited for; matrix products, arithmetic and copies ran while one was open for 36% of the time, Pallas kernels for 0%

profile of v14, /device:TPU:1, one launch (start us, length us, event | category | flops | bytes accessed | tf_op | source)
XLA Modules:
  0.0 98.1 jit_solution(15406247555254509986)
XLA Ops:
  0.6 0.8 copy_convert_fusion
  1.4 0.8 copy.95
  2.3 0.8 slice_bitcast_fusion
  3.2 0.9 concatenate.125
  4.1 3.7 %collective-permute-start.12 = (f32[5,8192]{1,0:T(8,128)}, f32[5,8192]{1,0:T(8,128)}, u32[]{:S(2)}, u32[]{:S(2)}) collective-permute-start(f32[5,8192]{1,0:T(8,128)} %concatenate.125), channel_id=1, source_target_pairs={{0,128},{128,0},{1,129},{129,1},{2,130},{130,2},{3,131},{131,3},{4... | collective-permute-start | bytes 491528 | tf_op jit(solution)/shard_map/ppermute | solution.py:109
  8.0 3.2 %fusion.80 = (f32[1,1,32,16,512]{4,3,2,1,0:T(8,128)}, f32[1,1,32,16,512]{4,3,2,1,0:T(8,128)S(1)}, f32[1,1,32,16,512]{4,3,2,1,0:T(8,128)S(1)}) fusion(f32[1,3,32,16,512]{4,3,2,1,0:T(8,128)} %param.13), kind=kLoop, calls=%fused_computation.140 | loop fusion | bytes 6291456 | tf_op jit(solution)/shard_map/slice | solution.py:81
  12.2 1.2 %collective-permute-start.3 = (f32[33,16,1]{0,1,2:T(8,128)S(1)}, f32[33,16,1]{0,1,2:T(8,128)S(1)}, u32[]{:S(2)}, u32[]{:S(2)}) collective-permute-start(f32[33,16,1]{0,1,2:T(8,128)S(1)} %maximum_select_fusion.3), channel_id=1, source_target_pairs={{0,1},{1,2},{2,3},{3,0},{4,5},{5,6},{6,7},{7,4},{8,9},{9,10},{10,1... | collective-permute-start | bytes 6344 | tf_op jit(solution)/shard_map/ppermute | solution.py:17
  13.7 1.5 %collective-permute-start.2 = (f32[33,16,1]{0,1,2:T(8,128)S(1)}, f32[33,16,1]{0,1,2:T(8,128)S(1)}, u32[]{:S(2)}, u32[]{:S(2)}) collective-permute-start(f32[33,16,1]{0,1,2:T(8,128)S(1)} %maximum_select_fusion.2), channel_id=1, source_target_pairs={{1,0},{2,1},{3,2},{0,3},{5,4},{6,5},{7,6},{4,7},{9,8},{10,9},{11,1... | collective-permute-start | bytes 6344 | tf_op jit(solution)/shard_map/ppermute | solution.py:18
  15.9 1.9 %collective-permute-start.1 = (f32[33,1,512]{2,0,1:T(8,128)S(1)}, f32[33,1,512]{2,0,1:T(8,128)S(1)}, u32[]{:S(2)}, u32[]{:S(2)}) collective-permute-start(f32[33,1,512]{2,0,1:T(8,128)S(1)} %maximum_select_fusion.1), channel_id=1, source_target_pairs={{0,4},{4,8},{8,12},{12,16},{16,20},{20,24},{24,28},{28,32},{32,36}... | collective-permute-start | bytes 202760 | tf_op jit(solution)/shard_map/ppermute | solution.py:17
  22.4 0.9 copy.74
  24.0 4.5 %fusion.6 = f32[32,16,512]{2,0,1:T(8,128)S(1)} fusion(f32[32,16,512]{2,0,1:T(8,128)S(1)} %bitcast.117, f32[32,16,1]{2,0,1:T(8,128)} %copy.74, f32[32,16,1]{2,0,1:T(8,128)S(1)} %copy.71, f32[32,16,512]{2,0,1:T(8,128)S(1)} %bitcast.120, f32[32,1,512]{2,0,1:T(8,128)S(1)} %slice.242, f32[32,1,512]{2,0,1:T(8,128)S(1)} %slice.239, ...), kind=kOutput, calls=%fused_computation.11 | convolution fusion | flops 105644032 | bytes 4366336 | tf_op jit(solution)/shard_map/lm,mxy->lxy/dot_general | solution.py:23
  28.5 0.7 slice_select_fusion.6
  29.5 2.7 %collective-permute-start.6 = (f32[32,16,2]{2,0,1:T(8,128)S(1)}, f32[32,16,2]{2,0,1:T(8,128)S(1)}, u32[]{:S(2)}, u32[]{:S(2)}) collective-permute-start(f32[32,16,2]{2,0,1:T(8,128)S(1)} %get-tuple-element.39), channel_id=1, source_target_pairs={{1,0},{2,1},{3,2},{0,3},{5,4},{6,5},{7,6},{4,7},{9,8},{10,9},{11,1... | collective-permute-start | bytes 12296 | tf_op jit(solution)/shard_map/ppermute | solution.py:18
  34.2 2.3 %collective-permute-start.5 = (f32[32,2,512]{2,0,1:T(8,128)}, f32[32,2,512]{2,0,1:T(8,128)}, u32[]{:S(2)}, u32[]{:S(2)}) collective-permute-start(f32[32,2,512]{2,0,1:T(8,128)} %get-tuple-element.36), channel_id=1, source_target_pairs={{0,4},{4,8},{8,12},{12,16},{16,20},{20,24},{24,28},{28,32},{32,36}... | collective-permute-start | bytes 393224 | tf_op jit(solution)/shard_map/ppermute | solution.py:17
  36.5 2.6 %collective-permute-start.4 = (f32[32,2,512]{2,0,1:T(8,128)}, f32[32,2,512]{2,0,1:T(8,128)}, u32[]{:S(2)}, u32[]{:S(2)}) collective-permute-start(f32[32,2,512]{2,0,1:T(8,128)} %get-tuple-element.37), channel_id=1, source_target_pairs={{4,0},{8,4},{12,8},{16,12},{20,16},{24,20},{28,24},{32,28},{36,32}... | collective-permute-start | bytes 393224 | tf_op jit(solution)/shard_map/ppermute | solution.py:18
  39.1 1.9 %fusion.7 = f32[32,16,514]{2,0,1:T(8,128)} fusion(f32[32,16,1]{2,0,1:T(8,128)S(1)} %copy.71, f32[32,16,512]{2,0,1:T(8,128)S(1)} %bitcast.118, f32[32,16,1]{2,0,1:T(8,128)S(1)} %copy-done.2, f32[32,16,2]{2,0,1:T(8,128)S(1)} %collective-permute-done.6, f32[32,16,512]{2,0,1:T(8,128)S(1)} %fusion.6, f32[32,16,2]{2,0,1:T(8,128)S(1)} %collective-permute-done.7, ...), kind=kLoop, calls=%fused_computation.13 | loop fusion | flops 2105344 | bytes 3195008 | tf_op jit(solution)/shard_map/mul | solution.py:52
  41.1 1.5 %fusion = bf16[8192,8]{0,1:T(8,128)(2,1)S(1)} fusion(f32[8,4]{0,1:T(4,128)S(1)} %copy-done.29, f32[5,8192]{1,0:T(8,128)} %collective-permute-done.12, f32[1,8192]{1,0:T(1,128)S(1)} %bitcast.138, f32[1,8192]{1,0:T(1,128)S(1)} %bitcast.140, f32[1,8192]{1,0:T(1,128)S(1)} %bitcast.144, f32[1,8192]{1,0:T(1,128)S(1)} %bitcast.142, pred[]{:T(512)S(6)} %eq.28), kind=kOutput, calls=%fused_computation.2 | convolution fusion | flops 3342336 | bytes 393345 | tf_op jit(solution)/shard_map/dot_general | solution.py:114
  43.3 2.9 %fusion.11 = bf16[64,8,128]{2,1,0:T(8,128)(2,1)S(1)} fusion(bf16[1,1,64,256,128]{4,3,2,1,0:T(8,128)(2,1)} %param.23, bf16[64,8,256]{2,1,0:T(8,128)(2,1)S(1)} %gather_fusion, pred[64]{0:T(512)(128)(4,1)} %compare_and_fusion), kind=kOutput, calls=%fused_computation.20 | convolution fusion | flops 33751040 | bytes 4587584 | tf_op jit(solution)/shard_map/fpi,pio->pfo/dot_general | solution.py:118
  47.6 11.7 %all-to-all-start = ((f32[32,5,128]{2,1,0:T(8,128)}), f32[32,5,128]{2,1,0:T(8,128)S(1)}, u32[]{:S(2)}, u32[]{:S(2)}) async-start(f32[32,5,128]{2,1,0:T(8,128)} %pad_maximum_fusion.10), calls=%async_computation | async-start | bytes 262144 | tf_op jit(solution)/shard_map/all_to_all | solution.py:139
  59.4 1.4 %fusion.9 = f32[32,18,512]{2,0,1:T(8,128)S(1)} fusion(f32[32,1,512]{2,0,1:T(8,128)S(1)} %copy-done.5, f32[32,16,512]{2,0,1:T(8,128)S(1)} %bitcast.121, f32[32,1,512]{2,0,1:T(8,128)S(1)} %slice.242, f32[32,2,512]{2,0,1:T(8,128)} %collective-permute-done.4, f32[32,16,512]{2,0,1:T(8,128)S(1)} %fusion.6, f32[32,2,512]{2,0,1:T(8,128)} %collective-permute-done.5, ...), kind=kLoop, calls=%fused_computation.17 | loop fusion | flops 2359296 | bytes 3706880 | tf_op jit(solution)/shard_map/mul | solution.py:51
  60.8 1.9 %fusion.5 = f32[32,16,512]{2,0,1:T(8,128)S(1)} fusion(f32[32,16,512]{2,0,1:T(8,128)S(1)} %fusion.6, f32[32,16,514]{2,0,1:T(8,128)S(1)} %copy-done.1, f32[32,18,512]{2,0,1:T(8,128)S(1)} %fusion.9, f32[16,512]{1,0:T(8,128)S(1)} %bitcast.155, f32[1,32,32]{2,1,0:T(8,128)S(1)} %copy-done), kind=kOutput, calls=%fused_computation.9 | convolution fusion | flops 103546880 | bytes 11616256 | tf_op jit(solution)/shard_map/lm,mxy->lxy/dot_general | solution.py:23
  63.2 1.5 %collective-permute-start.9 = (f32[32,1,512]{2,0,1:T(8,128)S(1)}, f32[32,1,512]{2,0,1:T(8,128)S(1)}, u32[]{:S(2)}, u32[]{:S(2)}) collective-permute-start(f32[32,1,512]{2,0,1:T(8,128)S(1)} %get-tuple-element.33), channel_id=1, source_target_pairs={{0,4},{4,8},{8,12},{12,16},{16,20},{20,24},{24,28},{28,32},{32,36}... | collective-permute-start | bytes 196616 | tf_op jit(solution)/shard_map/ppermute | solution.py:17
  64.7 1.3 %collective-permute-start.10 = (f32[32,16,1]{2,0,1:T(8,128)S(1)}, f32[32,16,1]{2,0,1:T(8,128)S(1)}, u32[]{:S(2)}, u32[]{:S(2)}) collective-permute-start(f32[32,16,1]{2,0,1:T(8,128)S(1)} %get-tuple-element.34), channel_id=1, source_target_pairs={{1,0},{2,1},{3,2},{0,3},{5,4},{6,5},{7,6},{4,7},{9,8},{10,9},{11,1... | collective-permute-start | bytes 6152 | tf_op jit(solution)/shard_map/ppermute | solution.py:18
  66.1 1.1 %fusion.83 = (f32[1,8192]{1,0:T(1,128)S(1)}, f32[1,8192]{1,0:T(1,128)S(1)}) fusion(f32[5,8192]{1,0:T(8,128)} %collective-permute-done.12), kind=kLoop, calls=%fused_computation.143 | loop fusion | bytes 131072 | tf_op jit(solution)/shard_map/slice | solution.py:111
  67.2 3.0 %collective-permute-done.10 = f32[32,16,1]{2,0,1:T(8,128)S(1)} collective-permute-done((f32[32,16,1]{2,0,1:T(8,128)S(1)}, f32[32,16,1]{2,0,1:T(8,128)S(1)}, u32[]{:S(2)}, u32[]{:S(2)}) %collective-permute-start.10) | collective-permute-done | bytes 2080 | tf_op jit(solution)/shard_map/ppermute | solution.py:18
  70.2 2.2 %collective-permute-done.11 = f32[32,16,1]{2,0,1:T(8,128)S(1)} collective-permute-done((f32[32,16,1]{2,0,1:T(8,128)S(1)}, f32[32,16,1]{2,0,1:T(8,128)S(1)}, u32[]{:S(2)}, u32[]{:S(2)}) %collective-permute-start.11) | collective-permute-done | bytes 2080 | tf_op jit(solution)/shard_map/ppermute | solution.py:17
  72.4 1.1 %fusion.24 = (f32[1,32,16,512]{3,1,2,0:T(8,128)S(1)}, f32[1,32,16,512]{3,1,2,0:T(8,128)S(1)}) fusion(f32[32,16,512]{2,0,1:T(8,128)S(1)} %fusion.5, f32[32,1,512]{2,0,1:T(8,128)S(1)} %collective-permute-done.9, f32[32,1,512]{2,0,1:T(8,128)S(1)} %collective-permute-done.8, f32[32,18,512]{2,0,1:T(8,128)S(1)} %fusion.9, f32[16,512]{1,0:T(8,128)S(1)} %bitcast.135, ...), kind=kLoop, calls=%fused_computation.36 | loop fusion | flops 3145728 | bytes 5410816 | tf_op jit(solution)/shard_map/stack | solution.py:89
  73.9 0.8 convolution_convert_fusion
  74.7 10.7 %all-to-all-start.1 = ((bf16[32,4,128]{2,1,0:T(4,128)(2,1)}), bf16[32,4,128]{2,1,0:T(4,128)(2,1)S(1)}, u32[]{:S(2)}, u32[]{:S(2)}) async-start(bf16[32,4,128]{2,1,0:T(4,128)(2,1)} %bitcast.35), calls=%async_computation.1 | async-start | bytes 65536 | tf_op jit(solution)/shard_map/all_to_all | solution.py:154
  85.8 3.5 %copy.81 = f32[1,3,32,16,512]{4,3,2,1,0:T(8,128)} copy(f32[1,3,32,16,512]{4,2,3,1,0:T(8,128)S(1)} %maximum_bitcast_fusion) | data formatting | bytes 6291456
  89.3 4.3 %all-to-all-done.1 = bf16[32,4,128]{2,1,0:T(4,128)(2,1)S(1)} async-done(((bf16[32,4,128]{2,1,0:T(4,128)(2,1)}), bf16[32,4,128]{2,1,0:T(4,128)(2,1)S(1)}, u32[]{:S(2)}, u32[]{:S(2)}) %all-to-all-start.1) | async-done | bytes 32800 | tf_op jit(solution)/shard_map/all_to_all | solution.py:154
  93.8 3.4 %fusion.1 = f32[64,1,256]{2,1,0:T(1,128)S(1)} fusion(bf16[1,1,64,256,128]{4,3,2,1,0:T(8,128)(2,1)} %param.23, bf16[64,128,1]{1,0,2:T(8,128)(2,1)S(1)} %fusion.14), kind=kOutput, calls=%fused_computation.3 | convolution fusion | flops 4194304 | bytes 4276224 | tf_op jit(solution)/shard_map/pio,po->pi/dot_general | solution.py:162
  (135 shorter events, 14.1 us)
Async XLA Ops:
  0.6 23.3 %copy-start = (f32[1,32,32]{2,1,0:T(8,128)S(1)}, f32[1,32,32]{2,1,0:T(8,128)}, u32[]{:S(2)}) copy-start(f32[1,32,32]{2,1,0:T(8,128)} %param.16) | copy-start | bytes 12292
  2.2 9.0 %copy-start.11 = (f32[1,1,16,512]{3,1,2,0:T(1,128)}, f32[1,1,16,512]{3,1,2,0:T(1,128)S(1)}, u32[]{:S(2)}) copy-start(f32[1,1,16,512]{3,1,2,0:T(1,128)S(1)} %copy.95) | copy-start | bytes 98308
  3.1 8.1 %copy-start.13 = (f32[1,1,16,512]{3,1,2,0:T(1,128)}, f32[1,1,16,512]{3,1,2,0:T(1,128)S(1)}, u32[]{:S(2)}) copy-start(f32[1,1,16,512]{3,1,2,0:T(1,128)S(1)} %copy.94) | copy-start | bytes 98308
  3.2 8.1 %copy-start.15 = (f32[1,1,16,512]{3,1,2,0:T(1,128)}, f32[1,1,16,512]{3,1,2,0:T(1,128)S(1)}, u32[]{:S(2)}) copy-start(f32[1,1,16,512]{3,1,2,0:T(1,128)S(1)} %copy.92) | copy-start | bytes 98308
  3.2 8.0 %copy-start.17 = (f32[1,1,16,512]{3,1,2,0:T(1,128)}, f32[1,1,16,512]{3,1,2,0:T(1,128)S(1)}, u32[]{:S(2)}) copy-start(f32[1,1,16,512]{3,1,2,0:T(1,128)S(1)} %copy.93) | copy-start | bytes 98308
  4.1 36.9 %collective-permute-start.12 = (f32[5,8192]{1,0:T(8,128)}, f32[5,8192]{1,0:T(8,128)}, u32[]{:S(2)}, u32[]{:S(2)}) collective-permute-start(f32[5,8192]{1,0:T(8,128)} %concatenate.125), channel_id=1, source_target_pairs={{0,128},{128,0},{1,129},{129,1},{2,130},{130,2},{3,131},{131,3},{4... | collective-permute-start | bytes 491528 | tf_op jit(solution)/shard_map/ppermute | solution.py:109
  12.2 9.0 %collective-permute-start.3 = (f32[33,16,1]{0,1,2:T(8,128)S(1)}, f32[33,16,1]{0,1,2:T(8,128)S(1)}, u32[]{:S(2)}, u32[]{:S(2)}) collective-permute-start(f32[33,16,1]{0,1,2:T(8,128)S(1)} %maximum_select_fusion.3), channel_id=1, source_target_pairs={{0,1},{1,2},{2,3},{3,0},{4,5},{5,6},{6,7},{7,4},{8,9},{9,10},{10,1... | collective-permute-start | bytes 6344 | tf_op jit(solution)/shard_map/ppermute | solution.py:17
  13.7 7.7 %collective-permute-start.2 = (f32[33,16,1]{0,1,2:T(8,128)S(1)}, f32[33,16,1]{0,1,2:T(8,128)S(1)}, u32[]{:S(2)}, u32[]{:S(2)}) collective-permute-start(f32[33,16,1]{0,1,2:T(8,128)S(1)} %maximum_select_fusion.2), channel_id=1, source_target_pairs={{1,0},{2,1},{3,2},{0,3},{5,4},{6,5},{7,6},{4,7},{9,8},{10,9},{11,1... | collective-permute-start | bytes 6344 | tf_op jit(solution)/shard_map/ppermute | solution.py:18
  15.2 4.7 %copy-start.3 = (f32[1,16,512]{2,1,0:T(8,128)S(1)}, f32[1,16,512]{2,1,0:T(8,128)}, u32[]{:S(2)}) copy-start(f32[1,16,512]{2,1,0:T(8,128)} %param.17) | copy-start | bytes 98308
  15.9 7.4 %collective-permute-start.1 = (f32[33,1,512]{2,0,1:T(8,128)S(1)}, f32[33,1,512]{2,0,1:T(8,128)S(1)}, u32[]{:S(2)}, u32[]{:S(2)}) collective-permute-start(f32[33,1,512]{2,0,1:T(8,128)S(1)} %maximum_select_fusion.1), channel_id=1, source_target_pairs={{0,4},{4,8},{8,12},{12,16},{16,20},{20,24},{24,28},{28,32},{32,36}... | collective-permute-start | bytes 202760 | tf_op jit(solution)/shard_map/ppermute | solution.py:17
  17.8 5.5 %collective-permute-start = (f32[33,1,512]{2,0,1:T(8,128)S(1)}, f32[33,1,512]{2,0,1:T(8,128)S(1)}, u32[]{:S(2)}, u32[]{:S(2)}) collective-permute-start(f32[33,1,512]{2,0,1:T(8,128)S(1)} %maximum_select_fusion), channel_id=1, source_target_pairs={{4,0},{8,4},{12,8},{16,12},{20,16},{24,20},{28,24},{32,28},{36,32}... | collective-permute-start | bytes 202760 | tf_op jit(solution)/shard_map/ppermute | solution.py:18
  23.3 5.1 %copy-start.4 = (f32[32,1,512]{2,0,1:T(8,128)}, f32[32,1,512]{2,0,1:T(8,128)S(1)}, u32[]{:S(2)}) copy-start(f32[32,1,512]{2,0,1:T(8,128)S(1)} %slice.239) | copy-start | bytes 196612
  28.5 10.6 %copy-start.2 = (f32[32,16,1]{2,0,1:T(8,128)S(1)}, f32[32,16,1]{2,0,1:T(8,128)}, u32[]{:S(2)}) copy-start(f32[32,16,1]{2,0,1:T(8,128)} %copy.74) | copy-start | bytes 6148
  28.5 10.6 %copy-start.7 = (f32[1,16,514]{2,1,0:T(8,128)S(1)}, f32[1,16,514]{2,1,0:T(8,128)}, u32[]{:S(2)}) copy-start(f32[1,16,514]{2,1,0:T(8,128)} %copy.121) | copy-start | bytes 98692
  29.4 9.7 %collective-permute-start.7 = (f32[32,16,2]{2,0,1:T(8,128)S(1)}, f32[32,16,2]{2,0,1:T(8,128)S(1)}, u32[]{:S(2)}, u32[]{:S(2)}) collective-permute-start(f32[32,16,2]{2,0,1:T(8,128)S(1)} %get-tuple-element.38), channel_id=1, source_target_pairs={{0,1},{1,2},{2,3},{3,0},{4,5},{5,6},{6,7},{7,4},{8,9},{9,10},{10,1... | collective-permute-start | bytes 12296 | tf_op jit(solution)/shard_map/ppermute | solution.py:17
  29.5 9.6 %collective-permute-start.6 = (f32[32,16,2]{2,0,1:T(8,128)S(1)}, f32[32,16,2]{2,0,1:T(8,128)S(1)}, u32[]{:S(2)}, u32[]{:S(2)}) collective-permute-start(f32[32,16,2]{2,0,1:T(8,128)S(1)} %get-tuple-element.39), channel_id=1, source_target_pairs={{1,0},{2,1},{3,2},{0,3},{5,4},{6,5},{7,6},{4,7},{9,8},{10,9},{11,1... | collective-permute-start | bytes 12296 | tf_op jit(solution)/shard_map/ppermute | solution.py:18
  34.2 25.1 %collective-permute-start.5 = (f32[32,2,512]{2,0,1:T(8,128)}, f32[32,2,512]{2,0,1:T(8,128)}, u32[]{:S(2)}, u32[]{:S(2)}) collective-permute-start(f32[32,2,512]{2,0,1:T(8,128)} %get-tuple-element.36), channel_id=1, source_target_pairs={{0,4},{4,8},{8,12},{12,16},{16,20},{20,24},{24,28},{28,32},{32,36}... | collective-permute-start | bytes 393224 | tf_op jit(solution)/shard_map/ppermute | solution.py:17
  36.5 22.8 %collective-permute-start.4 = (f32[32,2,512]{2,0,1:T(8,128)}, f32[32,2,512]{2,0,1:T(8,128)}, u32[]{:S(2)}, u32[]{:S(2)}) collective-permute-start(f32[32,2,512]{2,0,1:T(8,128)} %get-tuple-element.37), channel_id=1, source_target_pairs={{4,0},{8,4},{12,8},{16,12},{20,16},{24,20},{28,24},{32,28},{36,32}... | collective-permute-start | bytes 393224 | tf_op jit(solution)/shard_map/ppermute | solution.py:18
  43.3 3.3 %copy-start.26 = (s32[64]{0:T(128)S(1)}, s32[64]{0:T(128)}, u32[]{:S(2)}) copy-start(s32[64]{0:T(128)} %copy-done.25) | copy-start | bytes 772
  43.3 3.6 %copy-start.19 = (f32[32,1,128]{2,0,1:T(8,128)S(1)}, f32[32,1,128]{2,0,1:T(8,128)}, u32[]{:S(2)}) copy-start(f32[32,1,128]{2,0,1:T(8,128)} %scatter.4) | copy-start | bytes 49156
  43.3 16.0 %copy-start.5 = (f32[32,1,512]{2,0,1:T(8,128)S(1)}, f32[32,1,512]{2,0,1:T(8,128)}, u32[]{:S(2)}) copy-start(f32[32,1,512]{2,0,1:T(8,128)} %copy-done.4) | copy-start | bytes 196612
  43.3 16.0 %copy-start.6 = (f32[1,18,512]{2,1,0:T(8,128)S(1)}, f32[1,18,512]{2,1,0:T(8,128)}, u32[]{:S(2)}) copy-start(f32[1,18,512]{2,1,0:T(8,128)} %copy.120) | copy-start | bytes 110596
  47.6 26.0 %all-to-all-start = ((f32[32,5,128]{2,1,0:T(8,128)}), f32[32,5,128]{2,1,0:T(8,128)S(1)}, u32[]{:S(2)}, u32[]{:S(2)}) async-start(f32[32,5,128]{2,1,0:T(8,128)} %pad_maximum_fusion.10), calls=%async_computation | async-start | bytes 262144 | tf_op jit(solution)/shard_map/all_to_all | solution.py:139
  62.7 9.8 %copy-start.8 = (f32[1,16,512]{2,1,0:T(8,128)S(1)}, f32[1,16,512]{2,1,0:T(8,128)}, u32[]{:S(2)}) copy-start(f32[1,16,512]{2,1,0:T(8,128)} %copy.122) | copy-start | bytes 98308
  62.8 9.6 %collective-permute-start.8 = (f32[32,1,512]{2,0,1:T(8,128)S(1)}, f32[32,1,512]{2,0,1:T(8,128)S(1)}, u32[]{:S(2)}, u32[]{:S(2)}) collective-permute-start(f32[32,1,512]{2,0,1:T(8,128)S(1)} %get-tuple-element.32), channel_id=1, source_target_pairs={{4,0},{8,4},{12,8},{16,12},{20,16},{24,20},{28,24},{32,28},{36,32}... | collective-permute-start | bytes 196616 | tf_op jit(solution)/shard_map/ppermute | solution.py:18
  63.2 9.3 %collective-permute-start.9 = (f32[32,1,512]{2,0,1:T(8,128)S(1)}, f32[32,1,512]{2,0,1:T(8,128)S(1)}, u32[]{:S(2)}, u32[]{:S(2)}) collective-permute-start(f32[32,1,512]{2,0,1:T(8,128)S(1)} %get-tuple-element.33), channel_id=1, source_target_pairs={{0,4},{4,8},{8,12},{12,16},{16,20},{20,24},{24,28},{28,32},{32,36}... | collective-permute-start | bytes 196616 | tf_op jit(solution)/shard_map/ppermute | solution.py:17
  64.7 5.6 %collective-permute-start.10 = (f32[32,16,1]{2,0,1:T(8,128)S(1)}, f32[32,16,1]{2,0,1:T(8,128)S(1)}, u32[]{:S(2)}, u32[]{:S(2)}) collective-permute-start(f32[32,16,1]{2,0,1:T(8,128)S(1)} %get-tuple-element.34), channel_id=1, source_target_pairs={{1,0},{2,1},{3,2},{0,3},{5,4},{6,5},{7,6},{4,7},{9,8},{10,9},{11,1... | collective-permute-start | bytes 6152 | tf_op jit(solution)/shard_map/ppermute | solution.py:18
  66.0 6.4 %collective-permute-start.11 = (f32[32,16,1]{2,0,1:T(8,128)S(1)}, f32[32,16,1]{2,0,1:T(8,128)S(1)}, u32[]{:S(2)}, u32[]{:S(2)}) collective-permute-start(f32[32,16,1]{2,0,1:T(8,128)S(1)} %get-tuple-element.35), channel_id=1, source_target_pairs={{0,1},{1,2},{2,3},{3,0},{4,5},{5,6},{6,7},{7,4},{8,9},{9,10},{10,1... | collective-permute-start | bytes 6152 | tf_op jit(solution)/shard_map/ppermute | solution.py:17
  74.7 18.8 %all-to-all-start.1 = ((bf16[32,4,128]{2,1,0:T(4,128)(2,1)}), bf16[32,4,128]{2,1,0:T(4,128)(2,1)S(1)}, u32[]{:S(2)}, u32[]{:S(2)}) async-start(bf16[32,4,128]{2,1,0:T(4,128)(2,1)} %bitcast.35), calls=%async_computation.1 | async-start | bytes 65536 | tf_op jit(solution)/shard_map/all_to_all | solution.py:154
  85.8 7.8 %copy-start.27 = (s32[64]{0:T(128)S(1)}, s32[64]{0:T(128)}, u32[]{:S(2)}) copy-start(s32[64]{0:T(128)} %copy-done.25) | copy-start | bytes 772
  93.8 3.4 %copy-start.24 = (s32[1,1,64]{2,1,0:T(1,128)S(1)}, s32[1,1,64]{2,1,0:T(1,128)}, u32[]{:S(2)}) copy-start(s32[1,1,64]{2,1,0:T(1,128)} %param.21) | copy-start | bytes 772
  93.8 3.6 %copy-start.9 = (s32[1,16,512]{2,1,0:T(8,128)S(1)}, s32[1,16,512]{2,1,0:T(8,128)}, u32[]{:S(2)}) copy-start(s32[1,16,512]{2,1,0:T(8,128)} %param.15) | copy-start | bytes 98308
  (15 other events, 30.1 us)
